TPU v7x, 32 devices: a whole 2x2x4 slice. The times are simulated.
32 devices in a mesh: walk: 4 (over x, core), chol: 8 (over z, y).
Axes of the slice: x: 2, y: 2, z: 4, core: 2. Of those that a mesh axis runs over, the one named last changes fastest.
Arguments:
- old_walkers: bfloat16 [96, 2048, 128], P(('walk', 'chol'))
- half_chol: bfloat16 [16, 128, 2048], P('chol'), may hold values from -0.1875 to 0.1875
- parent: int32 [192], P(('walk', 'chol')), may hold values from -1 to 11, as said below
- field: float32 [192, 2048], P(('walk', 'chol')), may hold values from -0.8 to 0.8
Outputs:
- new_walkers: bfloat16 [192, 2048, 128], P(('walk', 'chol'))
- energy: float32 [192], P(('walk', 'chol'))
Inputs may be any that keep to these rules, and one draw needn't show every extreme that they name: `parent`: the 4 devices that share an index of chol form a column. On each device the live slots (value >= 0) come first among its 6 slots, the rest hold -1. Each column has exactly 12 live slots, every device of it at least one, and some device of it has all 6 slots live. A live value m names the walker that the column's walk index m // 3 holds as its local walker m % 3.
All inputs are finite; a program needn't handle non-finite values.
Results may differ from a plain program's by a relative error of at most 0.0062.
Values may be sent and summed in bfloat16 or wider, within the bound.
No kernel may reach another device: no remote copies, remote signals or barrier semaphores. Data moves between devices by JAX's collectives and lax.ppermute only.
A program may use at most 192 MiB of HBM per device.

v0:
```python
import jax
import jax.numpy as jnp
from jax import lax
from jax.sharding import PartitionSpec as P

ITERS = 3


def green_half(walkers):
    widened = walkers.astype(jnp.float32)
    electrons = walkers.shape[2]
    intersection = widened[:, :electrons, :]
    identity = jnp.eye(electrons, dtype=jnp.float32)
    diagonal = jnp.diagonal(intersection, axis1=1, axis2=2)
    inverse = identity[None, :, :] / diagonal[:, None, :]
    for sweep in range(ITERS):
        product = jnp.einsum("wij,wjk->wik", intersection, inverse, precision=lax.Precision.HIGHEST)
        inverse = jnp.einsum(
            "wij,wjk->wik",
            inverse,
            2.0 * identity[None, :, :] - product,
            precision=lax.Precision.HIGHEST,
        )
    theta = jnp.einsum("wnk,wkj->wnj", widened, inverse, precision=lax.Precision.HIGHEST)
    return theta.astype(jnp.bfloat16)


def block_energy(theta, vectors):
    blocks = jnp.einsum("gin,wnj->wgij", vectors, theta, preferred_element_type=jnp.float32)
    traces = jnp.einsum("wgii->wg", blocks)
    crossed = jnp.sum(blocks * jnp.swapaxes(blocks, 2, 3), axis=(2, 3))
    return 0.5 * jnp.sum(traces * traces - crossed, axis=1)


def body(old_walkers, half_chol, parent, field):
    slot_dev = parent.shape[0]
    column = lax.all_gather(old_walkers, "walk", axis=0, tiled=True)
    living = parent >= 0
    source = jnp.maximum(parent, 0)
    kicked = (jnp.exp(field)[:, :, None] * column[source].astype(jnp.float32)).astype(jnp.bfloat16)
    new_walkers = jnp.where(living[:, None, None], kicked, jnp.zeros_like(kicked))
    theta = green_half(kicked)
    energy = jnp.zeros((slot_dev,), jnp.float32) + block_energy(
        theta, lax.all_gather(half_chol, "chol", axis=0, tiled=True)
    )
    energy = jnp.where(living, energy, 0.0)
    return (new_walkers, energy)


def solution(mesh):
    return jax.shard_map(
        body,
        mesh=mesh,
        in_specs=(
            P(("walk", "chol"), None, None),
            P("chol", None, None),
            P(("walk", "chol")),
            P(("walk", "chol"), None),
        ),
        out_specs=(P(("walk", "chol"), None, None), P(("walk", "chol"))),
        check_vma=False,
    )
```

profile of v0, /device:TPU:0, one launch (start us, length us, event | category | flops | bytes accessed | tf_op | source)
XLA Modules:
  0.0 217.5 jit_solution(15850261391445615935)
XLA Ops:
  7.2 0.7 all-gather.3.cloned.1.call-update
  7.9 0.7 all-gather.5.cloned.1.call-update
  8.6 0.9 exp.3
  9.5 0.7 broadcast_maximum_fusion
  10.2 0.6 iota_compare_fusion.1
  10.8 0.6 fusion.15
  11.4 0.7 fusion.16
  12.1 0.7 broadcast_compare_fusion
  12.7 45.9 %all-gather.3.cloned.1.call-done = bf16[12,2048,128]{2,1,0:T(8,128)(2,1)} async-done(((bf16[3,2048,128]{2,1,0:T(8,128)(2,1)}), bf16[12,2048,128]{2,1,0:T(8,128)(2,1)}) %all-gather.3.cloned.1.call-update) | async-done | bytes 6291472 | tf_op jit(solution)/shard_map/all_gather | solution.py:37
  58.7 5.5 %gather_fusion = bf16[6,2048,128]{2,1,0:T(8,128)(2,1)} fusion(bf16[12,2048,128]{2,1,0:T(8,128)(2,1)} %all-gather.3.cloned.1.call-done, s32[1024]{0:T(1024)S(1)} %pad_clamp_fusion), kind=kCustom, calls=%fused_computation | custom fusion | bytes 6291480 | tf_op jit(solution)/shard_map/gather | solution.py:40
  64.2 5.1 %broadcast_select_fusion = (bf16[6,2048,128]{2,1,0:T(8,128)(2,1)}, bf16[6,2048,128]{2,1,0:T(8,128)(2,1)S(1)}) fusion(pred[6]{0:T(512)(128)(4,1)S(1)} %broadcast_compare_fusion, bf16[6,2048,128]{2,1,0:T(8,128)(2,1)} %gather_fusion, f32[6,2048]{1,0:T(8,128)S(1)} %exp.3), kind=kLoop, calls=%fused_computation.11 | loop fusion | flops 6291456 | bytes 9486342 | tf_op jit(solution)/shard_map/jit(_where)/select_n | solution.py:41
  69.3 4.7 %copy.17 = f32[6,128,128]{0,2,1:T(8,128)} copy(f32[6,128,128]{2,1,0:T(8,128)S(1)} %slice_convert_fusion) | data formatting | bytes 786432 | tf_op jit(solution)/shard_map/slice | solution.py:12
  74.0 1.8 gather_fusion.1
  75.8 1.3 convolution_subtract_fusion.2
  77.1 1.4 fusion.5
  78.5 0.3 convolution_subtract_fusion.1
  78.9 0.5 fusion.17
  79.7 0.5 fusion.18
  80.3 4.0 %convolution_convert_fusion = bf16[6,2048,128]{2,1,0:T(8,128)(2,1)} fusion(bf16[6,2048,128]{2,1,0:T(8,128)(2,1)S(1)} %get-tuple-element.7, f32[6,128,128]{2,1,0:T(8,128)S(1)} %fusion.18), kind=kOutput, calls=%fused_computation.9 | convolution fusion | flops 2417491968 | bytes 6684672 | tf_op jit(solution)/shard_map/wnk,wkj->wnj/dot_general | solution.py:24
  84.2 101.5 %all-gather.5.cloned.1.call-done = bf16[16,128,2048]{2,1,0:T(8,128)(2,1)} async-done(((bf16[2,128,2048]{2,1,0:T(8,128)(2,1)}), bf16[16,128,2048]{2,1,0:T(8,128)(2,1)}) %all-gather.5.cloned.1.call-update) | async-done | bytes 8388624 | tf_op jit(solution)/shard_map/all_gather | solution.py:44
  185.8 11.7 %fusion = f32[6,128,16,128]{3,1,2,0:T(8,128)} fusion(bf16[16,128,2048]{2,1,0:T(8,128)(2,1)} %all-gather.5.cloned.1.call-done, bf16[6,2048,128]{2,1,0:T(8,128)(2,1)} %convolution_convert_fusion), kind=kOutput, calls=%fused_computation.2 | convolution fusion | flops 6442450944 | bytes 17825792 | tf_op jit(solution)/shard_map/gin,wnj->wgij/dot_general | solution.py:29
  197.5 6.6 %copy.20 = f32[6,128,16,128]{1,3,2,0:T(8,128)} copy(f32[6,128,16,128]{3,1,2,0:T(8,128)} %fusion) | data formatting | bytes 12582912 | tf_op jit(solution)/shard_map/gin,wnj->wgij/dot_general | solution.py:29
  204.1 5.9 %fusion.3 = (f32[6,16]{1,0:T(8,128)S(1)}, f32[6,16]{1,0:T(8,128)S(1)}) fusion(f32[6,128,16,128]{1,3,2,0:T(8,128)} %copy.20, pred[128,128]{1,0:T(8,128)(4,1)S(1)} %copy-done.1, f32[6,128,16,128]{3,1,2,0:T(8,128)} %fusion), kind=kLoop, calls=%fused_computation.7 | loop fusion | flops 6291264 | bytes 12600064 | tf_op jit(solution)/shard_map/wgii->wg/reduce_sum | solution.py:30
  210.1 0.5 multiply_select_fusion
  (14 shorter events, 0.6 us)
Async XLA Ops:
  7.2 51.5 %all-gather.3.cloned.1.call-start = ((), (), s32[]{:S(2)}) async-start(), calls=%async_computation | async-start | bytes 7864320 | tf_op jit(solution)/shard_map/all_gather | solution.py:37
  7.9 177.9 %all-gather.5.cloned.1.call-start = ((), (), s32[]{:S(2)}) async-start(), calls=%async_computation.1 | async-start | bytes 9437184 | tf_op jit(solution)/shard_map/all_gather | solution.py:44
  74.0 4.5 %copy-start = (f32[128,128]{1,0:T(8,128)S(1)}, f32[128,128]{1,0:T(8,128)}, u32[]{:S(2)}) copy-start(f32[128,128]{1,0:T(8,128)} %fusion.15) | copy-start | bytes 196612
  197.5 6.6 %copy-start.1 = (pred[128,128]{1,0:T(8,128)(4,1)S(1)}, pred[128,128]{1,0:T(8,128)(4,1)}, u32[]{:S(2)}) copy-start(pred[128,128]{1,0:T(8,128)(4,1)} %iota_compare_fusion.1) | copy-start | bytes 49156
  204.1 6.0 %copy-start.2 = (s32[6]{0:T(128)S(1)}, s32[6]{0:T(128)}, u32[]{:S(2)}) copy-start(s32[6]{0:T(128)} %param.6) | copy-start | bytes 76
Sparse Core Ops, SparseCore 0:
  9.6 49.0 all-gather.2
  60.8 124.9 all-gather.4
where the time goes:
time: 218 us; the launch traced here: 217 us
  waiting for transfers between devices  149 us (68%)
  matrix products  20.1 us (9%)
  local copies, waits for them, and re-layouts  19.5 us (9%)
  other arithmetic  14.8 us (7%)
  between operations  14.1 us (6%)
    all_gather x1, waiting for transfers between devices, body(): lax.all_gather(half_chol, 'chol', axis=0, tiled=True)  102 us
    all_gather x1, waiting for transfers between devices, body(): column = lax.all_gather(old_walkers, 'walk', axis=0, tiled=True)  45.9 us
    dot_general x1, matrix products, block_energy(): jnp.einsum('gin,wnj->wgij', vectors, theta, preferred_element_type=jnp.fl...  11.7 us
    dot_general x1, local copies, waits for them, and re-layouts, block_energy(): jnp.einsum('gin,wnj->wgij', vectors, theta, preferred_element_type=jnp.fl...  6.6 us
    reduce_sum x1, other arithmetic, block_energy(): traces = jnp.einsum('wgii->wg', blocks)  5.87 us
    gather x1, local copies, waits for them, and re-layouts, body(): column[source].astype(jnp.float32)  5.5 us
    select_n x1, other arithmetic, body(): jnp.where(living[:, None, None], kicked, jnp.zeros_like(kicked))  5.09 us
    slice x1, local copies, waits for them, and re-layouts, green_half(): intersection = widened[:, :electrons, :]  4.72 us
  transfers between devices with their start and end apart: 2, of which 2 were waited for; matrix products, arithmetic and copies ran while one was open for 14% of the time, Pallas kernels for 0%

commit v1 on v0

--- a/solution.py
+++ b/solution.py
@@ -32,17 +32,37 @@
     return 0.5 * jnp.sum(traces * traces - crossed, axis=1)
 
 
+def swap_pairs(x, axis, size, bit):
+    perm = [(i, i ^ bit) for i in range(size)]
+    return lax.ppermute(x, axis, perm)
+
+
 def body(old_walkers, half_chol, parent, field):
+    n_walk = lax.axis_size("walk")
+    old_dev = old_walkers.shape[0]
     slot_dev = parent.shape[0]
-    column = lax.all_gather(old_walkers, "walk", axis=0, tiled=True)
+    walk_id = lax.axis_index("walk")
+    core = walk_id % 2
+
+    local_g = half_chol.shape[0]
+    half_g = local_g // 2
+    mine = lax.dynamic_slice_in_dim(half_chol, core * half_g, half_g, axis=0)
+    gathered = lax.all_gather(mine, "chol", axis=0, tiled=True)
+    other = swap_pairs(gathered, "walk", n_walk, 1)
+
+    across = swap_pairs(old_walkers, "walk", n_walk, 2)
+    beside = swap_pairs(old_walkers, "walk", n_walk, 1)
+    diagonal_peer = swap_pairs(across, "walk", n_walk, 1)
+    column = jnp.concatenate([old_walkers, beside, across, diagonal_peer], axis=0)
+
     living = parent >= 0
     source = jnp.maximum(parent, 0)
-    kicked = (jnp.exp(field)[:, :, None] * column[source].astype(jnp.float32)).astype(jnp.bfloat16)
+    relative = (source // old_dev) ^ walk_id
+    index = relative * old_dev + source % old_dev
+    kicked = (jnp.exp(field)[:, :, None] * column[index].astype(jnp.float32)).astype(jnp.bfloat16)
     new_walkers = jnp.where(living[:, None, None], kicked, jnp.zeros_like(kicked))
     theta = green_half(kicked)
-    energy = jnp.zeros((slot_dev,), jnp.float32) + block_energy(
-        theta, lax.all_gather(half_chol, "chol", axis=0, tiled=True)
-    )
+    energy = block_energy(theta, gathered) + block_energy(theta, other)
     energy = jnp.where(living, energy, 0.0)
     return (new_walkers, energy)
 

time: 218 us -> 154 us (0.71)
  waiting for transfers between devices: 149 us -> 72.3 us
  local copies, waits for them, and re-layouts: 19.5 us -> 25.4 us
  other arithmetic: 14.8 us -> 18.9 us
  starting transfers between devices: 0.08 us -> 3.05 us
    all_gather x2 -> x1, waiting for transfers between devices: 147 us -> 37.7 us  [body(): gathered = lax.all_gather(mine, 'chol', axis=0, tiled=True)]
    ppermute x0 -> x4, waiting for transfers between devices: none -> 34.6 us  [swap_pairs(): return lax.ppermute(x, axis, perm)]
    concatenate x0 -> x1, other arithmetic: none -> 5.84 us  [body(): jnp.concatenate([old_walkers, beside, across, diagonal_peer], axis=0)]
    unnamed x6 -> x12, local copies, waits for them, and re-layouts: 0.01 us -> 4.49 us
    ppermute x0 -> x4, starting transfers between devices: none -> 3.01 us  [swap_pairs(): return lax.ppermute(x, axis, perm)]
    dot_general x1 -> x2, matrix products: 11.7 us -> 12.5 us  [block_energy(): jnp.einsum('gin,wnj->wgij', vectors, theta, preferred_element_type=jnp.fl...]
    dot_general x1 -> x2, local copies, waits for them, and re-layouts: 6.6 us -> 7.09 us  [block_energy(): jnp.einsum('gin,wnj->wgij', vectors, theta, preferred_element_type=jnp.fl...]
  transfers between devices with their start and end apart: 2 -> 5, of which waited for: 2 -> 2; matrix products, arithmetic and copies ran while one was open for 14% -> 27% of each run, Pallas kernels for 0% -> 0%
where the time goes in v1:
time: 154 us
  waiting for transfers between devices  72.3 us (47%)
  local copies, waits for them, and re-layouts  25.4 us (16%)
  matrix products  20 us (13%)
  other arithmetic  18.9 us (12%)
  between operations  14.2 us (9%)
  starting transfers between devices  3.05 us (2%)
    all_gather x1, waiting for transfers between devices, body(): gathered = lax.all_gather(mine, 'chol', axis=0, tiled=True)  37.7 us
    ppermute x4, waiting for transfers between devices, swap_pairs(): return lax.ppermute(x, axis, perm)  34.6 us
    dot_general x2, matrix products, block_energy(): jnp.einsum('gin,wnj->wgij', vectors, theta, preferred_element_type=jnp.fl...  12.5 us
    dot_general x2, local copies, waits for them, and re-layouts, block_energy(): jnp.einsum('gin,wnj->wgij', vectors, theta, preferred_element_type=jnp.fl...  7.09 us
    reduce_sum x1, other arithmetic, block_energy(): traces = jnp.einsum('wgii->wg', blocks)  5.93 us
    concatenate x1, other arithmetic, body(): jnp.concatenate([old_walkers, beside, across, diagonal_peer], axis=0)  5.84 us
    gather x1, local copies, waits for them, and re-layouts, body(): column[index].astype(jnp.float32)  5.5 us
    select_n x1, other arithmetic, body(): jnp.where(living[:, None, None], kicked, jnp.zeros_like(kicked))  5.05 us
  transfers between devices with their start and end apart: 5, of which 2 were waited for; matrix products, arithmetic and copies ran while one was open for 27% of the time, Pallas kernels for 0%

profile of v1, /device:TPU:0, one launch (start us, length us, event | category | flops | bytes accessed | tf_op | source)
XLA Modules:
  0.0 153.8 jit_solution(10622074899993358610)
XLA Ops:
  7.2 1.2 copy-done
  8.4 0.8 constant_dynamic-slice_fusion
  9.3 3.0 %collective-permute-start.1 = (bf16[3,2048,128]{2,1,0:T(8,128)(2,1)}, bf16[3,2048,128]{2,1,0:T(8,128)(2,1)S(1)}, u32[]{:S(2)}, u32[]{:S(2)}) collective-permute-start(bf16[3,2048,128]{2,1,0:T(8,128)(2,1)} %param.4), channel_id=1, source_target_pairs={{0,16},{8,24},{16,0},{24,8},{1,17},{9,25},{17,1},{25,9},{2,18},{10... | collective-permute-start | bytes 4718600 | tf_op jit(solution)/shard_map/ppermute | solution.py:37
  12.3 34.6 %collective-permute-done.1 = bf16[3,2048,128]{2,1,0:T(8,128)(2,1)S(1)} collective-permute-done((bf16[3,2048,128]{2,1,0:T(8,128)(2,1)}, bf16[3,2048,128]{2,1,0:T(8,128)(2,1)S(1)}, u32[]{:S(2)}, u32[]{:S(2)}) %collective-permute-start.1) | collective-permute-done | bytes 1572896 | tf_op jit(solution)/shard_map/ppermute | solution.py:37
  46.9 0.9 exp.3
  47.8 0.7 compare_select_fusion
  48.5 0.7 broadcast_compare_fusion
  49.2 37.7 %all-gather.2.cloned.1.call-done = bf16[8,128,2048]{2,1,0:T(8,128)(2,1)} async-done(((bf16[1,128,2048]{2,1,0:T(8,128)(2,1)}), bf16[8,128,2048]{2,1,0:T(8,128)(2,1)}) %all-gather.2.cloned.1.call-update) | async-done | bytes 4194320 | tf_op jit(solution)/shard_map/all_gather | solution.py:50
  86.9 5.8 %pad_maximum_fusion = bf16[12,2048,128]{2,1,0:T(8,128)(2,1)} fusion(bf16[3,2048,128]{2,1,0:T(8,128)(2,1)} %collective-permute-done.2, bf16[3,2048,128]{2,1,0:T(8,128)(2,1)S(1)} %collective-permute-done.1, bf16[3,2048,128]{2,1,0:T(8,128)(2,1)} %collective-permute-done, bf16[3,2048,128]{2,1,0:T(8,128)(2,1)} %param.4), kind=kLoop, calls=%fused_computation.2 | loop fusion | flops 9437184 | bytes 12582912 | tf_op jit(solution)/shard_map/concatenate | solution.py:56
  92.7 5.5 %gather_fusion = bf16[6,2048,128]{2,1,0:T(8,128)(2,1)} fusion(bf16[12,2048,128]{2,1,0:T(8,128)(2,1)} %pad_maximum_fusion, s32[1024]{0:T(1024)S(1)} %pad_clamp_fusion), kind=kCustom, calls=%fused_computation | custom fusion | bytes 6291480 | tf_op jit(solution)/shard_map/gather | solution.py:62
  98.2 5.1 %broadcast_select_fusion = (bf16[6,2048,128]{2,1,0:T(8,128)(2,1)}, bf16[6,2048,128]{2,1,0:T(8,128)(2,1)S(1)}) fusion(pred[6]{0:T(512)(128)(4,1)S(1)} %broadcast_compare_fusion, bf16[6,2048,128]{2,1,0:T(8,128)(2,1)} %gather_fusion, f32[6,2048]{1,0:T(8,128)S(1)} %exp.3), kind=kLoop, calls=%fused_computation.19 | loop fusion | flops 6291456 | bytes 9486342 | tf_op jit(solution)/shard_map/jit(_where)/select_n | solution.py:63
  103.3 1.7 %copy-done.1 = bf16[6,2048,128]{2,1,0:T(8,128)(2,1)} copy-done((bf16[6,2048,128]{2,1,0:T(8,128)(2,1)}, bf16[6,2048,128]{2,1,0:T(8,128)(2,1)S(1)}, u32[]{:S(2)}) %copy-start.1) | copy-done | bytes 3145752
  104.9 4.7 %copy.26 = f32[6,128,128]{0,2,1:T(8,128)} copy(f32[6,128,128]{2,1,0:T(8,128)S(1)} %slice_convert_fusion) | data formatting | bytes 786432 | tf_op jit(solution)/shard_map/slice | solution.py:12
  109.7 1.8 %gather_fusion.1 = f32[128,6]{1,0:T(8,128)S(1)} fusion(f32[6,128,128]{0,2,1:T(8,128)} %copy.26, s32[128]{0:T(128)S(1)} %or_bitcast_fusion), kind=kCustom, calls=%fused_computation.1 | custom fusion | bytes 7168 | tf_op jit(solution)/shard_map/jit(diagonal)/gather | solution.py:14
  111.5 1.5 convolution_subtract_fusion.2
  113.0 0.5 fusion.10
  113.5 1.3 convolution_subtract_fusion.1
  116.3 2.8 %convolution_convert_fusion = bf16[6,2048,128]{2,1,0:T(8,128)(2,1)S(1)} fusion(bf16[6,2048,128]{2,1,0:T(8,128)(2,1)S(1)} %copy-done.2, f32[6,128,128]{2,1,0:T(8,128)S(1)} %fusion.24), kind=kOutput, calls=%fused_computation.8 | convolution fusion | flops 2417491968 | bytes 6684672 | tf_op jit(solution)/shard_map/wnk,wkj->wnj/dot_general | solution.py:24
  119.1 1.7 %copy-done.3 = bf16[6,2048,128]{2,1,0:T(8,128)(2,1)} copy-done((bf16[6,2048,128]{2,1,0:T(8,128)(2,1)}, bf16[6,2048,128]{2,1,0:T(8,128)(2,1)S(1)}, u32[]{:S(2)}) %copy-start.3) | copy-done | bytes 3145752
  120.7 5.1 %fusion.2 = f32[6,128,8,128]{3,1,2,0:T(8,128)} fusion(bf16[8,128,2048]{2,1,0:T(8,128)(2,1)S(1)} %copy-done.5, bf16[6,2048,128]{2,1,0:T(8,128)(2,1)S(1)} %convolution_convert_fusion), kind=kOutput, calls=%fused_computation.6 | convolution fusion | flops 3221225472 | bytes 10485760 | tf_op jit(solution)/shard_map/gin,wnj->wgij/dot_general | solution.py:29
  125.9 3.6 %copy.29 = f32[6,128,8,128]{1,3,2,0:T(8,128)} copy(f32[6,128,8,128]{3,1,2,0:T(8,128)} %fusion.2) | data formatting | bytes 6291456 | tf_op jit(solution)/shard_map/gin,wnj->wgij/dot_general | solution.py:29
  129.5 7.4 %fusion = f32[6,128,8,128]{3,1,2,0:T(8,128)} fusion(bf16[8,128,2048]{2,1,0:T(8,128)(2,1)} %collective-permute-done.3, bf16[6,2048,128]{2,1,0:T(8,128)(2,1)} %copy-done.3), kind=kOutput, calls=%fused_computation.4 | convolution fusion | flops 3221225472 | bytes 10485760 | tf_op jit(solution)/shard_map/gin,wnj->wgij/dot_general | solution.py:29
  136.9 3.5 %copy.31 = f32[6,128,8,128]{1,3,2,0:T(8,128)} copy(f32[6,128,8,128]{3,1,2,0:T(8,128)} %fusion) | data formatting | bytes 6291456 | tf_op jit(solution)/shard_map/gin,wnj->wgij/dot_general | solution.py:29
  140.4 5.9 %fusion.7 = (f32[6,8]{1,0:T(8,128)S(1)}, f32[6,8]{1,0:T(8,128)S(1)}, f32[6,8]{1,0:T(8,128)S(1)}, f32[6,8]{1,0:T(8,128)S(1)}) fusion(f32[6,128,8,128]{1,3,2,0:T(8,128)} %copy.31, pred[128,128]{1,0:T(8,128)(4,1)S(1)} %iota_compare_fusion.1, f32[6,128,8,128]{3,1,2,0:T(8,128)} %fusion, f32[6,128,8,128]{3,1,2,0:T(8,128)} %fusion.2, f32[6,128,8,128]{1,3,2,0:T(8,128)} %copy.29), kind=kLoop, calls=%fused_computation.14 | loop fusion | flops 6291264 | bytes 12600064 | tf_op jit(solution)/shard_map/wgii->wg/reduce_sum | solution.py:30
  (29 shorter events, 2.3 us)
Async XLA Ops:
  7.2 1.2 copy-start
  7.2 79.7 %all-gather.2.cloned.1.call-start = ((), (), s32[]{:S(2)}) async-start(), calls=%async_computation | async-start | bytes 4718592 | tf_op jit(solution)/shard_map/all_gather | solution.py:50
  9.3 37.6 %collective-permute-start.1 = (bf16[3,2048,128]{2,1,0:T(8,128)(2,1)}, bf16[3,2048,128]{2,1,0:T(8,128)(2,1)S(1)}, u32[]{:S(2)}, u32[]{:S(2)}) collective-permute-start(bf16[3,2048,128]{2,1,0:T(8,128)(2,1)} %param.4), channel_id=1, source_target_pairs={{0,16},{8,24},{16,0},{24,8},{1,17},{9,25},{17,1},{25,9},{2,18},{10... | collective-permute-start | bytes 4718600 | tf_op jit(solution)/shard_map/ppermute | solution.py:37
  12.3 74.6 %collective-permute-start = (bf16[3,2048,128]{2,1,0:T(8,128)(2,1)}, bf16[3,2048,128]{2,1,0:T(8,128)(2,1)}, u32[]{:S(2)}, u32[]{:S(2)}) collective-permute-start(bf16[3,2048,128]{2,1,0:T(8,128)(2,1)} %param.4), channel_id=1, source_target_pairs={{0,8},{8,0},{16,24},{24,16},{1,9},{9,1},{17,25},{25,17},{2,10},{10... | collective-permute-start | bytes 4718600 | tf_op jit(solution)/shard_map/ppermute | solution.py:37
  46.9 40.0 %collective-permute-start.2 = (bf16[3,2048,128]{2,1,0:T(8,128)(2,1)S(1)}, bf16[3,2048,128]{2,1,0:T(8,128)(2,1)}, u32[]{:S(2)}, u32[]{:S(2)}) collective-permute-start(bf16[3,2048,128]{2,1,0:T(8,128)(2,1)S(1)} %collective-permute-done.1), channel_id=1, source_target_pairs={{0,8},{8,0},{16,24},{24,16},{1,9},{9,1},{17,25},{25,17},{2,10},{10... | collective-permute-start | bytes 4718600 | tf_op jit(solution)/shard_map/ppermute | solution.py:37
  86.8 42.6 %collective-permute-start.3 = (bf16[8,128,2048]{2,1,0:T(8,128)(2,1)}, bf16[8,128,2048]{2,1,0:T(8,128)(2,1)}, u32[]{:S(2)}, u32[]{:S(2)}) collective-permute-start(bf16[8,128,2048]{2,1,0:T(8,128)(2,1)} %all-gather.2.cloned.1.call-done), channel_id=1, source_target_pairs={{0,8},{8,0},{16,24},{24,16},{1,9},{9,1},{17,25},{25,17},{2,10},{10... | collective-permute-start | bytes 12582920 | tf_op jit(solution)/shard_map/ppermute | solution.py:37
  103.2 1.7 %copy-start.1 = (bf16[6,2048,128]{2,1,0:T(8,128)(2,1)}, bf16[6,2048,128]{2,1,0:T(8,128)(2,1)S(1)}, u32[]{:S(2)}) copy-start(bf16[6,2048,128]{2,1,0:T(8,128)(2,1)S(1)} %get-tuple-element.11) | copy-start | bytes 9437188
  111.5 3.9 %copy-start.2 = (bf16[6,2048,128]{2,1,0:T(8,128)(2,1)S(1)}, bf16[6,2048,128]{2,1,0:T(8,128)(2,1)}, u32[]{:S(2)}) copy-start(bf16[6,2048,128]{2,1,0:T(8,128)(2,1)} %copy-done.1) | copy-start | bytes 9437188
  116.3 4.5 %copy-start.5 = (bf16[8,128,2048]{2,1,0:T(8,128)(2,1)S(1)}, bf16[8,128,2048]{2,1,0:T(8,128)(2,1)}, u32[]{:S(2)}) copy-start(bf16[8,128,2048]{2,1,0:T(8,128)(2,1)} %all-gather.2.cloned.1.call-done) | copy-start | bytes 12582916
  119.1 1.7 %copy-start.3 = (bf16[6,2048,128]{2,1,0:T(8,128)(2,1)}, bf16[6,2048,128]{2,1,0:T(8,128)(2,1)S(1)}, u32[]{:S(2)}) copy-start(bf16[6,2048,128]{2,1,0:T(8,128)(2,1)S(1)} %convolution_convert_fusion) | copy-start | bytes 9437188
  140.4 6.1 %copy-start.4 = (s32[6]{0:T(128)S(1)}, s32[6]{0:T(128)}, u32[]{:S(2)}) copy-start(s32[6]{0:T(128)} %param.6) | copy-start | bytes 76
Sparse Core Ops, SparseCore 0:
  10.7 76.0 all-gather.1

commit v2 on v1

--- a/solution.py
+++ b/solution.py
@@ -47,8 +47,22 @@
     local_g = half_chol.shape[0]
     half_g = local_g // 2
     mine = lax.dynamic_slice_in_dim(half_chol, core * half_g, half_g, axis=0)
-    gathered = lax.all_gather(mine, "chol", axis=0, tiled=True)
-    other = swap_pairs(gathered, "walk", n_walk, 1)
+    n_chol = lax.axis_size("chol")
+    order = list(range(0, n_chol, 2)) + list(range(n_chol - 1, 0, -2))
+    forward = [(order[i], order[(i + 1) % n_chol]) for i in range(n_chol)]
+    backward = [(b, a) for a, b in forward]
+    n_forward = n_chol // 2
+    pieces = []
+    current = mine
+    for step in range(n_forward):
+        current = lax.ppermute(current, "chol", forward)
+        pieces.append(current)
+    current = mine
+    for step in range(n_chol - 1 - n_forward):
+        current = lax.ppermute(current, "chol", backward)
+        pieces.append(current)
+    handed = [swap_pairs(piece, "walk", n_walk, 1) for piece in pieces]
+    vectors = jnp.concatenate([half_chol] + pieces + handed, axis=0)
 
     across = swap_pairs(old_walkers, "walk", n_walk, 2)
     beside = swap_pairs(old_walkers, "walk", n_walk, 1)
@@ -62,7 +76,7 @@
     kicked = (jnp.exp(field)[:, :, None] * column[index].astype(jnp.float32)).astype(jnp.bfloat16)
     new_walkers = jnp.where(living[:, None, None], kicked, jnp.zeros_like(kicked))
     theta = green_half(kicked)
-    energy = block_energy(theta, gathered) + block_energy(theta, other)
+    energy = block_energy(theta, vectors)
     energy = jnp.where(living, energy, 0.0)
     return (new_walkers, energy)
 

time: 154 us -> 128 us (0.83)
  waiting for transfers between devices: 72.3 us -> 50.3 us
  between operations: 14.2 us -> 0.91 us
  starting transfers between devices: 3.05 us -> 12.7 us
    ppermute x0 -> x7, waiting for transfers between devices: none -> 44.9 us  [the longest x4 30.8 us: body(): current = lax.ppermute(current, 'chol', forward)]
    all_gather x1 -> x0, waiting for transfers between devices: 37.7 us -> none  [body(): gathered = lax.all_gather(mine, 'chol', axis=0, tiled=True)]
    ppermute x4 -> x10, waiting for transfers between devices: 34.6 us -> 5.41 us  [swap_pairs(): return lax.ppermute(x, axis, perm)]
    ppermute x0 -> x7, starting transfers between devices: none -> 9.8 us  [the longest x4 7.73 us: body(): current = lax.ppermute(current, 'chol', forward)]
    concatenate x1, other arithmetic: 5.84 us -> 3.22 us  [body(): jnp.concatenate([old_walkers, beside, across, diagonal_peer], axis=0)]
    dot_general x2 -> x1, matrix products: 12.5 us -> 10.9 us  [block_energy(): jnp.einsum('gin,wnj->wgij', vectors, theta, preferred_element_type=jnp.fl...]
    unnamed x12 -> x22, local copies, waits for them, and re-layouts: 4.49 us -> 5.01 us
    dot_general x2 -> x1, local copies, waits for them, and re-layouts: 7.09 us -> 6.59 us  [block_energy(): jnp.einsum('gin,wnj->wgij', vectors, theta, preferred_element_type=jnp.fl...]
  transfers between devices with their start and end apart: 5 -> 17, of which waited for: 2 -> 11; matrix products, arithmetic and copies ran while one was open for 27% -> 5% of each run, Pallas kernels for 0% -> 0%
where the time goes in v2:
time: 128 us; the launch traced here: 127 us
  waiting for transfers between devices  50.3 us (39%)
  local copies, waits for them, and re-layouts  25.6 us (20%)
  matrix products  19.8 us (15%)
  other arithmetic  18 us (14%)
  starting transfers between devices  12.7 us (10%)
    ppermute x4, waiting for transfers between devices, body(): current = lax.ppermute(current, 'chol', forward)  30.8 us
    ppermute x3, waiting for transfers between devices, body(): current = lax.ppermute(current, 'chol', backward)  14 us
    dot_general x1, matrix products, block_energy(): jnp.einsum('gin,wnj->wgij', vectors, theta, preferred_element_type=jnp.fl...  10.9 us
    ppermute x4, starting transfers between devices, body(): current = lax.ppermute(current, 'chol', forward)  7.73 us
    dot_general x1, local copies, waits for them, and re-layouts, block_energy(): jnp.einsum('gin,wnj->wgij', vectors, theta, preferred_element_type=jnp.fl...  6.59 us
    reduce_sum x1, other arithmetic, block_energy(): traces = jnp.einsum('wgii->wg', blocks)  5.87 us
    gather x1, local copies, waits for them, and re-layouts, body(): column[index].astype(jnp.float32)  5.5 us
    ppermute x10, waiting for transfers between devices, swap_pairs(): return lax.ppermute(x, axis, perm)  5.41 us
  transfers between devices with their start and end apart: 17, of which 11 were waited for; matrix products, arithmetic and copies ran while one was open for 5% of the time, Pallas kernels for 0%

profile of v2, /device:TPU:0, one launch (start us, length us, event | category | flops | bytes accessed | tf_op | source)
XLA Modules:
  0.0 127.3 jit_solution(16564653508642874843)
XLA Ops:
  1.7 3.1 %collective-permute-start.3 = (bf16[1,128,2048]{2,1,0:T(8,128)(2,1)S(1)}, bf16[1,128,2048]{2,1,0:T(8,128)(2,1)S(1)}, u32[]{:S(2)}, u32[]{:S(2)}) collective-permute-start(bf16[1,128,2048]{2,1,0:T(8,128)(2,1)S(1)} %constant_dynamic-slice_fusion), channel_id=1, source_target_pairs={{0,2},{2,4},{4,6},{6,7},{7,5},{5,3},{3,1},{1,0},{8,10},{10,12},{12... | collective-permute-start | bytes 1572872 | tf_op jit(solution)/shard_map/ppermute | solution.py:58
  4.8 1.5 %collective-permute-start.1 = (bf16[3,2048,128]{2,1,0:T(8,128)(2,1)}, bf16[3,2048,128]{2,1,0:T(8,128)(2,1)S(1)}, u32[]{:S(2)}, u32[]{:S(2)}) collective-permute-start(bf16[3,2048,128]{2,1,0:T(8,128)(2,1)} %param.4), channel_id=1, source_target_pairs={{0,16},{8,24},{16,0},{24,8},{1,17},{9,25},{17,1},{25,9},{2,18},{10... | collective-permute-start | bytes 4718600 | tf_op jit(solution)/shard_map/ppermute | solution.py:37
  7.4 9.3 %collective-permute-done.3 = bf16[1,128,2048]{2,1,0:T(8,128)(2,1)S(1)} collective-permute-done((bf16[1,128,2048]{2,1,0:T(8,128)(2,1)S(1)}, bf16[1,128,2048]{2,1,0:T(8,128)(2,1)S(1)}, u32[]{:S(2)}, u32[]{:S(2)}) %collective-permute-start.3) | collective-permute-done | bytes 524320 | tf_op jit(solution)/shard_map/ppermute | solution.py:58
  16.7 1.8 %collective-permute-start.4 = (bf16[1,128,2048]{2,1,0:T(8,128)(2,1)S(1)}, bf16[1,128,2048]{2,1,0:T(8,128)(2,1)S(1)}, u32[]{:S(2)}, u32[]{:S(2)}) collective-permute-start(bf16[1,128,2048]{2,1,0:T(8,128)(2,1)S(1)} %collective-permute-done.3), channel_id=1, source_target_pairs={{0,2},{2,4},{4,6},{6,7},{7,5},{5,3},{3,1},{1,0},{8,10},{10,12},{12... | collective-permute-start | bytes 1572872 | tf_op jit(solution)/shard_map/ppermute | solution.py:58
  20.4 9.4 %collective-permute-done.4 = bf16[1,128,2048]{2,1,0:T(8,128)(2,1)S(1)} collective-permute-done((bf16[1,128,2048]{2,1,0:T(8,128)(2,1)S(1)}, bf16[1,128,2048]{2,1,0:T(8,128)(2,1)S(1)}, u32[]{:S(2)}, u32[]{:S(2)}) %collective-permute-start.4) | collective-permute-done | bytes 524320 | tf_op jit(solution)/shard_map/ppermute | solution.py:58
  29.8 1.5 %collective-permute-start.5 = (bf16[1,128,2048]{2,1,0:T(8,128)(2,1)S(1)}, bf16[1,128,2048]{2,1,0:T(8,128)(2,1)S(1)}, u32[]{:S(2)}, u32[]{:S(2)}) collective-permute-start(bf16[1,128,2048]{2,1,0:T(8,128)(2,1)S(1)} %collective-permute-done.4), channel_id=1, source_target_pairs={{0,2},{2,4},{4,6},{6,7},{7,5},{5,3},{3,1},{1,0},{8,10},{10,12},{12... | collective-permute-start | bytes 1572872 | tf_op jit(solution)/shard_map/ppermute | solution.py:58
  31.3 1.3 %constant_dynamic-update-slice_fusion.14 = bf16[16,128,2048]{2,1,0:T(8,128)(2,1)S(1)} fusion(bf16[2,128,2048]{2,1,0:T(8,128)(2,1)} %param.5), kind=kLoop, calls=%fused_computation.45 | loop fusion | bytes 2097152
  34.6 7.3 %collective-permute-done.5 = bf16[1,128,2048]{2,1,0:T(8,128)(2,1)S(1)} collective-permute-done((bf16[1,128,2048]{2,1,0:T(8,128)(2,1)S(1)}, bf16[1,128,2048]{2,1,0:T(8,128)(2,1)S(1)}, u32[]{:S(2)}, u32[]{:S(2)}) %collective-permute-start.5) | collective-permute-done | bytes 524320 | tf_op jit(solution)/shard_map/ppermute | solution.py:58
  42.0 1.4 %collective-permute-start.6 = (bf16[1,128,2048]{2,1,0:T(8,128)(2,1)S(1)}, bf16[1,128,2048]{2,1,0:T(8,128)(2,1)S(1)}, u32[]{:S(2)}, u32[]{:S(2)}) collective-permute-start(bf16[1,128,2048]{2,1,0:T(8,128)(2,1)S(1)} %collective-permute-done.5), channel_id=1, source_target_pairs={{0,2},{2,4},{4,6},{6,7},{7,5},{5,3},{3,1},{1,0},{8,10},{10,12},{12... | collective-permute-start | bytes 1572872 | tf_op jit(solution)/shard_map/ppermute | solution.py:58
  43.5 4.9 %collective-permute-done.8 = bf16[1,128,2048]{2,1,0:T(8,128)(2,1)S(1)} collective-permute-done((bf16[1,128,2048]{2,1,0:T(8,128)(2,1)S(1)}, bf16[1,128,2048]{2,1,0:T(8,128)(2,1)S(1)}, u32[]{:S(2)}, u32[]{:S(2)}) %collective-permute-start.8) | collective-permute-done | bytes 524320 | tf_op jit(solution)/shard_map/ppermute | solution.py:62
  48.4 4.8 %collective-permute-done.6 = bf16[1,128,2048]{2,1,0:T(8,128)(2,1)S(1)} collective-permute-done((bf16[1,128,2048]{2,1,0:T(8,128)(2,1)S(1)}, bf16[1,128,2048]{2,1,0:T(8,128)(2,1)S(1)}, u32[]{:S(2)}, u32[]{:S(2)}) %collective-permute-start.6) | collective-permute-done | bytes 524320 | tf_op jit(solution)/shard_map/ppermute | solution.py:58
  54.5 9.1 %collective-permute-done.9 = bf16[1,128,2048]{2,1,0:T(8,128)(2,1)S(1)} collective-permute-done((bf16[1,128,2048]{2,1,0:T(8,128)(2,1)S(1)}, bf16[1,128,2048]{2,1,0:T(8,128)(2,1)S(1)}, u32[]{:S(2)}, u32[]{:S(2)}) %collective-permute-start.9) | collective-permute-done | bytes 524320 | tf_op jit(solution)/shard_map/ppermute | solution.py:62
  65.7 2.8 %collective-permute-done.13 = bf16[1,128,2048]{2,1,0:T(8,128)(2,1)S(1)} collective-permute-done((bf16[1,128,2048]{2,1,0:T(8,128)(2,1)S(1)}, bf16[1,128,2048]{2,1,0:T(8,128)(2,1)S(1)}, u32[]{:S(2)}, u32[]{:S(2)}) %collective-permute-start.13) | collective-permute-done | bytes 524320 | tf_op jit(solution)/shard_map/ppermute | solution.py:37
  70.8 3.2 %copy-done.1 = bf16[16,128,2048]{2,1,0:T(8,128)(2,1)} copy-done((bf16[16,128,2048]{2,1,0:T(8,128)(2,1)}, bf16[16,128,2048]{2,1,0:T(8,128)(2,1)S(1)}, u32[]{:S(2)}) %copy-start.1) | copy-done | bytes 8388632
  74.0 3.2 %pad_maximum_fusion = bf16[12,2048,128]{2,1,0:T(8,128)(2,1)} fusion(bf16[3,2048,128]{2,1,0:T(8,128)(2,1)S(1)} %collective-permute-done.2, bf16[3,2048,128]{2,1,0:T(8,128)(2,1)S(1)} %collective-permute-done.1, bf16[3,2048,128]{2,1,0:T(8,128)(2,1)S(1)} %collective-permute-done, bf16[3,2048,128]{2,1,0:T(8,128)(2,1)S(1)} %copy-done), kind=kLoop, calls=%fused_computation.4 | loop fusion | flops 9437184 | bytes 12582912 | tf_op jit(solution)/shard_map/concatenate | solution.py:70
  77.2 5.5 %gather_fusion = bf16[6,2048,128]{2,1,0:T(8,128)(2,1)} fusion(bf16[12,2048,128]{2,1,0:T(8,128)(2,1)} %pad_maximum_fusion, s32[1024]{0:T(1024)S(1)} %pad_clamp_fusion), kind=kCustom, calls=%fused_computation | custom fusion | bytes 6291480 | tf_op jit(solution)/shard_map/gather | solution.py:76
  82.7 5.1 %broadcast_select_fusion = (bf16[6,2048,128]{2,1,0:T(8,128)(2,1)}, bf16[6,2048,128]{2,1,0:T(8,128)(2,1)S(1)}) fusion(pred[6]{0:T(512)(128)(4,1)S(1)} %broadcast_compare_fusion, bf16[6,2048,128]{2,1,0:T(8,128)(2,1)} %gather_fusion, f32[6,2048]{1,0:T(8,128)S(1)} %exp.3), kind=kLoop, calls=%fused_computation.12 | loop fusion | flops 6291456 | bytes 9486342 | tf_op jit(solution)/shard_map/jit(_where)/select_n | solution.py:77
  87.8 4.7 %copy.13 = f32[6,128,128]{0,2,1:T(8,128)} copy(f32[6,128,128]{2,1,0:T(8,128)S(1)} %slice_convert_fusion) | data formatting | bytes 786432 | tf_op jit(solution)/shard_map/slice | solution.py:12
  92.5 1.8 %gather_fusion.1 = f32[128,6]{1,0:T(8,128)S(1)} fusion(f32[6,128,128]{0,2,1:T(8,128)} %copy.13, s32[128]{0:T(128)S(1)} %or_bitcast_fusion), kind=kCustom, calls=%fused_computation.1 | custom fusion | bytes 7168 | tf_op jit(solution)/shard_map/jit(diagonal)/gather | solution.py:14
  95.6 1.4 %fusion.5 = f32[6,128,128]{2,1,0:T(8,128)S(1)} fusion(f32[6,128,128]{2,1,0:T(8,128)S(1)} %convolution_subtract_fusion.2, f32[6,128]{1,0:T(8,128)S(1)} %copy.14, f32[128,128]{1,0:T(8,128)} %fusion.16), kind=kOutput, calls=%fused_computation.16 | convolution fusion | flops 151093248 | bytes 855040 | tf_op jit(solution)/shard_map/wij,wjk->wik/dot_general | solution.py:18
  100.5 2.8 %convolution_convert_fusion = bf16[6,2048,128]{2,1,0:T(8,128)(2,1)S(1)} fusion(bf16[6,2048,128]{2,1,0:T(8,128)(2,1)S(1)} %get-tuple-element.7, f32[6,128,128]{2,1,0:T(8,128)S(1)} %fusion.19), kind=kOutput, calls=%fused_computation.10 | convolution fusion | flops 2417491968 | bytes 6684672 | tf_op jit(solution)/shard_map/wnk,wkj->wnj/dot_general | solution.py:24
  103.3 10.9 %fusion = f32[6,128,16,128]{3,1,2,0:T(8,128)} fusion(bf16[16,128,2048]{2,1,0:T(8,128)(2,1)} %copy-done.1, bf16[6,2048,128]{2,1,0:T(8,128)(2,1)S(1)} %convolution_convert_fusion), kind=kOutput, calls=%fused_computation.2 | convolution fusion | flops 6442450944 | bytes 17825792 | tf_op jit(solution)/shard_map/gin,wnj->wgij/dot_general | solution.py:29
  114.2 6.6 %copy.16 = f32[6,128,16,128]{1,3,2,0:T(8,128)} copy(f32[6,128,16,128]{3,1,2,0:T(8,128)} %fusion) | data formatting | bytes 12582912 | tf_op jit(solution)/shard_map/gin,wnj->wgij/dot_general | solution.py:29
  120.8 5.9 %fusion.3 = (f32[6,16]{1,0:T(8,128)S(1)}, f32[6,16]{1,0:T(8,128)S(1)}) fusion(f32[6,128,16,128]{1,3,2,0:T(8,128)} %copy.16, pred[128,128]{1,0:T(8,128)(4,1)S(1)} %copy-done.2, f32[6,128,16,128]{3,1,2,0:T(8,128)} %fusion), kind=kLoop, calls=%fused_computation.8 | loop fusion | flops 6291264 | bytes 12600064 | tf_op jit(solution)/shard_map/wgii->wg/reduce_sum | solution.py:30
  (61 shorter events, 17.2 us)
Async XLA Ops:
  1.7 14.9 %collective-permute-start.3 = (bf16[1,128,2048]{2,1,0:T(8,128)(2,1)S(1)}, bf16[1,128,2048]{2,1,0:T(8,128)(2,1)S(1)}, u32[]{:S(2)}, u32[]{:S(2)}) collective-permute-start(bf16[1,128,2048]{2,1,0:T(8,128)(2,1)S(1)} %constant_dynamic-slice_fusion), channel_id=1, source_target_pairs={{0,2},{2,4},{4,6},{6,7},{7,5},{5,3},{3,1},{1,0},{8,10},{10,12},{12... | collective-permute-start | bytes 1572872 | tf_op jit(solution)/shard_map/ppermute | solution.py:58
  4.8 58.8 %collective-permute-start.1 = (bf16[3,2048,128]{2,1,0:T(8,128)(2,1)}, bf16[3,2048,128]{2,1,0:T(8,128)(2,1)S(1)}, u32[]{:S(2)}, u32[]{:S(2)}) collective-permute-start(bf16[3,2048,128]{2,1,0:T(8,128)(2,1)} %param.4), channel_id=1, source_target_pairs={{0,16},{8,24},{16,0},{24,8},{1,17},{9,25},{17,1},{25,9},{2,18},{10... | collective-permute-start | bytes 4718600 | tf_op jit(solution)/shard_map/ppermute | solution.py:37
  6.3 64.5 %collective-permute-start = (bf16[3,2048,128]{2,1,0:T(8,128)(2,1)}, bf16[3,2048,128]{2,1,0:T(8,128)(2,1)S(1)}, u32[]{:S(2)}, u32[]{:S(2)}) collective-permute-start(bf16[3,2048,128]{2,1,0:T(8,128)(2,1)} %param.4), channel_id=1, source_target_pairs={{0,8},{8,0},{16,24},{24,16},{1,9},{9,1},{17,25},{25,17},{2,10},{10... | collective-permute-start | bytes 4718600 | tf_op jit(solution)/shard_map/ppermute | solution.py:37
  6.3 27.8 %collective-permute-start.7 = (bf16[1,128,2048]{2,1,0:T(8,128)(2,1)S(1)}, bf16[1,128,2048]{2,1,0:T(8,128)(2,1)S(1)}, u32[]{:S(2)}, u32[]{:S(2)}) collective-permute-start(bf16[1,128,2048]{2,1,0:T(8,128)(2,1)S(1)} %constant_dynamic-slice_fusion), channel_id=1, source_target_pairs={{2,0},{4,2},{6,4},{7,6},{5,7},{3,5},{1,3},{0,1},{10,8},{12,10},{14... | collective-permute-start | bytes 1572872 | tf_op jit(solution)/shard_map/ppermute | solution.py:62
  16.7 13.1 %collective-permute-start.4 = (bf16[1,128,2048]{2,1,0:T(8,128)(2,1)S(1)}, bf16[1,128,2048]{2,1,0:T(8,128)(2,1)S(1)}, u32[]{:S(2)}, u32[]{:S(2)}) collective-permute-start(bf16[1,128,2048]{2,1,0:T(8,128)(2,1)S(1)} %collective-permute-done.3), channel_id=1, source_target_pairs={{0,2},{2,4},{4,6},{6,7},{7,5},{5,3},{3,1},{1,0},{8,10},{10,12},{12... | collective-permute-start | bytes 1572872 | tf_op jit(solution)/shard_map/ppermute | solution.py:58
  29.8 12.2 %collective-permute-start.5 = (bf16[1,128,2048]{2,1,0:T(8,128)(2,1)S(1)}, bf16[1,128,2048]{2,1,0:T(8,128)(2,1)S(1)}, u32[]{:S(2)}, u32[]{:S(2)}) collective-permute-start(bf16[1,128,2048]{2,1,0:T(8,128)(2,1)S(1)} %collective-permute-done.4), channel_id=1, source_target_pairs={{0,2},{2,4},{4,6},{6,7},{7,5},{5,3},{3,1},{1,0},{8,10},{10,12},{12... | collective-permute-start | bytes 1572872 | tf_op jit(solution)/shard_map/ppermute | solution.py:58
  34.1 30.1 %collective-permute-start.10 = (bf16[1,128,2048]{2,1,0:T(8,128)(2,1)S(1)}, bf16[1,128,2048]{2,1,0:T(8,128)(2,1)S(1)}, u32[]{:S(2)}, u32[]{:S(2)}) collective-permute-start(bf16[1,128,2048]{2,1,0:T(8,128)(2,1)S(1)} %collective-permute-done.3), channel_id=1, source_target_pairs={{0,8},{8,0},{16,24},{24,16},{1,9},{9,1},{17,25},{25,17},{2,10},{10... | collective-permute-start | bytes 1572872 | tf_op jit(solution)/shard_map/ppermute | solution.py:37
  34.1 14.3 %collective-permute-start.8 = (bf16[1,128,2048]{2,1,0:T(8,128)(2,1)S(1)}, bf16[1,128,2048]{2,1,0:T(8,128)(2,1)S(1)}, u32[]{:S(2)}, u32[]{:S(2)}) collective-permute-start(bf16[1,128,2048]{2,1,0:T(8,128)(2,1)S(1)} %collective-permute-done.7), channel_id=1, source_target_pairs={{2,0},{4,2},{6,4},{7,6},{5,7},{3,5},{1,3},{0,1},{10,8},{12,10},{14... | collective-permute-start | bytes 1572872 | tf_op jit(solution)/shard_map/ppermute | solution.py:62
  42.0 11.3 %collective-permute-start.6 = (bf16[1,128,2048]{2,1,0:T(8,128)(2,1)S(1)}, bf16[1,128,2048]{2,1,0:T(8,128)(2,1)S(1)}, u32[]{:S(2)}, u32[]{:S(2)}) collective-permute-start(bf16[1,128,2048]{2,1,0:T(8,128)(2,1)S(1)} %collective-permute-done.5), channel_id=1, source_target_pairs={{0,2},{2,4},{4,6},{6,7},{7,5},{5,3},{3,1},{1,0},{8,10},{10,12},{12... | collective-permute-start | bytes 1572872 | tf_op jit(solution)/shard_map/ppermute | solution.py:58
  43.4 30.6 %copy-start = (bf16[3,2048,128]{2,1,0:T(8,128)(2,1)S(1)}, bf16[3,2048,128]{2,1,0:T(8,128)(2,1)}, u32[]{:S(2)}) copy-start(bf16[3,2048,128]{2,1,0:T(8,128)(2,1)} %param.4) | copy-start | bytes 4718596
  48.4 15.9 %collective-permute-start.11 = (bf16[1,128,2048]{2,1,0:T(8,128)(2,1)S(1)}, bf16[1,128,2048]{2,1,0:T(8,128)(2,1)S(1)}, u32[]{:S(2)}, u32[]{:S(2)}) collective-permute-start(bf16[1,128,2048]{2,1,0:T(8,128)(2,1)S(1)} %collective-permute-done.4), channel_id=1, source_target_pairs={{0,8},{8,0},{16,24},{24,16},{1,9},{9,1},{17,25},{25,17},{2,10},{10... | collective-permute-start | bytes 1572872 | tf_op jit(solution)/shard_map/ppermute | solution.py:37
  53.2 10.3 %collective-permute-start.9 = (bf16[1,128,2048]{2,1,0:T(8,128)(2,1)S(1)}, bf16[1,128,2048]{2,1,0:T(8,128)(2,1)S(1)}, u32[]{:S(2)}, u32[]{:S(2)}) collective-permute-start(bf16[1,128,2048]{2,1,0:T(8,128)(2,1)S(1)} %collective-permute-done.8), channel_id=1, source_target_pairs={{2,0},{4,2},{6,4},{7,6},{5,7},{3,5},{1,3},{0,1},{10,8},{12,10},{14... | collective-permute-start | bytes 1572872 | tf_op jit(solution)/shard_map/ppermute | solution.py:62
  63.6 1.9 %collective-permute-start.12 = (bf16[1,128,2048]{2,1,0:T(8,128)(2,1)S(1)}, bf16[1,128,2048]{2,1,0:T(8,128)(2,1)S(1)}, u32[]{:S(2)}, u32[]{:S(2)}) collective-permute-start(bf16[1,128,2048]{2,1,0:T(8,128)(2,1)S(1)} %collective-permute-done.5), channel_id=1, source_target_pairs={{0,8},{8,0},{16,24},{24,16},{1,9},{9,1},{17,25},{25,17},{2,10},{10... | collective-permute-start | bytes 1572872 | tf_op jit(solution)/shard_map/ppermute | solution.py:37
  63.6 10.4 %collective-permute-start.2 = (bf16[3,2048,128]{2,1,0:T(8,128)(2,1)S(1)}, bf16[3,2048,128]{2,1,0:T(8,128)(2,1)S(1)}, u32[]{:S(2)}, u32[]{:S(2)}) collective-permute-start(bf16[3,2048,128]{2,1,0:T(8,128)(2,1)S(1)} %collective-permute-done.1), channel_id=1, source_target_pairs={{0,8},{8,0},{16,24},{24,16},{1,9},{9,1},{17,25},{25,17},{2,10},{10... | collective-permute-start | bytes 4718600 | tf_op jit(solution)/shard_map/ppermute | solution.py:37
  64.2 4.3 %collective-permute-start.13 = (bf16[1,128,2048]{2,1,0:T(8,128)(2,1)S(1)}, bf16[1,128,2048]{2,1,0:T(8,128)(2,1)S(1)}, u32[]{:S(2)}, u32[]{:S(2)}) collective-permute-start(bf16[1,128,2048]{2,1,0:T(8,128)(2,1)S(1)} %collective-permute-done.6), channel_id=1, source_target_pairs={{0,8},{8,0},{16,24},{24,16},{1,9},{9,1},{17,25},{25,17},{2,10},{10... | collective-permute-start | bytes 1572872 | tf_op jit(solution)/shard_map/ppermute | solution.py:37
  64.3 5.0 %collective-permute-start.14 = (bf16[1,128,2048]{2,1,0:T(8,128)(2,1)S(1)}, bf16[1,128,2048]{2,1,0:T(8,128)(2,1)S(1)}, u32[]{:S(2)}, u32[]{:S(2)}) collective-permute-start(bf16[1,128,2048]{2,1,0:T(8,128)(2,1)S(1)} %collective-permute-done.7), channel_id=1, source_target_pairs={{0,8},{8,0},{16,24},{24,16},{1,9},{9,1},{17,25},{25,17},{2,10},{10... | collective-permute-start | bytes 1572872 | tf_op jit(solution)/shard_map/ppermute | solution.py:37
  65.5 4.5 %collective-permute-start.15 = (bf16[1,128,2048]{2,1,0:T(8,128)(2,1)S(1)}, bf16[1,128,2048]{2,1,0:T(8,128)(2,1)S(1)}, u32[]{:S(2)}, u32[]{:S(2)}) collective-permute-start(bf16[1,128,2048]{2,1,0:T(8,128)(2,1)S(1)} %collective-permute-done.8), channel_id=1, source_target_pairs={{0,8},{8,0},{16,24},{24,16},{1,9},{9,1},{17,25},{25,17},{2,10},{10... | collective-permute-start | bytes 1572872 | tf_op jit(solution)/shard_map/ppermute | solution.py:37
  68.5 2.2 %collective-permute-start.16 = (bf16[1,128,2048]{2,1,0:T(8,128)(2,1)S(1)}, bf16[1,128,2048]{2,1,0:T(8,128)(2,1)S(1)}, u32[]{:S(2)}, u32[]{:S(2)}) collective-permute-start(bf16[1,128,2048]{2,1,0:T(8,128)(2,1)S(1)} %collective-permute-done.9), channel_id=1, source_target_pairs={{0,8},{8,0},{16,24},{24,16},{1,9},{9,1},{17,25},{25,17},{2,10},{10... | collective-permute-start | bytes 1572872 | tf_op jit(solution)/shard_map/ppermute | solution.py:37
  70.8 3.2 %copy-start.1 = (bf16[16,128,2048]{2,1,0:T(8,128)(2,1)}, bf16[16,128,2048]{2,1,0:T(8,128)(2,1)S(1)}, u32[]{:S(2)}) copy-start(bf16[16,128,2048]{2,1,0:T(8,128)(2,1)S(1)} %constant_dynamic-update-slice_fusion) | copy-start | bytes 25165828
  114.2 6.6 %copy-start.2 = (pred[128,128]{1,0:T(8,128)(4,1)S(1)}, pred[128,128]{1,0:T(8,128)(4,1)}, u32[]{:S(2)}) copy-start(pred[128,128]{1,0:T(8,128)(4,1)} %iota_compare_fusion.1) | copy-start | bytes 49156
  120.8 6.0 %copy-start.3 = (s32[6]{0:T(128)S(1)}, s32[6]{0:T(128)}, u32[]{:S(2)}) copy-start(s32[6]{0:T(128)} %param.6) | copy-start | bytes 76

commit v3 on v2

--- a/solution.py
+++ b/solution.py
@@ -44,6 +44,9 @@
     walk_id = lax.axis_index("walk")
     core = walk_id % 2
 
+    across = swap_pairs(old_walkers, "walk", n_walk, 2)
+    beside = swap_pairs(old_walkers, "walk", n_walk, 1)
+    diagonal_peer = swap_pairs(across, "walk", n_walk, 1)
     local_g = half_chol.shape[0]
     half_g = local_g // 2
     mine = lax.dynamic_slice_in_dim(half_chol, core * half_g, half_g, axis=0)
@@ -52,21 +55,20 @@
     forward = [(order[i], order[(i + 1) % n_chol]) for i in range(n_chol)]
     backward = [(b, a) for a, b in forward]
     n_forward = n_chol // 2
+    n_backward = n_chol - 1 - n_forward
     pieces = []
-    current = mine
+    ahead = mine
+    behind = mine
     for step in range(n_forward):
-        current = lax.ppermute(current, "chol", forward)
-        pieces.append(current)
-    current = mine
-    for step in range(n_chol - 1 - n_forward):
-        current = lax.ppermute(current, "chol", backward)
-        pieces.append(current)
+        ahead = lax.ppermute(ahead, "chol", forward)
+        if step < n_backward:
+            behind = lax.ppermute(behind, "chol", backward)
+            ahead, behind = lax.optimization_barrier((ahead, behind))
+            pieces.append(behind)
+        pieces.append(ahead)
     handed = [swap_pairs(piece, "walk", n_walk, 1) for piece in pieces]
     vectors = jnp.concatenate([half_chol] + pieces + handed, axis=0)
 
-    across = swap_pairs(old_walkers, "walk", n_walk, 2)
-    beside = swap_pairs(old_walkers, "walk", n_walk, 1)
-    diagonal_peer = swap_pairs(across, "walk", n_walk, 1)
     column = jnp.concatenate([old_walkers, beside, across, diagonal_peer], axis=0)
 
     living = parent >= 0

time: 128 us -> 126 us (0.984)
  waiting for transfers between devices: 50.3 us -> 48.6 us
    ppermute x7, starting transfers between devices: 9.8 us -> 7.65 us  [the longest x4 6.3 us: body(): ahead = lax.ppermute(ahead, 'chol', forward)]
    ppermute x7, waiting for transfers between devices: 44.9 us -> 43.2 us  [the longest x4 39.3 us: body(): ahead = lax.ppermute(ahead, 'chol', forward)]
    ppermute x10, starting transfers between devices: 2.91 us -> 4.5 us  [swap_pairs(): return lax.ppermute(x, axis, perm)]
  transfers between devices with their start and end apart: 17 -> 17, of which waited for: 11 -> 12; matrix products, arithmetic and copies ran while one was open for 5% -> 6% of each run, Pallas kernels for 0% -> 0%
where the time goes in v3:
time: 126 us; the launch traced here: 125 us
  waiting for transfers between devices  48.6 us (39%)
  local copies, waits for them, and re-layouts  25.6 us (20%)
  matrix products  19.8 us (16%)
  other arithmetic  18 us (14%)
  starting transfers between devices  12.2 us (10%)
    ppermute x4, waiting for transfers between devices, body(): ahead = lax.ppermute(ahead, 'chol', forward)  39.3 us
    dot_general x1, matrix products, block_energy(): jnp.einsum('gin,wnj->wgij', vectors, theta, preferred_element_type=jnp.fl...  10.9 us
    dot_general x1, local copies, waits for them, and re-layouts, block_energy(): jnp.einsum('gin,wnj->wgij', vectors, theta, preferred_element_type=jnp.fl...  6.59 us
    ppermute x4, starting transfers between devices, body(): ahead = lax.ppermute(ahead, 'chol', forward)  6.3 us
    reduce_sum x1, other arithmetic, block_energy(): traces = jnp.einsum('wgii->wg', blocks)  5.87 us
    gather x1, local copies, waits for them, and re-layouts, body(): column[index].astype(jnp.float32)  5.5 us
    ppermute x10, waiting for transfers between devices, swap_pairs(): return lax.ppermute(x, axis, perm)  5.41 us
    select_n x1, other arithmetic, body(): jnp.where(living[:, None, None], kicked, jnp.zeros_like(kicked))  5.05 us
  transfers between devices with their start and end apart: 17, of which 12 were waited for; matrix products, arithmetic and copies ran while one was open for 6% of the time, Pallas kernels for 0%

profile of v3, /device:TPU:0, one launch (start us, length us, event | category | flops | bytes accessed | tf_op | source)
XLA Modules:
  0.0 125.0 jit_solution(8647457149457665766)
XLA Ops:
  0.6 3.0 %collective-permute-start.1 = (bf16[3,2048,128]{2,1,0:T(8,128)(2,1)}, bf16[3,2048,128]{2,1,0:T(8,128)(2,1)S(1)}, u32[]{:S(2)}, u32[]{:S(2)}) collective-permute-start(bf16[3,2048,128]{2,1,0:T(8,128)(2,1)} %param.4), channel_id=1, source_target_pairs={{0,16},{8,24},{16,0},{24,8},{1,17},{9,25},{17,1},{25,9},{2,18},{10... | collective-permute-start | bytes 4718600 | tf_op jit(solution)/shard_map/ppermute | solution.py:37
  4.7 1.6 %collective-permute-start.3 = (bf16[1,128,2048]{2,1,0:T(8,128)(2,1)S(1)}, bf16[1,128,2048]{2,1,0:T(8,128)(2,1)S(1)}, u32[]{:S(2)}, u32[]{:S(2)}) collective-permute-start(bf16[1,128,2048]{2,1,0:T(8,128)(2,1)S(1)} %constant_dynamic-slice_fusion), channel_id=1, source_target_pairs={{0,2},{2,4},{4,6},{6,7},{7,5},{5,3},{3,1},{1,0},{8,10},{10,12},{12... | collective-permute-start | bytes 1572872 | tf_op jit(solution)/shard_map/ppermute | solution.py:63
  9.4 9.7 %collective-permute-done.3 = bf16[1,128,2048]{2,1,0:T(8,128)(2,1)S(1)} collective-permute-done((bf16[1,128,2048]{2,1,0:T(8,128)(2,1)S(1)}, bf16[1,128,2048]{2,1,0:T(8,128)(2,1)S(1)}, u32[]{:S(2)}, u32[]{:S(2)}) %collective-permute-start.3) | collective-permute-done | bytes 524320 | tf_op jit(solution)/shard_map/ppermute | solution.py:63
  19.1 1.3 %collective-permute-done.4 = bf16[1,128,2048]{2,1,0:T(8,128)(2,1)S(1)} collective-permute-done((bf16[1,128,2048]{2,1,0:T(8,128)(2,1)S(1)}, bf16[1,128,2048]{2,1,0:T(8,128)(2,1)S(1)}, u32[]{:S(2)}, u32[]{:S(2)}) %collective-permute-start.4) | collective-permute-done | bytes 524320 | tf_op jit(solution)/shard_map/ppermute | solution.py:65
  20.4 1.6 %collective-permute-start.5 = (bf16[1,128,2048]{2,1,0:T(8,128)(2,1)S(1)}, bf16[1,128,2048]{2,1,0:T(8,128)(2,1)S(1)}, u32[]{:S(2)}, u32[]{:S(2)}) collective-permute-start(bf16[1,128,2048]{2,1,0:T(8,128)(2,1)S(1)} %collective-permute-done.3), channel_id=1, source_target_pairs={{0,2},{2,4},{4,6},{6,7},{7,5},{5,3},{3,1},{1,0},{8,10},{10,12},{12... | collective-permute-start | bytes 1572872 | tf_op jit(solution)/shard_map/ppermute | solution.py:63
  25.3 8.3 %collective-permute-done.5 = bf16[1,128,2048]{2,1,0:T(8,128)(2,1)S(1)} collective-permute-done((bf16[1,128,2048]{2,1,0:T(8,128)(2,1)S(1)}, bf16[1,128,2048]{2,1,0:T(8,128)(2,1)S(1)}, u32[]{:S(2)}, u32[]{:S(2)}) %collective-permute-start.5) | collective-permute-done | bytes 524320 | tf_op jit(solution)/shard_map/ppermute | solution.py:63
  33.6 1.3 %collective-permute-done.6 = bf16[1,128,2048]{2,1,0:T(8,128)(2,1)S(1)} collective-permute-done((bf16[1,128,2048]{2,1,0:T(8,128)(2,1)S(1)}, bf16[1,128,2048]{2,1,0:T(8,128)(2,1)S(1)}, u32[]{:S(2)}, u32[]{:S(2)}) %collective-permute-start.6) | collective-permute-done | bytes 524320 | tf_op jit(solution)/shard_map/ppermute | solution.py:65
  34.9 1.6 %collective-permute-start.7 = (bf16[1,128,2048]{2,1,0:T(8,128)(2,1)S(1)}, bf16[1,128,2048]{2,1,0:T(8,128)(2,1)S(1)}, u32[]{:S(2)}, u32[]{:S(2)}) collective-permute-start(bf16[1,128,2048]{2,1,0:T(8,128)(2,1)S(1)} %collective-permute-done.5), channel_id=1, source_target_pairs={{0,2},{2,4},{4,6},{6,7},{7,5},{5,3},{3,1},{1,0},{8,10},{10,12},{12... | collective-permute-start | bytes 1572872 | tf_op jit(solution)/shard_map/ppermute | solution.py:63
  37.1 9.8 %collective-permute-done.7 = bf16[1,128,2048]{2,1,0:T(8,128)(2,1)S(1)} collective-permute-done((bf16[1,128,2048]{2,1,0:T(8,128)(2,1)S(1)}, bf16[1,128,2048]{2,1,0:T(8,128)(2,1)S(1)}, u32[]{:S(2)}, u32[]{:S(2)}) %collective-permute-start.7) | collective-permute-done | bytes 524320 | tf_op jit(solution)/shard_map/ppermute | solution.py:63
  47.0 1.3 %collective-permute-done.8 = bf16[1,128,2048]{2,1,0:T(8,128)(2,1)S(1)} collective-permute-done((bf16[1,128,2048]{2,1,0:T(8,128)(2,1)S(1)}, bf16[1,128,2048]{2,1,0:T(8,128)(2,1)S(1)}, u32[]{:S(2)}, u32[]{:S(2)}) %collective-permute-start.8) | collective-permute-done | bytes 524320 | tf_op jit(solution)/shard_map/ppermute | solution.py:65
  48.3 1.5 %collective-permute-start.9 = (bf16[1,128,2048]{2,1,0:T(8,128)(2,1)S(1)}, bf16[1,128,2048]{2,1,0:T(8,128)(2,1)S(1)}, u32[]{:S(2)}, u32[]{:S(2)}) collective-permute-start(bf16[1,128,2048]{2,1,0:T(8,128)(2,1)S(1)} %collective-permute-done.7), channel_id=1, source_target_pairs={{0,2},{2,4},{4,6},{6,7},{7,5},{5,3},{3,1},{1,0},{8,10},{10,12},{12... | collective-permute-start | bytes 1572872 | tf_op jit(solution)/shard_map/ppermute | solution.py:63
  49.9 11.4 %collective-permute-done.9 = bf16[1,128,2048]{2,1,0:T(8,128)(2,1)S(1)} collective-permute-done((bf16[1,128,2048]{2,1,0:T(8,128)(2,1)S(1)}, bf16[1,128,2048]{2,1,0:T(8,128)(2,1)S(1)}, u32[]{:S(2)}, u32[]{:S(2)}) %collective-permute-start.9) | collective-permute-done | bytes 524320 | tf_op jit(solution)/shard_map/ppermute | solution.py:63
  64.2 2.8 %collective-permute-done.14 = bf16[1,128,2048]{2,1,0:T(8,128)(2,1)S(1)} collective-permute-done((bf16[1,128,2048]{2,1,0:T(8,128)(2,1)S(1)}, bf16[1,128,2048]{2,1,0:T(8,128)(2,1)S(1)}, u32[]{:S(2)}, u32[]{:S(2)}) %collective-permute-start.14) | collective-permute-done | bytes 524320 | tf_op jit(solution)/shard_map/ppermute | solution.py:37
  68.5 3.2 %copy-done.1 = bf16[16,128,2048]{2,1,0:T(8,128)(2,1)} copy-done((bf16[16,128,2048]{2,1,0:T(8,128)(2,1)}, bf16[16,128,2048]{2,1,0:T(8,128)(2,1)S(1)}, u32[]{:S(2)}) %copy-start.1) | copy-done | bytes 8388632
  71.7 3.2 %pad_maximum_fusion = bf16[12,2048,128]{2,1,0:T(8,128)(2,1)} fusion(bf16[3,2048,128]{2,1,0:T(8,128)(2,1)S(1)} %collective-permute-done.2, bf16[3,2048,128]{2,1,0:T(8,128)(2,1)S(1)} %collective-permute-done.1, bf16[3,2048,128]{2,1,0:T(8,128)(2,1)S(1)} %collective-permute-done, bf16[3,2048,128]{2,1,0:T(8,128)(2,1)S(1)} %copy-done), kind=kLoop, calls=%fused_computation.4 | loop fusion | flops 9437184 | bytes 12582912 | tf_op jit(solution)/shard_map/concatenate | solution.py:72
  75.0 5.5 %gather_fusion = bf16[6,2048,128]{2,1,0:T(8,128)(2,1)} fusion(bf16[12,2048,128]{2,1,0:T(8,128)(2,1)} %pad_maximum_fusion, s32[1024]{0:T(1024)S(1)} %pad_clamp_fusion), kind=kCustom, calls=%fused_computation | custom fusion | bytes 6291480 | tf_op jit(solution)/shard_map/gather | solution.py:78
  80.5 5.1 %broadcast_select_fusion = (bf16[6,2048,128]{2,1,0:T(8,128)(2,1)}, bf16[6,2048,128]{2,1,0:T(8,128)(2,1)S(1)}) fusion(pred[6]{0:T(512)(128)(4,1)S(1)} %broadcast_compare_fusion, bf16[6,2048,128]{2,1,0:T(8,128)(2,1)} %gather_fusion, f32[6,2048]{1,0:T(8,128)S(1)} %exp.3), kind=kLoop, calls=%fused_computation.12 | loop fusion | flops 6291456 | bytes 9486342 | tf_op jit(solution)/shard_map/jit(_where)/select_n | solution.py:79
  85.5 4.7 %copy.13 = f32[6,128,128]{0,2,1:T(8,128)} copy(f32[6,128,128]{2,1,0:T(8,128)S(1)} %slice_convert_fusion) | data formatting | bytes 786432 | tf_op jit(solution)/shard_map/slice | solution.py:12
  90.2 1.8 %gather_fusion.1 = f32[128,6]{1,0:T(8,128)S(1)} fusion(f32[6,128,128]{0,2,1:T(8,128)} %copy.13, s32[128]{0:T(128)S(1)} %or_bitcast_fusion), kind=kCustom, calls=%fused_computation.1 | custom fusion | bytes 7168 | tf_op jit(solution)/shard_map/jit(diagonal)/gather | solution.py:14
  93.4 1.4 %fusion.5 = f32[6,128,128]{2,1,0:T(8,128)S(1)} fusion(f32[6,128,128]{2,1,0:T(8,128)S(1)} %convolution_subtract_fusion.2, f32[6,128]{1,0:T(8,128)S(1)} %copy.14, f32[128,128]{1,0:T(8,128)} %fusion.16), kind=kOutput, calls=%fused_computation.16 | convolution fusion | flops 151093248 | bytes 855040 | tf_op jit(solution)/shard_map/wij,wjk->wik/dot_general | solution.py:18
  98.2 2.8 %convolution_convert_fusion = bf16[6,2048,128]{2,1,0:T(8,128)(2,1)S(1)} fusion(bf16[6,2048,128]{2,1,0:T(8,128)(2,1)S(1)} %get-tuple-element.19, f32[6,128,128]{2,1,0:T(8,128)S(1)} %fusion.19), kind=kOutput, calls=%fused_computation.10 | convolution fusion | flops 2417491968 | bytes 6684672 | tf_op jit(solution)/shard_map/wnk,wkj->wnj/dot_general | solution.py:24
  101.0 10.9 %fusion = f32[6,128,16,128]{3,1,2,0:T(8,128)} fusion(bf16[16,128,2048]{2,1,0:T(8,128)(2,1)} %copy-done.1, bf16[6,2048,128]{2,1,0:T(8,128)(2,1)S(1)} %convolution_convert_fusion), kind=kOutput, calls=%fused_computation.2 | convolution fusion | flops 6442450944 | bytes 17825792 | tf_op jit(solution)/shard_map/gin,wnj->wgij/dot_general | solution.py:29
  111.9 6.6 %copy.16 = f32[6,128,16,128]{1,3,2,0:T(8,128)} copy(f32[6,128,16,128]{3,1,2,0:T(8,128)} %fusion) | data formatting | bytes 12582912 | tf_op jit(solution)/shard_map/gin,wnj->wgij/dot_general | solution.py:29
  118.5 5.9 %fusion.3 = (f32[6,16]{1,0:T(8,128)S(1)}, f32[6,16]{1,0:T(8,128)S(1)}) fusion(f32[6,128,16,128]{1,3,2,0:T(8,128)} %copy.16, pred[128,128]{1,0:T(8,128)(4,1)S(1)} %copy-done.2, f32[6,128,16,128]{3,1,2,0:T(8,128)} %fusion), kind=kLoop, calls=%fused_computation.8 | loop fusion | flops 6291264 | bytes 12600064 | tf_op jit(solution)/shard_map/wgii->wg/reduce_sum | solution.py:30
  (61 shorter events, 17.8 us)
Async XLA Ops:
  0.6 61.3 %collective-permute-start.1 = (bf16[3,2048,128]{2,1,0:T(8,128)(2,1)}, bf16[3,2048,128]{2,1,0:T(8,128)(2,1)S(1)}, u32[]{:S(2)}, u32[]{:S(2)}) collective-permute-start(bf16[3,2048,128]{2,1,0:T(8,128)(2,1)} %param.4), channel_id=1, source_target_pairs={{0,16},{8,24},{16,0},{24,8},{1,17},{9,25},{17,1},{25,9},{2,18},{10... | collective-permute-start | bytes 4718600 | tf_op jit(solution)/shard_map/ppermute | solution.py:37
  3.6 64.9 %collective-permute-start = (bf16[3,2048,128]{2,1,0:T(8,128)(2,1)}, bf16[3,2048,128]{2,1,0:T(8,128)(2,1)S(1)}, u32[]{:S(2)}, u32[]{:S(2)}) collective-permute-start(bf16[3,2048,128]{2,1,0:T(8,128)(2,1)} %param.4), channel_id=1, source_target_pairs={{0,8},{8,0},{16,24},{24,16},{1,9},{9,1},{17,25},{25,17},{2,10},{10... | collective-permute-start | bytes 4718600 | tf_op jit(solution)/shard_map/ppermute | solution.py:37
  4.7 14.4 %collective-permute-start.3 = (bf16[1,128,2048]{2,1,0:T(8,128)(2,1)S(1)}, bf16[1,128,2048]{2,1,0:T(8,128)(2,1)S(1)}, u32[]{:S(2)}, u32[]{:S(2)}) collective-permute-start(bf16[1,128,2048]{2,1,0:T(8,128)(2,1)S(1)} %constant_dynamic-slice_fusion), channel_id=1, source_target_pairs={{0,2},{2,4},{4,6},{6,7},{7,5},{5,3},{3,1},{1,0},{8,10},{10,12},{12... | collective-permute-start | bytes 1572872 | tf_op jit(solution)/shard_map/ppermute | solution.py:63
  6.3 14.1 %collective-permute-start.4 = (bf16[1,128,2048]{2,1,0:T(8,128)(2,1)S(1)}, bf16[1,128,2048]{2,1,0:T(8,128)(2,1)S(1)}, u32[]{:S(2)}, u32[]{:S(2)}) collective-permute-start(bf16[1,128,2048]{2,1,0:T(8,128)(2,1)S(1)} %constant_dynamic-slice_fusion), channel_id=1, source_target_pairs={{2,0},{4,2},{6,4},{7,6},{5,7},{3,5},{1,3},{0,1},{10,8},{12,10},{14... | collective-permute-start | bytes 1572872 | tf_op jit(solution)/shard_map/ppermute | solution.py:65
  20.4 13.2 %collective-permute-start.5 = (bf16[1,128,2048]{2,1,0:T(8,128)(2,1)S(1)}, bf16[1,128,2048]{2,1,0:T(8,128)(2,1)S(1)}, u32[]{:S(2)}, u32[]{:S(2)}) collective-permute-start(bf16[1,128,2048]{2,1,0:T(8,128)(2,1)S(1)} %collective-permute-done.3), channel_id=1, source_target_pairs={{0,2},{2,4},{4,6},{6,7},{7,5},{5,3},{3,1},{1,0},{8,10},{10,12},{12... | collective-permute-start | bytes 1572872 | tf_op jit(solution)/shard_map/ppermute | solution.py:63
  22.0 13.0 %collective-permute-start.6 = (bf16[1,128,2048]{2,1,0:T(8,128)(2,1)S(1)}, bf16[1,128,2048]{2,1,0:T(8,128)(2,1)S(1)}, u32[]{:S(2)}, u32[]{:S(2)}) collective-permute-start(bf16[1,128,2048]{2,1,0:T(8,128)(2,1)S(1)} %collective-permute-done.4), channel_id=1, source_target_pairs={{2,0},{4,2},{6,4},{7,6},{5,7},{3,5},{1,3},{0,1},{10,8},{12,10},{14... | collective-permute-start | bytes 1572872 | tf_op jit(solution)/shard_map/ppermute | solution.py:65
  25.3 36.1 %collective-permute-start.10 = (bf16[1,128,2048]{2,1,0:T(8,128)(2,1)S(1)}, bf16[1,128,2048]{2,1,0:T(8,128)(2,1)S(1)}, u32[]{:S(2)}, u32[]{:S(2)}) collective-permute-start(bf16[1,128,2048]{2,1,0:T(8,128)(2,1)S(1)} %collective-permute-done.4), channel_id=1, source_target_pairs={{0,8},{8,0},{16,24},{24,16},{1,9},{9,1},{17,25},{25,17},{2,10},{10... | collective-permute-start | bytes 1572872 | tf_op jit(solution)/shard_map/ppermute | solution.py:37
  34.9 12.0 %collective-permute-start.7 = (bf16[1,128,2048]{2,1,0:T(8,128)(2,1)S(1)}, bf16[1,128,2048]{2,1,0:T(8,128)(2,1)S(1)}, u32[]{:S(2)}, u32[]{:S(2)}) collective-permute-start(bf16[1,128,2048]{2,1,0:T(8,128)(2,1)S(1)} %collective-permute-done.5), channel_id=1, source_target_pairs={{0,2},{2,4},{4,6},{6,7},{7,5},{5,3},{3,1},{1,0},{8,10},{10,12},{12... | collective-permute-start | bytes 1572872 | tf_op jit(solution)/shard_map/ppermute | solution.py:63
  36.5 11.8 %collective-permute-start.8 = (bf16[1,128,2048]{2,1,0:T(8,128)(2,1)S(1)}, bf16[1,128,2048]{2,1,0:T(8,128)(2,1)S(1)}, u32[]{:S(2)}, u32[]{:S(2)}) collective-permute-start(bf16[1,128,2048]{2,1,0:T(8,128)(2,1)S(1)} %collective-permute-done.6), channel_id=1, source_target_pairs={{2,0},{4,2},{6,4},{7,6},{5,7},{3,5},{1,3},{0,1},{10,8},{12,10},{14... | collective-permute-start | bytes 1572872 | tf_op jit(solution)/shard_map/ppermute | solution.py:65
  37.1 34.7 %copy-start = (bf16[3,2048,128]{2,1,0:T(8,128)(2,1)S(1)}, bf16[3,2048,128]{2,1,0:T(8,128)(2,1)}, u32[]{:S(2)}) copy-start(bf16[3,2048,128]{2,1,0:T(8,128)(2,1)} %param.4) | copy-start | bytes 4718596
  47.0 15.1 %collective-permute-start.11 = (bf16[1,128,2048]{2,1,0:T(8,128)(2,1)S(1)}, bf16[1,128,2048]{2,1,0:T(8,128)(2,1)S(1)}, u32[]{:S(2)}, u32[]{:S(2)}) collective-permute-start(bf16[1,128,2048]{2,1,0:T(8,128)(2,1)S(1)} %collective-permute-done.3), channel_id=1, source_target_pairs={{0,8},{8,0},{16,24},{24,16},{1,9},{9,1},{17,25},{25,17},{2,10},{10... | collective-permute-start | bytes 1572872 | tf_op jit(solution)/shard_map/ppermute | solution.py:37
  48.3 13.0 %collective-permute-start.9 = (bf16[1,128,2048]{2,1,0:T(8,128)(2,1)S(1)}, bf16[1,128,2048]{2,1,0:T(8,128)(2,1)S(1)}, u32[]{:S(2)}, u32[]{:S(2)}) collective-permute-start(bf16[1,128,2048]{2,1,0:T(8,128)(2,1)S(1)} %collective-permute-done.7), channel_id=1, source_target_pairs={{0,2},{2,4},{4,6},{6,7},{7,5},{5,3},{3,1},{1,0},{8,10},{10,12},{12... | collective-permute-start | bytes 1572872 | tf_op jit(solution)/shard_map/ppermute | solution.py:63
  61.3 1.9 %collective-permute-start.12 = (bf16[1,128,2048]{2,1,0:T(8,128)(2,1)S(1)}, bf16[1,128,2048]{2,1,0:T(8,128)(2,1)S(1)}, u32[]{:S(2)}, u32[]{:S(2)}) collective-permute-start(bf16[1,128,2048]{2,1,0:T(8,128)(2,1)S(1)} %collective-permute-done.6), channel_id=1, source_target_pairs={{0,8},{8,0},{16,24},{24,16},{1,9},{9,1},{17,25},{25,17},{2,10},{10... | collective-permute-start | bytes 1572872 | tf_op jit(solution)/shard_map/ppermute | solution.py:37
  61.4 2.6 %collective-permute-start.13 = (bf16[1,128,2048]{2,1,0:T(8,128)(2,1)S(1)}, bf16[1,128,2048]{2,1,0:T(8,128)(2,1)S(1)}, u32[]{:S(2)}, u32[]{:S(2)}) collective-permute-start(bf16[1,128,2048]{2,1,0:T(8,128)(2,1)S(1)} %collective-permute-done.5), channel_id=1, source_target_pairs={{0,8},{8,0},{16,24},{24,16},{1,9},{9,1},{17,25},{25,17},{2,10},{10... | collective-permute-start | bytes 1572872 | tf_op jit(solution)/shard_map/ppermute | solution.py:37
  61.9 9.8 %collective-permute-start.2 = (bf16[3,2048,128]{2,1,0:T(8,128)(2,1)S(1)}, bf16[3,2048,128]{2,1,0:T(8,128)(2,1)S(1)}, u32[]{:S(2)}, u32[]{:S(2)}) collective-permute-start(bf16[3,2048,128]{2,1,0:T(8,128)(2,1)S(1)} %collective-permute-done.1), channel_id=1, source_target_pairs={{0,8},{8,0},{16,24},{24,16},{1,9},{9,1},{17,25},{25,17},{2,10},{10... | collective-permute-start | bytes 4718600 | tf_op jit(solution)/shard_map/ppermute | solution.py:37
  62.1 4.9 %collective-permute-start.14 = (bf16[1,128,2048]{2,1,0:T(8,128)(2,1)S(1)}, bf16[1,128,2048]{2,1,0:T(8,128)(2,1)S(1)}, u32[]{:S(2)}, u32[]{:S(2)}) collective-permute-start(bf16[1,128,2048]{2,1,0:T(8,128)(2,1)S(1)} %collective-permute-done.8), channel_id=1, source_target_pairs={{0,8},{8,0},{16,24},{24,16},{1,9},{9,1},{17,25},{25,17},{2,10},{10... | collective-permute-start | bytes 1572872 | tf_op jit(solution)/shard_map/ppermute | solution.py:37
  63.2 4.5 %collective-permute-start.15 = (bf16[1,128,2048]{2,1,0:T(8,128)(2,1)S(1)}, bf16[1,128,2048]{2,1,0:T(8,128)(2,1)S(1)}, u32[]{:S(2)}, u32[]{:S(2)}) collective-permute-start(bf16[1,128,2048]{2,1,0:T(8,128)(2,1)S(1)} %collective-permute-done.7), channel_id=1, source_target_pairs={{0,8},{8,0},{16,24},{24,16},{1,9},{9,1},{17,25},{25,17},{2,10},{10... | collective-permute-start | bytes 1572872 | tf_op jit(solution)/shard_map/ppermute | solution.py:37
  64.0 4.5 %collective-permute-start.16 = (bf16[1,128,2048]{2,1,0:T(8,128)(2,1)S(1)}, bf16[1,128,2048]{2,1,0:T(8,128)(2,1)S(1)}, u32[]{:S(2)}, u32[]{:S(2)}) collective-permute-start(bf16[1,128,2048]{2,1,0:T(8,128)(2,1)S(1)} %collective-permute-done.9), channel_id=1, source_target_pairs={{0,8},{8,0},{16,24},{24,16},{1,9},{9,1},{17,25},{25,17},{2,10},{10... | collective-permute-start | bytes 1572872 | tf_op jit(solution)/shard_map/ppermute | solution.py:37
  68.5 3.2 %copy-start.1 = (bf16[16,128,2048]{2,1,0:T(8,128)(2,1)}, bf16[16,128,2048]{2,1,0:T(8,128)(2,1)S(1)}, u32[]{:S(2)}) copy-start(bf16[16,128,2048]{2,1,0:T(8,128)(2,1)S(1)} %constant_dynamic-update-slice_fusion) | copy-start | bytes 25165828
  111.9 6.6 %copy-start.2 = (pred[128,128]{1,0:T(8,128)(4,1)S(1)}, pred[128,128]{1,0:T(8,128)(4,1)}, u32[]{:S(2)}) copy-start(pred[128,128]{1,0:T(8,128)(4,1)} %iota_compare_fusion.1) | copy-start | bytes 49156
  118.5 6.0 %copy-start.3 = (s32[6]{0:T(128)S(1)}, s32[6]{0:T(128)}, u32[]{:S(2)}) copy-start(s32[6]{0:T(128)} %param.6) | copy-start | bytes 76

commit v4 on v3

--- a/solution.py
+++ b/solution.py
@@ -37,16 +37,26 @@
     return lax.ppermute(x, axis, perm)
 
 
+def kick(old_walkers, beside, across, diagonal_peer, parent, field, walk_id):
+    old_dev = old_walkers.shape[0]
+    column = jnp.concatenate([old_walkers, beside, across, diagonal_peer], axis=0)
+    living = parent >= 0
+    source = jnp.maximum(parent, 0)
+    relative = (source // old_dev) ^ walk_id
+    index = relative * old_dev + source % old_dev
+    kicked = (jnp.exp(field)[:, :, None] * column[index].astype(jnp.float32)).astype(jnp.bfloat16)
+    new_walkers = jnp.where(living[:, None, None], kicked, jnp.zeros_like(kicked))
+    return new_walkers, green_half(kicked)
+
+
 def body(old_walkers, half_chol, parent, field):
     n_walk = lax.axis_size("walk")
-    old_dev = old_walkers.shape[0]
-    slot_dev = parent.shape[0]
     walk_id = lax.axis_index("walk")
     core = walk_id % 2
 
     across = swap_pairs(old_walkers, "walk", n_walk, 2)
     beside = swap_pairs(old_walkers, "walk", n_walk, 1)
-    diagonal_peer = swap_pairs(across, "walk", n_walk, 1)
+
     local_g = half_chol.shape[0]
     half_g = local_g // 2
     mine = lax.dynamic_slice_in_dim(half_chol, core * half_g, half_g, axis=0)
@@ -56,28 +66,43 @@
     backward = [(b, a) for a, b in forward]
     n_forward = n_chol // 2
     n_backward = n_chol - 1 - n_forward
+    walker_step = max(n_forward - 2, 0)
     pieces = []
+    handed = []
     ahead = mine
     behind = mine
+    new_walkers = theta = None
     for step in range(n_forward):
         ahead = lax.ppermute(ahead, "chol", forward)
+        carried = [ahead]
         if step < n_backward:
             behind = lax.ppermute(behind, "chol", backward)
-            ahead, behind = lax.optimization_barrier((ahead, behind))
-            pieces.append(behind)
-        pieces.append(ahead)
-    handed = [swap_pairs(piece, "walk", n_walk, 1) for piece in pieces]
+            carried.append(behind)
+        if step == walker_step:
+            carried += [across, beside]
+        if step == n_forward - 1:
+            diagonal_peer = swap_pairs(across, "walk", n_walk, 1)
+            new_walkers, theta = kick(old_walkers, beside, across, diagonal_peer, parent, field, walk_id)
+            carried += [new_walkers, theta]
+        carried = list(lax.optimization_barrier(tuple(carried)))
+        ahead = carried.pop(0)
+        arrived = [ahead]
+        if step < n_backward:
+            behind = carried.pop(0)
+            arrived.append(behind)
+        if step == walker_step:
+            across, beside = carried.pop(0), carried.pop(0)
+        if step == n_forward - 1:
+            new_walkers, theta = carried.pop(0), carried.pop(0)
+        for piece in arrived:
+            pieces.append(piece)
+            handed.append(swap_pairs(piece, "walk", n_walk, 1))
+    if theta is None:
+        diagonal_peer = swap_pairs(across, "walk", n_walk, 1)
+        new_walkers, theta = kick(old_walkers, beside, across, diagonal_peer, parent, field, walk_id)
     vectors = jnp.concatenate([half_chol] + pieces + handed, axis=0)
 
-    column = jnp.concatenate([old_walkers, beside, across, diagonal_peer], axis=0)
-
     living = parent >= 0
-    source = jnp.maximum(parent, 0)
-    relative = (source // old_dev) ^ walk_id
-    index = relative * old_dev + source % old_dev
-    kicked = (jnp.exp(field)[:, :, None] * column[index].astype(jnp.float32)).astype(jnp.bfloat16)
-    new_walkers = jnp.where(living[:, None, None], kicked, jnp.zeros_like(kicked))
-    theta = green_half(kicked)
     energy = block_energy(theta, vectors)
     energy = jnp.where(living, energy, 0.0)
     return (new_walkers, energy)

time: 126 us -> 125 us (level)
  waiting for transfers between devices: 48.6 us -> 30.5 us
  local copies, waits for them, and re-layouts: 25.6 us -> 42.8 us
    unnamed x22 -> x26, local copies, waits for them, and re-layouts: 5.01 us -> 21.1 us
    ppermute x4, waiting for transfers between devices: 39.3 us -> 26.5 us  [body(): ahead = lax.ppermute(ahead, 'chol', forward)]
    ppermute x10, waiting for transfers between devices: 5.41 us -> 0.03 us  [swap_pairs(): return lax.ppermute(x, axis, perm)]
    ppermute x4, starting transfers between devices: 6.3 us -> 7.75 us  [body(): ahead = lax.ppermute(ahead, 'chol', forward)]
  transfers between devices with their start and end apart: 17 -> 17, of which waited for: 12 -> 6; matrix products, arithmetic and copies ran while one was open for 6% -> 41% of each run, Pallas kernels for 0% -> 0%
where the time goes in v4:
time: 125 us; the launch traced here: 124 us
  local copies, waits for them, and re-layouts  42.8 us (34%)
  waiting for transfers between devices  30.5 us (24%)
  matrix products  19.8 us (16%)
  other arithmetic  18.1 us (14%)
  starting transfers between devices  12.5 us (10%)
    ppermute x4, waiting for transfers between devices, body(): ahead = lax.ppermute(ahead, 'chol', forward)  26.5 us
    unnamed x26, local copies, waits for them, and re-layouts  21.1 us
    dot_general x1, matrix products, block_energy(): jnp.einsum('gin,wnj->wgij', vectors, theta, preferred_element_type=jnp.fl...  10.9 us
    ppermute x4, starting transfers between devices, body(): ahead = lax.ppermute(ahead, 'chol', forward)  7.75 us
    dot_general x1, local copies, waits for them, and re-layouts, block_energy(): jnp.einsum('gin,wnj->wgij', vectors, theta, preferred_element_type=jnp.fl...  6.6 us
    reduce_sum x1, other arithmetic, block_energy(): traces = jnp.einsum('wgii->wg', blocks)  5.87 us
    gather x1, local copies, waits for them, and re-layouts, kick(): column[index].astype(jnp.float32)  5.5 us
    select_n x1, other arithmetic, kick(): jnp.where(living[:, None, None], kicked, jnp.zeros_like(kicked))  5.05 us
  transfers between devices with their start and end apart: 17, of which 6 were waited for; matrix products, arithmetic and copies ran while one was open for 41% of the time, Pallas kernels for 0%

profile of v4, /device:TPU:0, one launch (start us, length us, event | category | flops | bytes accessed | tf_op | source)
XLA Modules:
  0.0 124.4 jit_solution(16435518007224625282)
XLA Ops:
  1.9 3.1 %collective-permute-start = (bf16[1,128,2048]{2,1,0:T(8,128)(2,1)S(1)}, bf16[1,128,2048]{2,1,0:T(8,128)(2,1)}, u32[]{:S(2)}, u32[]{:S(2)}) collective-permute-start(bf16[1,128,2048]{2,1,0:T(8,128)(2,1)S(1)} %constant_dynamic-slice_fusion), channel_id=1, source_target_pairs={{0,2},{2,4},{4,6},{6,7},{7,5},{5,3},{3,1},{1,0},{8,10},{10,12},{12... | collective-permute-start | bytes 1572872 | tf_op jit(solution)/shard_map/ppermute | solution.py:76
  4.9 1.9 %collective-permute-start.6 = (bf16[3,2048,128]{2,1,0:T(8,128)(2,1)}, bf16[3,2048,128]{2,1,0:T(8,128)(2,1)S(1)}, u32[]{:S(2)}, u32[]{:S(2)}) collective-permute-start(bf16[3,2048,128]{2,1,0:T(8,128)(2,1)} %param.4), channel_id=1, source_target_pairs={{0,16},{8,24},{16,0},{24,8},{1,17},{9,25},{17,1},{25,9},{2,18},{10... | collective-permute-start | bytes 4718600 | tf_op jit(solution)/shard_map/ppermute | solution.py:37
  6.9 10.0 %collective-permute-done = bf16[1,128,2048]{2,1,0:T(8,128)(2,1)} collective-permute-done((bf16[1,128,2048]{2,1,0:T(8,128)(2,1)S(1)}, bf16[1,128,2048]{2,1,0:T(8,128)(2,1)}, u32[]{:S(2)}, u32[]{:S(2)}) %collective-permute-start) | collective-permute-done | bytes 524320 | tf_op jit(solution)/shard_map/ppermute | solution.py:76
  16.9 1.5 %collective-permute-done.1 = bf16[1,128,2048]{2,1,0:T(8,128)(2,1)} collective-permute-done((bf16[1,128,2048]{2,1,0:T(8,128)(2,1)S(1)}, bf16[1,128,2048]{2,1,0:T(8,128)(2,1)}, u32[]{:S(2)}, u32[]{:S(2)}) %collective-permute-start.1) | collective-permute-done | bytes 524320 | tf_op jit(solution)/shard_map/ppermute | solution.py:79
  18.4 1.6 %collective-permute-start.2 = (bf16[1,128,2048]{2,1,0:T(8,128)(2,1)}, bf16[1,128,2048]{2,1,0:T(8,128)(2,1)}, u32[]{:S(2)}, u32[]{:S(2)}) collective-permute-start(bf16[1,128,2048]{2,1,0:T(8,128)(2,1)} %collective-permute-done), channel_id=1, source_target_pairs={{0,2},{2,4},{4,6},{6,7},{7,5},{5,3},{3,1},{1,0},{8,10},{10,12},{12... | collective-permute-start | bytes 1572872 | tf_op jit(solution)/shard_map/ppermute | solution.py:76
  22.4 8.8 %collective-permute-done.2 = bf16[1,128,2048]{2,1,0:T(8,128)(2,1)} collective-permute-done((bf16[1,128,2048]{2,1,0:T(8,128)(2,1)}, bf16[1,128,2048]{2,1,0:T(8,128)(2,1)}, u32[]{:S(2)}, u32[]{:S(2)}) %collective-permute-start.2) | collective-permute-done | bytes 524320 | tf_op jit(solution)/shard_map/ppermute | solution.py:76
  32.5 1.6 %collective-permute-start.4 = (bf16[1,128,2048]{2,1,0:T(8,128)(2,1)}, bf16[1,128,2048]{2,1,0:T(8,128)(2,1)}, u32[]{:S(2)}, u32[]{:S(2)}) collective-permute-start(bf16[1,128,2048]{2,1,0:T(8,128)(2,1)} %collective-permute-done.2), channel_id=1, source_target_pairs={{0,2},{2,4},{4,6},{6,7},{7,5},{5,3},{3,1},{1,0},{8,10},{10,12},{12... | collective-permute-start | bytes 1572872 | tf_op jit(solution)/shard_map/ppermute | solution.py:76
  36.5 7.6 %collective-permute-done.4 = bf16[1,128,2048]{2,1,0:T(8,128)(2,1)} collective-permute-done((bf16[1,128,2048]{2,1,0:T(8,128)(2,1)}, bf16[1,128,2048]{2,1,0:T(8,128)(2,1)}, u32[]{:S(2)}, u32[]{:S(2)}) %collective-permute-start.4) | collective-permute-done | bytes 524320 | tf_op jit(solution)/shard_map/ppermute | solution.py:76
  53.5 3.2 %copy-done.3 = bf16[16,128,2048]{2,1,0:T(8,128)(2,1)} copy-done((bf16[16,128,2048]{2,1,0:T(8,128)(2,1)}, bf16[16,128,2048]{2,1,0:T(8,128)(2,1)S(1)}, u32[]{:S(2)}) %copy-start.3) | copy-done | bytes 8388632
  56.7 1.5 %collective-permute-start.8 = (bf16[1,128,2048]{2,1,0:T(8,128)(2,1)}, bf16[1,128,2048]{2,1,0:T(8,128)(2,1)}, u32[]{:S(2)}, u32[]{:S(2)}) collective-permute-start(bf16[1,128,2048]{2,1,0:T(8,128)(2,1)} %collective-permute-done.4), channel_id=1, source_target_pairs={{0,2},{2,4},{4,6},{6,7},{7,5},{5,3},{3,1},{1,0},{8,10},{10,12},{12... | collective-permute-start | bytes 1572872 | tf_op jit(solution)/shard_map/ppermute | solution.py:76
  58.3 3.2 %pad_maximum_fusion = bf16[12,2048,128]{2,1,0:T(8,128)(2,1)} fusion(bf16[3,2048,128]{2,1,0:T(8,128)(2,1)S(1)} %collective-permute-done.9, bf16[3,2048,128]{2,1,0:T(8,128)(2,1)S(1)} %collective-permute-done.6, bf16[3,2048,128]{2,1,0:T(8,128)(2,1)S(1)} %collective-permute-done.7, bf16[3,2048,128]{2,1,0:T(8,128)(2,1)S(1)} %copy-done), kind=kLoop, calls=%fused_computation.4 | loop fusion | flops 9437184 | bytes 12582912 | tf_op jit(solution)/shard_map/concatenate | solution.py:42
  61.5 5.5 %gather_fusion = bf16[6,2048,128]{2,1,0:T(8,128)(2,1)} fusion(bf16[12,2048,128]{2,1,0:T(8,128)(2,1)} %pad_maximum_fusion, s32[1024]{0:T(1024)S(1)} %pad_clamp_fusion), kind=kCustom, calls=%fused_computation | custom fusion | bytes 6291480 | tf_op jit(solution)/shard_map/gather | solution.py:47
  67.0 5.1 %broadcast_select_fusion = (bf16[6,2048,128]{2,1,0:T(8,128)(2,1)}, bf16[6,2048,128]{2,1,0:T(8,128)(2,1)S(1)}) fusion(pred[6]{0:T(512)(128)(4,1)S(1)} %broadcast_compare_fusion, bf16[6,2048,128]{2,1,0:T(8,128)(2,1)} %gather_fusion, f32[6,2048]{1,0:T(8,128)S(1)} %exp.3), kind=kLoop, calls=%fused_computation.12 | loop fusion | flops 6291456 | bytes 9486342 | tf_op jit(solution)/shard_map/jit(_where)/select_n | solution.py:48
  72.1 4.7 %copy.16 = f32[6,128,128]{0,2,1:T(8,128)} copy(f32[6,128,128]{2,1,0:T(8,128)S(1)} %slice_convert_fusion) | data formatting | bytes 786432 | tf_op jit(solution)/shard_map/slice | solution.py:12
  76.8 1.8 %gather_fusion.1 = f32[128,6]{1,0:T(8,128)S(1)} fusion(f32[6,128,128]{0,2,1:T(8,128)} %copy.16, s32[128]{0:T(128)S(1)} %or_bitcast_fusion), kind=kCustom, calls=%fused_computation.1 | custom fusion | bytes 7168 | tf_op jit(solution)/shard_map/jit(diagonal)/gather | solution.py:14
  84.8 2.8 %convolution_convert_fusion = bf16[6,2048,128]{2,1,0:T(8,128)(2,1)S(1)} fusion(bf16[6,2048,128]{2,1,0:T(8,128)(2,1)S(1)} %get-tuple-element.29, f32[6,128,128]{2,1,0:T(8,128)S(1)} %fusion.19), kind=kOutput, calls=%fused_computation.10 | convolution fusion | flops 2417491968 | bytes 6684672 | tf_op jit(solution)/shard_map/wnk,wkj->wnj/dot_general | solution.py:24
  87.8 1.9 %constant_dynamic-update-slice_fusion.7 = bf16[16,128,2048]{2,1,0:T(8,128)(2,1)} fusion(bf16[16,128,2048]{2,1,0:T(8,128)(2,1)} %copy-done.3, bf16[1,128,2048]{2,1,0:T(8,128)(2,1)} %collective-permute-done.8), kind=kLoop, calls=%fused_computation.38 | loop fusion | bytes 1048576
  90.1 1.9 %constant_dynamic-update-slice_fusion.6 = bf16[16,128,2048]{2,1,0:T(8,128)(2,1)} fusion(bf16[16,128,2048]{2,1,0:T(8,128)(2,1)} %constant_dynamic-update-slice_fusion.7, bf16[1,128,2048]{2,1,0:T(8,128)(2,1)} %collective-permute-done.10), kind=kLoop, calls=%fused_computation.37 | loop fusion | bytes 1048576
  92.1 1.9 %constant_dynamic-update-slice_fusion.5 = bf16[16,128,2048]{2,1,0:T(8,128)(2,1)} fusion(bf16[16,128,2048]{2,1,0:T(8,128)(2,1)} %constant_dynamic-update-slice_fusion.6, bf16[1,128,2048]{2,1,0:T(8,128)(2,1)} %collective-permute-done.11), kind=kLoop, calls=%fused_computation.36 | loop fusion | bytes 1048576
  94.1 1.9 %constant_dynamic-update-slice_fusion.4 = bf16[16,128,2048]{2,1,0:T(8,128)(2,1)} fusion(bf16[16,128,2048]{2,1,0:T(8,128)(2,1)} %constant_dynamic-update-slice_fusion.5, bf16[1,128,2048]{2,1,0:T(8,128)(2,1)} %collective-permute-done.12), kind=kLoop, calls=%fused_computation.35 | loop fusion | bytes 1048576
  96.0 1.9 %constant_dynamic-update-slice_fusion.3 = bf16[16,128,2048]{2,1,0:T(8,128)(2,1)} fusion(bf16[16,128,2048]{2,1,0:T(8,128)(2,1)} %constant_dynamic-update-slice_fusion.4, bf16[1,128,2048]{2,1,0:T(8,128)(2,1)} %collective-permute-done.13), kind=kLoop, calls=%fused_computation.34 | loop fusion | bytes 1048576
  100.4 10.9 %fusion = f32[6,128,16,128]{3,1,2,0:T(8,128)} fusion(bf16[16,128,2048]{2,1,0:T(8,128)(2,1)} %constant_dynamic-update-slice_fusion, bf16[6,2048,128]{2,1,0:T(8,128)(2,1)S(1)} %convolution_convert_fusion), kind=kOutput, calls=%fused_computation.2 | convolution fusion | flops 6442450944 | bytes 17825792 | tf_op jit(solution)/shard_map/gin,wnj->wgij/dot_general | solution.py:29
  111.3 6.6 %copy.19 = f32[6,128,16,128]{1,3,2,0:T(8,128)} copy(f32[6,128,16,128]{3,1,2,0:T(8,128)} %fusion) | data formatting | bytes 12582912 | tf_op jit(solution)/shard_map/gin,wnj->wgij/dot_general | solution.py:29
  117.9 5.9 %fusion.3 = (f32[6,16]{1,0:T(8,128)S(1)}, f32[6,16]{1,0:T(8,128)S(1)}) fusion(f32[6,128,16,128]{1,3,2,0:T(8,128)} %copy.19, pred[128,128]{1,0:T(8,128)(4,1)S(1)} %copy-done.4, f32[6,128,16,128]{3,1,2,0:T(8,128)} %fusion), kind=kLoop, calls=%fused_computation.8 | loop fusion | flops 6291264 | bytes 12600064 | tf_op jit(solution)/shard_map/wgii->wg/reduce_sum | solution.py:30
  (65 shorter events, 26.8 us)
Async XLA Ops:
  0.6 57.6 %copy-start = (bf16[3,2048,128]{2,1,0:T(8,128)(2,1)S(1)}, bf16[3,2048,128]{2,1,0:T(8,128)(2,1)}, u32[]{:S(2)}) copy-start(bf16[3,2048,128]{2,1,0:T(8,128)(2,1)} %param.4) | copy-start | bytes 4718596
  1.9 15.0 %collective-permute-start = (bf16[1,128,2048]{2,1,0:T(8,128)(2,1)S(1)}, bf16[1,128,2048]{2,1,0:T(8,128)(2,1)}, u32[]{:S(2)}, u32[]{:S(2)}) collective-permute-start(bf16[1,128,2048]{2,1,0:T(8,128)(2,1)S(1)} %constant_dynamic-slice_fusion), channel_id=1, source_target_pairs={{0,2},{2,4},{4,6},{6,7},{7,5},{5,3},{3,1},{1,0},{8,10},{10,12},{12... | collective-permute-start | bytes 1572872 | tf_op jit(solution)/shard_map/ppermute | solution.py:76
  4.9 13.5 %collective-permute-start.1 = (bf16[1,128,2048]{2,1,0:T(8,128)(2,1)S(1)}, bf16[1,128,2048]{2,1,0:T(8,128)(2,1)}, u32[]{:S(2)}, u32[]{:S(2)}) collective-permute-start(bf16[1,128,2048]{2,1,0:T(8,128)(2,1)S(1)} %constant_dynamic-slice_fusion), channel_id=1, source_target_pairs={{2,0},{4,2},{6,4},{7,6},{5,7},{3,5},{1,3},{0,1},{10,8},{12,10},{14... | collective-permute-start | bytes 1572872 | tf_op jit(solution)/shard_map/ppermute | solution.py:79
  4.9 40.4 %collective-permute-start.6 = (bf16[3,2048,128]{2,1,0:T(8,128)(2,1)}, bf16[3,2048,128]{2,1,0:T(8,128)(2,1)S(1)}, u32[]{:S(2)}, u32[]{:S(2)}) collective-permute-start(bf16[3,2048,128]{2,1,0:T(8,128)(2,1)} %param.4), channel_id=1, source_target_pairs={{0,16},{8,24},{16,0},{24,8},{1,17},{9,25},{17,1},{25,9},{2,18},{10... | collective-permute-start | bytes 4718600 | tf_op jit(solution)/shard_map/ppermute | solution.py:37
  6.9 38.4 %collective-permute-start.7 = (bf16[3,2048,128]{2,1,0:T(8,128)(2,1)}, bf16[3,2048,128]{2,1,0:T(8,128)(2,1)S(1)}, u32[]{:S(2)}, u32[]{:S(2)}) collective-permute-start(bf16[3,2048,128]{2,1,0:T(8,128)(2,1)} %param.4), channel_id=1, source_target_pairs={{0,8},{8,0},{16,24},{24,16},{1,9},{9,1},{17,25},{25,17},{2,10},{10... | collective-permute-start | bytes 4718600 | tf_op jit(solution)/shard_map/ppermute | solution.py:37
  18.4 12.8 %collective-permute-start.2 = (bf16[1,128,2048]{2,1,0:T(8,128)(2,1)}, bf16[1,128,2048]{2,1,0:T(8,128)(2,1)}, u32[]{:S(2)}, u32[]{:S(2)}) collective-permute-start(bf16[1,128,2048]{2,1,0:T(8,128)(2,1)} %collective-permute-done), channel_id=1, source_target_pairs={{0,2},{2,4},{4,6},{6,7},{7,5},{5,3},{3,1},{1,0},{8,10},{10,12},{12... | collective-permute-start | bytes 1572872 | tf_op jit(solution)/shard_map/ppermute | solution.py:76
  20.0 12.5 %collective-permute-start.3 = (bf16[1,128,2048]{2,1,0:T(8,128)(2,1)}, bf16[1,128,2048]{2,1,0:T(8,128)(2,1)}, u32[]{:S(2)}, u32[]{:S(2)}) collective-permute-start(bf16[1,128,2048]{2,1,0:T(8,128)(2,1)} %collective-permute-done.1), channel_id=1, source_target_pairs={{2,0},{4,2},{6,4},{7,6},{5,7},{3,5},{1,3},{0,1},{10,8},{12,10},{14... | collective-permute-start | bytes 1572872 | tf_op jit(solution)/shard_map/ppermute | solution.py:79
  32.5 11.6 %collective-permute-start.4 = (bf16[1,128,2048]{2,1,0:T(8,128)(2,1)}, bf16[1,128,2048]{2,1,0:T(8,128)(2,1)}, u32[]{:S(2)}, u32[]{:S(2)}) collective-permute-start(bf16[1,128,2048]{2,1,0:T(8,128)(2,1)} %collective-permute-done.2), channel_id=1, source_target_pairs={{0,2},{2,4},{4,6},{6,7},{7,5},{5,3},{3,1},{1,0},{8,10},{10,12},{12... | collective-permute-start | bytes 1572872 | tf_op jit(solution)/shard_map/ppermute | solution.py:76
  34.1 11.2 %collective-permute-start.5 = (bf16[1,128,2048]{2,1,0:T(8,128)(2,1)}, bf16[1,128,2048]{2,1,0:T(8,128)(2,1)S(1)}, u32[]{:S(2)}, u32[]{:S(2)}) collective-permute-start(bf16[1,128,2048]{2,1,0:T(8,128)(2,1)} %collective-permute-done.3), channel_id=1, source_target_pairs={{2,0},{4,2},{6,4},{7,6},{5,7},{3,5},{1,3},{0,1},{10,8},{12,10},{14... | collective-permute-start | bytes 1572872 | tf_op jit(solution)/shard_map/ppermute | solution.py:79
  45.3 8.2 %copy-start.1 = (bf16[1,128,2048]{2,1,0:T(8,128)(2,1)}, bf16[1,128,2048]{2,1,0:T(8,128)(2,1)S(1)}, u32[]{:S(2)}) copy-start(bf16[1,128,2048]{2,1,0:T(8,128)(2,1)S(1)} %collective-permute-done.5) | copy-start | bytes 1572868
  45.3 8.2 %collective-permute-start.9 = (bf16[3,2048,128]{2,1,0:T(8,128)(2,1)S(1)}, bf16[3,2048,128]{2,1,0:T(8,128)(2,1)S(1)}, u32[]{:S(2)}, u32[]{:S(2)}) collective-permute-start(bf16[3,2048,128]{2,1,0:T(8,128)(2,1)S(1)} %collective-permute-done.6), channel_id=1, source_target_pairs={{0,8},{8,0},{16,24},{24,16},{1,9},{9,1},{17,25},{25,17},{2,10},{10... | collective-permute-start | bytes 4718600 | tf_op jit(solution)/shard_map/ppermute | solution.py:37
  47.0 42.8 %collective-permute-start.10 = (bf16[1,128,2048]{2,1,0:T(8,128)(2,1)}, bf16[1,128,2048]{2,1,0:T(8,128)(2,1)}, u32[]{:S(2)}, u32[]{:S(2)}) collective-permute-start(bf16[1,128,2048]{2,1,0:T(8,128)(2,1)} %collective-permute-done), channel_id=1, source_target_pairs={{0,8},{8,0},{16,24},{24,16},{1,9},{9,1},{17,25},{25,17},{2,10},{10... | collective-permute-start | bytes 1572872 | tf_op jit(solution)/shard_map/ppermute | solution.py:37
  47.4 44.6 %collective-permute-start.11 = (bf16[1,128,2048]{2,1,0:T(8,128)(2,1)}, bf16[1,128,2048]{2,1,0:T(8,128)(2,1)}, u32[]{:S(2)}, u32[]{:S(2)}) collective-permute-start(bf16[1,128,2048]{2,1,0:T(8,128)(2,1)} %collective-permute-done.1), channel_id=1, source_target_pairs={{0,8},{8,0},{16,24},{24,16},{1,9},{9,1},{17,25},{25,17},{2,10},{10... | collective-permute-start | bytes 1572872 | tf_op jit(solution)/shard_map/ppermute | solution.py:37
  49.6 44.4 %collective-permute-start.12 = (bf16[1,128,2048]{2,1,0:T(8,128)(2,1)}, bf16[1,128,2048]{2,1,0:T(8,128)(2,1)}, u32[]{:S(2)}, u32[]{:S(2)}) collective-permute-start(bf16[1,128,2048]{2,1,0:T(8,128)(2,1)} %collective-permute-done.2), channel_id=1, source_target_pairs={{0,8},{8,0},{16,24},{24,16},{1,9},{9,1},{17,25},{25,17},{2,10},{10... | collective-permute-start | bytes 1572872 | tf_op jit(solution)/shard_map/ppermute | solution.py:37
  50.1 45.9 %collective-permute-start.13 = (bf16[1,128,2048]{2,1,0:T(8,128)(2,1)}, bf16[1,128,2048]{2,1,0:T(8,128)(2,1)}, u32[]{:S(2)}, u32[]{:S(2)}) collective-permute-start(bf16[1,128,2048]{2,1,0:T(8,128)(2,1)} %collective-permute-done.3), channel_id=1, source_target_pairs={{0,8},{8,0},{16,24},{24,16},{1,9},{9,1},{17,25},{25,17},{2,10},{10... | collective-permute-start | bytes 1572872 | tf_op jit(solution)/shard_map/ppermute | solution.py:37
  53.5 3.2 %copy-start.3 = (bf16[16,128,2048]{2,1,0:T(8,128)(2,1)}, bf16[16,128,2048]{2,1,0:T(8,128)(2,1)S(1)}, u32[]{:S(2)}) copy-start(bf16[16,128,2048]{2,1,0:T(8,128)(2,1)S(1)} %constant_dynamic-update-slice_fusion.8) | copy-start | bytes 25165828
  56.7 30.9 %collective-permute-start.8 = (bf16[1,128,2048]{2,1,0:T(8,128)(2,1)}, bf16[1,128,2048]{2,1,0:T(8,128)(2,1)}, u32[]{:S(2)}, u32[]{:S(2)}) collective-permute-start(bf16[1,128,2048]{2,1,0:T(8,128)(2,1)} %collective-permute-done.4), channel_id=1, source_target_pairs={{0,2},{2,4},{4,6},{6,7},{7,5},{5,3},{3,1},{1,0},{8,10},{10,12},{12... | collective-permute-start | bytes 1572872 | tf_op jit(solution)/shard_map/ppermute | solution.py:76
  81.3 8.5 %copy-start.2 = (bf16[1,128,2048]{2,1,0:T(8,128)(2,1)S(1)}, bf16[1,128,2048]{2,1,0:T(8,128)(2,1)}, u32[]{:S(2)}) copy-start(bf16[1,128,2048]{2,1,0:T(8,128)(2,1)} %copy-done.1) | copy-start | bytes 1572868
  87.6 10.2 %collective-permute-start.14 = (bf16[1,128,2048]{2,1,0:T(8,128)(2,1)}, bf16[1,128,2048]{2,1,0:T(8,128)(2,1)S(1)}, u32[]{:S(2)}, u32[]{:S(2)}) collective-permute-start(bf16[1,128,2048]{2,1,0:T(8,128)(2,1)} %collective-permute-done.4), channel_id=1, source_target_pairs={{0,8},{8,0},{16,24},{24,16},{1,9},{9,1},{17,25},{25,17},{2,10},{10... | collective-permute-start | bytes 1572872 | tf_op jit(solution)/shard_map/ppermute | solution.py:37
  89.7 9.0 %collective-permute-start.15 = (bf16[1,128,2048]{2,1,0:T(8,128)(2,1)S(1)}, bf16[1,128,2048]{2,1,0:T(8,128)(2,1)S(1)}, u32[]{:S(2)}, u32[]{:S(2)}) collective-permute-start(bf16[1,128,2048]{2,1,0:T(8,128)(2,1)S(1)} %copy-done.2), channel_id=1, source_target_pairs={{0,8},{8,0},{16,24},{24,16},{1,9},{9,1},{17,25},{25,17},{2,10},{10... | collective-permute-start | bytes 1572872 | tf_op jit(solution)/shard_map/ppermute | solution.py:37
  92.0 7.6 %collective-permute-start.16 = (bf16[1,128,2048]{2,1,0:T(8,128)(2,1)}, bf16[1,128,2048]{2,1,0:T(8,128)(2,1)S(1)}, u32[]{:S(2)}, u32[]{:S(2)}) collective-permute-start(bf16[1,128,2048]{2,1,0:T(8,128)(2,1)} %collective-permute-done.8), channel_id=1, source_target_pairs={{0,8},{8,0},{16,24},{24,16},{1,9},{9,1},{17,25},{25,17},{2,10},{10... | collective-permute-start | bytes 1572872 | tf_op jit(solution)/shard_map/ppermute | solution.py:37
  111.3 6.6 %copy-start.4 = (pred[128,128]{1,0:T(8,128)(4,1)S(1)}, pred[128,128]{1,0:T(8,128)(4,1)}, u32[]{:S(2)}) copy-start(pred[128,128]{1,0:T(8,128)(4,1)} %iota_compare_fusion) | copy-start | bytes 49156
  117.9 6.0 %copy-start.5 = (s32[6]{0:T(128)S(1)}, s32[6]{0:T(128)}, u32[]{:S(2)}) copy-start(s32[6]{0:T(128)} %param.6) | copy-start | bytes 76

commit v5 on v4

--- a/solution.py
+++ b/solution.py
@@ -2,6 +2,8 @@
 import jax.numpy as jnp
 from jax import lax
 from jax.sharding import PartitionSpec as P
+from jax.experimental import pallas as pl
+from jax.experimental.pallas import tpu as pltpu
 
 ITERS = 3
 
@@ -25,11 +27,44 @@
     return theta.astype(jnp.bfloat16)
 
 
-def block_energy(theta, vectors):
-    blocks = jnp.einsum("gin,wnj->wgij", vectors, theta, preferred_element_type=jnp.float32)
-    traces = jnp.einsum("wgii->wg", blocks)
-    crossed = jnp.sum(blocks * jnp.swapaxes(blocks, 2, 3), axis=(2, 3))
-    return 0.5 * jnp.sum(traces * traces - crossed, axis=1)
+def energy_kernel(*refs):
+    theta_ref = refs[0]
+    chol_refs = refs[1:-1]
+    out_ref = refs[-1]
+    n_slot, _, electrons = theta_ref.shape
+    rows = lax.broadcasted_iota(jnp.int32, (electrons, electrons), 0)
+    cols = lax.broadcasted_iota(jnp.int32, (electrons, electrons), 1)
+    diagonal = rows == cols
+    out_ref[...] = jnp.zeros(out_ref.shape, jnp.float32)
+    for chol_ref in chol_refs:
+        def per_vector(g, carry, chol_ref=chol_ref):
+            vector = chol_ref[g]
+
+            def per_slot(s, inner):
+                blocks = jnp.dot(vector, theta_ref[s], preferred_element_type=jnp.float32)
+                trace = jnp.sum(jnp.where(diagonal, blocks, 0.0), keepdims=True)
+                crossed = jnp.sum(blocks * blocks.T, keepdims=True)
+                value = 0.5 * (trace * trace - crossed)
+                out_ref[pl.ds(s, 1), :] += jnp.broadcast_to(value, (1, out_ref.shape[1]))
+                return inner
+
+            return lax.fori_loop(0, n_slot, per_slot, carry)
+
+        lax.fori_loop(0, chol_ref.shape[0], per_vector, 0)
+
+
+def block_energy(theta, pieces):
+    n_slot = theta.shape[0]
+    vmem = pltpu.MemorySpace.VMEM
+    held = sum(p.size * p.dtype.itemsize for p in pieces) + theta.size * theta.dtype.itemsize
+    out = pl.pallas_call(
+        energy_kernel,
+        out_shape=jax.ShapeDtypeStruct((n_slot, 128), jnp.float32),
+        in_specs=[pl.BlockSpec(memory_space=vmem)] * (1 + len(pieces)),
+        out_specs=pl.BlockSpec(memory_space=vmem),
+        compiler_params=pltpu.CompilerParams(vmem_limit_bytes=int(held + (16 << 20))),
+    )(theta, *pieces)
+    return out[:, 0]
 
 
 def swap_pairs(x, axis, size, bit):
@@ -100,10 +135,9 @@
     if theta is None:
         diagonal_peer = swap_pairs(across, "walk", n_walk, 1)
         new_walkers, theta = kick(old_walkers, beside, across, diagonal_peer, parent, field, walk_id)
-    vectors = jnp.concatenate([half_chol] + pieces + handed, axis=0)
 
     living = parent >= 0
-    energy = block_energy(theta, vectors)
+    energy = block_energy(theta, [half_chol] + pieces + handed)
     energy = jnp.where(living, energy, 0.0)
     return (new_walkers, energy)
 

time: 125 us -> 135 us (1.080)
  Pallas kernels: 0 us -> 48.2 us
  local copies, waits for them, and re-layouts: 42.8 us -> 15.8 us
  matrix products: 19.8 us -> 8.36 us
  waiting for transfers between devices: 30.5 us -> 36.6 us
  other arithmetic: 18.1 us -> 12.6 us
    pallas_call x0 -> x1, Pallas kernels: none -> 48.2 us  [block_energy(): pl.pallas_call(energy_kernel, out_shape=jax.ShapeDtypeStruct((n_slot, 128...]
    unnamed x26 -> x10, local copies, waits for them, and re-layouts: 21.1 us -> 1.73 us
    dot_general x1 -> x0, matrix products: 10.9 us -> none  [block_energy(): jnp.einsum('gin,wnj->wgij', vectors, theta, preferred_element_type=jnp.fl...]
    dot_general x1 -> x0, local copies, waits for them, and re-layouts: 6.6 us -> none  [block_energy(): jnp.einsum('gin,wnj->wgij', vectors, theta, preferred_element_type=jnp.fl...]
    reduce_sum x2 -> x0, other arithmetic: 5.99 us -> none  [the longest x1 5.87 us: block_energy(): traces = jnp.einsum('wgii->wg', blocks)]
    ppermute x4, waiting for transfers between devices: 26.5 us -> 29.6 us  [body(): ahead = lax.ppermute(ahead, 'chol', forward)]
    ppermute x10, waiting for transfers between devices: 0.03 us -> 2.89 us  [swap_pairs(): return lax.ppermute(x, axis, perm)]
  transfers between devices with their start and end apart: 17 -> 17, of which waited for: 6 -> 9; matrix products, arithmetic and copies ran while one was open for 41% -> 25% of each run, Pallas kernels for 0% -> 0%
where the time goes in v5:
time: 135 us
  Pallas kernels  48.2 us (36%)
  waiting for transfers between devices  36.6 us (27%)
  local copies, waits for them, and re-layouts  15.8 us (12%)
  other arithmetic  12.6 us (9%)
  starting transfers between devices  12.4 us (9%)
  matrix products  8.36 us (6%)
    pallas_call x1, Pallas kernels, block_energy(): pl.pallas_call(energy_kernel, out_shape=jax.ShapeDtypeStruct((n_slot, 128...  48.2 us
    ppermute x4, waiting for transfers between devices, body(): ahead = lax.ppermute(ahead, 'chol', forward)  29.6 us
    ppermute x4, starting transfers between devices, body(): ahead = lax.ppermute(ahead, 'chol', forward)  7.75 us
    gather x1, local copies, waits for them, and re-layouts, kick(): column[index].astype(jnp.float32)  5.5 us
    select_n x1, other arithmetic, kick(): jnp.where(living[:, None, None], kicked, jnp.zeros_like(kicked))  5.05 us
    slice x1, local copies, waits for them, and re-layouts, green_half(): intersection = widened[:, :electrons, :]  4.72 us
    concatenate x1, other arithmetic, kick(): jnp.concatenate([old_walkers, beside, across, diagonal_peer], axis=0)  4.42 us
    ppermute x3, waiting for transfers between devices, body(): behind = lax.ppermute(behind, 'chol', backward)  4.11 us
  transfers between devices with their start and end apart: 17, of which 9 were waited for; matrix products, arithmetic and copies ran while one was open for 25% of the time, Pallas kernels for 0%

profile of v5, /device:TPU:0, one launch (start us, length us, event | category | flops | bytes accessed | tf_op | source)
XLA Modules:
  0.0 134.8 jit_solution(306553736168879911)
XLA Ops:
  1.7 3.1 %collective-permute-start = (bf16[1,128,2048]{2,1,0:T(8,128)(2,1)S(1)}, bf16[1,128,2048]{2,1,0:T(8,128)(2,1)S(1)}, u32[]{:S(2)}, u32[]{:S(2)}) collective-permute-start(bf16[1,128,2048]{2,1,0:T(8,128)(2,1)S(1)} %constant_dynamic-slice_fusion), channel_id=1, source_target_pairs={{0,2},{2,4},{4,6},{6,7},{7,5},{5,3},{3,1},{1,0},{8,10},{10,12},{12... | collective-permute-start | bytes 1572872 | tf_op jit(solution)/shard_map/ppermute | solution.py:111
  4.8 1.9 %collective-permute-start.6 = (bf16[3,2048,128]{2,1,0:T(8,128)(2,1)}, bf16[3,2048,128]{2,1,0:T(8,128)(2,1)S(1)}, u32[]{:S(2)}, u32[]{:S(2)}) collective-permute-start(bf16[3,2048,128]{2,1,0:T(8,128)(2,1)} %param.4), channel_id=1, source_target_pairs={{0,16},{8,24},{16,0},{24,8},{1,17},{9,25},{17,1},{25,9},{2,18},{10... | collective-permute-start | bytes 4718600 | tf_op jit(solution)/shard_map/ppermute | solution.py:72
  6.8 9.9 %collective-permute-done.refs_2_ = bf16[1,128,2048]{2,1,0:T(8,128)(2,1)S(1)} collective-permute-done((bf16[1,128,2048]{2,1,0:T(8,128)(2,1)S(1)}, bf16[1,128,2048]{2,1,0:T(8,128)(2,1)S(1)}, u32[]{:S(2)}, u32[]{:S(2)}) %collective-permute-start) | collective-permute-done | bytes 524320 | tf_op jit(solution)/shard_map/ppermute | solution.py:111
  16.7 1.5 %collective-permute-done.1.refs_3_ = bf16[1,128,2048]{2,1,0:T(8,128)(2,1)S(1)} collective-permute-done((bf16[1,128,2048]{2,1,0:T(8,128)(2,1)S(1)}, bf16[1,128,2048]{2,1,0:T(8,128)(2,1)S(1)}, u32[]{:S(2)}, u32[]{:S(2)}) %collective-permute-start.1) | collective-permute-done | bytes 524320 | tf_op jit(solution)/shard_map/ppermute | solution.py:114
  18.2 1.6 %collective-permute-start.2 = (bf16[1,128,2048]{2,1,0:T(8,128)(2,1)S(1)}, bf16[1,128,2048]{2,1,0:T(8,128)(2,1)S(1)}, u32[]{:S(2)}, u32[]{:S(2)}) collective-permute-start(bf16[1,128,2048]{2,1,0:T(8,128)(2,1)S(1)} %collective-permute-done.refs_2_), channel_id=1, source_target_pairs={{0,2},{2,4},{4,6},{6,7},{7,5},{5,3},{3,1},{1,0},{8,10},{10,12},{12... | collective-permute-start | bytes 1572872 | tf_op jit(solution)/shard_map/ppermute | solution.py:111
  20.2 10.4 %collective-permute-done.2.refs_4_ = bf16[1,128,2048]{2,1,0:T(8,128)(2,1)S(1)} collective-permute-done((bf16[1,128,2048]{2,1,0:T(8,128)(2,1)S(1)}, bf16[1,128,2048]{2,1,0:T(8,128)(2,1)S(1)}, u32[]{:S(2)}, u32[]{:S(2)}) %collective-permute-start.2) | collective-permute-done | bytes 524320 | tf_op jit(solution)/shard_map/ppermute | solution.py:111
  30.7 1.3 collective-permute-done.3.refs_5_
  32.0 1.6 %collective-permute-start.4 = (bf16[1,128,2048]{2,1,0:T(8,128)(2,1)S(1)}, bf16[1,128,2048]{2,1,0:T(8,128)(2,1)S(1)}, u32[]{:S(2)}, u32[]{:S(2)}) collective-permute-start(bf16[1,128,2048]{2,1,0:T(8,128)(2,1)S(1)} %collective-permute-done.2.refs_4_), channel_id=1, source_target_pairs={{0,2},{2,4},{4,6},{6,7},{7,5},{5,3},{3,1},{1,0},{8,10},{10,12},{12... | collective-permute-start | bytes 1572872 | tf_op jit(solution)/shard_map/ppermute | solution.py:111
  34.0 9.2 %collective-permute-done.4.refs_6_ = bf16[1,128,2048]{2,1,0:T(8,128)(2,1)S(1)} collective-permute-done((bf16[1,128,2048]{2,1,0:T(8,128)(2,1)S(1)}, bf16[1,128,2048]{2,1,0:T(8,128)(2,1)S(1)}, u32[]{:S(2)}, u32[]{:S(2)}) %collective-permute-start.4) | collective-permute-done | bytes 524320 | tf_op jit(solution)/shard_map/ppermute | solution.py:111
  43.2 1.3 collective-permute-done.5.refs_7_
  49.1 1.5 %collective-permute-start.8 = (bf16[1,128,2048]{2,1,0:T(8,128)(2,1)S(1)}, bf16[1,128,2048]{2,1,0:T(8,128)(2,1)}, u32[]{:S(2)}, u32[]{:S(2)}) collective-permute-start(bf16[1,128,2048]{2,1,0:T(8,128)(2,1)S(1)} %collective-permute-done.4.refs_6_), channel_id=1, source_target_pairs={{0,2},{2,4},{4,6},{6,7},{7,5},{5,3},{3,1},{1,0},{8,10},{10,12},{12... | collective-permute-start | bytes 1572872 | tf_op jit(solution)/shard_map/ppermute | solution.py:111
  50.6 4.4 %pad_maximum_fusion = bf16[12,2048,128]{2,1,0:T(8,128)(2,1)} fusion(bf16[3,2048,128]{2,1,0:T(8,128)(2,1)S(1)} %collective-permute-done.9, bf16[3,2048,128]{2,1,0:T(8,128)(2,1)S(1)} %collective-permute-done.6, bf16[3,2048,128]{2,1,0:T(8,128)(2,1)S(1)} %collective-permute-done.7, bf16[3,2048,128]{2,1,0:T(8,128)(2,1)} %param.4), kind=kLoop, calls=%fused_computation.2 | loop fusion | flops 9437184 | bytes 12582912 | tf_op jit(solution)/shard_map/concatenate | solution.py:77
  55.0 5.5 %gather_fusion = bf16[6,2048,128]{2,1,0:T(8,128)(2,1)} fusion(bf16[12,2048,128]{2,1,0:T(8,128)(2,1)} %pad_maximum_fusion, s32[1024]{0:T(1024)S(1)} %pad_clamp_fusion), kind=kCustom, calls=%fused_computation | custom fusion | bytes 6291480 | tf_op jit(solution)/shard_map/gather | solution.py:82
  60.5 5.1 %broadcast_select_fusion = (bf16[6,2048,128]{2,1,0:T(8,128)(2,1)}, bf16[6,2048,128]{2,1,0:T(8,128)(2,1)S(1)}) fusion(pred[6]{0:T(512)(128)(4,1)S(1)} %broadcast_compare_fusion, bf16[6,2048,128]{2,1,0:T(8,128)(2,1)} %gather_fusion, f32[6,2048]{1,0:T(8,128)S(1)} %exp.3), kind=kLoop, calls=%fused_computation.5 | loop fusion | flops 6291456 | bytes 9486342 | tf_op jit(solution)/shard_map/jit(_where)/select_n | solution.py:83
  65.6 1.7 %copy-done.1 = bf16[6,2048,128]{2,1,0:T(8,128)(2,1)} copy-done((bf16[6,2048,128]{2,1,0:T(8,128)(2,1)}, bf16[6,2048,128]{2,1,0:T(8,128)(2,1)S(1)}, u32[]{:S(2)}) %copy-start.1) | copy-done | bytes 3145752
  67.3 4.7 %copy.10 = f32[6,128,128]{0,2,1:T(8,128)} copy(f32[6,128,128]{2,1,0:T(8,128)S(1)} %slice_convert_fusion) | data formatting | bytes 786432 | tf_op jit(solution)/shard_map/slice | solution.py:14
  72.0 1.8 %gather_fusion.1 = f32[128,6]{1,0:T(8,128)S(1)} fusion(f32[6,128,128]{0,2,1:T(8,128)} %copy.10, s32[128]{0:T(128)S(1)} %or_bitcast_fusion), kind=kCustom, calls=%fused_computation.1 | custom fusion | bytes 7168 | tf_op jit(solution)/shard_map/jit(diagonal)/gather | solution.py:16
  73.9 1.5 %convolution_subtract_fusion.2 = f32[6,128,128]{2,1,0:T(8,128)S(1)} fusion(f32[128,128]{1,0:T(8,128)} %fusion.10, f32[6,128]{1,0:T(8,128)S(1)} %copy.11, f32[128,128]{1,0:T(8,128)} %fusion.11, bf16[6,2048,128]{2,1,0:T(8,128)(2,1)} %copy-done.1), kind=kOutput, calls=%fused_computation.8 | convolution fusion | flops 151191552 | bytes 723968 | tf_op jit(solution)/shard_map/wij,wjk->wik/dot_general | solution.py:19
  75.4 1.4 %fusion = f32[6,128,128]{2,1,0:T(8,128)S(1)} fusion(f32[6,128,128]{2,1,0:T(8,128)S(1)} %convolution_subtract_fusion.2, f32[6,128]{1,0:T(8,128)S(1)} %copy.11, f32[128,128]{1,0:T(8,128)} %fusion.11), kind=kOutput, calls=%fused_computation.9 | convolution fusion | flops 151093248 | bytes 855040 | tf_op jit(solution)/shard_map/wij,wjk->wik/dot_general | solution.py:20
  76.8 1.3 convolution_subtract_fusion.1
  79.5 2.8 %convolution_convert_fusion.refs_0_ = bf16[6,2048,128]{2,1,0:T(8,128)(2,1)S(1)} fusion(bf16[6,2048,128]{2,1,0:T(8,128)(2,1)S(1)} %copy-done.2, f32[6,128,128]{2,1,0:T(8,128)S(1)} %fusion.14), kind=kOutput, calls=%fused_computation.4 | convolution fusion | flops 2417491968 | bytes 6684672 | tf_op jit(solution)/shard_map/wnk,wkj->wnj/dot_general | solution.py:26
  83.1 1.2 collective-permute-done.14.refs_13_
  84.3 1.5 %collective-permute-done.15.refs_14_ = bf16[1,128,2048]{2,1,0:T(8,128)(2,1)S(1)} collective-permute-done((bf16[1,128,2048]{2,1,0:T(8,128)(2,1)S(1)}, bf16[1,128,2048]{2,1,0:T(8,128)(2,1)S(1)}, u32[]{:S(2)}, u32[]{:S(2)}) %collective-permute-start.15) | collective-permute-done | bytes 524320 | tf_op jit(solution)/shard_map/ppermute | solution.py:72
  86.0 48.2 %shard_map.59 = f32[6,128]{1,0:T(8,128)S(1)} custom-call(bf16[6,2048,128]{2,1,0:T(8,128)(2,1)S(1)} %convolution_convert_fusion.refs_0_, bf16[2,128,2048]{2,1,0:T(8,128)(2,1)S(1)} %copy-done, bf16[1,128,2048]{2,1,0:T(8,128)(2,1)S(1)} %collective-permute-done.refs_2_, bf16[1,128,2048]{2,1,0:T(8,128)(2,1)S(1)} %collective-permute-done.1.refs_3_, ...), custom_call_target="tpu_custom_call" | custom-call | tf_op jit(solution)/shard_map/pallas_call | solution.py:60
  (45 shorter events, 9.7 us)
Async XLA Ops:
  1.7 14.9 %collective-permute-start = (bf16[1,128,2048]{2,1,0:T(8,128)(2,1)S(1)}, bf16[1,128,2048]{2,1,0:T(8,128)(2,1)S(1)}, u32[]{:S(2)}, u32[]{:S(2)}) collective-permute-start(bf16[1,128,2048]{2,1,0:T(8,128)(2,1)S(1)} %constant_dynamic-slice_fusion), channel_id=1, source_target_pairs={{0,2},{2,4},{4,6},{6,7},{7,5},{5,3},{3,1},{1,0},{8,10},{10,12},{12... | collective-permute-start | bytes 1572872 | tf_op jit(solution)/shard_map/ppermute | solution.py:111
  4.8 13.4 %collective-permute-start.1 = (bf16[1,128,2048]{2,1,0:T(8,128)(2,1)S(1)}, bf16[1,128,2048]{2,1,0:T(8,128)(2,1)S(1)}, u32[]{:S(2)}, u32[]{:S(2)}) collective-permute-start(bf16[1,128,2048]{2,1,0:T(8,128)(2,1)S(1)} %constant_dynamic-slice_fusion), channel_id=1, source_target_pairs={{2,0},{4,2},{6,4},{7,6},{5,7},{3,5},{1,3},{0,1},{10,8},{12,10},{14... | collective-permute-start | bytes 1572872 | tf_op jit(solution)/shard_map/ppermute | solution.py:114
  4.8 39.7 %collective-permute-start.6 = (bf16[3,2048,128]{2,1,0:T(8,128)(2,1)}, bf16[3,2048,128]{2,1,0:T(8,128)(2,1)S(1)}, u32[]{:S(2)}, u32[]{:S(2)}) collective-permute-start(bf16[3,2048,128]{2,1,0:T(8,128)(2,1)} %param.4), channel_id=1, source_target_pairs={{0,16},{8,24},{16,0},{24,8},{1,17},{9,25},{17,1},{25,9},{2,18},{10... | collective-permute-start | bytes 4718600 | tf_op jit(solution)/shard_map/ppermute | solution.py:72
  6.8 37.8 %collective-permute-start.7 = (bf16[3,2048,128]{2,1,0:T(8,128)(2,1)}, bf16[3,2048,128]{2,1,0:T(8,128)(2,1)S(1)}, u32[]{:S(2)}, u32[]{:S(2)}) collective-permute-start(bf16[3,2048,128]{2,1,0:T(8,128)(2,1)} %param.4), channel_id=1, source_target_pairs={{0,8},{8,0},{16,24},{24,16},{1,9},{9,1},{17,25},{25,17},{2,10},{10... | collective-permute-start | bytes 4718600 | tf_op jit(solution)/shard_map/ppermute | solution.py:72
  18.2 12.5 %collective-permute-start.2 = (bf16[1,128,2048]{2,1,0:T(8,128)(2,1)S(1)}, bf16[1,128,2048]{2,1,0:T(8,128)(2,1)S(1)}, u32[]{:S(2)}, u32[]{:S(2)}) collective-permute-start(bf16[1,128,2048]{2,1,0:T(8,128)(2,1)S(1)} %collective-permute-done.refs_2_), channel_id=1, source_target_pairs={{0,2},{2,4},{4,6},{6,7},{7,5},{5,3},{3,1},{1,0},{8,10},{10,12},{12... | collective-permute-start | bytes 1572872 | tf_op jit(solution)/shard_map/ppermute | solution.py:111
  19.8 12.2 %collective-permute-start.3 = (bf16[1,128,2048]{2,1,0:T(8,128)(2,1)S(1)}, bf16[1,128,2048]{2,1,0:T(8,128)(2,1)S(1)}, u32[]{:S(2)}, u32[]{:S(2)}) collective-permute-start(bf16[1,128,2048]{2,1,0:T(8,128)(2,1)S(1)} %collective-permute-done.1.refs_3_), channel_id=1, source_target_pairs={{2,0},{4,2},{6,4},{7,6},{5,7},{3,5},{1,3},{0,1},{10,8},{12,10},{14... | collective-permute-start | bytes 1572872 | tf_op jit(solution)/shard_map/ppermute | solution.py:114
  32.0 11.3 %collective-permute-start.4 = (bf16[1,128,2048]{2,1,0:T(8,128)(2,1)S(1)}, bf16[1,128,2048]{2,1,0:T(8,128)(2,1)S(1)}, u32[]{:S(2)}, u32[]{:S(2)}) collective-permute-start(bf16[1,128,2048]{2,1,0:T(8,128)(2,1)S(1)} %collective-permute-done.2.refs_4_), channel_id=1, source_target_pairs={{0,2},{2,4},{4,6},{6,7},{7,5},{5,3},{3,1},{1,0},{8,10},{10,12},{12... | collective-permute-start | bytes 1572872 | tf_op jit(solution)/shard_map/ppermute | solution.py:111
  33.5 11.0 %collective-permute-start.5 = (bf16[1,128,2048]{2,1,0:T(8,128)(2,1)S(1)}, bf16[1,128,2048]{2,1,0:T(8,128)(2,1)S(1)}, u32[]{:S(2)}, u32[]{:S(2)}) collective-permute-start(bf16[1,128,2048]{2,1,0:T(8,128)(2,1)S(1)} %collective-permute-done.3.refs_5_), channel_id=1, source_target_pairs={{2,0},{4,2},{6,4},{7,6},{5,7},{3,5},{1,3},{0,1},{10,8},{12,10},{14... | collective-permute-start | bytes 1572872 | tf_op jit(solution)/shard_map/ppermute | solution.py:114
  44.5 4.5 %collective-permute-start.9 = (bf16[3,2048,128]{2,1,0:T(8,128)(2,1)S(1)}, bf16[3,2048,128]{2,1,0:T(8,128)(2,1)S(1)}, u32[]{:S(2)}, u32[]{:S(2)}) collective-permute-start(bf16[3,2048,128]{2,1,0:T(8,128)(2,1)S(1)} %collective-permute-done.6), channel_id=1, source_target_pairs={{0,8},{8,0},{16,24},{24,16},{1,9},{9,1},{17,25},{25,17},{2,10},{10... | collective-permute-start | bytes 4718600 | tf_op jit(solution)/shard_map/ppermute | solution.py:72
  48.1 34.6 %collective-permute-start.10 = (bf16[1,128,2048]{2,1,0:T(8,128)(2,1)S(1)}, bf16[1,128,2048]{2,1,0:T(8,128)(2,1)}, u32[]{:S(2)}, u32[]{:S(2)}) collective-permute-start(bf16[1,128,2048]{2,1,0:T(8,128)(2,1)S(1)} %collective-permute-done.refs_2_), channel_id=1, source_target_pairs={{0,8},{8,0},{16,24},{24,16},{1,9},{9,1},{17,25},{25,17},{2,10},{10... | collective-permute-start | bytes 1572872 | tf_op jit(solution)/shard_map/ppermute | solution.py:72
  48.6 34.4 %collective-permute-start.11 = (bf16[1,128,2048]{2,1,0:T(8,128)(2,1)S(1)}, bf16[1,128,2048]{2,1,0:T(8,128)(2,1)}, u32[]{:S(2)}, u32[]{:S(2)}) collective-permute-start(bf16[1,128,2048]{2,1,0:T(8,128)(2,1)S(1)} %collective-permute-done.1.refs_3_), channel_id=1, source_target_pairs={{0,8},{8,0},{16,24},{24,16},{1,9},{9,1},{17,25},{25,17},{2,10},{10... | collective-permute-start | bytes 1572872 | tf_op jit(solution)/shard_map/ppermute | solution.py:72
  48.6 34.6 %collective-permute-start.12 = (bf16[1,128,2048]{2,1,0:T(8,128)(2,1)S(1)}, bf16[1,128,2048]{2,1,0:T(8,128)(2,1)}, u32[]{:S(2)}, u32[]{:S(2)}) collective-permute-start(bf16[1,128,2048]{2,1,0:T(8,128)(2,1)S(1)} %collective-permute-done.2.refs_4_), channel_id=1, source_target_pairs={{0,8},{8,0},{16,24},{24,16},{1,9},{9,1},{17,25},{25,17},{2,10},{10... | collective-permute-start | bytes 1572872 | tf_op jit(solution)/shard_map/ppermute | solution.py:72
  49.1 34.1 %collective-permute-start.13 = (bf16[1,128,2048]{2,1,0:T(8,128)(2,1)S(1)}, bf16[1,128,2048]{2,1,0:T(8,128)(2,1)}, u32[]{:S(2)}, u32[]{:S(2)}) collective-permute-start(bf16[1,128,2048]{2,1,0:T(8,128)(2,1)S(1)} %collective-permute-done.3.refs_5_), channel_id=1, source_target_pairs={{0,8},{8,0},{16,24},{24,16},{1,9},{9,1},{17,25},{25,17},{2,10},{10... | collective-permute-start | bytes 1572872 | tf_op jit(solution)/shard_map/ppermute | solution.py:72
  49.1 33.2 %collective-permute-start.8 = (bf16[1,128,2048]{2,1,0:T(8,128)(2,1)S(1)}, bf16[1,128,2048]{2,1,0:T(8,128)(2,1)}, u32[]{:S(2)}, u32[]{:S(2)}) collective-permute-start(bf16[1,128,2048]{2,1,0:T(8,128)(2,1)S(1)} %collective-permute-done.4.refs_6_), channel_id=1, source_target_pairs={{0,2},{2,4},{4,6},{6,7},{7,5},{5,3},{3,1},{1,0},{8,10},{10,12},{12... | collective-permute-start | bytes 1572872 | tf_op jit(solution)/shard_map/ppermute | solution.py:111
  65.6 1.7 %copy-start.1 = (bf16[6,2048,128]{2,1,0:T(8,128)(2,1)}, bf16[6,2048,128]{2,1,0:T(8,128)(2,1)S(1)}, u32[]{:S(2)}) copy-start(bf16[6,2048,128]{2,1,0:T(8,128)(2,1)S(1)} %get-tuple-element.27) | copy-start | bytes 9437188
  72.0 4.7 %copy-start.3 = (f32[128,128]{1,0:T(8,128)S(1)}, f32[128,128]{1,0:T(8,128)}, u32[]{:S(2)}) copy-start(f32[128,128]{1,0:T(8,128)} %fusion.10) | copy-start | bytes 196612
  73.9 4.7 %copy-start.2 = (bf16[6,2048,128]{2,1,0:T(8,128)(2,1)S(1)}, bf16[6,2048,128]{2,1,0:T(8,128)(2,1)}, u32[]{:S(2)}) copy-start(bf16[6,2048,128]{2,1,0:T(8,128)(2,1)} %copy-done.1) | copy-start | bytes 9437188
  79.5 6.5 %copy-start = (bf16[2,128,2048]{2,1,0:T(8,128)(2,1)S(1)}, bf16[2,128,2048]{2,1,0:T(8,128)(2,1)}, u32[]{:S(2)}) copy-start(bf16[2,128,2048]{2,1,0:T(8,128)(2,1)} %refs_1_.1) | copy-start | bytes 3145732
  82.3 2.0 %collective-permute-start.14 = (bf16[1,128,2048]{2,1,0:T(8,128)(2,1)S(1)}, bf16[1,128,2048]{2,1,0:T(8,128)(2,1)S(1)}, u32[]{:S(2)}, u32[]{:S(2)}) collective-permute-start(bf16[1,128,2048]{2,1,0:T(8,128)(2,1)S(1)} %collective-permute-done.4.refs_6_), channel_id=1, source_target_pairs={{0,8},{8,0},{16,24},{24,16},{1,9},{9,1},{17,25},{25,17},{2,10},{10... | collective-permute-start | bytes 1572872 | tf_op jit(solution)/shard_map/ppermute | solution.py:72
  82.6 51.7 %copy-start.4 = (s32[6]{0:T(128)S(1)}, s32[6]{0:T(128)}, u32[]{:S(2)}) copy-start(s32[6]{0:T(128)} %param.6) | copy-start | bytes 76
  82.6 3.2 %collective-permute-start.15 = (bf16[1,128,2048]{2,1,0:T(8,128)(2,1)S(1)}, bf16[1,128,2048]{2,1,0:T(8,128)(2,1)S(1)}, u32[]{:S(2)}, u32[]{:S(2)}) collective-permute-start(bf16[1,128,2048]{2,1,0:T(8,128)(2,1)S(1)} %collective-permute-done.5.refs_7_), channel_id=1, source_target_pairs={{0,8},{8,0},{16,24},{24,16},{1,9},{9,1},{17,25},{25,17},{2,10},{10... | collective-permute-start | bytes 1572872 | tf_op jit(solution)/shard_map/ppermute | solution.py:72
  82.9 3.1 %collective-permute-start.16 = (bf16[1,128,2048]{2,1,0:T(8,128)(2,1)}, bf16[1,128,2048]{2,1,0:T(8,128)(2,1)S(1)}, u32[]{:S(2)}, u32[]{:S(2)}) collective-permute-start(bf16[1,128,2048]{2,1,0:T(8,128)(2,1)} %collective-permute-done.8.refs_8_), channel_id=1, source_target_pairs={{0,8},{8,0},{16,24},{24,16},{1,9},{9,1},{17,25},{25,17},{2,10},{10... | collective-permute-start | bytes 1572872 | tf_op jit(solution)/shard_map/ppermute | solution.py:72

commit v6 on v5

--- a/solution.py
+++ b/solution.py
@@ -29,32 +29,34 @@
 
 def energy_kernel(*refs):
     theta_ref = refs[0]
-    chol_refs = refs[1:-1]
-    out_ref = refs[-1]
+    chol_refs = refs[1:-3]
+    out_ref, crossed_ref, square_ref = refs[-3:]
     n_slot, _, electrons = theta_ref.shape
+    lanes = out_ref.shape[1]
     rows = lax.broadcasted_iota(jnp.int32, (electrons, electrons), 0)
     cols = lax.broadcasted_iota(jnp.int32, (electrons, electrons), 1)
     diagonal = rows == cols
-    out_ref[...] = jnp.zeros(out_ref.shape, jnp.float32)
+    crossed_ref[...] = jnp.zeros(crossed_ref.shape, jnp.float32)
+    square_ref[...] = jnp.zeros(square_ref.shape, jnp.float32)
     for chol_ref in chol_refs:
         def per_vector(g, carry, chol_ref=chol_ref):
             vector = chol_ref[g]
-
-            def per_slot(s, inner):
+            for s in range(n_slot):
                 blocks = jnp.dot(vector, theta_ref[s], preferred_element_type=jnp.float32)
-                trace = jnp.sum(jnp.where(diagonal, blocks, 0.0), keepdims=True)
-                crossed = jnp.sum(blocks * blocks.T, keepdims=True)
-                value = 0.5 * (trace * trace - crossed)
-                out_ref[pl.ds(s, 1), :] += jnp.broadcast_to(value, (1, out_ref.shape[1]))
-                return inner
-
-            return lax.fori_loop(0, n_slot, per_slot, carry)
+                crossed_ref[s] += blocks * blocks.T
+                diag = jnp.sum(jnp.where(diagonal, blocks, 0.0), axis=0, keepdims=True)
+                trace = jnp.sum(diag, axis=1, keepdims=True)
+                square_ref[pl.ds(s, 1), :] += jnp.broadcast_to(trace * trace, (1, lanes))
+            return carry
 
         lax.fori_loop(0, chol_ref.shape[0], per_vector, 0)
+    for s in range(n_slot):
+        crossed = jnp.sum(crossed_ref[s], keepdims=True)
+        out_ref[pl.ds(s, 1), :] = 0.5 * (square_ref[pl.ds(s, 1), :] - jnp.broadcast_to(crossed, (1, lanes)))
 
 
 def block_energy(theta, pieces):
-    n_slot = theta.shape[0]
+    n_slot, _, electrons = theta.shape
     vmem = pltpu.MemorySpace.VMEM
     held = sum(p.size * p.dtype.itemsize for p in pieces) + theta.size * theta.dtype.itemsize
     out = pl.pallas_call(
@@ -62,6 +64,10 @@
         out_shape=jax.ShapeDtypeStruct((n_slot, 128), jnp.float32),
         in_specs=[pl.BlockSpec(memory_space=vmem)] * (1 + len(pieces)),
         out_specs=pl.BlockSpec(memory_space=vmem),
+        scratch_shapes=[
+            pltpu.VMEM((n_slot, electrons, electrons), jnp.float32),
+            pltpu.VMEM((n_slot, 128), jnp.float32),
+        ],
         compiler_params=pltpu.CompilerParams(vmem_limit_bytes=int(held + (16 << 20))),
     )(theta, *pieces)
     return out[:, 0]

time: 135 us -> 103 us (0.76)
  Pallas kernels: 48.2 us -> 16 us
    pallas_call x1, Pallas kernels: 48.2 us -> 16 us  [block_energy(): pl.pallas_call(energy_kernel, out_shape=jax.ShapeDtypeStruct((n_slot, 128...]
  transfers between devices with their start and end apart: 17 -> 17, of which waited for: 9 -> 9; matrix products, arithmetic and copies ran while one was open for 25% -> 33% of each run, Pallas kernels for 0% -> 0%
where the time goes in v6:
time: 103 us
  waiting for transfers between devices  36.6 us (36%)
  Pallas kernels  16 us (16%)
  local copies, waits for them, and re-layouts  15.8 us (15%)
  other arithmetic  12.6 us (12%)
  starting transfers between devices  12.4 us (12%)
  matrix products  8.37 us (8%)
    ppermute x4, waiting for transfers between devices, body(): ahead = lax.ppermute(ahead, 'chol', forward)  29.6 us
    pallas_call x1, Pallas kernels, block_energy(): pl.pallas_call(energy_kernel, out_shape=jax.ShapeDtypeStruct((n_slot, 128...  16 us
    ppermute x4, starting transfers between devices, body(): ahead = lax.ppermute(ahead, 'chol', forward)  7.75 us
    gather x1, local copies, waits for them, and re-layouts, kick(): column[index].astype(jnp.float32)  5.5 us
    select_n x1, other arithmetic, kick(): jnp.where(living[:, None, None], kicked, jnp.zeros_like(kicked))  5.05 us
    slice x1, local copies, waits for them, and re-layouts, green_half(): intersection = widened[:, :electrons, :]  4.72 us
    concatenate x1, other arithmetic, kick(): jnp.concatenate([old_walkers, beside, across, diagonal_peer], axis=0)  4.42 us
    ppermute x3, waiting for transfers between devices, body(): behind = lax.ppermute(behind, 'chol', backward)  4.11 us
  transfers between devices with their start and end apart: 17, of which 9 were waited for; matrix products, arithmetic and copies ran while one was open for 33% of the time, Pallas kernels for 0%

profile of v6, /device:TPU:0, one launch (start us, length us, event | category | flops | bytes accessed | tf_op | source)
XLA Modules:
  0.0 102.6 jit_solution(6881486776178071881)
XLA Ops:
  1.7 3.1 %collective-permute-start = (bf16[1,128,2048]{2,1,0:T(8,128)(2,1)S(1)}, bf16[1,128,2048]{2,1,0:T(8,128)(2,1)S(1)}, u32[]{:S(2)}, u32[]{:S(2)}) collective-permute-start(bf16[1,128,2048]{2,1,0:T(8,128)(2,1)S(1)} %constant_dynamic-slice_fusion), channel_id=1, source_target_pairs={{0,2},{2,4},{4,6},{6,7},{7,5},{5,3},{3,1},{1,0},{8,10},{10,12},{12... | collective-permute-start | bytes 1572872 | tf_op jit(solution)/shard_map/ppermute | solution.py:117
  4.8 1.9 %collective-permute-start.6 = (bf16[3,2048,128]{2,1,0:T(8,128)(2,1)}, bf16[3,2048,128]{2,1,0:T(8,128)(2,1)S(1)}, u32[]{:S(2)}, u32[]{:S(2)}) collective-permute-start(bf16[3,2048,128]{2,1,0:T(8,128)(2,1)} %param.4), channel_id=1, source_target_pairs={{0,16},{8,24},{16,0},{24,8},{1,17},{9,25},{17,1},{25,9},{2,18},{10... | collective-permute-start | bytes 4718600 | tf_op jit(solution)/shard_map/ppermute | solution.py:78
  6.8 9.9 %collective-permute-done.refs_2_ = bf16[1,128,2048]{2,1,0:T(8,128)(2,1)S(1)} collective-permute-done((bf16[1,128,2048]{2,1,0:T(8,128)(2,1)S(1)}, bf16[1,128,2048]{2,1,0:T(8,128)(2,1)S(1)}, u32[]{:S(2)}, u32[]{:S(2)}) %collective-permute-start) | collective-permute-done | bytes 524320 | tf_op jit(solution)/shard_map/ppermute | solution.py:117
  16.7 1.5 %collective-permute-done.1.refs_3_ = bf16[1,128,2048]{2,1,0:T(8,128)(2,1)S(1)} collective-permute-done((bf16[1,128,2048]{2,1,0:T(8,128)(2,1)S(1)}, bf16[1,128,2048]{2,1,0:T(8,128)(2,1)S(1)}, u32[]{:S(2)}, u32[]{:S(2)}) %collective-permute-start.1) | collective-permute-done | bytes 524320 | tf_op jit(solution)/shard_map/ppermute | solution.py:120
  18.2 1.6 %collective-permute-start.2 = (bf16[1,128,2048]{2,1,0:T(8,128)(2,1)S(1)}, bf16[1,128,2048]{2,1,0:T(8,128)(2,1)S(1)}, u32[]{:S(2)}, u32[]{:S(2)}) collective-permute-start(bf16[1,128,2048]{2,1,0:T(8,128)(2,1)S(1)} %collective-permute-done.refs_2_), channel_id=1, source_target_pairs={{0,2},{2,4},{4,6},{6,7},{7,5},{5,3},{3,1},{1,0},{8,10},{10,12},{12... | collective-permute-start | bytes 1572872 | tf_op jit(solution)/shard_map/ppermute | solution.py:117
  20.2 10.4 %collective-permute-done.2.refs_4_ = bf16[1,128,2048]{2,1,0:T(8,128)(2,1)S(1)} collective-permute-done((bf16[1,128,2048]{2,1,0:T(8,128)(2,1)S(1)}, bf16[1,128,2048]{2,1,0:T(8,128)(2,1)S(1)}, u32[]{:S(2)}, u32[]{:S(2)}) %collective-permute-start.2) | collective-permute-done | bytes 524320 | tf_op jit(solution)/shard_map/ppermute | solution.py:117
  30.7 1.3 %collective-permute-done.3.refs_5_ = bf16[1,128,2048]{2,1,0:T(8,128)(2,1)S(1)} collective-permute-done((bf16[1,128,2048]{2,1,0:T(8,128)(2,1)S(1)}, bf16[1,128,2048]{2,1,0:T(8,128)(2,1)S(1)}, u32[]{:S(2)}, u32[]{:S(2)}) %collective-permute-start.3) | collective-permute-done | bytes 524320 | tf_op jit(solution)/shard_map/ppermute | solution.py:120
  32.0 1.6 %collective-permute-start.4 = (bf16[1,128,2048]{2,1,0:T(8,128)(2,1)S(1)}, bf16[1,128,2048]{2,1,0:T(8,128)(2,1)S(1)}, u32[]{:S(2)}, u32[]{:S(2)}) collective-permute-start(bf16[1,128,2048]{2,1,0:T(8,128)(2,1)S(1)} %collective-permute-done.2.refs_4_), channel_id=1, source_target_pairs={{0,2},{2,4},{4,6},{6,7},{7,5},{5,3},{3,1},{1,0},{8,10},{10,12},{12... | collective-permute-start | bytes 1572872 | tf_op jit(solution)/shard_map/ppermute | solution.py:117
  34.0 9.2 %collective-permute-done.4.refs_6_ = bf16[1,128,2048]{2,1,0:T(8,128)(2,1)S(1)} collective-permute-done((bf16[1,128,2048]{2,1,0:T(8,128)(2,1)S(1)}, bf16[1,128,2048]{2,1,0:T(8,128)(2,1)S(1)}, u32[]{:S(2)}, u32[]{:S(2)}) %collective-permute-start.4) | collective-permute-done | bytes 524320 | tf_op jit(solution)/shard_map/ppermute | solution.py:117
  43.2 1.3 %collective-permute-done.5.refs_7_ = bf16[1,128,2048]{2,1,0:T(8,128)(2,1)S(1)} collective-permute-done((bf16[1,128,2048]{2,1,0:T(8,128)(2,1)S(1)}, bf16[1,128,2048]{2,1,0:T(8,128)(2,1)S(1)}, u32[]{:S(2)}, u32[]{:S(2)}) %collective-permute-start.5) | collective-permute-done | bytes 524320 | tf_op jit(solution)/shard_map/ppermute | solution.py:120
  49.1 1.5 %collective-permute-start.8 = (bf16[1,128,2048]{2,1,0:T(8,128)(2,1)S(1)}, bf16[1,128,2048]{2,1,0:T(8,128)(2,1)}, u32[]{:S(2)}, u32[]{:S(2)}) collective-permute-start(bf16[1,128,2048]{2,1,0:T(8,128)(2,1)S(1)} %collective-permute-done.4.refs_6_), channel_id=1, source_target_pairs={{0,2},{2,4},{4,6},{6,7},{7,5},{5,3},{3,1},{1,0},{8,10},{10,12},{12... | collective-permute-start | bytes 1572872 | tf_op jit(solution)/shard_map/ppermute | solution.py:117
  50.6 4.4 %pad_maximum_fusion = bf16[12,2048,128]{2,1,0:T(8,128)(2,1)} fusion(bf16[3,2048,128]{2,1,0:T(8,128)(2,1)S(1)} %collective-permute-done.9, bf16[3,2048,128]{2,1,0:T(8,128)(2,1)S(1)} %collective-permute-done.6, bf16[3,2048,128]{2,1,0:T(8,128)(2,1)S(1)} %collective-permute-done.7, bf16[3,2048,128]{2,1,0:T(8,128)(2,1)} %param.4), kind=kLoop, calls=%fused_computation.2 | loop fusion | flops 9437184 | bytes 12582912 | tf_op jit(solution)/shard_map/concatenate | solution.py:83
  55.0 5.5 %gather_fusion = bf16[6,2048,128]{2,1,0:T(8,128)(2,1)} fusion(bf16[12,2048,128]{2,1,0:T(8,128)(2,1)} %pad_maximum_fusion, s32[1024]{0:T(1024)S(1)} %pad_clamp_fusion), kind=kCustom, calls=%fused_computation | custom fusion | bytes 6291480 | tf_op jit(solution)/shard_map/gather | solution.py:88
  60.5 5.1 %broadcast_select_fusion = (bf16[6,2048,128]{2,1,0:T(8,128)(2,1)}, bf16[6,2048,128]{2,1,0:T(8,128)(2,1)S(1)}) fusion(pred[6]{0:T(512)(128)(4,1)S(1)} %broadcast_compare_fusion, bf16[6,2048,128]{2,1,0:T(8,128)(2,1)} %gather_fusion, f32[6,2048]{1,0:T(8,128)S(1)} %exp.3), kind=kLoop, calls=%fused_computation.5 | loop fusion | flops 6291456 | bytes 9486342 | tf_op jit(solution)/shard_map/jit(_where)/select_n | solution.py:89
  65.6 1.7 %copy-done.1 = bf16[6,2048,128]{2,1,0:T(8,128)(2,1)} copy-done((bf16[6,2048,128]{2,1,0:T(8,128)(2,1)}, bf16[6,2048,128]{2,1,0:T(8,128)(2,1)S(1)}, u32[]{:S(2)}) %copy-start.1) | copy-done | bytes 3145752
  67.3 4.7 %copy.10 = f32[6,128,128]{0,2,1:T(8,128)} copy(f32[6,128,128]{2,1,0:T(8,128)S(1)} %slice_convert_fusion) | data formatting | bytes 786432 | tf_op jit(solution)/shard_map/slice | solution.py:14
  72.0 1.8 %gather_fusion.1 = f32[128,6]{1,0:T(8,128)S(1)} fusion(f32[6,128,128]{0,2,1:T(8,128)} %copy.10, s32[128]{0:T(128)S(1)} %or_bitcast_fusion), kind=kCustom, calls=%fused_computation.1 | custom fusion | bytes 7168 | tf_op jit(solution)/shard_map/jit(diagonal)/gather | solution.py:16
  73.9 1.5 %convolution_subtract_fusion.2 = f32[6,128,128]{2,1,0:T(8,128)S(1)} fusion(f32[128,128]{1,0:T(8,128)} %fusion.10, f32[6,128]{1,0:T(8,128)S(1)} %copy.11, f32[128,128]{1,0:T(8,128)} %fusion.11, bf16[6,2048,128]{2,1,0:T(8,128)(2,1)} %copy-done.1), kind=kOutput, calls=%fused_computation.8 | convolution fusion | flops 151191552 | bytes 723968 | tf_op jit(solution)/shard_map/wij,wjk->wik/dot_general | solution.py:19
  75.4 1.4 %fusion = f32[6,128,128]{2,1,0:T(8,128)S(1)} fusion(f32[6,128,128]{2,1,0:T(8,128)S(1)} %convolution_subtract_fusion.2, f32[6,128]{1,0:T(8,128)S(1)} %copy.11, f32[128,128]{1,0:T(8,128)} %fusion.11), kind=kOutput, calls=%fused_computation.9 | convolution fusion | flops 151093248 | bytes 855040 | tf_op jit(solution)/shard_map/wij,wjk->wik/dot_general | solution.py:20
  76.8 1.3 %convolution_subtract_fusion.1 = f32[6,128,128]{2,1,0:T(8,128)S(1)} fusion(f32[6,128,128]{2,1,0:T(8,128)S(1)} %fusion, f32[128,128]{1,0:T(8,128)S(1)} %copy-done.3, bf16[6,2048,128]{2,1,0:T(8,128)(2,1)} %copy-done.1), kind=kOutput, calls=%fused_computation.7 | convolution fusion | flops 151093248 | bytes 1048576 | tf_op jit(solution)/shard_map/wij,wjk->wik/dot_general | solution.py:19
  79.5 2.8 %convolution_convert_fusion.refs_0_ = bf16[6,2048,128]{2,1,0:T(8,128)(2,1)S(1)} fusion(bf16[6,2048,128]{2,1,0:T(8,128)(2,1)S(1)} %copy-done.2, f32[6,128,128]{2,1,0:T(8,128)S(1)} %fusion.14), kind=kOutput, calls=%fused_computation.4 | convolution fusion | flops 2417491968 | bytes 6684672 | tf_op jit(solution)/shard_map/wnk,wkj->wnj/dot_general | solution.py:26
  83.1 1.2 %collective-permute-done.14.refs_13_ = bf16[1,128,2048]{2,1,0:T(8,128)(2,1)S(1)} collective-permute-done((bf16[1,128,2048]{2,1,0:T(8,128)(2,1)S(1)}, bf16[1,128,2048]{2,1,0:T(8,128)(2,1)S(1)}, u32[]{:S(2)}, u32[]{:S(2)}) %collective-permute-start.14) | collective-permute-done | bytes 524320 | tf_op jit(solution)/shard_map/ppermute | solution.py:78
  84.3 1.5 %collective-permute-done.15.refs_14_ = bf16[1,128,2048]{2,1,0:T(8,128)(2,1)S(1)} collective-permute-done((bf16[1,128,2048]{2,1,0:T(8,128)(2,1)S(1)}, bf16[1,128,2048]{2,1,0:T(8,128)(2,1)S(1)}, u32[]{:S(2)}, u32[]{:S(2)}) %collective-permute-start.15) | collective-permute-done | bytes 524320 | tf_op jit(solution)/shard_map/ppermute | solution.py:78
  86.0 16.0 %shard_map.59 = f32[6,128]{1,0:T(8,128)S(1)} custom-call(bf16[6,2048,128]{2,1,0:T(8,128)(2,1)S(1)} %convolution_convert_fusion.refs_0_, bf16[2,128,2048]{2,1,0:T(8,128)(2,1)S(1)} %copy-done, bf16[1,128,2048]{2,1,0:T(8,128)(2,1)S(1)} %collective-permute-done.refs_2_, bf16[1,128,2048]{2,1,0:T(8,128)(2,1)S(1)} %collective-permute-done.1.refs_3_, ...), custom_call_target="tpu_custom_call" | custom-call | tf_op jit(solution)/shard_map/pallas_call | solution.py:62
  (45 shorter events, 9.7 us)
Async XLA Ops:
  1.7 14.9 %collective-permute-start = (bf16[1,128,2048]{2,1,0:T(8,128)(2,1)S(1)}, bf16[1,128,2048]{2,1,0:T(8,128)(2,1)S(1)}, u32[]{:S(2)}, u32[]{:S(2)}) collective-permute-start(bf16[1,128,2048]{2,1,0:T(8,128)(2,1)S(1)} %constant_dynamic-slice_fusion), channel_id=1, source_target_pairs={{0,2},{2,4},{4,6},{6,7},{7,5},{5,3},{3,1},{1,0},{8,10},{10,12},{12... | collective-permute-start | bytes 1572872 | tf_op jit(solution)/shard_map/ppermute | solution.py:117
  4.8 13.4 %collective-permute-start.1 = (bf16[1,128,2048]{2,1,0:T(8,128)(2,1)S(1)}, bf16[1,128,2048]{2,1,0:T(8,128)(2,1)S(1)}, u32[]{:S(2)}, u32[]{:S(2)}) collective-permute-start(bf16[1,128,2048]{2,1,0:T(8,128)(2,1)S(1)} %constant_dynamic-slice_fusion), channel_id=1, source_target_pairs={{2,0},{4,2},{6,4},{7,6},{5,7},{3,5},{1,3},{0,1},{10,8},{12,10},{14... | collective-permute-start | bytes 1572872 | tf_op jit(solution)/shard_map/ppermute | solution.py:120
  4.8 39.7 %collective-permute-start.6 = (bf16[3,2048,128]{2,1,0:T(8,128)(2,1)}, bf16[3,2048,128]{2,1,0:T(8,128)(2,1)S(1)}, u32[]{:S(2)}, u32[]{:S(2)}) collective-permute-start(bf16[3,2048,128]{2,1,0:T(8,128)(2,1)} %param.4), channel_id=1, source_target_pairs={{0,16},{8,24},{16,0},{24,8},{1,17},{9,25},{17,1},{25,9},{2,18},{10... | collective-permute-start | bytes 4718600 | tf_op jit(solution)/shard_map/ppermute | solution.py:78
  6.8 37.8 %collective-permute-start.7 = (bf16[3,2048,128]{2,1,0:T(8,128)(2,1)}, bf16[3,2048,128]{2,1,0:T(8,128)(2,1)S(1)}, u32[]{:S(2)}, u32[]{:S(2)}) collective-permute-start(bf16[3,2048,128]{2,1,0:T(8,128)(2,1)} %param.4), channel_id=1, source_target_pairs={{0,8},{8,0},{16,24},{24,16},{1,9},{9,1},{17,25},{25,17},{2,10},{10... | collective-permute-start | bytes 4718600 | tf_op jit(solution)/shard_map/ppermute | solution.py:78
  18.2 12.5 %collective-permute-start.2 = (bf16[1,128,2048]{2,1,0:T(8,128)(2,1)S(1)}, bf16[1,128,2048]{2,1,0:T(8,128)(2,1)S(1)}, u32[]{:S(2)}, u32[]{:S(2)}) collective-permute-start(bf16[1,128,2048]{2,1,0:T(8,128)(2,1)S(1)} %collective-permute-done.refs_2_), channel_id=1, source_target_pairs={{0,2},{2,4},{4,6},{6,7},{7,5},{5,3},{3,1},{1,0},{8,10},{10,12},{12... | collective-permute-start | bytes 1572872 | tf_op jit(solution)/shard_map/ppermute | solution.py:117
  19.8 12.2 %collective-permute-start.3 = (bf16[1,128,2048]{2,1,0:T(8,128)(2,1)S(1)}, bf16[1,128,2048]{2,1,0:T(8,128)(2,1)S(1)}, u32[]{:S(2)}, u32[]{:S(2)}) collective-permute-start(bf16[1,128,2048]{2,1,0:T(8,128)(2,1)S(1)} %collective-permute-done.1.refs_3_), channel_id=1, source_target_pairs={{2,0},{4,2},{6,4},{7,6},{5,7},{3,5},{1,3},{0,1},{10,8},{12,10},{14... | collective-permute-start | bytes 1572872 | tf_op jit(solution)/shard_map/ppermute | solution.py:120
  32.0 11.3 %collective-permute-start.4 = (bf16[1,128,2048]{2,1,0:T(8,128)(2,1)S(1)}, bf16[1,128,2048]{2,1,0:T(8,128)(2,1)S(1)}, u32[]{:S(2)}, u32[]{:S(2)}) collective-permute-start(bf16[1,128,2048]{2,1,0:T(8,128)(2,1)S(1)} %collective-permute-done.2.refs_4_), channel_id=1, source_target_pairs={{0,2},{2,4},{4,6},{6,7},{7,5},{5,3},{3,1},{1,0},{8,10},{10,12},{12... | collective-permute-start | bytes 1572872 | tf_op jit(solution)/shard_map/ppermute | solution.py:117
  33.5 11.0 %collective-permute-start.5 = (bf16[1,128,2048]{2,1,0:T(8,128)(2,1)S(1)}, bf16[1,128,2048]{2,1,0:T(8,128)(2,1)S(1)}, u32[]{:S(2)}, u32[]{:S(2)}) collective-permute-start(bf16[1,128,2048]{2,1,0:T(8,128)(2,1)S(1)} %collective-permute-done.3.refs_5_), channel_id=1, source_target_pairs={{2,0},{4,2},{6,4},{7,6},{5,7},{3,5},{1,3},{0,1},{10,8},{12,10},{14... | collective-permute-start | bytes 1572872 | tf_op jit(solution)/shard_map/ppermute | solution.py:120
  44.5 4.5 %collective-permute-start.9 = (bf16[3,2048,128]{2,1,0:T(8,128)(2,1)S(1)}, bf16[3,2048,128]{2,1,0:T(8,128)(2,1)S(1)}, u32[]{:S(2)}, u32[]{:S(2)}) collective-permute-start(bf16[3,2048,128]{2,1,0:T(8,128)(2,1)S(1)} %collective-permute-done.6), channel_id=1, source_target_pairs={{0,8},{8,0},{16,24},{24,16},{1,9},{9,1},{17,25},{25,17},{2,10},{10... | collective-permute-start | bytes 4718600 | tf_op jit(solution)/shard_map/ppermute | solution.py:78
  48.1 34.6 %collective-permute-start.10 = (bf16[1,128,2048]{2,1,0:T(8,128)(2,1)S(1)}, bf16[1,128,2048]{2,1,0:T(8,128)(2,1)}, u32[]{:S(2)}, u32[]{:S(2)}) collective-permute-start(bf16[1,128,2048]{2,1,0:T(8,128)(2,1)S(1)} %collective-permute-done.refs_2_), channel_id=1, source_target_pairs={{0,8},{8,0},{16,24},{24,16},{1,9},{9,1},{17,25},{25,17},{2,10},{10... | collective-permute-start | bytes 1572872 | tf_op jit(solution)/shard_map/ppermute | solution.py:78
  48.6 34.4 %collective-permute-start.11 = (bf16[1,128,2048]{2,1,0:T(8,128)(2,1)S(1)}, bf16[1,128,2048]{2,1,0:T(8,128)(2,1)}, u32[]{:S(2)}, u32[]{:S(2)}) collective-permute-start(bf16[1,128,2048]{2,1,0:T(8,128)(2,1)S(1)} %collective-permute-done.1.refs_3_), channel_id=1, source_target_pairs={{0,8},{8,0},{16,24},{24,16},{1,9},{9,1},{17,25},{25,17},{2,10},{10... | collective-permute-start | bytes 1572872 | tf_op jit(solution)/shard_map/ppermute | solution.py:78
  48.6 34.6 %collective-permute-start.12 = (bf16[1,128,2048]{2,1,0:T(8,128)(2,1)S(1)}, bf16[1,128,2048]{2,1,0:T(8,128)(2,1)}, u32[]{:S(2)}, u32[]{:S(2)}) collective-permute-start(bf16[1,128,2048]{2,1,0:T(8,128)(2,1)S(1)} %collective-permute-done.2.refs_4_), channel_id=1, source_target_pairs={{0,8},{8,0},{16,24},{24,16},{1,9},{9,1},{17,25},{25,17},{2,10},{10... | collective-permute-start | bytes 1572872 | tf_op jit(solution)/shard_map/ppermute | solution.py:78
  49.1 34.1 %collective-permute-start.13 = (bf16[1,128,2048]{2,1,0:T(8,128)(2,1)S(1)}, bf16[1,128,2048]{2,1,0:T(8,128)(2,1)}, u32[]{:S(2)}, u32[]{:S(2)}) collective-permute-start(bf16[1,128,2048]{2,1,0:T(8,128)(2,1)S(1)} %collective-permute-done.3.refs_5_), channel_id=1, source_target_pairs={{0,8},{8,0},{16,24},{24,16},{1,9},{9,1},{17,25},{25,17},{2,10},{10... | collective-permute-start | bytes 1572872 | tf_op jit(solution)/shard_map/ppermute | solution.py:78
  49.1 33.2 %collective-permute-start.8 = (bf16[1,128,2048]{2,1,0:T(8,128)(2,1)S(1)}, bf16[1,128,2048]{2,1,0:T(8,128)(2,1)}, u32[]{:S(2)}, u32[]{:S(2)}) collective-permute-start(bf16[1,128,2048]{2,1,0:T(8,128)(2,1)S(1)} %collective-permute-done.4.refs_6_), channel_id=1, source_target_pairs={{0,2},{2,4},{4,6},{6,7},{7,5},{5,3},{3,1},{1,0},{8,10},{10,12},{12... | collective-permute-start | bytes 1572872 | tf_op jit(solution)/shard_map/ppermute | solution.py:117
  65.6 1.7 %copy-start.1 = (bf16[6,2048,128]{2,1,0:T(8,128)(2,1)}, bf16[6,2048,128]{2,1,0:T(8,128)(2,1)S(1)}, u32[]{:S(2)}) copy-start(bf16[6,2048,128]{2,1,0:T(8,128)(2,1)S(1)} %get-tuple-element.27) | copy-start | bytes 9437188
  72.0 4.7 %copy-start.3 = (f32[128,128]{1,0:T(8,128)S(1)}, f32[128,128]{1,0:T(8,128)}, u32[]{:S(2)}) copy-start(f32[128,128]{1,0:T(8,128)} %fusion.10) | copy-start | bytes 196612
  73.9 4.7 %copy-start.2 = (bf16[6,2048,128]{2,1,0:T(8,128)(2,1)S(1)}, bf16[6,2048,128]{2,1,0:T(8,128)(2,1)}, u32[]{:S(2)}) copy-start(bf16[6,2048,128]{2,1,0:T(8,128)(2,1)} %copy-done.1) | copy-start | bytes 9437188
  79.5 6.5 %copy-start = (bf16[2,128,2048]{2,1,0:T(8,128)(2,1)S(1)}, bf16[2,128,2048]{2,1,0:T(8,128)(2,1)}, u32[]{:S(2)}) copy-start(bf16[2,128,2048]{2,1,0:T(8,128)(2,1)} %refs_1_.1) | copy-start | bytes 3145732
  82.3 2.0 %collective-permute-start.14 = (bf16[1,128,2048]{2,1,0:T(8,128)(2,1)S(1)}, bf16[1,128,2048]{2,1,0:T(8,128)(2,1)S(1)}, u32[]{:S(2)}, u32[]{:S(2)}) collective-permute-start(bf16[1,128,2048]{2,1,0:T(8,128)(2,1)S(1)} %collective-permute-done.4.refs_6_), channel_id=1, source_target_pairs={{0,8},{8,0},{16,24},{24,16},{1,9},{9,1},{17,25},{25,17},{2,10},{10... | collective-permute-start | bytes 1572872 | tf_op jit(solution)/shard_map/ppermute | solution.py:78
  82.6 19.5 %copy-start.4 = (s32[6]{0:T(128)S(1)}, s32[6]{0:T(128)}, u32[]{:S(2)}) copy-start(s32[6]{0:T(128)} %param.6) | copy-start | bytes 76
  82.6 3.2 %collective-permute-start.15 = (bf16[1,128,2048]{2,1,0:T(8,128)(2,1)S(1)}, bf16[1,128,2048]{2,1,0:T(8,128)(2,1)S(1)}, u32[]{:S(2)}, u32[]{:S(2)}) collective-permute-start(bf16[1,128,2048]{2,1,0:T(8,128)(2,1)S(1)} %collective-permute-done.5.refs_7_), channel_id=1, source_target_pairs={{0,8},{8,0},{16,24},{24,16},{1,9},{9,1},{17,25},{25,17},{2,10},{10... | collective-permute-start | bytes 1572872 | tf_op jit(solution)/shard_map/ppermute | solution.py:78
  82.9 3.1 %collective-permute-start.16 = (bf16[1,128,2048]{2,1,0:T(8,128)(2,1)}, bf16[1,128,2048]{2,1,0:T(8,128)(2,1)S(1)}, u32[]{:S(2)}, u32[]{:S(2)}) collective-permute-start(bf16[1,128,2048]{2,1,0:T(8,128)(2,1)} %collective-permute-done.8.refs_8_), channel_id=1, source_target_pairs={{0,8},{8,0},{16,24},{24,16},{1,9},{9,1},{17,25},{25,17},{2,10},{10... | collective-permute-start | bytes 1572872 | tf_op jit(solution)/shard_map/ppermute | solution.py:78

commit v7 on v6

--- a/solution.py
+++ b/solution.py
@@ -78,16 +78,68 @@
     return lax.ppermute(x, axis, perm)
 
 
+def kick_kernel(source_ref, living_ref, *refs):
+    walker_refs = refs[:4]
+    field_ref, new_ref, theta_ref, buffer, copy_sem = refs[4:]
+    s = pl.program_id(0)
+    old_dev = walker_refs[0].shape[0]
+    source = source_ref[s]
+    for r, walker_ref in enumerate(walker_refs):
+        @pl.when(source // old_dev == r)
+        def _(walker_ref=walker_ref):
+            copy = pltpu.make_async_copy(walker_ref.at[source % old_dev], buffer, copy_sem)
+            copy.start()
+            copy.wait()
+
+    orbitals, electrons = buffer.shape
+    lanes = field_ref.shape[0]
+    scale = jnp.transpose(jnp.exp(field_ref[...]))
+    pick = lax.broadcasted_iota(jnp.int32, scale.shape, 1) == s
+    scale = jnp.sum(jnp.where(pick, scale, 0.0), axis=1, keepdims=True)
+    kicked = (scale * buffer[...].astype(jnp.float32)).astype(jnp.bfloat16)
+    live = living_ref[s] > 0
+    new_ref[0] = jnp.where(live, kicked, jnp.zeros_like(kicked))
+
+    widened = kicked.astype(jnp.float32)
+    intersection = widened[:electrons, :]
+    rows = lax.broadcasted_iota(jnp.int32, (electrons, electrons), 0)
+    cols = lax.broadcasted_iota(jnp.int32, (electrons, electrons), 1)
+    eye = rows == cols
+    identity = eye.astype(jnp.float32)
+    diagonal = jnp.sum(jnp.where(eye, intersection, 0.0), axis=0, keepdims=True)
+    inverse = jnp.where(eye, 1.0 / diagonal, 0.0)
+    for sweep in range(ITERS):
+        product = jnp.dot(intersection, inverse, precision=lax.Precision.HIGHEST, preferred_element_type=jnp.float32)
+        inverse = jnp.dot(inverse, 2.0 * identity - product, precision=lax.Precision.HIGHEST, preferred_element_type=jnp.float32)
+    theta = jnp.dot(widened, inverse, precision=lax.Precision.HIGHEST, preferred_element_type=jnp.float32)
+    theta_ref[0] = theta.astype(jnp.bfloat16)
+
+
 def kick(old_walkers, beside, across, diagonal_peer, parent, field, walk_id):
-    old_dev = old_walkers.shape[0]
-    column = jnp.concatenate([old_walkers, beside, across, diagonal_peer], axis=0)
-    living = parent >= 0
+    old_dev, orbitals, electrons = old_walkers.shape
+    slot_dev = parent.shape[0]
+    living = (parent >= 0).astype(jnp.int32)
     source = jnp.maximum(parent, 0)
     relative = (source // old_dev) ^ walk_id
-    index = relative * old_dev + source % old_dev
-    kicked = (jnp.exp(field)[:, :, None] * column[index].astype(jnp.float32)).astype(jnp.bfloat16)
-    new_walkers = jnp.where(living[:, None, None], kicked, jnp.zeros_like(kicked))
-    return new_walkers, green_half(kicked)
+    index = (relative * old_dev + source % old_dev).astype(jnp.int32)
+    lanes = max(8, -(-slot_dev // 8) * 8)
+    padded = jnp.zeros((lanes, orbitals), jnp.float32).at[:slot_dev].set(field)
+    any_space = pl.BlockSpec(memory_space=pl.ANY)
+    slot_block = pl.BlockSpec((1, orbitals, electrons), lambda s, *_: (s, 0, 0))
+    grid_spec = pltpu.PrefetchScalarGridSpec(
+        num_scalar_prefetch=2,
+        grid=(slot_dev,),
+        in_specs=[any_space] * 4 + [pl.BlockSpec((lanes, orbitals), lambda s, *_: (0, 0))],
+        out_specs=[slot_block, slot_block],
+        scratch_shapes=[pltpu.VMEM((orbitals, electrons), old_walkers.dtype), pltpu.SemaphoreType.DMA(())],
+    )
+    shape = jax.ShapeDtypeStruct((slot_dev, orbitals, electrons), jnp.bfloat16)
+    new_walkers, theta = pl.pallas_call(
+        kick_kernel,
+        out_shape=[shape, shape],
+        grid_spec=grid_spec,
+    )(index, living, old_walkers, beside, across, diagonal_peer, padded)
+    return new_walkers, theta
 
 
 def body(old_walkers, half_chol, parent, field):

time: 103 us -> 101 us (0.981)
  Pallas kernels: 16 us -> 40.7 us
  other arithmetic: 12.6 us -> 2.84 us
  local copies, waits for them, and re-layouts: 15.8 us -> 6.75 us
  matrix products: 8.37 us -> 0 us
    pallas_call x0 -> x1, Pallas kernels: none -> 24.6 us  [kick(): pl.pallas_call(kick_kernel, out_shape=[shape, shape], grid_spec=grid_spec)]
    dot_general x7 -> x0, matrix products: 8.37 us -> none  [the longest x3 3.12 us: green_half(): jnp.einsum('wij,wjk->wik', intersection, inverse, precision=lax.Precision...]
    gather x3 -> x0, local copies, waits for them, and re-layouts: 7.33 us -> none  [the longest x1 5.5 us: kick(): column[index].astype(jnp.float32)]
    select_n x2 -> x0, other arithmetic: 5.73 us -> none  [the longest x1 5.05 us: kick(): jnp.where(living[:, None, None], kicked, jnp.zeros_like(kicked))]
    slice x1 -> x0, local copies, waits for them, and re-layouts: 4.72 us -> none  [green_half(): intersection = widened[:, :electrons, :]]
    concatenate x2 -> x0, other arithmetic: 4.43 us -> none  [the longest x1 4.42 us: kick(): jnp.concatenate([old_walkers, beside, across, diagonal_peer], axis=0)]
    unnamed x10 -> x16, local copies, waits for them, and re-layouts: 1.73 us -> 4.09 us
    scatter x0 -> x1, local copies, waits for them, and re-layouts: none -> 1.46 us  [kick(): padded = jnp.zeros((lanes, orbitals), jnp.float32).at[:slot_dev].set(field)]
  transfers between devices with their start and end apart: 17 -> 17, of which waited for: 9 -> 9; matrix products, arithmetic and copies ran while one was open for 33% -> 4% of each run, Pallas kernels for 0% -> 25%
where the time goes in v7:
time: 101 us; the launch traced here: 100 us
  Pallas kernels  40.7 us (40%)
  waiting for transfers between devices  36.7 us (36%)
  starting transfers between devices  12.5 us (12%)
  local copies, waits for them, and re-layouts  6.75 us (7%)
  other arithmetic  2.84 us (3%)
    ppermute x4, waiting for transfers between devices, body(): ahead = lax.ppermute(ahead, 'chol', forward)  29.7 us
    pallas_call x1, Pallas kernels, kick(): pl.pallas_call(kick_kernel, out_shape=[shape, shape], grid_spec=grid_spec)  24.6 us
    pallas_call x1, Pallas kernels, block_energy(): pl.pallas_call(energy_kernel, out_shape=jax.ShapeDtypeStruct((n_slot, 128...  16.1 us
    ppermute x4, starting transfers between devices, body(): ahead = lax.ppermute(ahead, 'chol', forward)  7.8 us
    unnamed x16, local copies, waits for them, and re-layouts  4.09 us
    ppermute x3, waiting for transfers between devices, body(): behind = lax.ppermute(behind, 'chol', backward)  4 us
    ppermute x10, starting transfers between devices, swap_pairs(): return lax.ppermute(x, axis, perm)  3.77 us
    ppermute x10, waiting for transfers between devices, swap_pairs(): return lax.ppermute(x, axis, perm)  2.94 us
  transfers between devices with their start and end apart: 17, of which 9 were waited for; matrix products, arithmetic and copies ran while one was open for 4% of the time, Pallas kernels for 25%

profile of v7, /device:TPU:0, one launch (start us, length us, event | category | flops | bytes accessed | tf_op | source)
XLA Modules:
  0.0 100.1 jit_solution(3824250121735822088)
XLA Ops:
  0.6 1.1 %constant_dynamic-slice_fusion = bf16[1,128,2048]{2,1,0:T(8,128)(2,1)S(1)} fusion(bf16[2,128,2048]{2,1,0:T(8,128)(2,1)} %refs_1_.1, s32[]{:T(128)S(6)} %select_n.26), kind=kLoop, calls=%fused_computation.6 | loop fusion | bytes 1048580 | tf_op jit(solution)/shard_map/dynamic_slice | solution.py:155
  1.7 3.1 %collective-permute-start = (bf16[1,128,2048]{2,1,0:T(8,128)(2,1)S(1)}, bf16[1,128,2048]{2,1,0:T(8,128)(2,1)S(1)}, u32[]{:S(2)}, u32[]{:S(2)}) collective-permute-start(bf16[1,128,2048]{2,1,0:T(8,128)(2,1)S(1)} %constant_dynamic-slice_fusion), channel_id=1, source_target_pairs={{0,2},{2,4},{4,6},{6,7},{7,5},{5,3},{3,1},{1,0},{8,10},{10,12},{12... | collective-permute-start | bytes 1572872 | tf_op jit(solution)/shard_map/ppermute | solution.py:169
  4.8 1.9 %collective-permute-start.6 = (bf16[3,2048,128]{2,1,0:T(8,128)(2,1)}, bf16[3,2048,128]{2,1,0:T(8,128)(2,1)S(1)}, u32[]{:S(2)}, u32[]{:S(2)}) collective-permute-start(bf16[3,2048,128]{2,1,0:T(8,128)(2,1)} %refs_0_.1), channel_id=1, source_target_pairs={{0,16},{8,24},{16,0},{24,8},{1,17},{9,25},{17,1},{25,9},{2,18},{10... | collective-permute-start | bytes 4718600 | tf_op jit(solution)/shard_map/ppermute | solution.py:78
  6.7 9.9 %collective-permute-done.refs_2_ = bf16[1,128,2048]{2,1,0:T(8,128)(2,1)S(1)} collective-permute-done((bf16[1,128,2048]{2,1,0:T(8,128)(2,1)S(1)}, bf16[1,128,2048]{2,1,0:T(8,128)(2,1)S(1)}, u32[]{:S(2)}, u32[]{:S(2)}) %collective-permute-start) | collective-permute-done | bytes 524320 | tf_op jit(solution)/shard_map/ppermute | solution.py:169
  16.7 1.5 %collective-permute-done.1.refs_3_ = bf16[1,128,2048]{2,1,0:T(8,128)(2,1)S(1)} collective-permute-done((bf16[1,128,2048]{2,1,0:T(8,128)(2,1)S(1)}, bf16[1,128,2048]{2,1,0:T(8,128)(2,1)S(1)}, u32[]{:S(2)}, u32[]{:S(2)}) %collective-permute-start.1) | collective-permute-done | bytes 524320 | tf_op jit(solution)/shard_map/ppermute | solution.py:172
  18.2 1.6 %collective-permute-start.2 = (bf16[1,128,2048]{2,1,0:T(8,128)(2,1)S(1)}, bf16[1,128,2048]{2,1,0:T(8,128)(2,1)S(1)}, u32[]{:S(2)}, u32[]{:S(2)}) collective-permute-start(bf16[1,128,2048]{2,1,0:T(8,128)(2,1)S(1)} %collective-permute-done.refs_2_), channel_id=1, source_target_pairs={{0,2},{2,4},{4,6},{6,7},{7,5},{5,3},{3,1},{1,0},{8,10},{10,12},{12... | collective-permute-start | bytes 1572872 | tf_op jit(solution)/shard_map/ppermute | solution.py:169
  20.2 10.4 %collective-permute-done.2.refs_4_ = bf16[1,128,2048]{2,1,0:T(8,128)(2,1)S(1)} collective-permute-done((bf16[1,128,2048]{2,1,0:T(8,128)(2,1)S(1)}, bf16[1,128,2048]{2,1,0:T(8,128)(2,1)S(1)}, u32[]{:S(2)}, u32[]{:S(2)}) %collective-permute-start.2) | collective-permute-done | bytes 524320 | tf_op jit(solution)/shard_map/ppermute | solution.py:169
  30.7 1.3 %collective-permute-done.3.refs_5_ = bf16[1,128,2048]{2,1,0:T(8,128)(2,1)S(1)} collective-permute-done((bf16[1,128,2048]{2,1,0:T(8,128)(2,1)S(1)}, bf16[1,128,2048]{2,1,0:T(8,128)(2,1)S(1)}, u32[]{:S(2)}, u32[]{:S(2)}) %collective-permute-start.3) | collective-permute-done | bytes 524320 | tf_op jit(solution)/shard_map/ppermute | solution.py:172
  32.0 1.6 %collective-permute-start.4 = (bf16[1,128,2048]{2,1,0:T(8,128)(2,1)S(1)}, bf16[1,128,2048]{2,1,0:T(8,128)(2,1)}, u32[]{:S(2)}, u32[]{:S(2)}) collective-permute-start(bf16[1,128,2048]{2,1,0:T(8,128)(2,1)S(1)} %collective-permute-done.2.refs_4_), channel_id=1, source_target_pairs={{0,2},{2,4},{4,6},{6,7},{7,5},{5,3},{3,1},{1,0},{8,10},{10,12},{12... | collective-permute-start | bytes 1572872 | tf_op jit(solution)/shard_map/ppermute | solution.py:169
  34.0 9.4 %collective-permute-done.4.refs_6_ = bf16[1,128,2048]{2,1,0:T(8,128)(2,1)} collective-permute-done((bf16[1,128,2048]{2,1,0:T(8,128)(2,1)S(1)}, bf16[1,128,2048]{2,1,0:T(8,128)(2,1)}, u32[]{:S(2)}, u32[]{:S(2)}) %collective-permute-start.4) | collective-permute-done | bytes 524320 | tf_op jit(solution)/shard_map/ppermute | solution.py:169
  43.3 1.2 %collective-permute-done.5.refs_7_ = bf16[1,128,2048]{2,1,0:T(8,128)(2,1)S(1)} collective-permute-done((bf16[1,128,2048]{2,1,0:T(8,128)(2,1)S(1)}, bf16[1,128,2048]{2,1,0:T(8,128)(2,1)S(1)}, u32[]{:S(2)}, u32[]{:S(2)}) %collective-permute-start.5) | collective-permute-done | bytes 524320 | tf_op jit(solution)/shard_map/ppermute | solution.py:172
  44.6 1.6 %collective-permute-start.8 = (bf16[1,128,2048]{2,1,0:T(8,128)(2,1)}, bf16[1,128,2048]{2,1,0:T(8,128)(2,1)}, u32[]{:S(2)}, u32[]{:S(2)}) collective-permute-start(bf16[1,128,2048]{2,1,0:T(8,128)(2,1)} %collective-permute-done.4.refs_6_), channel_id=1, source_target_pairs={{0,2},{2,4},{4,6},{6,7},{7,5},{5,3},{3,1},{1,0},{8,10},{10,12},{12... | collective-permute-start | bytes 1572872 | tf_op jit(solution)/shard_map/ppermute | solution.py:169
  46.7 1.5 %scatter.4.refs_4_ = f32[8,2048]{1,0:T(8,128)} pad(f32[6,2048]{1,0:T(8,128)} %param.9, f32[]{:T(128)} %constant.67.clone.1), padding=0_2x0_0 | pad | bytes 114692 | tf_op jit(solution)/shard_map/scatter | solution.py:126
  48.2 1.2 %fusion.source_ref = s32[6]{0:T(128)} fusion(s32[6]{0:T(128)} %param.8, s32[]{:T(128)S(6)} %axis_index.15), kind=kLoop, calls=%fused_computation.5 | loop fusion | flops 96 | bytes 52 | tf_op jit(solution)/shard_map/add | solution.py:124
  49.4 1.1 %compare_convert_fusion.living_ref = s32[6]{0:T(128)} fusion(s32[6]{0:T(128)} %param.8), kind=kLoop, calls=%fused_computation.4 | loop fusion | flops 12 | bytes 48 | tf_op jit(solution)/shard_map/convert_element_type | solution.py:121
  50.7 1.1 %copy-done.6 = bf16[3,2048,128]{2,1,0:T(8,128)(2,1)} copy-done((bf16[3,2048,128]{2,1,0:T(8,128)(2,1)}, bf16[3,2048,128]{2,1,0:T(8,128)(2,1)S(1)}, u32[]{:S(2)}) %copy-start.6) | copy-done | bytes 1572888
  52.2 24.6 %shard_map.59 = (bf16[6,2048,128]{2,1,0:T(8,128)(2,1)}, bf16[6,2048,128]{2,1,0:T(8,128)(2,1)}) custom-call(s32[6]{0:T(128)} %fusion.source_ref, s32[6]{0:T(128)} %compare_convert_fusion.living_ref, bf16[3,2048,128]{2,1,0:T(8,128)(2,1)} %refs_0_.1, bf16[3,2048,128]{2,1,0:T(8,128)(2,1)} %copy-done.5, bf16[3,2048,128]{2,1,0:T(8,128)(2,1)} %copy-done.4, ...), custom_call_target="tpu_custom_call" | custom-call | tf_op jit(solution)/shard_map/pallas_call | solution.py:137
  77.5 1.4 %collective-permute-done.14.refs_13_ = bf16[1,128,2048]{2,1,0:T(8,128)(2,1)S(1)} collective-permute-done((bf16[1,128,2048]{2,1,0:T(8,128)(2,1)}, bf16[1,128,2048]{2,1,0:T(8,128)(2,1)S(1)}, u32[]{:S(2)}, u32[]{:S(2)}) %collective-permute-start.14) | collective-permute-done | bytes 524320 | tf_op jit(solution)/shard_map/ppermute | solution.py:78
  79.0 0.7 collective-permute-done.15.refs_14_
  79.7 0.7 collective-permute-done.16.refs_15_
  80.5 1.9 %copy-done = bf16[6,2048,128]{2,1,0:T(8,128)(2,1)S(1)} copy-done((bf16[6,2048,128]{2,1,0:T(8,128)(2,1)S(1)}, bf16[6,2048,128]{2,1,0:T(8,128)(2,1)}, u32[]{:S(2)}) %copy-start) | copy-done | bytes 3145752
  82.3 1.0 %copy-done.3 = bf16[1,128,2048]{2,1,0:T(8,128)(2,1)S(1)} copy-done((bf16[1,128,2048]{2,1,0:T(8,128)(2,1)S(1)}, bf16[1,128,2048]{2,1,0:T(8,128)(2,1)}, u32[]{:S(2)}) %copy-start.3) | copy-done | bytes 524312
  83.4 16.1 %shard_map.60 = f32[6,128]{1,0:T(8,128)S(1)} custom-call(bf16[6,2048,128]{2,1,0:T(8,128)(2,1)S(1)} %copy-done, bf16[2,128,2048]{2,1,0:T(8,128)(2,1)S(1)} %copy-done.1, bf16[1,128,2048]{2,1,0:T(8,128)(2,1)S(1)} %collective-permute-done.refs_2_, bf16[1,128,2048]{2,1,0:T(8,128)(2,1)S(1)} %collective-permute-done.1.refs_3_, ...), custom_call_target="tpu_custom_call" | custom-call | tf_op jit(solution)/shard_map/pallas_call | solution.py:62
  99.6 0.5 compare_select_fusion
  (34 shorter events, 2.9 us)
Async XLA Ops:
  1.7 14.9 %collective-permute-start = (bf16[1,128,2048]{2,1,0:T(8,128)(2,1)S(1)}, bf16[1,128,2048]{2,1,0:T(8,128)(2,1)S(1)}, u32[]{:S(2)}, u32[]{:S(2)}) collective-permute-start(bf16[1,128,2048]{2,1,0:T(8,128)(2,1)S(1)} %constant_dynamic-slice_fusion), channel_id=1, source_target_pairs={{0,2},{2,4},{4,6},{6,7},{7,5},{5,3},{3,1},{1,0},{8,10},{10,12},{12... | collective-permute-start | bytes 1572872 | tf_op jit(solution)/shard_map/ppermute | solution.py:169
  4.8 13.4 %collective-permute-start.1 = (bf16[1,128,2048]{2,1,0:T(8,128)(2,1)S(1)}, bf16[1,128,2048]{2,1,0:T(8,128)(2,1)S(1)}, u32[]{:S(2)}, u32[]{:S(2)}) collective-permute-start(bf16[1,128,2048]{2,1,0:T(8,128)(2,1)S(1)} %constant_dynamic-slice_fusion), channel_id=1, source_target_pairs={{2,0},{4,2},{6,4},{7,6},{5,7},{3,5},{1,3},{0,1},{10,8},{12,10},{14... | collective-permute-start | bytes 1572872 | tf_op jit(solution)/shard_map/ppermute | solution.py:172
  4.8 39.7 %collective-permute-start.6 = (bf16[3,2048,128]{2,1,0:T(8,128)(2,1)}, bf16[3,2048,128]{2,1,0:T(8,128)(2,1)S(1)}, u32[]{:S(2)}, u32[]{:S(2)}) collective-permute-start(bf16[3,2048,128]{2,1,0:T(8,128)(2,1)} %refs_0_.1), channel_id=1, source_target_pairs={{0,16},{8,24},{16,0},{24,8},{1,17},{9,25},{17,1},{25,9},{2,18},{10... | collective-permute-start | bytes 4718600 | tf_op jit(solution)/shard_map/ppermute | solution.py:78
  6.7 37.8 %collective-permute-start.7 = (bf16[3,2048,128]{2,1,0:T(8,128)(2,1)}, bf16[3,2048,128]{2,1,0:T(8,128)(2,1)S(1)}, u32[]{:S(2)}, u32[]{:S(2)}) collective-permute-start(bf16[3,2048,128]{2,1,0:T(8,128)(2,1)} %refs_0_.1), channel_id=1, source_target_pairs={{0,8},{8,0},{16,24},{24,16},{1,9},{9,1},{17,25},{25,17},{2,10},{10... | collective-permute-start | bytes 4718600 | tf_op jit(solution)/shard_map/ppermute | solution.py:78
  18.2 12.5 %collective-permute-start.2 = (bf16[1,128,2048]{2,1,0:T(8,128)(2,1)S(1)}, bf16[1,128,2048]{2,1,0:T(8,128)(2,1)S(1)}, u32[]{:S(2)}, u32[]{:S(2)}) collective-permute-start(bf16[1,128,2048]{2,1,0:T(8,128)(2,1)S(1)} %collective-permute-done.refs_2_), channel_id=1, source_target_pairs={{0,2},{2,4},{4,6},{6,7},{7,5},{5,3},{3,1},{1,0},{8,10},{10,12},{12... | collective-permute-start | bytes 1572872 | tf_op jit(solution)/shard_map/ppermute | solution.py:169
  19.8 12.2 %collective-permute-start.3 = (bf16[1,128,2048]{2,1,0:T(8,128)(2,1)S(1)}, bf16[1,128,2048]{2,1,0:T(8,128)(2,1)S(1)}, u32[]{:S(2)}, u32[]{:S(2)}) collective-permute-start(bf16[1,128,2048]{2,1,0:T(8,128)(2,1)S(1)} %collective-permute-done.1.refs_3_), channel_id=1, source_target_pairs={{2,0},{4,2},{6,4},{7,6},{5,7},{3,5},{1,3},{0,1},{10,8},{12,10},{14... | collective-permute-start | bytes 1572872 | tf_op jit(solution)/shard_map/ppermute | solution.py:172
  32.0 11.4 %collective-permute-start.4 = (bf16[1,128,2048]{2,1,0:T(8,128)(2,1)S(1)}, bf16[1,128,2048]{2,1,0:T(8,128)(2,1)}, u32[]{:S(2)}, u32[]{:S(2)}) collective-permute-start(bf16[1,128,2048]{2,1,0:T(8,128)(2,1)S(1)} %collective-permute-done.2.refs_4_), channel_id=1, source_target_pairs={{0,2},{2,4},{4,6},{6,7},{7,5},{5,3},{3,1},{1,0},{8,10},{10,12},{12... | collective-permute-start | bytes 1572872 | tf_op jit(solution)/shard_map/ppermute | solution.py:169
  33.5 11.0 %collective-permute-start.5 = (bf16[1,128,2048]{2,1,0:T(8,128)(2,1)S(1)}, bf16[1,128,2048]{2,1,0:T(8,128)(2,1)S(1)}, u32[]{:S(2)}, u32[]{:S(2)}) collective-permute-start(bf16[1,128,2048]{2,1,0:T(8,128)(2,1)S(1)} %collective-permute-done.3.refs_5_), channel_id=1, source_target_pairs={{2,0},{4,2},{6,4},{7,6},{5,7},{3,5},{1,3},{0,1},{10,8},{12,10},{14... | collective-permute-start | bytes 1572872 | tf_op jit(solution)/shard_map/ppermute | solution.py:172
  44.5 1.7 %copy-start.2 = (bf16[1,128,2048]{2,1,0:T(8,128)(2,1)}, bf16[1,128,2048]{2,1,0:T(8,128)(2,1)S(1)}, u32[]{:S(2)}) copy-start(bf16[1,128,2048]{2,1,0:T(8,128)(2,1)S(1)} %collective-permute-done.5.refs_7_) | copy-start | bytes 1572868
  44.5 6.1 %copy-start.4 = (bf16[3,2048,128]{2,1,0:T(8,128)(2,1)}, bf16[3,2048,128]{2,1,0:T(8,128)(2,1)S(1)}, u32[]{:S(2)}) copy-start(bf16[3,2048,128]{2,1,0:T(8,128)(2,1)S(1)} %collective-permute-done.6.refs_2_) | copy-start | bytes 4718596
  44.5 1.8 %copy-start.5 = (bf16[3,2048,128]{2,1,0:T(8,128)(2,1)}, bf16[3,2048,128]{2,1,0:T(8,128)(2,1)S(1)}, u32[]{:S(2)}) copy-start(bf16[3,2048,128]{2,1,0:T(8,128)(2,1)S(1)} %collective-permute-done.7.refs_1_) | copy-start | bytes 4718596
  44.6 6.1 %collective-permute-start.9 = (bf16[3,2048,128]{2,1,0:T(8,128)(2,1)S(1)}, bf16[3,2048,128]{2,1,0:T(8,128)(2,1)S(1)}, u32[]{:S(2)}, u32[]{:S(2)}) collective-permute-start(bf16[3,2048,128]{2,1,0:T(8,128)(2,1)S(1)} %collective-permute-done.6.refs_2_), channel_id=1, source_target_pairs={{0,8},{8,0},{16,24},{24,16},{1,9},{9,1},{17,25},{25,17},{2,10},{10... | collective-permute-start | bytes 4718600 | tf_op jit(solution)/shard_map/ppermute | solution.py:78
  44.6 32.1 %collective-permute-start.8 = (bf16[1,128,2048]{2,1,0:T(8,128)(2,1)}, bf16[1,128,2048]{2,1,0:T(8,128)(2,1)}, u32[]{:S(2)}, u32[]{:S(2)}) collective-permute-start(bf16[1,128,2048]{2,1,0:T(8,128)(2,1)} %collective-permute-done.4.refs_6_), channel_id=1, source_target_pairs={{0,2},{2,4},{4,6},{6,7},{7,5},{5,3},{3,1},{1,0},{8,10},{10,12},{12... | collective-permute-start | bytes 1572872 | tf_op jit(solution)/shard_map/ppermute | solution.py:169
  46.2 30.8 %collective-permute-start.10 = (bf16[1,128,2048]{2,1,0:T(8,128)(2,1)S(1)}, bf16[1,128,2048]{2,1,0:T(8,128)(2,1)}, u32[]{:S(2)}, u32[]{:S(2)}) collective-permute-start(bf16[1,128,2048]{2,1,0:T(8,128)(2,1)S(1)} %collective-permute-done.refs_2_), channel_id=1, source_target_pairs={{0,8},{8,0},{16,24},{24,16},{1,9},{9,1},{17,25},{25,17},{2,10},{10... | collective-permute-start | bytes 1572872 | tf_op jit(solution)/shard_map/ppermute | solution.py:78
  46.4 31.0 %collective-permute-start.11 = (bf16[1,128,2048]{2,1,0:T(8,128)(2,1)S(1)}, bf16[1,128,2048]{2,1,0:T(8,128)(2,1)}, u32[]{:S(2)}, u32[]{:S(2)}) collective-permute-start(bf16[1,128,2048]{2,1,0:T(8,128)(2,1)S(1)} %collective-permute-done.1.refs_3_), channel_id=1, source_target_pairs={{0,8},{8,0},{16,24},{24,16},{1,9},{9,1},{17,25},{25,17},{2,10},{10... | collective-permute-start | bytes 1572872 | tf_op jit(solution)/shard_map/ppermute | solution.py:78
  50.5 29.9 %copy-start.1 = (bf16[2,128,2048]{2,1,0:T(8,128)(2,1)S(1)}, bf16[2,128,2048]{2,1,0:T(8,128)(2,1)}, u32[]{:S(2)}) copy-start(bf16[2,128,2048]{2,1,0:T(8,128)(2,1)} %refs_1_.1) | copy-start | bytes 3145732
  50.5 27.0 %collective-permute-start.12 = (bf16[1,128,2048]{2,1,0:T(8,128)(2,1)S(1)}, bf16[1,128,2048]{2,1,0:T(8,128)(2,1)}, u32[]{:S(2)}, u32[]{:S(2)}) collective-permute-start(bf16[1,128,2048]{2,1,0:T(8,128)(2,1)S(1)} %collective-permute-done.2.refs_4_), channel_id=1, source_target_pairs={{0,8},{8,0},{16,24},{24,16},{1,9},{9,1},{17,25},{25,17},{2,10},{10... | collective-permute-start | bytes 1572872 | tf_op jit(solution)/shard_map/ppermute | solution.py:78
  50.7 1.1 %copy-start.6 = (bf16[3,2048,128]{2,1,0:T(8,128)(2,1)}, bf16[3,2048,128]{2,1,0:T(8,128)(2,1)S(1)}, u32[]{:S(2)}) copy-start(bf16[3,2048,128]{2,1,0:T(8,128)(2,1)S(1)} %collective-permute-done.9.refs_3_) | copy-start | bytes 4718596
  51.8 25.7 %collective-permute-start.13 = (bf16[1,128,2048]{2,1,0:T(8,128)(2,1)S(1)}, bf16[1,128,2048]{2,1,0:T(8,128)(2,1)}, u32[]{:S(2)}, u32[]{:S(2)}) collective-permute-start(bf16[1,128,2048]{2,1,0:T(8,128)(2,1)S(1)} %collective-permute-done.3.refs_5_), channel_id=1, source_target_pairs={{0,8},{8,0},{16,24},{24,16},{1,9},{9,1},{17,25},{25,17},{2,10},{10... | collective-permute-start | bytes 1572872 | tf_op jit(solution)/shard_map/ppermute | solution.py:78
  76.8 2.2 %collective-permute-start.14 = (bf16[1,128,2048]{2,1,0:T(8,128)(2,1)}, bf16[1,128,2048]{2,1,0:T(8,128)(2,1)S(1)}, u32[]{:S(2)}, u32[]{:S(2)}) collective-permute-start(bf16[1,128,2048]{2,1,0:T(8,128)(2,1)} %collective-permute-done.4.refs_6_), channel_id=1, source_target_pairs={{0,8},{8,0},{16,24},{24,16},{1,9},{9,1},{17,25},{25,17},{2,10},{10... | collective-permute-start | bytes 1572872 | tf_op jit(solution)/shard_map/ppermute | solution.py:78
  77.0 22.6 %copy-start.7 = (s32[6]{0:T(128)S(1)}, s32[6]{0:T(128)}, u32[]{:S(2)}) copy-start(s32[6]{0:T(128)} %param.8) | copy-start | bytes 76
  77.0 2.7 %collective-permute-start.15 = (bf16[1,128,2048]{2,1,0:T(8,128)(2,1)}, bf16[1,128,2048]{2,1,0:T(8,128)(2,1)S(1)}, u32[]{:S(2)}, u32[]{:S(2)}) collective-permute-start(bf16[1,128,2048]{2,1,0:T(8,128)(2,1)} %copy-done.2), channel_id=1, source_target_pairs={{0,8},{8,0},{16,24},{24,16},{1,9},{9,1},{17,25},{25,17},{2,10},{10... | collective-permute-start | bytes 1572872 | tf_op jit(solution)/shard_map/ppermute | solution.py:78
  77.4 3.1 %collective-permute-start.16 = (bf16[1,128,2048]{2,1,0:T(8,128)(2,1)}, bf16[1,128,2048]{2,1,0:T(8,128)(2,1)S(1)}, u32[]{:S(2)}, u32[]{:S(2)}) collective-permute-start(bf16[1,128,2048]{2,1,0:T(8,128)(2,1)} %collective-permute-done.8.refs_8_), channel_id=1, source_target_pairs={{0,8},{8,0},{16,24},{24,16},{1,9},{9,1},{17,25},{25,17},{2,10},{10... | collective-permute-start | bytes 1572872 | tf_op jit(solution)/shard_map/ppermute | solution.py:78
  80.5 1.9 %copy-start = (bf16[6,2048,128]{2,1,0:T(8,128)(2,1)S(1)}, bf16[6,2048,128]{2,1,0:T(8,128)(2,1)}, u32[]{:S(2)}) copy-start(bf16[6,2048,128]{2,1,0:T(8,128)(2,1)} %get-tuple-element.37.refs_0_) | copy-start | bytes 9437188
  (1 other events, 1.0 us)

commit v8 on v7

--- a/solution.py
+++ b/solution.py
@@ -80,7 +80,7 @@
 
 def kick_kernel(source_ref, living_ref, *refs):
     walker_refs = refs[:4]
-    field_ref, new_ref, theta_ref, buffer, copy_sem = refs[4:]
+    field_ref, new_ref, kicked_ref, buffer, copy_sem = refs[4:]
     s = pl.program_id(0)
     old_dev = walker_refs[0].shape[0]
     source = source_ref[s]
@@ -100,19 +100,7 @@
     live = living_ref[s] > 0
     new_ref[0] = jnp.where(live, kicked, jnp.zeros_like(kicked))
 
-    widened = kicked.astype(jnp.float32)
-    intersection = widened[:electrons, :]
-    rows = lax.broadcasted_iota(jnp.int32, (electrons, electrons), 0)
-    cols = lax.broadcasted_iota(jnp.int32, (electrons, electrons), 1)
-    eye = rows == cols
-    identity = eye.astype(jnp.float32)
-    diagonal = jnp.sum(jnp.where(eye, intersection, 0.0), axis=0, keepdims=True)
-    inverse = jnp.where(eye, 1.0 / diagonal, 0.0)
-    for sweep in range(ITERS):
-        product = jnp.dot(intersection, inverse, precision=lax.Precision.HIGHEST, preferred_element_type=jnp.float32)
-        inverse = jnp.dot(inverse, 2.0 * identity - product, precision=lax.Precision.HIGHEST, preferred_element_type=jnp.float32)
-    theta = jnp.dot(widened, inverse, precision=lax.Precision.HIGHEST, preferred_element_type=jnp.float32)
-    theta_ref[0] = theta.astype(jnp.bfloat16)
+    kicked_ref[0] = kicked
 
 
 def kick(old_walkers, beside, across, diagonal_peer, parent, field, walk_id):
@@ -134,12 +122,12 @@
         scratch_shapes=[pltpu.VMEM((orbitals, electrons), old_walkers.dtype), pltpu.SemaphoreType.DMA(())],
     )
     shape = jax.ShapeDtypeStruct((slot_dev, orbitals, electrons), jnp.bfloat16)
-    new_walkers, theta = pl.pallas_call(
+    new_walkers, kicked = pl.pallas_call(
         kick_kernel,
         out_shape=[shape, shape],
         grid_spec=grid_spec,
     )(index, living, old_walkers, beside, across, diagonal_peer, padded)
-    return new_walkers, theta
+    return new_walkers, green_half(kicked)
 
 
 def body(old_walkers, half_chol, parent, field):

time: 101 us -> 105 us (1.040)
  Pallas kernels: 40.7 us -> 30.5 us
  matrix products: 0 us -> 8.37 us
  local copies, waits for them, and re-layouts: 6.75 us -> 10.5 us
  other arithmetic: 2.84 us -> 5.14 us
    pallas_call x1, Pallas kernels: 24.6 us -> 14.6 us  [kick(): pl.pallas_call(kick_kernel, out_shape=[shape, shape], grid_spec=grid_spec)]
    dot_general x0 -> x7, matrix products: none -> 8.37 us  [the longest x3 3.12 us: green_half(): jnp.einsum('wij,wjk->wik', intersection, inverse, precision=lax.Precision...]
    slice x0 -> x1, local copies, waits for them, and re-layouts: none -> 4.73 us  [green_half(): intersection = widened[:, :electrons, :]]
    unnamed x16 -> x12, local copies, waits for them, and re-layouts: 4.09 us -> 1.18 us
    gather x0 -> x2, local copies, waits for them, and re-layouts: none -> 1.83 us  [green_half(): diagonal = jnp.diagonal(intersection, axis1=1, axis2=2)]
  transfers between devices with their start and end apart: 17 -> 17, of which waited for: 9 -> 9; matrix products, arithmetic and copies ran while one was open for 4% -> 20% of each run, Pallas kernels for 25% -> 14%
where the time goes in v8:
time: 105 us; the launch traced here: 104 us
  waiting for transfers between devices  36.7 us (35%)
  Pallas kernels  30.5 us (29%)
  starting transfers between devices  12.4 us (12%)
  local copies, waits for them, and re-layouts  10.5 us (10%)
  matrix products  8.37 us (8%)
  other arithmetic  5.14 us (5%)
    ppermute x4, waiting for transfers between devices, body(): ahead = lax.ppermute(ahead, 'chol', forward)  29.6 us
    pallas_call x1, Pallas kernels, block_energy(): pl.pallas_call(energy_kernel, out_shape=jax.ShapeDtypeStruct((n_slot, 128...  16 us
    pallas_call x1, Pallas kernels, kick(): pl.pallas_call(kick_kernel, out_shape=[shape, shape], grid_spec=grid_spec)  14.6 us
    ppermute x4, starting transfers between devices, body(): ahead = lax.ppermute(ahead, 'chol', forward)  7.75 us
    slice x1, local copies, waits for them, and re-layouts, green_half(): intersection = widened[:, :electrons, :]  4.73 us
    ppermute x3, waiting for transfers between devices, body(): behind = lax.ppermute(behind, 'chol', backward)  4.11 us
    ppermute x10, starting transfers between devices, swap_pairs(): return lax.ppermute(x, axis, perm)  3.75 us
    dot_general x3, matrix products, green_half(): jnp.einsum('wij,wjk->wik', intersection, inverse, precision=lax.Precision...  3.12 us
  transfers between devices with their start and end apart: 17, of which 9 were waited for; matrix products, arithmetic and copies ran while one was open for 20% of the time, Pallas kernels for 14%

profile of v8, /device:TPU:0, one launch (start us, length us, event | category | flops | bytes accessed | tf_op | source)
XLA Modules:
  0.0 104.4 jit_solution(2943888558526018748)
XLA Ops:
  1.7 3.1 %collective-permute-start = (bf16[1,128,2048]{2,1,0:T(8,128)(2,1)S(1)}, bf16[1,128,2048]{2,1,0:T(8,128)(2,1)S(1)}, u32[]{:S(2)}, u32[]{:S(2)}) collective-permute-start(bf16[1,128,2048]{2,1,0:T(8,128)(2,1)S(1)} %constant_dynamic-slice_fusion), channel_id=1, source_target_pairs={{0,2},{2,4},{4,6},{6,7},{7,5},{5,3},{3,1},{1,0},{8,10},{10,12},{12... | collective-permute-start | bytes 1572872 | tf_op jit(solution)/shard_map/ppermute | solution.py:157
  4.8 1.9 %collective-permute-start.6 = (bf16[3,2048,128]{2,1,0:T(8,128)(2,1)}, bf16[3,2048,128]{2,1,0:T(8,128)(2,1)S(1)}, u32[]{:S(2)}, u32[]{:S(2)}) collective-permute-start(bf16[3,2048,128]{2,1,0:T(8,128)(2,1)} %refs_0_.1), channel_id=1, source_target_pairs={{0,16},{8,24},{16,0},{24,8},{1,17},{9,25},{17,1},{25,9},{2,18},{10... | collective-permute-start | bytes 4718600 | tf_op jit(solution)/shard_map/ppermute | solution.py:78
  6.8 9.9 %collective-permute-done.refs_2_ = bf16[1,128,2048]{2,1,0:T(8,128)(2,1)S(1)} collective-permute-done((bf16[1,128,2048]{2,1,0:T(8,128)(2,1)S(1)}, bf16[1,128,2048]{2,1,0:T(8,128)(2,1)S(1)}, u32[]{:S(2)}, u32[]{:S(2)}) %collective-permute-start) | collective-permute-done | bytes 524320 | tf_op jit(solution)/shard_map/ppermute | solution.py:157
  16.7 1.5 %collective-permute-done.1.refs_3_ = bf16[1,128,2048]{2,1,0:T(8,128)(2,1)S(1)} collective-permute-done((bf16[1,128,2048]{2,1,0:T(8,128)(2,1)S(1)}, bf16[1,128,2048]{2,1,0:T(8,128)(2,1)S(1)}, u32[]{:S(2)}, u32[]{:S(2)}) %collective-permute-start.1) | collective-permute-done | bytes 524320 | tf_op jit(solution)/shard_map/ppermute | solution.py:160
  18.2 1.6 %collective-permute-start.2 = (bf16[1,128,2048]{2,1,0:T(8,128)(2,1)S(1)}, bf16[1,128,2048]{2,1,0:T(8,128)(2,1)S(1)}, u32[]{:S(2)}, u32[]{:S(2)}) collective-permute-start(bf16[1,128,2048]{2,1,0:T(8,128)(2,1)S(1)} %collective-permute-done.refs_2_), channel_id=1, source_target_pairs={{0,2},{2,4},{4,6},{6,7},{7,5},{5,3},{3,1},{1,0},{8,10},{10,12},{12... | collective-permute-start | bytes 1572872 | tf_op jit(solution)/shard_map/ppermute | solution.py:157
  20.2 10.4 %collective-permute-done.2.refs_4_ = bf16[1,128,2048]{2,1,0:T(8,128)(2,1)S(1)} collective-permute-done((bf16[1,128,2048]{2,1,0:T(8,128)(2,1)S(1)}, bf16[1,128,2048]{2,1,0:T(8,128)(2,1)S(1)}, u32[]{:S(2)}, u32[]{:S(2)}) %collective-permute-start.2) | collective-permute-done | bytes 524320 | tf_op jit(solution)/shard_map/ppermute | solution.py:157
  30.7 1.3 %collective-permute-done.3.refs_5_ = bf16[1,128,2048]{2,1,0:T(8,128)(2,1)S(1)} collective-permute-done((bf16[1,128,2048]{2,1,0:T(8,128)(2,1)S(1)}, bf16[1,128,2048]{2,1,0:T(8,128)(2,1)S(1)}, u32[]{:S(2)}, u32[]{:S(2)}) %collective-permute-start.3) | collective-permute-done | bytes 524320 | tf_op jit(solution)/shard_map/ppermute | solution.py:160
  32.0 1.6 %collective-permute-start.4 = (bf16[1,128,2048]{2,1,0:T(8,128)(2,1)S(1)}, bf16[1,128,2048]{2,1,0:T(8,128)(2,1)S(1)}, u32[]{:S(2)}, u32[]{:S(2)}) collective-permute-start(bf16[1,128,2048]{2,1,0:T(8,128)(2,1)S(1)} %collective-permute-done.2.refs_4_), channel_id=1, source_target_pairs={{0,2},{2,4},{4,6},{6,7},{7,5},{5,3},{3,1},{1,0},{8,10},{10,12},{12... | collective-permute-start | bytes 1572872 | tf_op jit(solution)/shard_map/ppermute | solution.py:157
  34.0 9.2 %collective-permute-done.4.refs_6_ = bf16[1,128,2048]{2,1,0:T(8,128)(2,1)S(1)} collective-permute-done((bf16[1,128,2048]{2,1,0:T(8,128)(2,1)S(1)}, bf16[1,128,2048]{2,1,0:T(8,128)(2,1)S(1)}, u32[]{:S(2)}, u32[]{:S(2)}) %collective-permute-start.4) | collective-permute-done | bytes 524320 | tf_op jit(solution)/shard_map/ppermute | solution.py:157
  43.2 1.3 %collective-permute-done.5.refs_7_ = bf16[1,128,2048]{2,1,0:T(8,128)(2,1)S(1)} collective-permute-done((bf16[1,128,2048]{2,1,0:T(8,128)(2,1)S(1)}, bf16[1,128,2048]{2,1,0:T(8,128)(2,1)S(1)}, u32[]{:S(2)}, u32[]{:S(2)}) %collective-permute-start.5) | collective-permute-done | bytes 524320 | tf_op jit(solution)/shard_map/ppermute | solution.py:160
  44.6 1.6 %scatter.4.refs_4_ = f32[8,2048]{1,0:T(8,128)} pad(f32[6,2048]{1,0:T(8,128)} %param.9, f32[]{:T(128)} %constant.74.clone.1), padding=0_2x0_0 | pad | bytes 114692 | tf_op jit(solution)/shard_map/scatter | solution.py:114
  47.4 1.2 %fusion.12.source_ref = s32[6]{0:T(128)} fusion(s32[6]{0:T(128)} %param.8, s32[]{:T(128)S(6)} %axis_index.15), kind=kLoop, calls=%fused_computation.24 | loop fusion | flops 96 | bytes 52 | tf_op jit(solution)/shard_map/add | solution.py:112
  48.6 1.2 %compare_convert_fusion.living_ref = s32[6]{0:T(128)} fusion(s32[6]{0:T(128)} %param.8), kind=kLoop, calls=%fused_computation.23 | loop fusion | flops 12 | bytes 48 | tf_op jit(solution)/shard_map/convert_element_type | solution.py:109
  52.0 1.5 %collective-permute-start.8 = (bf16[1,128,2048]{2,1,0:T(8,128)(2,1)S(1)}, bf16[1,128,2048]{2,1,0:T(8,128)(2,1)}, u32[]{:S(2)}, u32[]{:S(2)}) collective-permute-start(bf16[1,128,2048]{2,1,0:T(8,128)(2,1)S(1)} %collective-permute-done.4.refs_6_), channel_id=1, source_target_pairs={{0,2},{2,4},{4,6},{6,7},{7,5},{5,3},{3,1},{1,0},{8,10},{10,12},{12... | collective-permute-start | bytes 1572872 | tf_op jit(solution)/shard_map/ppermute | solution.py:157
  53.6 14.6 %shard_map.59 = (bf16[6,2048,128]{2,1,0:T(8,128)(2,1)}, bf16[6,2048,128]{2,1,0:T(8,128)(2,1)}) custom-call(s32[6]{0:T(128)} %fusion.12.source_ref, s32[6]{0:T(128)} %compare_convert_fusion.living_ref, bf16[3,2048,128]{2,1,0:T(8,128)(2,1)} %refs_0_.1, bf16[3,2048,128]{2,1,0:T(8,128)(2,1)} %collective-permute-done.7.refs_1_, bf16[3,2048,128]{2,1,0:T(8,128)(2,1)} %copy-done.2, ...), custom_call_target="tpu_custom_call" | custom-call | tf_op jit(solution)/shard_map/pallas_call | solution.py:125
  69.1 4.7 %copy.8 = f32[6,128,128]{0,2,1:T(8,128)} copy(f32[6,128,128]{2,1,0:T(8,128)S(1)} %slice_convert_fusion) | data formatting | bytes 786432 | tf_op jit(solution)/shard_map/slice | solution.py:14
  73.9 1.8 %gather_fusion = f32[128,6]{1,0:T(8,128)S(1)} fusion(f32[6,128,128]{0,2,1:T(8,128)} %copy.8, s32[128]{0:T(128)S(1)} %or_bitcast_fusion), kind=kCustom, calls=%fused_computation | custom fusion | bytes 7168 | tf_op jit(solution)/shard_map/jit(diagonal)/gather | solution.py:16
  75.7 1.5 %convolution_subtract_fusion.2 = f32[6,128,128]{2,1,0:T(8,128)S(1)} fusion(f32[128,128]{1,0:T(8,128)} %fusion.10, f32[6,128]{1,0:T(8,128)S(1)} %copy.9, f32[128,128]{1,0:T(8,128)} %fusion.11, bf16[6,2048,128]{2,1,0:T(8,128)(2,1)} %get-tuple-element.35), kind=kOutput, calls=%fused_computation.4 | convolution fusion | flops 151191552 | bytes 723968 | tf_op jit(solution)/shard_map/wij,wjk->wik/dot_general | solution.py:19
  77.2 1.4 %fusion = f32[6,128,128]{2,1,0:T(8,128)S(1)} fusion(f32[6,128,128]{2,1,0:T(8,128)S(1)} %convolution_subtract_fusion.2, f32[6,128]{1,0:T(8,128)S(1)} %copy.9, f32[128,128]{1,0:T(8,128)} %fusion.11), kind=kOutput, calls=%fused_computation.5 | convolution fusion | flops 151093248 | bytes 855040 | tf_op jit(solution)/shard_map/wij,wjk->wik/dot_general | solution.py:20
  78.6 1.3 %convolution_subtract_fusion.1 = f32[6,128,128]{2,1,0:T(8,128)S(1)} fusion(f32[6,128,128]{2,1,0:T(8,128)S(1)} %fusion, f32[128,128]{1,0:T(8,128)S(1)} %copy-done.4, bf16[6,2048,128]{2,1,0:T(8,128)(2,1)} %get-tuple-element.35), kind=kOutput, calls=%fused_computation.3 | convolution fusion | flops 151093248 | bytes 1048576 | tf_op jit(solution)/shard_map/wij,wjk->wik/dot_general | solution.py:19
  81.3 2.8 %convolution_convert_fusion.refs_0_ = bf16[6,2048,128]{2,1,0:T(8,128)(2,1)S(1)} fusion(bf16[6,2048,128]{2,1,0:T(8,128)(2,1)S(1)} %copy-done.1, f32[6,128,128]{2,1,0:T(8,128)S(1)} %fusion.14), kind=kOutput, calls=%fused_computation.1 | convolution fusion | flops 2417491968 | bytes 6684672 | tf_op jit(solution)/shard_map/wnk,wkj->wnj/dot_general | solution.py:26
  84.9 1.2 %collective-permute-done.14.refs_13_ = bf16[1,128,2048]{2,1,0:T(8,128)(2,1)S(1)} collective-permute-done((bf16[1,128,2048]{2,1,0:T(8,128)(2,1)S(1)}, bf16[1,128,2048]{2,1,0:T(8,128)(2,1)S(1)}, u32[]{:S(2)}, u32[]{:S(2)}) %collective-permute-start.14) | collective-permute-done | bytes 524320 | tf_op jit(solution)/shard_map/ppermute | solution.py:78
  86.1 1.5 %collective-permute-done.15.refs_14_ = bf16[1,128,2048]{2,1,0:T(8,128)(2,1)S(1)} collective-permute-done((bf16[1,128,2048]{2,1,0:T(8,128)(2,1)S(1)}, bf16[1,128,2048]{2,1,0:T(8,128)(2,1)S(1)}, u32[]{:S(2)}, u32[]{:S(2)}) %collective-permute-start.15) | collective-permute-done | bytes 524320 | tf_op jit(solution)/shard_map/ppermute | solution.py:78
  87.8 16.0 %shard_map.60 = f32[6,128]{1,0:T(8,128)S(1)} custom-call(bf16[6,2048,128]{2,1,0:T(8,128)(2,1)S(1)} %convolution_convert_fusion.refs_0_, bf16[2,128,2048]{2,1,0:T(8,128)(2,1)S(1)} %copy-done, bf16[1,128,2048]{2,1,0:T(8,128)(2,1)S(1)} %collective-permute-done.refs_2_, bf16[1,128,2048]{2,1,0:T(8,128)(2,1)S(1)} %collective-permute-done.1.refs_3_, ...), custom_call_target="tpu_custom_call" | custom-call | tf_op jit(solution)/shard_map/pallas_call | solution.py:62
  (44 shorter events, 9.5 us)
Async XLA Ops:
  1.7 14.9 %collective-permute-start = (bf16[1,128,2048]{2,1,0:T(8,128)(2,1)S(1)}, bf16[1,128,2048]{2,1,0:T(8,128)(2,1)S(1)}, u32[]{:S(2)}, u32[]{:S(2)}) collective-permute-start(bf16[1,128,2048]{2,1,0:T(8,128)(2,1)S(1)} %constant_dynamic-slice_fusion), channel_id=1, source_target_pairs={{0,2},{2,4},{4,6},{6,7},{7,5},{5,3},{3,1},{1,0},{8,10},{10,12},{12... | collective-permute-start | bytes 1572872 | tf_op jit(solution)/shard_map/ppermute | solution.py:157
  4.8 13.4 %collective-permute-start.1 = (bf16[1,128,2048]{2,1,0:T(8,128)(2,1)S(1)}, bf16[1,128,2048]{2,1,0:T(8,128)(2,1)S(1)}, u32[]{:S(2)}, u32[]{:S(2)}) collective-permute-start(bf16[1,128,2048]{2,1,0:T(8,128)(2,1)S(1)} %constant_dynamic-slice_fusion), channel_id=1, source_target_pairs={{2,0},{4,2},{6,4},{7,6},{5,7},{3,5},{1,3},{0,1},{10,8},{12,10},{14... | collective-permute-start | bytes 1572872 | tf_op jit(solution)/shard_map/ppermute | solution.py:160
  4.8 39.7 %collective-permute-start.6 = (bf16[3,2048,128]{2,1,0:T(8,128)(2,1)}, bf16[3,2048,128]{2,1,0:T(8,128)(2,1)S(1)}, u32[]{:S(2)}, u32[]{:S(2)}) collective-permute-start(bf16[3,2048,128]{2,1,0:T(8,128)(2,1)} %refs_0_.1), channel_id=1, source_target_pairs={{0,16},{8,24},{16,0},{24,8},{1,17},{9,25},{17,1},{25,9},{2,18},{10... | collective-permute-start | bytes 4718600 | tf_op jit(solution)/shard_map/ppermute | solution.py:78
  6.8 37.8 %collective-permute-start.7 = (bf16[3,2048,128]{2,1,0:T(8,128)(2,1)}, bf16[3,2048,128]{2,1,0:T(8,128)(2,1)}, u32[]{:S(2)}, u32[]{:S(2)}) collective-permute-start(bf16[3,2048,128]{2,1,0:T(8,128)(2,1)} %refs_0_.1), channel_id=1, source_target_pairs={{0,8},{8,0},{16,24},{24,16},{1,9},{9,1},{17,25},{25,17},{2,10},{10... | collective-permute-start | bytes 4718600 | tf_op jit(solution)/shard_map/ppermute | solution.py:78
  18.2 12.5 %collective-permute-start.2 = (bf16[1,128,2048]{2,1,0:T(8,128)(2,1)S(1)}, bf16[1,128,2048]{2,1,0:T(8,128)(2,1)S(1)}, u32[]{:S(2)}, u32[]{:S(2)}) collective-permute-start(bf16[1,128,2048]{2,1,0:T(8,128)(2,1)S(1)} %collective-permute-done.refs_2_), channel_id=1, source_target_pairs={{0,2},{2,4},{4,6},{6,7},{7,5},{5,3},{3,1},{1,0},{8,10},{10,12},{12... | collective-permute-start | bytes 1572872 | tf_op jit(solution)/shard_map/ppermute | solution.py:157
  19.8 12.2 %collective-permute-start.3 = (bf16[1,128,2048]{2,1,0:T(8,128)(2,1)S(1)}, bf16[1,128,2048]{2,1,0:T(8,128)(2,1)S(1)}, u32[]{:S(2)}, u32[]{:S(2)}) collective-permute-start(bf16[1,128,2048]{2,1,0:T(8,128)(2,1)S(1)} %collective-permute-done.1.refs_3_), channel_id=1, source_target_pairs={{2,0},{4,2},{6,4},{7,6},{5,7},{3,5},{1,3},{0,1},{10,8},{12,10},{14... | collective-permute-start | bytes 1572872 | tf_op jit(solution)/shard_map/ppermute | solution.py:160
  32.0 11.3 %collective-permute-start.4 = (bf16[1,128,2048]{2,1,0:T(8,128)(2,1)S(1)}, bf16[1,128,2048]{2,1,0:T(8,128)(2,1)S(1)}, u32[]{:S(2)}, u32[]{:S(2)}) collective-permute-start(bf16[1,128,2048]{2,1,0:T(8,128)(2,1)S(1)} %collective-permute-done.2.refs_4_), channel_id=1, source_target_pairs={{0,2},{2,4},{4,6},{6,7},{7,5},{5,3},{3,1},{1,0},{8,10},{10,12},{12... | collective-permute-start | bytes 1572872 | tf_op jit(solution)/shard_map/ppermute | solution.py:157
  33.5 11.0 %collective-permute-start.5 = (bf16[1,128,2048]{2,1,0:T(8,128)(2,1)S(1)}, bf16[1,128,2048]{2,1,0:T(8,128)(2,1)S(1)}, u32[]{:S(2)}, u32[]{:S(2)}) collective-permute-start(bf16[1,128,2048]{2,1,0:T(8,128)(2,1)S(1)} %collective-permute-done.3.refs_5_), channel_id=1, source_target_pairs={{2,0},{4,2},{6,4},{7,6},{5,7},{3,5},{1,3},{0,1},{10,8},{12,10},{14... | collective-permute-start | bytes 1572872 | tf_op jit(solution)/shard_map/ppermute | solution.py:160
  44.5 6.3 %copy-start.2 = (bf16[3,2048,128]{2,1,0:T(8,128)(2,1)}, bf16[3,2048,128]{2,1,0:T(8,128)(2,1)S(1)}, u32[]{:S(2)}) copy-start(bf16[3,2048,128]{2,1,0:T(8,128)(2,1)S(1)} %collective-permute-done.6.refs_2_) | copy-start | bytes 4718596
  44.6 6.3 %collective-permute-start.9 = (bf16[3,2048,128]{2,1,0:T(8,128)(2,1)S(1)}, bf16[3,2048,128]{2,1,0:T(8,128)(2,1)S(1)}, u32[]{:S(2)}, u32[]{:S(2)}) collective-permute-start(bf16[3,2048,128]{2,1,0:T(8,128)(2,1)S(1)} %collective-permute-done.6.refs_2_), channel_id=1, source_target_pairs={{0,8},{8,0},{16,24},{24,16},{1,9},{9,1},{17,25},{25,17},{2,10},{10... | collective-permute-start | bytes 4718600 | tf_op jit(solution)/shard_map/ppermute | solution.py:78
  49.9 34.5 %collective-permute-start.10 = (bf16[1,128,2048]{2,1,0:T(8,128)(2,1)S(1)}, bf16[1,128,2048]{2,1,0:T(8,128)(2,1)}, u32[]{:S(2)}, u32[]{:S(2)}) collective-permute-start(bf16[1,128,2048]{2,1,0:T(8,128)(2,1)S(1)} %collective-permute-done.refs_2_), channel_id=1, source_target_pairs={{0,8},{8,0},{16,24},{24,16},{1,9},{9,1},{17,25},{25,17},{2,10},{10... | collective-permute-start | bytes 1572872 | tf_op jit(solution)/shard_map/ppermute | solution.py:78
  50.3 34.5 %collective-permute-start.11 = (bf16[1,128,2048]{2,1,0:T(8,128)(2,1)S(1)}, bf16[1,128,2048]{2,1,0:T(8,128)(2,1)}, u32[]{:S(2)}, u32[]{:S(2)}) collective-permute-start(bf16[1,128,2048]{2,1,0:T(8,128)(2,1)S(1)} %collective-permute-done.1.refs_3_), channel_id=1, source_target_pairs={{0,8},{8,0},{16,24},{24,16},{1,9},{9,1},{17,25},{25,17},{2,10},{10... | collective-permute-start | bytes 1572872 | tf_op jit(solution)/shard_map/ppermute | solution.py:78
  50.4 34.5 %collective-permute-start.12 = (bf16[1,128,2048]{2,1,0:T(8,128)(2,1)S(1)}, bf16[1,128,2048]{2,1,0:T(8,128)(2,1)}, u32[]{:S(2)}, u32[]{:S(2)}) collective-permute-start(bf16[1,128,2048]{2,1,0:T(8,128)(2,1)S(1)} %collective-permute-done.2.refs_4_), channel_id=1, source_target_pairs={{0,8},{8,0},{16,24},{24,16},{1,9},{9,1},{17,25},{25,17},{2,10},{10... | collective-permute-start | bytes 1572872 | tf_op jit(solution)/shard_map/ppermute | solution.py:78
  50.8 34.1 %collective-permute-start.13 = (bf16[1,128,2048]{2,1,0:T(8,128)(2,1)S(1)}, bf16[1,128,2048]{2,1,0:T(8,128)(2,1)}, u32[]{:S(2)}, u32[]{:S(2)}) collective-permute-start(bf16[1,128,2048]{2,1,0:T(8,128)(2,1)S(1)} %collective-permute-done.3.refs_5_), channel_id=1, source_target_pairs={{0,8},{8,0},{16,24},{24,16},{1,9},{9,1},{17,25},{25,17},{2,10},{10... | collective-permute-start | bytes 1572872 | tf_op jit(solution)/shard_map/ppermute | solution.py:78
  50.9 1.2 %copy-start.3 = (bf16[3,2048,128]{2,1,0:T(8,128)(2,1)}, bf16[3,2048,128]{2,1,0:T(8,128)(2,1)S(1)}, u32[]{:S(2)}) copy-start(bf16[3,2048,128]{2,1,0:T(8,128)(2,1)S(1)} %collective-permute-done.9.refs_3_) | copy-start | bytes 4718596
  52.0 32.1 %collective-permute-start.8 = (bf16[1,128,2048]{2,1,0:T(8,128)(2,1)S(1)}, bf16[1,128,2048]{2,1,0:T(8,128)(2,1)}, u32[]{:S(2)}, u32[]{:S(2)}) collective-permute-start(bf16[1,128,2048]{2,1,0:T(8,128)(2,1)S(1)} %collective-permute-done.4.refs_6_), channel_id=1, source_target_pairs={{0,2},{2,4},{4,6},{6,7},{7,5},{5,3},{3,1},{1,0},{8,10},{10,12},{12... | collective-permute-start | bytes 1572872 | tf_op jit(solution)/shard_map/ppermute | solution.py:157
  73.9 4.7 %copy-start.4 = (f32[128,128]{1,0:T(8,128)S(1)}, f32[128,128]{1,0:T(8,128)}, u32[]{:S(2)}) copy-start(f32[128,128]{1,0:T(8,128)} %fusion.10) | copy-start | bytes 196612
  75.7 4.7 %copy-start.1 = (bf16[6,2048,128]{2,1,0:T(8,128)(2,1)S(1)}, bf16[6,2048,128]{2,1,0:T(8,128)(2,1)}, u32[]{:S(2)}) copy-start(bf16[6,2048,128]{2,1,0:T(8,128)(2,1)} %get-tuple-element.35) | copy-start | bytes 9437188
  81.3 6.5 %copy-start = (bf16[2,128,2048]{2,1,0:T(8,128)(2,1)S(1)}, bf16[2,128,2048]{2,1,0:T(8,128)(2,1)}, u32[]{:S(2)}) copy-start(bf16[2,128,2048]{2,1,0:T(8,128)(2,1)} %refs_1_.1) | copy-start | bytes 3145732
  84.2 2.0 %collective-permute-start.14 = (bf16[1,128,2048]{2,1,0:T(8,128)(2,1)S(1)}, bf16[1,128,2048]{2,1,0:T(8,128)(2,1)S(1)}, u32[]{:S(2)}, u32[]{:S(2)}) collective-permute-start(bf16[1,128,2048]{2,1,0:T(8,128)(2,1)S(1)} %collective-permute-done.4.refs_6_), channel_id=1, source_target_pairs={{0,8},{8,0},{16,24},{24,16},{1,9},{9,1},{17,25},{25,17},{2,10},{10... | collective-permute-start | bytes 1572872 | tf_op jit(solution)/shard_map/ppermute | solution.py:78
  84.4 19.6 %copy-start.5 = (s32[6]{0:T(128)S(1)}, s32[6]{0:T(128)}, u32[]{:S(2)}) copy-start(s32[6]{0:T(128)} %param.8) | copy-start | bytes 76
  84.4 3.3 %collective-permute-start.15 = (bf16[1,128,2048]{2,1,0:T(8,128)(2,1)S(1)}, bf16[1,128,2048]{2,1,0:T(8,128)(2,1)S(1)}, u32[]{:S(2)}, u32[]{:S(2)}) collective-permute-start(bf16[1,128,2048]{2,1,0:T(8,128)(2,1)S(1)} %collective-permute-done.5.refs_7_), channel_id=1, source_target_pairs={{0,8},{8,0},{16,24},{24,16},{1,9},{9,1},{17,25},{25,17},{2,10},{10... | collective-permute-start | bytes 1572872 | tf_op jit(solution)/shard_map/ppermute | solution.py:78
  84.7 3.1 %collective-permute-start.16 = (bf16[1,128,2048]{2,1,0:T(8,128)(2,1)}, bf16[1,128,2048]{2,1,0:T(8,128)(2,1)S(1)}, u32[]{:S(2)}, u32[]{:S(2)}) collective-permute-start(bf16[1,128,2048]{2,1,0:T(8,128)(2,1)} %collective-permute-done.8.refs_8_), channel_id=1, source_target_pairs={{0,8},{8,0},{16,24},{24,16},{1,9},{9,1},{17,25},{25,17},{2,10},{10... | collective-permute-start | bytes 1572872 | tf_op jit(solution)/shard_map/ppermute | solution.py:78

commit v9 on v8

--- a/solution.py
+++ b/solution.py
@@ -80,7 +80,7 @@
 
 def kick_kernel(source_ref, living_ref, *refs):
     walker_refs = refs[:4]
-    field_ref, new_ref, kicked_ref, buffer, copy_sem = refs[4:]
+    scale_ref, new_ref, kicked_ref, buffer, copy_sem = refs[4:]
     s = pl.program_id(0)
     old_dev = walker_refs[0].shape[0]
     source = source_ref[s]
@@ -91,12 +91,7 @@
             copy.start()
             copy.wait()
 
-    orbitals, electrons = buffer.shape
-    lanes = field_ref.shape[0]
-    scale = jnp.transpose(jnp.exp(field_ref[...]))
-    pick = lax.broadcasted_iota(jnp.int32, scale.shape, 1) == s
-    scale = jnp.sum(jnp.where(pick, scale, 0.0), axis=1, keepdims=True)
-    kicked = (scale * buffer[...].astype(jnp.float32)).astype(jnp.bfloat16)
+    kicked = (scale_ref[0] * buffer[...].astype(jnp.float32)).astype(jnp.bfloat16)
     live = living_ref[s] > 0
     new_ref[0] = jnp.where(live, kicked, jnp.zeros_like(kicked))
 
@@ -110,14 +105,13 @@
     source = jnp.maximum(parent, 0)
     relative = (source // old_dev) ^ walk_id
     index = (relative * old_dev + source % old_dev).astype(jnp.int32)
-    lanes = max(8, -(-slot_dev // 8) * 8)
-    padded = jnp.zeros((lanes, orbitals), jnp.float32).at[:slot_dev].set(field)
+    scale = jnp.broadcast_to(jnp.exp(field)[:, :, None], (slot_dev, orbitals, electrons))
     any_space = pl.BlockSpec(memory_space=pl.ANY)
     slot_block = pl.BlockSpec((1, orbitals, electrons), lambda s, *_: (s, 0, 0))
     grid_spec = pltpu.PrefetchScalarGridSpec(
         num_scalar_prefetch=2,
         grid=(slot_dev,),
-        in_specs=[any_space] * 4 + [pl.BlockSpec((lanes, orbitals), lambda s, *_: (0, 0))],
+        in_specs=[any_space] * 4 + [pl.BlockSpec((1, orbitals, electrons), lambda s, *_: (s, 0, 0))],
         out_specs=[slot_block, slot_block],
         scratch_shapes=[pltpu.VMEM((orbitals, electrons), old_walkers.dtype), pltpu.SemaphoreType.DMA(())],
     )
@@ -126,7 +120,7 @@
         kick_kernel,
         out_shape=[shape, shape],
         grid_spec=grid_spec,
-    )(index, living, old_walkers, beside, across, diagonal_peer, padded)
+    )(index, living, old_walkers, beside, across, diagonal_peer, scale)
     return new_walkers, green_half(kicked)
 
 

time: 105 us -> 107 us (1.019)
  local copies, waits for them, and re-layouts: 10.5 us -> 13.6 us
  Pallas kernels: 30.5 us -> 29.2 us
    broadcast_in_dim x0 -> x1, local copies, waits for them, and re-layouts: none -> 3.7 us  [kick(): jnp.broadcast_to(jnp.exp(field)[:, :, None], (slot_dev, orbitals, electro...]
    scatter x1 -> x0, local copies, waits for them, and re-layouts: 1.55 us -> none  [kick(): padded = jnp.zeros((lanes, orbitals), jnp.float32).at[:slot_dev].set(field)]
    pallas_call x1, Pallas kernels: 14.6 us -> 13.2 us  [kick(): pl.pallas_call(kick_kernel, out_shape=[shape, shape], grid_spec=grid_spec)]
  transfers between devices with their start and end apart: 17 -> 17, of which waited for: 9 -> 9; matrix products, arithmetic and copies ran while one was open for 20% -> 23% of each run, Pallas kernels for 14% -> 12%
where the time goes in v9:
time: 107 us; the launch traced here: 106 us
  waiting for transfers between devices  36.7 us (34%)
  Pallas kernels  29.2 us (27%)
  local copies, waits for them, and re-layouts  13.6 us (13%)
  starting transfers between devices  12.4 us (12%)
  matrix products  8.37 us (8%)
  other arithmetic  5.1 us (5%)
    ppermute x4, waiting for transfers between devices, body(): ahead = lax.ppermute(ahead, 'chol', forward)  29.6 us
    pallas_call x1, Pallas kernels, block_energy(): pl.pallas_call(energy_kernel, out_shape=jax.ShapeDtypeStruct((n_slot, 128...  16 us
    pallas_call x1, Pallas kernels, kick(): pl.pallas_call(kick_kernel, out_shape=[shape, shape], grid_spec=grid_spec)  13.2 us
    ppermute x4, starting transfers between devices, body(): ahead = lax.ppermute(ahead, 'chol', forward)  7.75 us
    slice x1, local copies, waits for them, and re-layouts, green_half(): intersection = widened[:, :electrons, :]  4.73 us
    ppermute x3, waiting for transfers between devices, body(): behind = lax.ppermute(behind, 'chol', backward)  4.11 us
    ppermute x10, starting transfers between devices, swap_pairs(): return lax.ppermute(x, axis, perm)  3.75 us
    broadcast_in_dim x1, local copies, waits for them, and re-layouts, kick(): jnp.broadcast_to(jnp.exp(field)[:, :, None], (slot_dev, orbitals, electro...  3.7 us
  transfers between devices with their start and end apart: 17, of which 9 were waited for; matrix products, arithmetic and copies ran while one was open for 23% of the time, Pallas kernels for 12%

profile of v9, /device:TPU:0, one launch (start us, length us, event | category | flops | bytes accessed | tf_op | source)
XLA Modules:
  0.0 106.1 jit_solution(3816693475420420595)
XLA Ops:
  1.7 3.1 %collective-permute-start = (bf16[1,128,2048]{2,1,0:T(8,128)(2,1)S(1)}, bf16[1,128,2048]{2,1,0:T(8,128)(2,1)S(1)}, u32[]{:S(2)}, u32[]{:S(2)}) collective-permute-start(bf16[1,128,2048]{2,1,0:T(8,128)(2,1)S(1)} %constant_dynamic-slice_fusion), channel_id=1, source_target_pairs={{0,2},{2,4},{4,6},{6,7},{7,5},{5,3},{3,1},{1,0},{8,10},{10,12},{12... | collective-permute-start | bytes 1572872 | tf_op jit(solution)/shard_map/ppermute | solution.py:151
  4.8 1.9 %collective-permute-start.6 = (bf16[3,2048,128]{2,1,0:T(8,128)(2,1)}, bf16[3,2048,128]{2,1,0:T(8,128)(2,1)S(1)}, u32[]{:S(2)}, u32[]{:S(2)}) collective-permute-start(bf16[3,2048,128]{2,1,0:T(8,128)(2,1)} %refs_0_.1), channel_id=1, source_target_pairs={{0,16},{8,24},{16,0},{24,8},{1,17},{9,25},{17,1},{25,9},{2,18},{10... | collective-permute-start | bytes 4718600 | tf_op jit(solution)/shard_map/ppermute | solution.py:78
  6.8 9.9 %collective-permute-done.refs_2_ = bf16[1,128,2048]{2,1,0:T(8,128)(2,1)S(1)} collective-permute-done((bf16[1,128,2048]{2,1,0:T(8,128)(2,1)S(1)}, bf16[1,128,2048]{2,1,0:T(8,128)(2,1)S(1)}, u32[]{:S(2)}, u32[]{:S(2)}) %collective-permute-start) | collective-permute-done | bytes 524320 | tf_op jit(solution)/shard_map/ppermute | solution.py:151
  16.7 1.5 %collective-permute-done.1.refs_3_ = bf16[1,128,2048]{2,1,0:T(8,128)(2,1)S(1)} collective-permute-done((bf16[1,128,2048]{2,1,0:T(8,128)(2,1)S(1)}, bf16[1,128,2048]{2,1,0:T(8,128)(2,1)S(1)}, u32[]{:S(2)}, u32[]{:S(2)}) %collective-permute-start.1) | collective-permute-done | bytes 524320 | tf_op jit(solution)/shard_map/ppermute | solution.py:154
  18.2 1.6 %collective-permute-start.2 = (bf16[1,128,2048]{2,1,0:T(8,128)(2,1)S(1)}, bf16[1,128,2048]{2,1,0:T(8,128)(2,1)S(1)}, u32[]{:S(2)}, u32[]{:S(2)}) collective-permute-start(bf16[1,128,2048]{2,1,0:T(8,128)(2,1)S(1)} %collective-permute-done.refs_2_), channel_id=1, source_target_pairs={{0,2},{2,4},{4,6},{6,7},{7,5},{5,3},{3,1},{1,0},{8,10},{10,12},{12... | collective-permute-start | bytes 1572872 | tf_op jit(solution)/shard_map/ppermute | solution.py:151
  20.2 10.4 %collective-permute-done.2.refs_4_ = bf16[1,128,2048]{2,1,0:T(8,128)(2,1)S(1)} collective-permute-done((bf16[1,128,2048]{2,1,0:T(8,128)(2,1)S(1)}, bf16[1,128,2048]{2,1,0:T(8,128)(2,1)S(1)}, u32[]{:S(2)}, u32[]{:S(2)}) %collective-permute-start.2) | collective-permute-done | bytes 524320 | tf_op jit(solution)/shard_map/ppermute | solution.py:151
  30.7 1.3 %collective-permute-done.3.refs_5_ = bf16[1,128,2048]{2,1,0:T(8,128)(2,1)S(1)} collective-permute-done((bf16[1,128,2048]{2,1,0:T(8,128)(2,1)S(1)}, bf16[1,128,2048]{2,1,0:T(8,128)(2,1)S(1)}, u32[]{:S(2)}, u32[]{:S(2)}) %collective-permute-start.3) | collective-permute-done | bytes 524320 | tf_op jit(solution)/shard_map/ppermute | solution.py:154
  32.0 1.6 %collective-permute-start.4 = (bf16[1,128,2048]{2,1,0:T(8,128)(2,1)S(1)}, bf16[1,128,2048]{2,1,0:T(8,128)(2,1)S(1)}, u32[]{:S(2)}, u32[]{:S(2)}) collective-permute-start(bf16[1,128,2048]{2,1,0:T(8,128)(2,1)S(1)} %collective-permute-done.2.refs_4_), channel_id=1, source_target_pairs={{0,2},{2,4},{4,6},{6,7},{7,5},{5,3},{3,1},{1,0},{8,10},{10,12},{12... | collective-permute-start | bytes 1572872 | tf_op jit(solution)/shard_map/ppermute | solution.py:151
  34.0 9.2 %collective-permute-done.4.refs_6_ = bf16[1,128,2048]{2,1,0:T(8,128)(2,1)S(1)} collective-permute-done((bf16[1,128,2048]{2,1,0:T(8,128)(2,1)S(1)}, bf16[1,128,2048]{2,1,0:T(8,128)(2,1)S(1)}, u32[]{:S(2)}, u32[]{:S(2)}) %collective-permute-start.4) | collective-permute-done | bytes 524320 | tf_op jit(solution)/shard_map/ppermute | solution.py:151
  43.2 1.3 %collective-permute-done.5.refs_7_ = bf16[1,128,2048]{2,1,0:T(8,128)(2,1)S(1)} collective-permute-done((bf16[1,128,2048]{2,1,0:T(8,128)(2,1)S(1)}, bf16[1,128,2048]{2,1,0:T(8,128)(2,1)S(1)}, u32[]{:S(2)}, u32[]{:S(2)}) %collective-permute-start.5) | collective-permute-done | bytes 524320 | tf_op jit(solution)/shard_map/ppermute | solution.py:154
  46.9 1.2 %fusion.12.source_ref = s32[6]{0:T(128)} fusion(s32[6]{0:T(128)} %param.6, s32[]{:T(128)S(6)} %axis_index.15), kind=kLoop, calls=%fused_computation.24 | loop fusion | flops 96 | bytes 52 | tf_op jit(solution)/shard_map/add | solution.py:107
  48.0 1.2 %compare_convert_fusion.living_ref = s32[6]{0:T(128)} fusion(s32[6]{0:T(128)} %param.6), kind=kLoop, calls=%fused_computation.23 | loop fusion | flops 12 | bytes 48 | tf_op jit(solution)/shard_map/convert_element_type | solution.py:104
  51.4 1.5 %collective-permute-start.8 = (bf16[1,128,2048]{2,1,0:T(8,128)(2,1)S(1)}, bf16[1,128,2048]{2,1,0:T(8,128)(2,1)}, u32[]{:S(2)}, u32[]{:S(2)}) collective-permute-start(bf16[1,128,2048]{2,1,0:T(8,128)(2,1)S(1)} %collective-permute-done.4.refs_6_), channel_id=1, source_target_pairs={{0,2},{2,4},{4,6},{6,7},{7,5},{5,3},{3,1},{1,0},{8,10},{10,12},{12... | collective-permute-start | bytes 1572872 | tf_op jit(solution)/shard_map/ppermute | solution.py:151
  52.9 3.7 %broadcast_in_dim.9.refs_4_ = f32[6,2048,128]{2,1,0:T(8,128)} broadcast(f32[6,2048]{1,0:T(8,128)S(1)} %exp.3), dimensions={0,1} | broadcast | bytes 6340608 | tf_op jit(solution)/shard_map/broadcast_in_dim | solution.py:108
  56.6 13.2 %shard_map.59 = (bf16[6,2048,128]{2,1,0:T(8,128)(2,1)}, bf16[6,2048,128]{2,1,0:T(8,128)(2,1)}) custom-call(s32[6]{0:T(128)} %fusion.12.source_ref, s32[6]{0:T(128)} %compare_convert_fusion.living_ref, bf16[3,2048,128]{2,1,0:T(8,128)(2,1)} %refs_0_.1, bf16[3,2048,128]{2,1,0:T(8,128)(2,1)} %collective-permute-done.7.refs_1_, bf16[3,2048,128]{2,1,0:T(8,128)(2,1)} %copy-done.2, ...), custom_call_target="tpu_custom_call" | custom-call | tf_op jit(solution)/shard_map/pallas_call | solution.py:119
  70.8 4.7 %copy.8 = f32[6,128,128]{0,2,1:T(8,128)} copy(f32[6,128,128]{2,1,0:T(8,128)S(1)} %slice_convert_fusion) | data formatting | bytes 786432 | tf_op jit(solution)/shard_map/slice | solution.py:14
  75.6 1.8 %gather_fusion = f32[128,6]{1,0:T(8,128)S(1)} fusion(f32[6,128,128]{0,2,1:T(8,128)} %copy.8, s32[128]{0:T(128)S(1)} %or_bitcast_fusion), kind=kCustom, calls=%fused_computation | custom fusion | bytes 7168 | tf_op jit(solution)/shard_map/jit(diagonal)/gather | solution.py:16
  77.4 1.5 %convolution_subtract_fusion.2 = f32[6,128,128]{2,1,0:T(8,128)S(1)} fusion(f32[128,128]{1,0:T(8,128)} %fusion.10, f32[6,128]{1,0:T(8,128)S(1)} %copy.9, f32[128,128]{1,0:T(8,128)} %fusion.11, bf16[6,2048,128]{2,1,0:T(8,128)(2,1)} %get-tuple-element.23), kind=kOutput, calls=%fused_computation.4 | convolution fusion | flops 151191552 | bytes 723968 | tf_op jit(solution)/shard_map/wij,wjk->wik/dot_general | solution.py:19
  78.9 1.4 %fusion = f32[6,128,128]{2,1,0:T(8,128)S(1)} fusion(f32[6,128,128]{2,1,0:T(8,128)S(1)} %convolution_subtract_fusion.2, f32[6,128]{1,0:T(8,128)S(1)} %copy.9, f32[128,128]{1,0:T(8,128)} %fusion.11), kind=kOutput, calls=%fused_computation.5 | convolution fusion | flops 151093248 | bytes 855040 | tf_op jit(solution)/shard_map/wij,wjk->wik/dot_general | solution.py:20
  80.3 1.3 %convolution_subtract_fusion.1 = f32[6,128,128]{2,1,0:T(8,128)S(1)} fusion(f32[6,128,128]{2,1,0:T(8,128)S(1)} %fusion, f32[128,128]{1,0:T(8,128)S(1)} %copy-done.4, bf16[6,2048,128]{2,1,0:T(8,128)(2,1)} %get-tuple-element.23), kind=kOutput, calls=%fused_computation.3 | convolution fusion | flops 151093248 | bytes 1048576 | tf_op jit(solution)/shard_map/wij,wjk->wik/dot_general | solution.py:19
  83.0 2.8 %convolution_convert_fusion.refs_0_ = bf16[6,2048,128]{2,1,0:T(8,128)(2,1)S(1)} fusion(bf16[6,2048,128]{2,1,0:T(8,128)(2,1)S(1)} %copy-done.1, f32[6,128,128]{2,1,0:T(8,128)S(1)} %fusion.14), kind=kOutput, calls=%fused_computation.1 | convolution fusion | flops 2417491968 | bytes 6684672 | tf_op jit(solution)/shard_map/wnk,wkj->wnj/dot_general | solution.py:26
  86.6 1.2 %collective-permute-done.14.refs_13_ = bf16[1,128,2048]{2,1,0:T(8,128)(2,1)S(1)} collective-permute-done((bf16[1,128,2048]{2,1,0:T(8,128)(2,1)S(1)}, bf16[1,128,2048]{2,1,0:T(8,128)(2,1)S(1)}, u32[]{:S(2)}, u32[]{:S(2)}) %collective-permute-start.14) | collective-permute-done | bytes 524320 | tf_op jit(solution)/shard_map/ppermute | solution.py:78
  87.8 1.5 %collective-permute-done.15.refs_14_ = bf16[1,128,2048]{2,1,0:T(8,128)(2,1)S(1)} collective-permute-done((bf16[1,128,2048]{2,1,0:T(8,128)(2,1)S(1)}, bf16[1,128,2048]{2,1,0:T(8,128)(2,1)S(1)}, u32[]{:S(2)}, u32[]{:S(2)}) %collective-permute-start.15) | collective-permute-done | bytes 524320 | tf_op jit(solution)/shard_map/ppermute | solution.py:78
  89.5 16.0 %shard_map.60 = f32[6,128]{1,0:T(8,128)S(1)} custom-call(bf16[6,2048,128]{2,1,0:T(8,128)(2,1)S(1)} %convolution_convert_fusion.refs_0_, bf16[2,128,2048]{2,1,0:T(8,128)(2,1)S(1)} %copy-done, bf16[1,128,2048]{2,1,0:T(8,128)(2,1)S(1)} %collective-permute-done.refs_2_, bf16[1,128,2048]{2,1,0:T(8,128)(2,1)S(1)} %collective-permute-done.1.refs_3_, ...), custom_call_target="tpu_custom_call" | custom-call | tf_op jit(solution)/shard_map/pallas_call | solution.py:62
  (45 shorter events, 10.5 us)
Async XLA Ops:
  1.7 14.9 %collective-permute-start = (bf16[1,128,2048]{2,1,0:T(8,128)(2,1)S(1)}, bf16[1,128,2048]{2,1,0:T(8,128)(2,1)S(1)}, u32[]{:S(2)}, u32[]{:S(2)}) collective-permute-start(bf16[1,128,2048]{2,1,0:T(8,128)(2,1)S(1)} %constant_dynamic-slice_fusion), channel_id=1, source_target_pairs={{0,2},{2,4},{4,6},{6,7},{7,5},{5,3},{3,1},{1,0},{8,10},{10,12},{12... | collective-permute-start | bytes 1572872 | tf_op jit(solution)/shard_map/ppermute | solution.py:151
  4.8 13.4 %collective-permute-start.1 = (bf16[1,128,2048]{2,1,0:T(8,128)(2,1)S(1)}, bf16[1,128,2048]{2,1,0:T(8,128)(2,1)S(1)}, u32[]{:S(2)}, u32[]{:S(2)}) collective-permute-start(bf16[1,128,2048]{2,1,0:T(8,128)(2,1)S(1)} %constant_dynamic-slice_fusion), channel_id=1, source_target_pairs={{2,0},{4,2},{6,4},{7,6},{5,7},{3,5},{1,3},{0,1},{10,8},{12,10},{14... | collective-permute-start | bytes 1572872 | tf_op jit(solution)/shard_map/ppermute | solution.py:154
  4.8 39.7 %collective-permute-start.6 = (bf16[3,2048,128]{2,1,0:T(8,128)(2,1)}, bf16[3,2048,128]{2,1,0:T(8,128)(2,1)S(1)}, u32[]{:S(2)}, u32[]{:S(2)}) collective-permute-start(bf16[3,2048,128]{2,1,0:T(8,128)(2,1)} %refs_0_.1), channel_id=1, source_target_pairs={{0,16},{8,24},{16,0},{24,8},{1,17},{9,25},{17,1},{25,9},{2,18},{10... | collective-permute-start | bytes 4718600 | tf_op jit(solution)/shard_map/ppermute | solution.py:78
  6.8 37.8 %collective-permute-start.7 = (bf16[3,2048,128]{2,1,0:T(8,128)(2,1)}, bf16[3,2048,128]{2,1,0:T(8,128)(2,1)}, u32[]{:S(2)}, u32[]{:S(2)}) collective-permute-start(bf16[3,2048,128]{2,1,0:T(8,128)(2,1)} %refs_0_.1), channel_id=1, source_target_pairs={{0,8},{8,0},{16,24},{24,16},{1,9},{9,1},{17,25},{25,17},{2,10},{10... | collective-permute-start | bytes 4718600 | tf_op jit(solution)/shard_map/ppermute | solution.py:78
  18.2 12.5 %collective-permute-start.2 = (bf16[1,128,2048]{2,1,0:T(8,128)(2,1)S(1)}, bf16[1,128,2048]{2,1,0:T(8,128)(2,1)S(1)}, u32[]{:S(2)}, u32[]{:S(2)}) collective-permute-start(bf16[1,128,2048]{2,1,0:T(8,128)(2,1)S(1)} %collective-permute-done.refs_2_), channel_id=1, source_target_pairs={{0,2},{2,4},{4,6},{6,7},{7,5},{5,3},{3,1},{1,0},{8,10},{10,12},{12... | collective-permute-start | bytes 1572872 | tf_op jit(solution)/shard_map/ppermute | solution.py:151
  19.8 12.2 %collective-permute-start.3 = (bf16[1,128,2048]{2,1,0:T(8,128)(2,1)S(1)}, bf16[1,128,2048]{2,1,0:T(8,128)(2,1)S(1)}, u32[]{:S(2)}, u32[]{:S(2)}) collective-permute-start(bf16[1,128,2048]{2,1,0:T(8,128)(2,1)S(1)} %collective-permute-done.1.refs_3_), channel_id=1, source_target_pairs={{2,0},{4,2},{6,4},{7,6},{5,7},{3,5},{1,3},{0,1},{10,8},{12,10},{14... | collective-permute-start | bytes 1572872 | tf_op jit(solution)/shard_map/ppermute | solution.py:154
  32.0 11.3 %collective-permute-start.4 = (bf16[1,128,2048]{2,1,0:T(8,128)(2,1)S(1)}, bf16[1,128,2048]{2,1,0:T(8,128)(2,1)S(1)}, u32[]{:S(2)}, u32[]{:S(2)}) collective-permute-start(bf16[1,128,2048]{2,1,0:T(8,128)(2,1)S(1)} %collective-permute-done.2.refs_4_), channel_id=1, source_target_pairs={{0,2},{2,4},{4,6},{6,7},{7,5},{5,3},{3,1},{1,0},{8,10},{10,12},{12... | collective-permute-start | bytes 1572872 | tf_op jit(solution)/shard_map/ppermute | solution.py:151
  33.5 11.0 %collective-permute-start.5 = (bf16[1,128,2048]{2,1,0:T(8,128)(2,1)S(1)}, bf16[1,128,2048]{2,1,0:T(8,128)(2,1)S(1)}, u32[]{:S(2)}, u32[]{:S(2)}) collective-permute-start(bf16[1,128,2048]{2,1,0:T(8,128)(2,1)S(1)} %collective-permute-done.3.refs_5_), channel_id=1, source_target_pairs={{2,0},{4,2},{6,4},{7,6},{5,7},{3,5},{1,3},{0,1},{10,8},{12,10},{14... | collective-permute-start | bytes 1572872 | tf_op jit(solution)/shard_map/ppermute | solution.py:154
  44.5 5.7 %copy-start.2 = (bf16[3,2048,128]{2,1,0:T(8,128)(2,1)}, bf16[3,2048,128]{2,1,0:T(8,128)(2,1)S(1)}, u32[]{:S(2)}) copy-start(bf16[3,2048,128]{2,1,0:T(8,128)(2,1)S(1)} %collective-permute-done.6.refs_2_) | copy-start | bytes 4718596
  44.6 5.7 %collective-permute-start.9 = (bf16[3,2048,128]{2,1,0:T(8,128)(2,1)S(1)}, bf16[3,2048,128]{2,1,0:T(8,128)(2,1)S(1)}, u32[]{:S(2)}, u32[]{:S(2)}) collective-permute-start(bf16[3,2048,128]{2,1,0:T(8,128)(2,1)S(1)} %collective-permute-done.6.refs_2_), channel_id=1, source_target_pairs={{0,8},{8,0},{16,24},{24,16},{1,9},{9,1},{17,25},{25,17},{2,10},{10... | collective-permute-start | bytes 4718600 | tf_op jit(solution)/shard_map/ppermute | solution.py:78
  49.2 36.9 %collective-permute-start.10 = (bf16[1,128,2048]{2,1,0:T(8,128)(2,1)S(1)}, bf16[1,128,2048]{2,1,0:T(8,128)(2,1)}, u32[]{:S(2)}, u32[]{:S(2)}) collective-permute-start(bf16[1,128,2048]{2,1,0:T(8,128)(2,1)S(1)} %collective-permute-done.refs_2_), channel_id=1, source_target_pairs={{0,8},{8,0},{16,24},{24,16},{1,9},{9,1},{17,25},{25,17},{2,10},{10... | collective-permute-start | bytes 1572872 | tf_op jit(solution)/shard_map/ppermute | solution.py:78
  49.6 36.8 %collective-permute-start.11 = (bf16[1,128,2048]{2,1,0:T(8,128)(2,1)S(1)}, bf16[1,128,2048]{2,1,0:T(8,128)(2,1)}, u32[]{:S(2)}, u32[]{:S(2)}) collective-permute-start(bf16[1,128,2048]{2,1,0:T(8,128)(2,1)S(1)} %collective-permute-done.1.refs_3_), channel_id=1, source_target_pairs={{0,8},{8,0},{16,24},{24,16},{1,9},{9,1},{17,25},{25,17},{2,10},{10... | collective-permute-start | bytes 1572872 | tf_op jit(solution)/shard_map/ppermute | solution.py:78
  49.7 36.9 %collective-permute-start.12 = (bf16[1,128,2048]{2,1,0:T(8,128)(2,1)S(1)}, bf16[1,128,2048]{2,1,0:T(8,128)(2,1)}, u32[]{:S(2)}, u32[]{:S(2)}) collective-permute-start(bf16[1,128,2048]{2,1,0:T(8,128)(2,1)S(1)} %collective-permute-done.2.refs_4_), channel_id=1, source_target_pairs={{0,8},{8,0},{16,24},{24,16},{1,9},{9,1},{17,25},{25,17},{2,10},{10... | collective-permute-start | bytes 1572872 | tf_op jit(solution)/shard_map/ppermute | solution.py:78
  50.1 36.5 %collective-permute-start.13 = (bf16[1,128,2048]{2,1,0:T(8,128)(2,1)S(1)}, bf16[1,128,2048]{2,1,0:T(8,128)(2,1)}, u32[]{:S(2)}, u32[]{:S(2)}) collective-permute-start(bf16[1,128,2048]{2,1,0:T(8,128)(2,1)S(1)} %collective-permute-done.3.refs_5_), channel_id=1, source_target_pairs={{0,8},{8,0},{16,24},{24,16},{1,9},{9,1},{17,25},{25,17},{2,10},{10... | collective-permute-start | bytes 1572872 | tf_op jit(solution)/shard_map/ppermute | solution.py:78
  50.2 1.1 %copy-start.3 = (bf16[3,2048,128]{2,1,0:T(8,128)(2,1)}, bf16[3,2048,128]{2,1,0:T(8,128)(2,1)S(1)}, u32[]{:S(2)}) copy-start(bf16[3,2048,128]{2,1,0:T(8,128)(2,1)S(1)} %collective-permute-done.9.refs_3_) | copy-start | bytes 4718596
  51.4 34.5 %collective-permute-start.8 = (bf16[1,128,2048]{2,1,0:T(8,128)(2,1)S(1)}, bf16[1,128,2048]{2,1,0:T(8,128)(2,1)}, u32[]{:S(2)}, u32[]{:S(2)}) collective-permute-start(bf16[1,128,2048]{2,1,0:T(8,128)(2,1)S(1)} %collective-permute-done.4.refs_6_), channel_id=1, source_target_pairs={{0,2},{2,4},{4,6},{6,7},{7,5},{5,3},{3,1},{1,0},{8,10},{10,12},{12... | collective-permute-start | bytes 1572872 | tf_op jit(solution)/shard_map/ppermute | solution.py:151
  75.6 4.7 %copy-start.4 = (f32[128,128]{1,0:T(8,128)S(1)}, f32[128,128]{1,0:T(8,128)}, u32[]{:S(2)}) copy-start(f32[128,128]{1,0:T(8,128)} %fusion.10) | copy-start | bytes 196612
  77.4 4.7 %copy-start.1 = (bf16[6,2048,128]{2,1,0:T(8,128)(2,1)S(1)}, bf16[6,2048,128]{2,1,0:T(8,128)(2,1)}, u32[]{:S(2)}) copy-start(bf16[6,2048,128]{2,1,0:T(8,128)(2,1)} %get-tuple-element.23) | copy-start | bytes 9437188
  83.0 6.5 %copy-start = (bf16[2,128,2048]{2,1,0:T(8,128)(2,1)S(1)}, bf16[2,128,2048]{2,1,0:T(8,128)(2,1)}, u32[]{:S(2)}) copy-start(bf16[2,128,2048]{2,1,0:T(8,128)(2,1)} %refs_1_.1) | copy-start | bytes 3145732
  85.9 2.0 %collective-permute-start.14 = (bf16[1,128,2048]{2,1,0:T(8,128)(2,1)S(1)}, bf16[1,128,2048]{2,1,0:T(8,128)(2,1)S(1)}, u32[]{:S(2)}, u32[]{:S(2)}) collective-permute-start(bf16[1,128,2048]{2,1,0:T(8,128)(2,1)S(1)} %collective-permute-done.4.refs_6_), channel_id=1, source_target_pairs={{0,8},{8,0},{16,24},{24,16},{1,9},{9,1},{17,25},{25,17},{2,10},{10... | collective-permute-start | bytes 1572872 | tf_op jit(solution)/shard_map/ppermute | solution.py:78
  86.1 19.6 %copy-start.5 = (s32[6]{0:T(128)S(1)}, s32[6]{0:T(128)}, u32[]{:S(2)}) copy-start(s32[6]{0:T(128)} %param.6) | copy-start | bytes 76
  86.1 3.3 %collective-permute-start.15 = (bf16[1,128,2048]{2,1,0:T(8,128)(2,1)S(1)}, bf16[1,128,2048]{2,1,0:T(8,128)(2,1)S(1)}, u32[]{:S(2)}, u32[]{:S(2)}) collective-permute-start(bf16[1,128,2048]{2,1,0:T(8,128)(2,1)S(1)} %collective-permute-done.5.refs_7_), channel_id=1, source_target_pairs={{0,8},{8,0},{16,24},{24,16},{1,9},{9,1},{17,25},{25,17},{2,10},{10... | collective-permute-start | bytes 1572872 | tf_op jit(solution)/shard_map/ppermute | solution.py:78
  86.4 3.1 %collective-permute-start.16 = (bf16[1,128,2048]{2,1,0:T(8,128)(2,1)}, bf16[1,128,2048]{2,1,0:T(8,128)(2,1)S(1)}, u32[]{:S(2)}, u32[]{:S(2)}) collective-permute-start(bf16[1,128,2048]{2,1,0:T(8,128)(2,1)} %collective-permute-done.8.refs_8_), channel_id=1, source_target_pairs={{0,8},{8,0},{16,24},{24,16},{1,9},{9,1},{17,25},{25,17},{2,10},{10... | collective-permute-start | bytes 1572872 | tf_op jit(solution)/shard_map/ppermute | solution.py:78

commit v10 on v7

--- a/solution.py
+++ b/solution.py
@@ -80,39 +80,60 @@
 
 def kick_kernel(source_ref, living_ref, *refs):
     walker_refs = refs[:4]
-    field_ref, new_ref, theta_ref, buffer, copy_sem = refs[4:]
-    s = pl.program_id(0)
+    field_ref, new_hbm, theta_hbm, walkers, kicked_buf, new_buf, theta_buf, in_sem, out_sem = refs[4:]
     old_dev = walker_refs[0].shape[0]
-    source = source_ref[s]
-    for r, walker_ref in enumerate(walker_refs):
-        @pl.when(source // old_dev == r)
-        def _(walker_ref=walker_ref):
-            copy = pltpu.make_async_copy(walker_ref.at[source % old_dev], buffer, copy_sem)
-            copy.start()
-            copy.wait()
-
-    orbitals, electrons = buffer.shape
-    lanes = field_ref.shape[0]
-    scale = jnp.transpose(jnp.exp(field_ref[...]))
-    pick = lax.broadcasted_iota(jnp.int32, scale.shape, 1) == s
-    scale = jnp.sum(jnp.where(pick, scale, 0.0), axis=1, keepdims=True)
-    kicked = (scale * buffer[...].astype(jnp.float32)).astype(jnp.bfloat16)
-    live = living_ref[s] > 0
-    new_ref[0] = jnp.where(live, kicked, jnp.zeros_like(kicked))
-
-    widened = kicked.astype(jnp.float32)
-    intersection = widened[:electrons, :]
+    n_slot, orbitals, electrons = walkers.shape
+
+    for s in range(n_slot):
+        source = source_ref[s]
+        for r, walker_ref in enumerate(walker_refs):
+            group = source // old_dev
+            chosen = group >= r if r == len(walker_refs) - 1 else group == r
+
+            @pl.when(chosen)
+            def _(walker_ref=walker_ref, source=source, s=s):
+                pltpu.make_async_copy(walker_ref.at[source % old_dev], walkers.at[s], in_sem.at[s]).start()
+
+    scale_all = jnp.transpose(jnp.exp(field_ref[...]))
     rows = lax.broadcasted_iota(jnp.int32, (electrons, electrons), 0)
     cols = lax.broadcasted_iota(jnp.int32, (electrons, electrons), 1)
     eye = rows == cols
     identity = eye.astype(jnp.float32)
-    diagonal = jnp.sum(jnp.where(eye, intersection, 0.0), axis=0, keepdims=True)
-    inverse = jnp.where(eye, 1.0 / diagonal, 0.0)
+    out_copies = []
+    intersections = []
+    inverses = []
+    for s in range(n_slot):
+        pltpu.make_async_copy(walker_refs[0].at[0], walkers.at[s], in_sem.at[s]).wait()
+        kicked = (scale_all[:, s:s + 1] * walkers[s].astype(jnp.float32)).astype(jnp.bfloat16)
+        kicked_buf[s] = kicked
+        new_buf[s] = jnp.where(living_ref[s] > 0, kicked, jnp.zeros_like(kicked))
+        copy = pltpu.make_async_copy(new_buf.at[s], new_hbm.at[s], out_sem.at[0, s])
+        copy.start()
+        out_copies.append(copy)
+        intersection = kicked[:electrons, :].astype(jnp.float32)
+        diagonal = jnp.sum(jnp.where(eye, intersection, 0.0), axis=0, keepdims=True)
+        intersections.append(intersection)
+        inverses.append(jnp.where(eye, 1.0 / diagonal, 0.0))
+
     for sweep in range(ITERS):
-        product = jnp.dot(intersection, inverse, precision=lax.Precision.HIGHEST, preferred_element_type=jnp.float32)
-        inverse = jnp.dot(inverse, 2.0 * identity - product, precision=lax.Precision.HIGHEST, preferred_element_type=jnp.float32)
-    theta = jnp.dot(widened, inverse, precision=lax.Precision.HIGHEST, preferred_element_type=jnp.float32)
-    theta_ref[0] = theta.astype(jnp.bfloat16)
+        products = [
+            jnp.dot(x, inv, precision=lax.Precision.HIGHEST, preferred_element_type=jnp.float32)
+            for x, inv in zip(intersections, inverses)
+        ]
+        inverses = [
+            jnp.dot(inv, 2.0 * identity - p, precision=lax.Precision.HIGHEST, preferred_element_type=jnp.float32)
+            for inv, p in zip(inverses, products)
+        ]
+
+    for s in range(n_slot):
+        widened = kicked_buf[s].astype(jnp.float32)
+        theta = jnp.dot(widened, inverses[s], precision=lax.Precision.HIGHEST, preferred_element_type=jnp.float32)
+        theta_buf[s] = theta.astype(jnp.bfloat16)
+        copy = pltpu.make_async_copy(theta_buf.at[s], theta_hbm.at[s], out_sem.at[1, s])
+        copy.start()
+        out_copies.append(copy)
+    for copy in out_copies:
+        copy.wait()
 
 
 def kick(old_walkers, beside, across, diagonal_peer, parent, field, walk_id):
@@ -125,15 +146,22 @@
     lanes = max(8, -(-slot_dev // 8) * 8)
     padded = jnp.zeros((lanes, orbitals), jnp.float32).at[:slot_dev].set(field)
     any_space = pl.BlockSpec(memory_space=pl.ANY)
-    slot_block = pl.BlockSpec((1, orbitals, electrons), lambda s, *_: (s, 0, 0))
+    slots = (slot_dev, orbitals, electrons)
     grid_spec = pltpu.PrefetchScalarGridSpec(
         num_scalar_prefetch=2,
-        grid=(slot_dev,),
-        in_specs=[any_space] * 4 + [pl.BlockSpec((lanes, orbitals), lambda s, *_: (0, 0))],
-        out_specs=[slot_block, slot_block],
-        scratch_shapes=[pltpu.VMEM((orbitals, electrons), old_walkers.dtype), pltpu.SemaphoreType.DMA(())],
+        grid=(1,),
+        in_specs=[any_space] * 4 + [pl.BlockSpec((lanes, orbitals), lambda i, *_: (0, 0))],
+        out_specs=[any_space, any_space],
+        scratch_shapes=[
+            pltpu.VMEM(slots, jnp.bfloat16),
+            pltpu.VMEM(slots, jnp.bfloat16),
+            pltpu.VMEM(slots, jnp.bfloat16),
+            pltpu.VMEM(slots, jnp.bfloat16),
+            pltpu.SemaphoreType.DMA((slot_dev,)),
+            pltpu.SemaphoreType.DMA((2, slot_dev)),
+        ],
     )
-    shape = jax.ShapeDtypeStruct((slot_dev, orbitals, electrons), jnp.bfloat16)
+    shape = jax.ShapeDtypeStruct(slots, jnp.bfloat16)
     new_walkers, theta = pl.pallas_call(
         kick_kernel,
         out_shape=[shape, shape],

time: 101 us -> 88.9 us (0.88)
  Pallas kernels: 40.7 us -> 29.1 us
    pallas_call x1, Pallas kernels: 24.6 us -> 13 us  [kick(): pl.pallas_call(kick_kernel, out_shape=[shape, shape], grid_spec=grid_spec)]
  transfers between devices with their start and end apart: 17 -> 17, of which waited for: 9 -> 9; matrix products, arithmetic and copies ran while one was open for 4% -> 4% of each run, Pallas kernels for 25% -> 15%
where the time goes in v10:
time: 88.9 us; the launch traced here: 88.5 us
  waiting for transfers between devices  36.7 us (41%)
  Pallas kernels  29.1 us (33%)
  starting transfers between devices  12.5 us (14%)
  local copies, waits for them, and re-layouts  6.75 us (8%)
  other arithmetic  2.84 us (3%)
    ppermute x4, waiting for transfers between devices, body(): ahead = lax.ppermute(ahead, 'chol', forward)  29.7 us
    pallas_call x1, Pallas kernels, block_energy(): pl.pallas_call(energy_kernel, out_shape=jax.ShapeDtypeStruct((n_slot, 128...  16.1 us
    pallas_call x1, Pallas kernels, kick(): pl.pallas_call(kick_kernel, out_shape=[shape, shape], grid_spec=grid_spec)  13 us
    ppermute x4, starting transfers between devices, body(): ahead = lax.ppermute(ahead, 'chol', forward)  7.8 us
    unnamed x16, local copies, waits for them, and re-layouts  4.09 us
    ppermute x3, waiting for transfers between devices, body(): behind = lax.ppermute(behind, 'chol', backward)  4 us
    ppermute x10, starting transfers between devices, swap_pairs(): return lax.ppermute(x, axis, perm)  3.77 us
    ppermute x10, waiting for transfers between devices, swap_pairs(): return lax.ppermute(x, axis, perm)  2.95 us
  transfers between devices with their start and end apart: 17, of which 9 were waited for; matrix products, arithmetic and copies ran while one was open for 4% of the time, Pallas kernels for 15%

profile of v10, /device:TPU:0, one launch (start us, length us, event | category | flops | bytes accessed | tf_op | source)
XLA Modules:
  0.0 88.5 jit_solution(17081762309088206797)
XLA Ops:
  0.6 1.1 %constant_dynamic-slice_fusion = bf16[1,128,2048]{2,1,0:T(8,128)(2,1)S(1)} fusion(bf16[2,128,2048]{2,1,0:T(8,128)(2,1)} %refs_1_.1, s32[]{:T(128)S(6)} %select_n.26), kind=kLoop, calls=%fused_computation.6 | loop fusion | bytes 1048580 | tf_op jit(solution)/shard_map/dynamic_slice | solution.py:183
  1.7 3.1 %collective-permute-start = (bf16[1,128,2048]{2,1,0:T(8,128)(2,1)S(1)}, bf16[1,128,2048]{2,1,0:T(8,128)(2,1)S(1)}, u32[]{:S(2)}, u32[]{:S(2)}) collective-permute-start(bf16[1,128,2048]{2,1,0:T(8,128)(2,1)S(1)} %constant_dynamic-slice_fusion), channel_id=1, source_target_pairs={{0,2},{2,4},{4,6},{6,7},{7,5},{5,3},{3,1},{1,0},{8,10},{10,12},{12... | collective-permute-start | bytes 1572872 | tf_op jit(solution)/shard_map/ppermute | solution.py:197
  4.8 1.9 %collective-permute-start.6 = (bf16[3,2048,128]{2,1,0:T(8,128)(2,1)}, bf16[3,2048,128]{2,1,0:T(8,128)(2,1)S(1)}, u32[]{:S(2)}, u32[]{:S(2)}) collective-permute-start(bf16[3,2048,128]{2,1,0:T(8,128)(2,1)} %refs_0_.1), channel_id=1, source_target_pairs={{0,16},{8,24},{16,0},{24,8},{1,17},{9,25},{17,1},{25,9},{2,18},{10... | collective-permute-start | bytes 4718600 | tf_op jit(solution)/shard_map/ppermute | solution.py:78
  6.7 9.9 %collective-permute-done.refs_2_ = bf16[1,128,2048]{2,1,0:T(8,128)(2,1)S(1)} collective-permute-done((bf16[1,128,2048]{2,1,0:T(8,128)(2,1)S(1)}, bf16[1,128,2048]{2,1,0:T(8,128)(2,1)S(1)}, u32[]{:S(2)}, u32[]{:S(2)}) %collective-permute-start) | collective-permute-done | bytes 524320 | tf_op jit(solution)/shard_map/ppermute | solution.py:197
  16.7 1.5 %collective-permute-done.1.refs_3_ = bf16[1,128,2048]{2,1,0:T(8,128)(2,1)S(1)} collective-permute-done((bf16[1,128,2048]{2,1,0:T(8,128)(2,1)S(1)}, bf16[1,128,2048]{2,1,0:T(8,128)(2,1)S(1)}, u32[]{:S(2)}, u32[]{:S(2)}) %collective-permute-start.1) | collective-permute-done | bytes 524320 | tf_op jit(solution)/shard_map/ppermute | solution.py:200
  18.2 1.6 %collective-permute-start.2 = (bf16[1,128,2048]{2,1,0:T(8,128)(2,1)S(1)}, bf16[1,128,2048]{2,1,0:T(8,128)(2,1)S(1)}, u32[]{:S(2)}, u32[]{:S(2)}) collective-permute-start(bf16[1,128,2048]{2,1,0:T(8,128)(2,1)S(1)} %collective-permute-done.refs_2_), channel_id=1, source_target_pairs={{0,2},{2,4},{4,6},{6,7},{7,5},{5,3},{3,1},{1,0},{8,10},{10,12},{12... | collective-permute-start | bytes 1572872 | tf_op jit(solution)/shard_map/ppermute | solution.py:197
  20.2 10.4 %collective-permute-done.2.refs_4_ = bf16[1,128,2048]{2,1,0:T(8,128)(2,1)S(1)} collective-permute-done((bf16[1,128,2048]{2,1,0:T(8,128)(2,1)S(1)}, bf16[1,128,2048]{2,1,0:T(8,128)(2,1)S(1)}, u32[]{:S(2)}, u32[]{:S(2)}) %collective-permute-start.2) | collective-permute-done | bytes 524320 | tf_op jit(solution)/shard_map/ppermute | solution.py:197
  30.7 1.3 %collective-permute-done.3.refs_5_ = bf16[1,128,2048]{2,1,0:T(8,128)(2,1)S(1)} collective-permute-done((bf16[1,128,2048]{2,1,0:T(8,128)(2,1)S(1)}, bf16[1,128,2048]{2,1,0:T(8,128)(2,1)S(1)}, u32[]{:S(2)}, u32[]{:S(2)}) %collective-permute-start.3) | collective-permute-done | bytes 524320 | tf_op jit(solution)/shard_map/ppermute | solution.py:200
  32.0 1.6 %collective-permute-start.4 = (bf16[1,128,2048]{2,1,0:T(8,128)(2,1)S(1)}, bf16[1,128,2048]{2,1,0:T(8,128)(2,1)}, u32[]{:S(2)}, u32[]{:S(2)}) collective-permute-start(bf16[1,128,2048]{2,1,0:T(8,128)(2,1)S(1)} %collective-permute-done.2.refs_4_), channel_id=1, source_target_pairs={{0,2},{2,4},{4,6},{6,7},{7,5},{5,3},{3,1},{1,0},{8,10},{10,12},{12... | collective-permute-start | bytes 1572872 | tf_op jit(solution)/shard_map/ppermute | solution.py:197
  34.0 9.4 %collective-permute-done.4.refs_6_ = bf16[1,128,2048]{2,1,0:T(8,128)(2,1)} collective-permute-done((bf16[1,128,2048]{2,1,0:T(8,128)(2,1)S(1)}, bf16[1,128,2048]{2,1,0:T(8,128)(2,1)}, u32[]{:S(2)}, u32[]{:S(2)}) %collective-permute-start.4) | collective-permute-done | bytes 524320 | tf_op jit(solution)/shard_map/ppermute | solution.py:197
  43.3 1.2 %collective-permute-done.5.refs_7_ = bf16[1,128,2048]{2,1,0:T(8,128)(2,1)S(1)} collective-permute-done((bf16[1,128,2048]{2,1,0:T(8,128)(2,1)S(1)}, bf16[1,128,2048]{2,1,0:T(8,128)(2,1)S(1)}, u32[]{:S(2)}, u32[]{:S(2)}) %collective-permute-start.5) | collective-permute-done | bytes 524320 | tf_op jit(solution)/shard_map/ppermute | solution.py:200
  44.6 1.6 %collective-permute-start.8 = (bf16[1,128,2048]{2,1,0:T(8,128)(2,1)}, bf16[1,128,2048]{2,1,0:T(8,128)(2,1)}, u32[]{:S(2)}, u32[]{:S(2)}) collective-permute-start(bf16[1,128,2048]{2,1,0:T(8,128)(2,1)} %collective-permute-done.4.refs_6_), channel_id=1, source_target_pairs={{0,2},{2,4},{4,6},{6,7},{7,5},{5,3},{3,1},{1,0},{8,10},{10,12},{12... | collective-permute-start | bytes 1572872 | tf_op jit(solution)/shard_map/ppermute | solution.py:197
  46.7 1.5 %scatter.4.refs_4_ = f32[8,2048]{1,0:T(8,128)} pad(f32[6,2048]{1,0:T(8,128)} %param.9, f32[]{:T(128)} %constant.67.clone.1), padding=0_2x0_0 | pad | bytes 114692 | tf_op jit(solution)/shard_map/scatter | solution.py:147
  48.2 1.2 %fusion.source_ref = s32[6]{0:T(128)} fusion(s32[6]{0:T(128)} %param.8, s32[]{:T(128)S(6)} %axis_index.15), kind=kLoop, calls=%fused_computation.5 | loop fusion | flops 96 | bytes 52 | tf_op jit(solution)/shard_map/add | solution.py:145
  49.4 1.1 %compare_convert_fusion.living_ref = s32[6]{0:T(128)} fusion(s32[6]{0:T(128)} %param.8), kind=kLoop, calls=%fused_computation.4 | loop fusion | flops 12 | bytes 48 | tf_op jit(solution)/shard_map/convert_element_type | solution.py:142
  50.7 1.1 %copy-done.6 = bf16[3,2048,128]{2,1,0:T(8,128)(2,1)} copy-done((bf16[3,2048,128]{2,1,0:T(8,128)(2,1)}, bf16[3,2048,128]{2,1,0:T(8,128)(2,1)S(1)}, u32[]{:S(2)}) %copy-start.6) | copy-done | bytes 1572888
  52.2 13.0 %shard_map.59 = (bf16[6,2048,128]{2,1,0:T(8,128)(2,1)}, bf16[6,2048,128]{2,1,0:T(8,128)(2,1)}) custom-call(s32[6]{0:T(128)} %fusion.source_ref, s32[6]{0:T(128)} %compare_convert_fusion.living_ref, bf16[3,2048,128]{2,1,0:T(8,128)(2,1)} %refs_0_.1, bf16[3,2048,128]{2,1,0:T(8,128)(2,1)} %copy-done.5, bf16[3,2048,128]{2,1,0:T(8,128)(2,1)} %copy-done.4, ...), custom_call_target="tpu_custom_call" | custom-call | tf_op jit(solution)/shard_map/pallas_call | solution.py:165
  65.9 1.4 %collective-permute-done.14.refs_13_ = bf16[1,128,2048]{2,1,0:T(8,128)(2,1)S(1)} collective-permute-done((bf16[1,128,2048]{2,1,0:T(8,128)(2,1)}, bf16[1,128,2048]{2,1,0:T(8,128)(2,1)S(1)}, u32[]{:S(2)}, u32[]{:S(2)}) %collective-permute-start.14) | collective-permute-done | bytes 524320 | tf_op jit(solution)/shard_map/ppermute | solution.py:78
  67.3 0.7 collective-permute-done.15.refs_14_
  68.1 0.7 collective-permute-done.16.refs_15_
  68.8 1.9 %copy-done = bf16[6,2048,128]{2,1,0:T(8,128)(2,1)S(1)} copy-done((bf16[6,2048,128]{2,1,0:T(8,128)(2,1)S(1)}, bf16[6,2048,128]{2,1,0:T(8,128)(2,1)}, u32[]{:S(2)}) %copy-start) | copy-done | bytes 3145752
  70.7 1.0 %copy-done.3 = bf16[1,128,2048]{2,1,0:T(8,128)(2,1)S(1)} copy-done((bf16[1,128,2048]{2,1,0:T(8,128)(2,1)S(1)}, bf16[1,128,2048]{2,1,0:T(8,128)(2,1)}, u32[]{:S(2)}) %copy-start.3) | copy-done | bytes 524312
  71.8 16.1 %shard_map.60 = f32[6,128]{1,0:T(8,128)S(1)} custom-call(bf16[6,2048,128]{2,1,0:T(8,128)(2,1)S(1)} %copy-done, bf16[2,128,2048]{2,1,0:T(8,128)(2,1)S(1)} %copy-done.1, bf16[1,128,2048]{2,1,0:T(8,128)(2,1)S(1)} %collective-permute-done.refs_2_, bf16[1,128,2048]{2,1,0:T(8,128)(2,1)S(1)} %collective-permute-done.1.refs_3_, ...), custom_call_target="tpu_custom_call" | custom-call | tf_op jit(solution)/shard_map/pallas_call | solution.py:62
  88.0 0.5 compare_select_fusion
  (34 shorter events, 2.9 us)
Async XLA Ops:
  1.7 14.9 %collective-permute-start = (bf16[1,128,2048]{2,1,0:T(8,128)(2,1)S(1)}, bf16[1,128,2048]{2,1,0:T(8,128)(2,1)S(1)}, u32[]{:S(2)}, u32[]{:S(2)}) collective-permute-start(bf16[1,128,2048]{2,1,0:T(8,128)(2,1)S(1)} %constant_dynamic-slice_fusion), channel_id=1, source_target_pairs={{0,2},{2,4},{4,6},{6,7},{7,5},{5,3},{3,1},{1,0},{8,10},{10,12},{12... | collective-permute-start | bytes 1572872 | tf_op jit(solution)/shard_map/ppermute | solution.py:197
  4.8 13.4 %collective-permute-start.1 = (bf16[1,128,2048]{2,1,0:T(8,128)(2,1)S(1)}, bf16[1,128,2048]{2,1,0:T(8,128)(2,1)S(1)}, u32[]{:S(2)}, u32[]{:S(2)}) collective-permute-start(bf16[1,128,2048]{2,1,0:T(8,128)(2,1)S(1)} %constant_dynamic-slice_fusion), channel_id=1, source_target_pairs={{2,0},{4,2},{6,4},{7,6},{5,7},{3,5},{1,3},{0,1},{10,8},{12,10},{14... | collective-permute-start | bytes 1572872 | tf_op jit(solution)/shard_map/ppermute | solution.py:200
  4.8 39.7 %collective-permute-start.6 = (bf16[3,2048,128]{2,1,0:T(8,128)(2,1)}, bf16[3,2048,128]{2,1,0:T(8,128)(2,1)S(1)}, u32[]{:S(2)}, u32[]{:S(2)}) collective-permute-start(bf16[3,2048,128]{2,1,0:T(8,128)(2,1)} %refs_0_.1), channel_id=1, source_target_pairs={{0,16},{8,24},{16,0},{24,8},{1,17},{9,25},{17,1},{25,9},{2,18},{10... | collective-permute-start | bytes 4718600 | tf_op jit(solution)/shard_map/ppermute | solution.py:78
  6.7 37.8 %collective-permute-start.7 = (bf16[3,2048,128]{2,1,0:T(8,128)(2,1)}, bf16[3,2048,128]{2,1,0:T(8,128)(2,1)S(1)}, u32[]{:S(2)}, u32[]{:S(2)}) collective-permute-start(bf16[3,2048,128]{2,1,0:T(8,128)(2,1)} %refs_0_.1), channel_id=1, source_target_pairs={{0,8},{8,0},{16,24},{24,16},{1,9},{9,1},{17,25},{25,17},{2,10},{10... | collective-permute-start | bytes 4718600 | tf_op jit(solution)/shard_map/ppermute | solution.py:78
  18.2 12.5 %collective-permute-start.2 = (bf16[1,128,2048]{2,1,0:T(8,128)(2,1)S(1)}, bf16[1,128,2048]{2,1,0:T(8,128)(2,1)S(1)}, u32[]{:S(2)}, u32[]{:S(2)}) collective-permute-start(bf16[1,128,2048]{2,1,0:T(8,128)(2,1)S(1)} %collective-permute-done.refs_2_), channel_id=1, source_target_pairs={{0,2},{2,4},{4,6},{6,7},{7,5},{5,3},{3,1},{1,0},{8,10},{10,12},{12... | collective-permute-start | bytes 1572872 | tf_op jit(solution)/shard_map/ppermute | solution.py:197
  19.8 12.2 %collective-permute-start.3 = (bf16[1,128,2048]{2,1,0:T(8,128)(2,1)S(1)}, bf16[1,128,2048]{2,1,0:T(8,128)(2,1)S(1)}, u32[]{:S(2)}, u32[]{:S(2)}) collective-permute-start(bf16[1,128,2048]{2,1,0:T(8,128)(2,1)S(1)} %collective-permute-done.1.refs_3_), channel_id=1, source_target_pairs={{2,0},{4,2},{6,4},{7,6},{5,7},{3,5},{1,3},{0,1},{10,8},{12,10},{14... | collective-permute-start | bytes 1572872 | tf_op jit(solution)/shard_map/ppermute | solution.py:200
  32.0 11.4 %collective-permute-start.4 = (bf16[1,128,2048]{2,1,0:T(8,128)(2,1)S(1)}, bf16[1,128,2048]{2,1,0:T(8,128)(2,1)}, u32[]{:S(2)}, u32[]{:S(2)}) collective-permute-start(bf16[1,128,2048]{2,1,0:T(8,128)(2,1)S(1)} %collective-permute-done.2.refs_4_), channel_id=1, source_target_pairs={{0,2},{2,4},{4,6},{6,7},{7,5},{5,3},{3,1},{1,0},{8,10},{10,12},{12... | collective-permute-start | bytes 1572872 | tf_op jit(solution)/shard_map/ppermute | solution.py:197
  33.5 11.0 %collective-permute-start.5 = (bf16[1,128,2048]{2,1,0:T(8,128)(2,1)S(1)}, bf16[1,128,2048]{2,1,0:T(8,128)(2,1)S(1)}, u32[]{:S(2)}, u32[]{:S(2)}) collective-permute-start(bf16[1,128,2048]{2,1,0:T(8,128)(2,1)S(1)} %collective-permute-done.3.refs_5_), channel_id=1, source_target_pairs={{2,0},{4,2},{6,4},{7,6},{5,7},{3,5},{1,3},{0,1},{10,8},{12,10},{14... | collective-permute-start | bytes 1572872 | tf_op jit(solution)/shard_map/ppermute | solution.py:200
  44.5 1.7 %copy-start.2 = (bf16[1,128,2048]{2,1,0:T(8,128)(2,1)}, bf16[1,128,2048]{2,1,0:T(8,128)(2,1)S(1)}, u32[]{:S(2)}) copy-start(bf16[1,128,2048]{2,1,0:T(8,128)(2,1)S(1)} %collective-permute-done.5.refs_7_) | copy-start | bytes 1572868
  44.5 6.1 %copy-start.4 = (bf16[3,2048,128]{2,1,0:T(8,128)(2,1)}, bf16[3,2048,128]{2,1,0:T(8,128)(2,1)S(1)}, u32[]{:S(2)}) copy-start(bf16[3,2048,128]{2,1,0:T(8,128)(2,1)S(1)} %collective-permute-done.6.refs_2_) | copy-start | bytes 4718596
  44.5 1.8 %copy-start.5 = (bf16[3,2048,128]{2,1,0:T(8,128)(2,1)}, bf16[3,2048,128]{2,1,0:T(8,128)(2,1)S(1)}, u32[]{:S(2)}) copy-start(bf16[3,2048,128]{2,1,0:T(8,128)(2,1)S(1)} %collective-permute-done.7.refs_1_) | copy-start | bytes 4718596
  44.6 6.1 %collective-permute-start.9 = (bf16[3,2048,128]{2,1,0:T(8,128)(2,1)S(1)}, bf16[3,2048,128]{2,1,0:T(8,128)(2,1)S(1)}, u32[]{:S(2)}, u32[]{:S(2)}) collective-permute-start(bf16[3,2048,128]{2,1,0:T(8,128)(2,1)S(1)} %collective-permute-done.6.refs_2_), channel_id=1, source_target_pairs={{0,8},{8,0},{16,24},{24,16},{1,9},{9,1},{17,25},{25,17},{2,10},{10... | collective-permute-start | bytes 4718600 | tf_op jit(solution)/shard_map/ppermute | solution.py:78
  44.6 20.5 %collective-permute-start.8 = (bf16[1,128,2048]{2,1,0:T(8,128)(2,1)}, bf16[1,128,2048]{2,1,0:T(8,128)(2,1)}, u32[]{:S(2)}, u32[]{:S(2)}) collective-permute-start(bf16[1,128,2048]{2,1,0:T(8,128)(2,1)} %collective-permute-done.4.refs_6_), channel_id=1, source_target_pairs={{0,2},{2,4},{4,6},{6,7},{7,5},{5,3},{3,1},{1,0},{8,10},{10,12},{12... | collective-permute-start | bytes 1572872 | tf_op jit(solution)/shard_map/ppermute | solution.py:197
  46.2 19.2 %collective-permute-start.10 = (bf16[1,128,2048]{2,1,0:T(8,128)(2,1)S(1)}, bf16[1,128,2048]{2,1,0:T(8,128)(2,1)}, u32[]{:S(2)}, u32[]{:S(2)}) collective-permute-start(bf16[1,128,2048]{2,1,0:T(8,128)(2,1)S(1)} %collective-permute-done.refs_2_), channel_id=1, source_target_pairs={{0,8},{8,0},{16,24},{24,16},{1,9},{9,1},{17,25},{25,17},{2,10},{10... | collective-permute-start | bytes 1572872 | tf_op jit(solution)/shard_map/ppermute | solution.py:78
  46.4 19.4 %collective-permute-start.11 = (bf16[1,128,2048]{2,1,0:T(8,128)(2,1)S(1)}, bf16[1,128,2048]{2,1,0:T(8,128)(2,1)}, u32[]{:S(2)}, u32[]{:S(2)}) collective-permute-start(bf16[1,128,2048]{2,1,0:T(8,128)(2,1)S(1)} %collective-permute-done.1.refs_3_), channel_id=1, source_target_pairs={{0,8},{8,0},{16,24},{24,16},{1,9},{9,1},{17,25},{25,17},{2,10},{10... | collective-permute-start | bytes 1572872 | tf_op jit(solution)/shard_map/ppermute | solution.py:78
  50.5 18.3 %copy-start.1 = (bf16[2,128,2048]{2,1,0:T(8,128)(2,1)S(1)}, bf16[2,128,2048]{2,1,0:T(8,128)(2,1)}, u32[]{:S(2)}) copy-start(bf16[2,128,2048]{2,1,0:T(8,128)(2,1)} %refs_1_.1) | copy-start | bytes 3145732
  50.5 15.4 %collective-permute-start.12 = (bf16[1,128,2048]{2,1,0:T(8,128)(2,1)S(1)}, bf16[1,128,2048]{2,1,0:T(8,128)(2,1)}, u32[]{:S(2)}, u32[]{:S(2)}) collective-permute-start(bf16[1,128,2048]{2,1,0:T(8,128)(2,1)S(1)} %collective-permute-done.2.refs_4_), channel_id=1, source_target_pairs={{0,8},{8,0},{16,24},{24,16},{1,9},{9,1},{17,25},{25,17},{2,10},{10... | collective-permute-start | bytes 1572872 | tf_op jit(solution)/shard_map/ppermute | solution.py:78
  50.7 1.1 %copy-start.6 = (bf16[3,2048,128]{2,1,0:T(8,128)(2,1)}, bf16[3,2048,128]{2,1,0:T(8,128)(2,1)S(1)}, u32[]{:S(2)}) copy-start(bf16[3,2048,128]{2,1,0:T(8,128)(2,1)S(1)} %collective-permute-done.9.refs_3_) | copy-start | bytes 4718596
  51.8 14.1 %collective-permute-start.13 = (bf16[1,128,2048]{2,1,0:T(8,128)(2,1)S(1)}, bf16[1,128,2048]{2,1,0:T(8,128)(2,1)}, u32[]{:S(2)}, u32[]{:S(2)}) collective-permute-start(bf16[1,128,2048]{2,1,0:T(8,128)(2,1)S(1)} %collective-permute-done.3.refs_5_), channel_id=1, source_target_pairs={{0,8},{8,0},{16,24},{24,16},{1,9},{9,1},{17,25},{25,17},{2,10},{10... | collective-permute-start | bytes 1572872 | tf_op jit(solution)/shard_map/ppermute | solution.py:78
  65.1 2.2 %collective-permute-start.14 = (bf16[1,128,2048]{2,1,0:T(8,128)(2,1)}, bf16[1,128,2048]{2,1,0:T(8,128)(2,1)S(1)}, u32[]{:S(2)}, u32[]{:S(2)}) collective-permute-start(bf16[1,128,2048]{2,1,0:T(8,128)(2,1)} %collective-permute-done.4.refs_6_), channel_id=1, source_target_pairs={{0,8},{8,0},{16,24},{24,16},{1,9},{9,1},{17,25},{25,17},{2,10},{10... | collective-permute-start | bytes 1572872 | tf_op jit(solution)/shard_map/ppermute | solution.py:78
  65.4 22.6 %copy-start.7 = (s32[6]{0:T(128)S(1)}, s32[6]{0:T(128)}, u32[]{:S(2)}) copy-start(s32[6]{0:T(128)} %param.8) | copy-start | bytes 76
  65.4 2.7 %collective-permute-start.15 = (bf16[1,128,2048]{2,1,0:T(8,128)(2,1)}, bf16[1,128,2048]{2,1,0:T(8,128)(2,1)S(1)}, u32[]{:S(2)}, u32[]{:S(2)}) collective-permute-start(bf16[1,128,2048]{2,1,0:T(8,128)(2,1)} %copy-done.2), channel_id=1, source_target_pairs={{0,8},{8,0},{16,24},{24,16},{1,9},{9,1},{17,25},{25,17},{2,10},{10... | collective-permute-start | bytes 1572872 | tf_op jit(solution)/shard_map/ppermute | solution.py:78
  65.7 3.1 %collective-permute-start.16 = (bf16[1,128,2048]{2,1,0:T(8,128)(2,1)}, bf16[1,128,2048]{2,1,0:T(8,128)(2,1)S(1)}, u32[]{:S(2)}, u32[]{:S(2)}) collective-permute-start(bf16[1,128,2048]{2,1,0:T(8,128)(2,1)} %collective-permute-done.8.refs_8_), channel_id=1, source_target_pairs={{0,8},{8,0},{16,24},{24,16},{1,9},{9,1},{17,25},{25,17},{2,10},{10... | collective-permute-start | bytes 1572872 | tf_op jit(solution)/shard_map/ppermute | solution.py:78
  68.8 1.9 %copy-start = (bf16[6,2048,128]{2,1,0:T(8,128)(2,1)S(1)}, bf16[6,2048,128]{2,1,0:T(8,128)(2,1)}, u32[]{:S(2)}) copy-start(bf16[6,2048,128]{2,1,0:T(8,128)(2,1)} %get-tuple-element.37.refs_0_) | copy-start | bytes 9437188
  (1 other events, 1.0 us)

commit v11 on v10

--- a/solution.py
+++ b/solution.py
@@ -136,15 +136,21 @@
         copy.wait()
 
 
-def kick(old_walkers, beside, across, diagonal_peer, parent, field, walk_id):
-    old_dev, orbitals, electrons = old_walkers.shape
-    slot_dev = parent.shape[0]
+def kick_operands(old_dev, parent, field, walk_id):
+    slot_dev, orbitals = field.shape
     living = (parent >= 0).astype(jnp.int32)
     source = jnp.maximum(parent, 0)
     relative = (source // old_dev) ^ walk_id
     index = (relative * old_dev + source % old_dev).astype(jnp.int32)
     lanes = max(8, -(-slot_dev // 8) * 8)
     padded = jnp.zeros((lanes, orbitals), jnp.float32).at[:slot_dev].set(field)
+    return index, living, padded
+
+
+def kick(old_walkers, beside, across, diagonal_peer, index, living, padded):
+    old_dev, orbitals, electrons = old_walkers.shape
+    slot_dev = index.shape[0]
+    lanes = padded.shape[0]
     any_space = pl.BlockSpec(memory_space=pl.ANY)
     slots = (slot_dev, orbitals, electrons)
     grid_spec = pltpu.PrefetchScalarGridSpec(
@@ -193,6 +199,7 @@
     ahead = mine
     behind = mine
     new_walkers = theta = None
+    operands = kick_operands(old_walkers.shape[0], parent, field, walk_id)
     for step in range(n_forward):
         ahead = lax.ppermute(ahead, "chol", forward)
         carried = [ahead]
@@ -201,9 +208,11 @@
             carried.append(behind)
         if step == walker_step:
             carried += [across, beside]
+        if step == 0:
+            carried += list(operands)
         if step == n_forward - 1:
             diagonal_peer = swap_pairs(across, "walk", n_walk, 1)
-            new_walkers, theta = kick(old_walkers, beside, across, diagonal_peer, parent, field, walk_id)
+            new_walkers, theta = kick(old_walkers, beside, across, diagonal_peer, *operands)
             carried += [new_walkers, theta]
         carried = list(lax.optimization_barrier(tuple(carried)))
         ahead = carried.pop(0)
@@ -213,6 +222,8 @@
             arrived.append(behind)
         if step == walker_step:
             across, beside = carried.pop(0), carried.pop(0)
+        if step == 0:
+            operands = [carried.pop(0) for item in operands]
         if step == n_forward - 1:
             new_walkers, theta = carried.pop(0), carried.pop(0)
         for piece in arrived:
@@ -220,7 +231,7 @@
             handed.append(swap_pairs(piece, "walk", n_walk, 1))
     if theta is None:
         diagonal_peer = swap_pairs(across, "walk", n_walk, 1)
-        new_walkers, theta = kick(old_walkers, beside, across, diagonal_peer, parent, field, walk_id)
+        new_walkers, theta = kick(old_walkers, beside, across, diagonal_peer, *operands)
 
     living = parent >= 0
     energy = block_energy(theta, [half_chol] + pieces + handed)

time: 88.9 us -> 86.1 us (0.969)
  waiting for transfers between devices: 36.7 us -> 33.8 us
    ppermute x4, waiting for transfers between devices: 29.7 us -> 25.9 us  [body(): ahead = lax.ppermute(ahead, 'chol', forward)]
    ppermute x10, waiting for transfers between devices: 2.95 us -> 3.88 us  [swap_pairs(): return lax.ppermute(x, axis, perm)]
  transfers between devices with their start and end apart: 17 -> 17, of which waited for: 9 -> 10; matrix products, arithmetic and copies ran while one was open for 4% -> 4% of each run, Pallas kernels for 15% -> 15%
where the time goes in v11:
time: 86.1 us; the launch traced here: 85.7 us
  waiting for transfers between devices  33.8 us (39%)
  Pallas kernels  29.1 us (34%)
  starting transfers between devices  12.5 us (15%)
  local copies, waits for them, and re-layouts  6.76 us (8%)
  other arithmetic  2.84 us (3%)
    ppermute x4, waiting for transfers between devices, body(): ahead = lax.ppermute(ahead, 'chol', forward)  25.9 us
    pallas_call x1, Pallas kernels, block_energy(): pl.pallas_call(energy_kernel, out_shape=jax.ShapeDtypeStruct((n_slot, 128...  16.1 us
    pallas_call x1, Pallas kernels, kick(): pl.pallas_call(kick_kernel, out_shape=[shape, shape], grid_spec=grid_spec)  12.9 us
    ppermute x4, starting transfers between devices, body(): ahead = lax.ppermute(ahead, 'chol', forward)  7.8 us
    unnamed x16, local copies, waits for them, and re-layouts  4.09 us
    ppermute x3, waiting for transfers between devices, body(): behind = lax.ppermute(behind, 'chol', backward)  4 us
    ppermute x10, waiting for transfers between devices, swap_pairs(): return lax.ppermute(x, axis, perm)  3.88 us
    ppermute x10, starting transfers between devices, swap_pairs(): return lax.ppermute(x, axis, perm)  3.77 us
  transfers between devices with their start and end apart: 17, of which 10 were waited for; matrix products, arithmetic and copies ran while one was open for 4% of the time, Pallas kernels for 15%

profile of v11, /device:TPU:0, one launch (start us, length us, event | category | flops | bytes accessed | tf_op | source)
XLA Modules:
  0.0 85.7 jit_solution(15236562557215302339)
XLA Ops:
  0.6 1.1 %constant_dynamic-slice_fusion = bf16[1,128,2048]{2,1,0:T(8,128)(2,1)S(1)} fusion(bf16[2,128,2048]{2,1,0:T(8,128)(2,1)} %refs_1_.1, s32[]{:T(128)S(6)} %select_n.26), kind=kLoop, calls=%fused_computation.6 | loop fusion | bytes 1048580 | tf_op jit(solution)/shard_map/dynamic_slice | solution.py:189
  1.7 3.1 %collective-permute-start = (bf16[1,128,2048]{2,1,0:T(8,128)(2,1)S(1)}, bf16[1,128,2048]{2,1,0:T(8,128)(2,1)S(1)}, u32[]{:S(2)}, u32[]{:S(2)}) collective-permute-start(bf16[1,128,2048]{2,1,0:T(8,128)(2,1)S(1)} %constant_dynamic-slice_fusion), channel_id=1, source_target_pairs={{0,2},{2,4},{4,6},{6,7},{7,5},{5,3},{3,1},{1,0},{8,10},{10,12},{12... | collective-permute-start | bytes 1572872 | tf_op jit(solution)/shard_map/ppermute | solution.py:204
  4.8 1.9 %collective-permute-start.6 = (bf16[3,2048,128]{2,1,0:T(8,128)(2,1)}, bf16[3,2048,128]{2,1,0:T(8,128)(2,1)S(1)}, u32[]{:S(2)}, u32[]{:S(2)}) collective-permute-start(bf16[3,2048,128]{2,1,0:T(8,128)(2,1)} %refs_0_.1), channel_id=1, source_target_pairs={{0,16},{8,24},{16,0},{24,8},{1,17},{9,25},{17,1},{25,9},{2,18},{10... | collective-permute-start | bytes 4718600 | tf_op jit(solution)/shard_map/ppermute | solution.py:78
  6.8 1.5 %scatter.4.refs_4_ = f32[8,2048]{1,0:T(8,128)} pad(f32[6,2048]{1,0:T(8,128)} %param.9, f32[]{:T(128)} %constant.67.clone.1), padding=0_2x0_0 | pad | bytes 114692 | tf_op jit(solution)/shard_map/scatter | solution.py:146
  8.2 1.2 %fusion.source_ref = s32[6]{0:T(128)} fusion(s32[6]{0:T(128)} %param.8, s32[]{:T(128)S(6)} %axis_index.15), kind=kLoop, calls=%fused_computation.5 | loop fusion | flops 96 | bytes 52 | tf_op jit(solution)/shard_map/add | solution.py:144
  9.4 1.1 %compare_convert_fusion.living_ref = s32[6]{0:T(128)} fusion(s32[6]{0:T(128)} %param.8), kind=kLoop, calls=%fused_computation.4 | loop fusion | flops 12 | bytes 48 | tf_op jit(solution)/shard_map/convert_element_type | solution.py:141
  10.5 6.1 %collective-permute-done.refs_2_ = bf16[1,128,2048]{2,1,0:T(8,128)(2,1)S(1)} collective-permute-done((bf16[1,128,2048]{2,1,0:T(8,128)(2,1)S(1)}, bf16[1,128,2048]{2,1,0:T(8,128)(2,1)S(1)}, u32[]{:S(2)}, u32[]{:S(2)}) %collective-permute-start) | collective-permute-done | bytes 524320 | tf_op jit(solution)/shard_map/ppermute | solution.py:204
  16.7 1.5 %collective-permute-done.1.refs_3_ = bf16[1,128,2048]{2,1,0:T(8,128)(2,1)S(1)} collective-permute-done((bf16[1,128,2048]{2,1,0:T(8,128)(2,1)S(1)}, bf16[1,128,2048]{2,1,0:T(8,128)(2,1)S(1)}, u32[]{:S(2)}, u32[]{:S(2)}) %collective-permute-start.1) | collective-permute-done | bytes 524320 | tf_op jit(solution)/shard_map/ppermute | solution.py:207
  18.2 1.6 %collective-permute-start.2 = (bf16[1,128,2048]{2,1,0:T(8,128)(2,1)S(1)}, bf16[1,128,2048]{2,1,0:T(8,128)(2,1)S(1)}, u32[]{:S(2)}, u32[]{:S(2)}) collective-permute-start(bf16[1,128,2048]{2,1,0:T(8,128)(2,1)S(1)} %collective-permute-done.refs_2_), channel_id=1, source_target_pairs={{0,2},{2,4},{4,6},{6,7},{7,5},{5,3},{3,1},{1,0},{8,10},{10,12},{12... | collective-permute-start | bytes 1572872 | tf_op jit(solution)/shard_map/ppermute | solution.py:204
  20.2 10.4 %collective-permute-done.2.refs_4_ = bf16[1,128,2048]{2,1,0:T(8,128)(2,1)S(1)} collective-permute-done((bf16[1,128,2048]{2,1,0:T(8,128)(2,1)S(1)}, bf16[1,128,2048]{2,1,0:T(8,128)(2,1)S(1)}, u32[]{:S(2)}, u32[]{:S(2)}) %collective-permute-start.2) | collective-permute-done | bytes 524320 | tf_op jit(solution)/shard_map/ppermute | solution.py:204
  30.7 1.3 %collective-permute-done.3.refs_5_ = bf16[1,128,2048]{2,1,0:T(8,128)(2,1)S(1)} collective-permute-done((bf16[1,128,2048]{2,1,0:T(8,128)(2,1)S(1)}, bf16[1,128,2048]{2,1,0:T(8,128)(2,1)S(1)}, u32[]{:S(2)}, u32[]{:S(2)}) %collective-permute-start.3) | collective-permute-done | bytes 524320 | tf_op jit(solution)/shard_map/ppermute | solution.py:207
  32.0 1.6 %collective-permute-start.4 = (bf16[1,128,2048]{2,1,0:T(8,128)(2,1)S(1)}, bf16[1,128,2048]{2,1,0:T(8,128)(2,1)}, u32[]{:S(2)}, u32[]{:S(2)}) collective-permute-start(bf16[1,128,2048]{2,1,0:T(8,128)(2,1)S(1)} %collective-permute-done.2.refs_4_), channel_id=1, source_target_pairs={{0,2},{2,4},{4,6},{6,7},{7,5},{5,3},{3,1},{1,0},{8,10},{10,12},{12... | collective-permute-start | bytes 1572872 | tf_op jit(solution)/shard_map/ppermute | solution.py:204
  34.0 9.4 %collective-permute-done.4.refs_6_ = bf16[1,128,2048]{2,1,0:T(8,128)(2,1)} collective-permute-done((bf16[1,128,2048]{2,1,0:T(8,128)(2,1)S(1)}, bf16[1,128,2048]{2,1,0:T(8,128)(2,1)}, u32[]{:S(2)}, u32[]{:S(2)}) %collective-permute-start.4) | collective-permute-done | bytes 524320 | tf_op jit(solution)/shard_map/ppermute | solution.py:204
  43.3 1.2 %collective-permute-done.5.refs_7_ = bf16[1,128,2048]{2,1,0:T(8,128)(2,1)S(1)} collective-permute-done((bf16[1,128,2048]{2,1,0:T(8,128)(2,1)S(1)}, bf16[1,128,2048]{2,1,0:T(8,128)(2,1)S(1)}, u32[]{:S(2)}, u32[]{:S(2)}) %collective-permute-start.5) | collective-permute-done | bytes 524320 | tf_op jit(solution)/shard_map/ppermute | solution.py:207
  44.6 1.6 %collective-permute-start.8 = (bf16[1,128,2048]{2,1,0:T(8,128)(2,1)}, bf16[1,128,2048]{2,1,0:T(8,128)(2,1)}, u32[]{:S(2)}, u32[]{:S(2)}) collective-permute-start(bf16[1,128,2048]{2,1,0:T(8,128)(2,1)} %collective-permute-done.4.refs_6_), channel_id=1, source_target_pairs={{0,2},{2,4},{4,6},{6,7},{7,5},{5,3},{3,1},{1,0},{8,10},{10,12},{12... | collective-permute-start | bytes 1572872 | tf_op jit(solution)/shard_map/ppermute | solution.py:204
  46.9 1.1 %collective-permute-done.9.refs_3_ = bf16[3,2048,128]{2,1,0:T(8,128)(2,1)S(1)} collective-permute-done((bf16[3,2048,128]{2,1,0:T(8,128)(2,1)S(1)}, bf16[3,2048,128]{2,1,0:T(8,128)(2,1)S(1)}, u32[]{:S(2)}, u32[]{:S(2)}) %collective-permute-start.9) | collective-permute-done | bytes 1572896 | tf_op jit(solution)/shard_map/ppermute | solution.py:78
  48.0 1.1 %copy-done.6 = bf16[3,2048,128]{2,1,0:T(8,128)(2,1)} copy-done((bf16[3,2048,128]{2,1,0:T(8,128)(2,1)}, bf16[3,2048,128]{2,1,0:T(8,128)(2,1)S(1)}, u32[]{:S(2)}) %copy-start.6) | copy-done | bytes 1572888
  49.3 12.9 %shard_map.59 = (bf16[6,2048,128]{2,1,0:T(8,128)(2,1)}, bf16[6,2048,128]{2,1,0:T(8,128)(2,1)}) custom-call(s32[6]{0:T(128)} %fusion.source_ref, s32[6]{0:T(128)} %compare_convert_fusion.living_ref, bf16[3,2048,128]{2,1,0:T(8,128)(2,1)} %refs_0_.1, bf16[3,2048,128]{2,1,0:T(8,128)(2,1)} %copy-done.5, bf16[3,2048,128]{2,1,0:T(8,128)(2,1)} %copy-done.4, ...), custom_call_target="tpu_custom_call" | custom-call | tf_op jit(solution)/shard_map/pallas_call | solution.py:171
  63.3 1.2 %collective-permute-done.14.refs_13_ = bf16[1,128,2048]{2,1,0:T(8,128)(2,1)S(1)} collective-permute-done((bf16[1,128,2048]{2,1,0:T(8,128)(2,1)}, bf16[1,128,2048]{2,1,0:T(8,128)(2,1)S(1)}, u32[]{:S(2)}, u32[]{:S(2)}) %collective-permute-start.14) | collective-permute-done | bytes 524320 | tf_op jit(solution)/shard_map/ppermute | solution.py:78
  64.5 0.7 collective-permute-done.15.refs_14_
  65.2 0.7 collective-permute-done.16.refs_15_
  66.0 1.9 %copy-done = bf16[6,2048,128]{2,1,0:T(8,128)(2,1)S(1)} copy-done((bf16[6,2048,128]{2,1,0:T(8,128)(2,1)S(1)}, bf16[6,2048,128]{2,1,0:T(8,128)(2,1)}, u32[]{:S(2)}) %copy-start) | copy-done | bytes 3145752
  67.9 1.0 %copy-done.3 = bf16[1,128,2048]{2,1,0:T(8,128)(2,1)S(1)} copy-done((bf16[1,128,2048]{2,1,0:T(8,128)(2,1)S(1)}, bf16[1,128,2048]{2,1,0:T(8,128)(2,1)}, u32[]{:S(2)}) %copy-start.3) | copy-done | bytes 524312
  68.9 16.1 %shard_map.60 = f32[6,128]{1,0:T(8,128)S(1)} custom-call(bf16[6,2048,128]{2,1,0:T(8,128)(2,1)S(1)} %copy-done, bf16[2,128,2048]{2,1,0:T(8,128)(2,1)S(1)} %copy-done.1, bf16[1,128,2048]{2,1,0:T(8,128)(2,1)S(1)} %collective-permute-done.refs_2_, bf16[1,128,2048]{2,1,0:T(8,128)(2,1)S(1)} %collective-permute-done.1.refs_3_, ...), custom_call_target="tpu_custom_call" | custom-call | tf_op jit(solution)/shard_map/pallas_call | solution.py:62
  (34 shorter events, 3.4 us)
Async XLA Ops:
  1.7 14.9 %collective-permute-start = (bf16[1,128,2048]{2,1,0:T(8,128)(2,1)S(1)}, bf16[1,128,2048]{2,1,0:T(8,128)(2,1)S(1)}, u32[]{:S(2)}, u32[]{:S(2)}) collective-permute-start(bf16[1,128,2048]{2,1,0:T(8,128)(2,1)S(1)} %constant_dynamic-slice_fusion), channel_id=1, source_target_pairs={{0,2},{2,4},{4,6},{6,7},{7,5},{5,3},{3,1},{1,0},{8,10},{10,12},{12... | collective-permute-start | bytes 1572872 | tf_op jit(solution)/shard_map/ppermute | solution.py:204
  4.8 13.4 %collective-permute-start.1 = (bf16[1,128,2048]{2,1,0:T(8,128)(2,1)S(1)}, bf16[1,128,2048]{2,1,0:T(8,128)(2,1)S(1)}, u32[]{:S(2)}, u32[]{:S(2)}) collective-permute-start(bf16[1,128,2048]{2,1,0:T(8,128)(2,1)S(1)} %constant_dynamic-slice_fusion), channel_id=1, source_target_pairs={{2,0},{4,2},{6,4},{7,6},{5,7},{3,5},{1,3},{0,1},{10,8},{12,10},{14... | collective-permute-start | bytes 1572872 | tf_op jit(solution)/shard_map/ppermute | solution.py:207
  4.8 39.7 %collective-permute-start.6 = (bf16[3,2048,128]{2,1,0:T(8,128)(2,1)}, bf16[3,2048,128]{2,1,0:T(8,128)(2,1)S(1)}, u32[]{:S(2)}, u32[]{:S(2)}) collective-permute-start(bf16[3,2048,128]{2,1,0:T(8,128)(2,1)} %refs_0_.1), channel_id=1, source_target_pairs={{0,16},{8,24},{16,0},{24,8},{1,17},{9,25},{17,1},{25,9},{2,18},{10... | collective-permute-start | bytes 4718600 | tf_op jit(solution)/shard_map/ppermute | solution.py:78
  6.8 37.8 %collective-permute-start.7 = (bf16[3,2048,128]{2,1,0:T(8,128)(2,1)}, bf16[3,2048,128]{2,1,0:T(8,128)(2,1)S(1)}, u32[]{:S(2)}, u32[]{:S(2)}) collective-permute-start(bf16[3,2048,128]{2,1,0:T(8,128)(2,1)} %refs_0_.1), channel_id=1, source_target_pairs={{0,8},{8,0},{16,24},{24,16},{1,9},{9,1},{17,25},{25,17},{2,10},{10... | collective-permute-start | bytes 4718600 | tf_op jit(solution)/shard_map/ppermute | solution.py:78
  10.5 55.4 %copy-start.1 = (bf16[2,128,2048]{2,1,0:T(8,128)(2,1)S(1)}, bf16[2,128,2048]{2,1,0:T(8,128)(2,1)}, u32[]{:S(2)}) copy-start(bf16[2,128,2048]{2,1,0:T(8,128)(2,1)} %refs_1_.1) | copy-start | bytes 3145732
  18.2 12.5 %collective-permute-start.2 = (bf16[1,128,2048]{2,1,0:T(8,128)(2,1)S(1)}, bf16[1,128,2048]{2,1,0:T(8,128)(2,1)S(1)}, u32[]{:S(2)}, u32[]{:S(2)}) collective-permute-start(bf16[1,128,2048]{2,1,0:T(8,128)(2,1)S(1)} %collective-permute-done.refs_2_), channel_id=1, source_target_pairs={{0,2},{2,4},{4,6},{6,7},{7,5},{5,3},{3,1},{1,0},{8,10},{10,12},{12... | collective-permute-start | bytes 1572872 | tf_op jit(solution)/shard_map/ppermute | solution.py:204
  19.8 12.2 %collective-permute-start.3 = (bf16[1,128,2048]{2,1,0:T(8,128)(2,1)S(1)}, bf16[1,128,2048]{2,1,0:T(8,128)(2,1)S(1)}, u32[]{:S(2)}, u32[]{:S(2)}) collective-permute-start(bf16[1,128,2048]{2,1,0:T(8,128)(2,1)S(1)} %collective-permute-done.1.refs_3_), channel_id=1, source_target_pairs={{2,0},{4,2},{6,4},{7,6},{5,7},{3,5},{1,3},{0,1},{10,8},{12,10},{14... | collective-permute-start | bytes 1572872 | tf_op jit(solution)/shard_map/ppermute | solution.py:207
  32.0 11.4 %collective-permute-start.4 = (bf16[1,128,2048]{2,1,0:T(8,128)(2,1)S(1)}, bf16[1,128,2048]{2,1,0:T(8,128)(2,1)}, u32[]{:S(2)}, u32[]{:S(2)}) collective-permute-start(bf16[1,128,2048]{2,1,0:T(8,128)(2,1)S(1)} %collective-permute-done.2.refs_4_), channel_id=1, source_target_pairs={{0,2},{2,4},{4,6},{6,7},{7,5},{5,3},{3,1},{1,0},{8,10},{10,12},{12... | collective-permute-start | bytes 1572872 | tf_op jit(solution)/shard_map/ppermute | solution.py:204
  33.5 11.0 %collective-permute-start.5 = (bf16[1,128,2048]{2,1,0:T(8,128)(2,1)S(1)}, bf16[1,128,2048]{2,1,0:T(8,128)(2,1)S(1)}, u32[]{:S(2)}, u32[]{:S(2)}) collective-permute-start(bf16[1,128,2048]{2,1,0:T(8,128)(2,1)S(1)} %collective-permute-done.3.refs_5_), channel_id=1, source_target_pairs={{2,0},{4,2},{6,4},{7,6},{5,7},{3,5},{1,3},{0,1},{10,8},{12,10},{14... | collective-permute-start | bytes 1572872 | tf_op jit(solution)/shard_map/ppermute | solution.py:207
  44.5 2.4 %copy-start.2 = (bf16[1,128,2048]{2,1,0:T(8,128)(2,1)}, bf16[1,128,2048]{2,1,0:T(8,128)(2,1)S(1)}, u32[]{:S(2)}) copy-start(bf16[1,128,2048]{2,1,0:T(8,128)(2,1)S(1)} %collective-permute-done.5.refs_7_) | copy-start | bytes 1572868
  44.5 3.5 %copy-start.4 = (bf16[3,2048,128]{2,1,0:T(8,128)(2,1)}, bf16[3,2048,128]{2,1,0:T(8,128)(2,1)S(1)}, u32[]{:S(2)}) copy-start(bf16[3,2048,128]{2,1,0:T(8,128)(2,1)S(1)} %collective-permute-done.6.refs_2_) | copy-start | bytes 4718596
  44.6 3.5 %copy-start.5 = (bf16[3,2048,128]{2,1,0:T(8,128)(2,1)}, bf16[3,2048,128]{2,1,0:T(8,128)(2,1)S(1)}, u32[]{:S(2)}) copy-start(bf16[3,2048,128]{2,1,0:T(8,128)(2,1)S(1)} %collective-permute-done.7.refs_1_) | copy-start | bytes 4718596
  44.6 3.5 %collective-permute-start.9 = (bf16[3,2048,128]{2,1,0:T(8,128)(2,1)S(1)}, bf16[3,2048,128]{2,1,0:T(8,128)(2,1)S(1)}, u32[]{:S(2)}, u32[]{:S(2)}) collective-permute-start(bf16[3,2048,128]{2,1,0:T(8,128)(2,1)S(1)} %collective-permute-done.6.refs_2_), channel_id=1, source_target_pairs={{0,8},{8,0},{16,24},{24,16},{1,9},{9,1},{17,25},{25,17},{2,10},{10... | collective-permute-start | bytes 4718600 | tf_op jit(solution)/shard_map/ppermute | solution.py:78
  44.6 17.6 %collective-permute-start.8 = (bf16[1,128,2048]{2,1,0:T(8,128)(2,1)}, bf16[1,128,2048]{2,1,0:T(8,128)(2,1)}, u32[]{:S(2)}, u32[]{:S(2)}) collective-permute-start(bf16[1,128,2048]{2,1,0:T(8,128)(2,1)} %collective-permute-done.4.refs_6_), channel_id=1, source_target_pairs={{0,2},{2,4},{4,6},{6,7},{7,5},{5,3},{3,1},{1,0},{8,10},{10,12},{12... | collective-permute-start | bytes 1572872 | tf_op jit(solution)/shard_map/ppermute | solution.py:204
  46.2 16.5 %collective-permute-start.10 = (bf16[1,128,2048]{2,1,0:T(8,128)(2,1)S(1)}, bf16[1,128,2048]{2,1,0:T(8,128)(2,1)}, u32[]{:S(2)}, u32[]{:S(2)}) collective-permute-start(bf16[1,128,2048]{2,1,0:T(8,128)(2,1)S(1)} %collective-permute-done.refs_2_), channel_id=1, source_target_pairs={{0,8},{8,0},{16,24},{24,16},{1,9},{9,1},{17,25},{25,17},{2,10},{10... | collective-permute-start | bytes 1572872 | tf_op jit(solution)/shard_map/ppermute | solution.py:78
  46.4 16.5 %collective-permute-start.11 = (bf16[1,128,2048]{2,1,0:T(8,128)(2,1)S(1)}, bf16[1,128,2048]{2,1,0:T(8,128)(2,1)}, u32[]{:S(2)}, u32[]{:S(2)}) collective-permute-start(bf16[1,128,2048]{2,1,0:T(8,128)(2,1)S(1)} %collective-permute-done.1.refs_3_), channel_id=1, source_target_pairs={{0,8},{8,0},{16,24},{24,16},{1,9},{9,1},{17,25},{25,17},{2,10},{10... | collective-permute-start | bytes 1572872 | tf_op jit(solution)/shard_map/ppermute | solution.py:78
  46.7 16.5 %collective-permute-start.12 = (bf16[1,128,2048]{2,1,0:T(8,128)(2,1)S(1)}, bf16[1,128,2048]{2,1,0:T(8,128)(2,1)}, u32[]{:S(2)}, u32[]{:S(2)}) collective-permute-start(bf16[1,128,2048]{2,1,0:T(8,128)(2,1)S(1)} %collective-permute-done.2.refs_4_), channel_id=1, source_target_pairs={{0,8},{8,0},{16,24},{24,16},{1,9},{9,1},{17,25},{25,17},{2,10},{10... | collective-permute-start | bytes 1572872 | tf_op jit(solution)/shard_map/ppermute | solution.py:78
  48.0 1.1 %copy-start.6 = (bf16[3,2048,128]{2,1,0:T(8,128)(2,1)}, bf16[3,2048,128]{2,1,0:T(8,128)(2,1)S(1)}, u32[]{:S(2)}) copy-start(bf16[3,2048,128]{2,1,0:T(8,128)(2,1)S(1)} %collective-permute-done.9.refs_3_) | copy-start | bytes 4718596
  49.2 14.1 %collective-permute-start.13 = (bf16[1,128,2048]{2,1,0:T(8,128)(2,1)S(1)}, bf16[1,128,2048]{2,1,0:T(8,128)(2,1)}, u32[]{:S(2)}, u32[]{:S(2)}) collective-permute-start(bf16[1,128,2048]{2,1,0:T(8,128)(2,1)S(1)} %collective-permute-done.3.refs_5_), channel_id=1, source_target_pairs={{0,8},{8,0},{16,24},{24,16},{1,9},{9,1},{17,25},{25,17},{2,10},{10... | collective-permute-start | bytes 1572872 | tf_op jit(solution)/shard_map/ppermute | solution.py:78
  62.3 2.2 %collective-permute-start.14 = (bf16[1,128,2048]{2,1,0:T(8,128)(2,1)}, bf16[1,128,2048]{2,1,0:T(8,128)(2,1)S(1)}, u32[]{:S(2)}, u32[]{:S(2)}) collective-permute-start(bf16[1,128,2048]{2,1,0:T(8,128)(2,1)} %collective-permute-done.4.refs_6_), channel_id=1, source_target_pairs={{0,8},{8,0},{16,24},{24,16},{1,9},{9,1},{17,25},{25,17},{2,10},{10... | collective-permute-start | bytes 1572872 | tf_op jit(solution)/shard_map/ppermute | solution.py:78
  62.7 22.4 %copy-start.7 = (s32[6]{0:T(128)S(1)}, s32[6]{0:T(128)}, u32[]{:S(2)}) copy-start(s32[6]{0:T(128)} %param.8) | copy-start | bytes 76
  62.7 2.5 %collective-permute-start.15 = (bf16[1,128,2048]{2,1,0:T(8,128)(2,1)}, bf16[1,128,2048]{2,1,0:T(8,128)(2,1)S(1)}, u32[]{:S(2)}, u32[]{:S(2)}) collective-permute-start(bf16[1,128,2048]{2,1,0:T(8,128)(2,1)} %copy-done.2), channel_id=1, source_target_pairs={{0,8},{8,0},{16,24},{24,16},{1,9},{9,1},{17,25},{25,17},{2,10},{10... | collective-permute-start | bytes 1572872 | tf_op jit(solution)/shard_map/ppermute | solution.py:78
  62.9 3.1 %collective-permute-start.16 = (bf16[1,128,2048]{2,1,0:T(8,128)(2,1)}, bf16[1,128,2048]{2,1,0:T(8,128)(2,1)S(1)}, u32[]{:S(2)}, u32[]{:S(2)}) collective-permute-start(bf16[1,128,2048]{2,1,0:T(8,128)(2,1)} %collective-permute-done.8.refs_8_), channel_id=1, source_target_pairs={{0,8},{8,0},{16,24},{24,16},{1,9},{9,1},{17,25},{25,17},{2,10},{10... | collective-permute-start | bytes 1572872 | tf_op jit(solution)/shard_map/ppermute | solution.py:78
  66.0 1.9 %copy-start = (bf16[6,2048,128]{2,1,0:T(8,128)(2,1)S(1)}, bf16[6,2048,128]{2,1,0:T(8,128)(2,1)}, u32[]{:S(2)}) copy-start(bf16[6,2048,128]{2,1,0:T(8,128)(2,1)} %get-tuple-element.43.refs_0_) | copy-start | bytes 9437188
  (1 other events, 1.0 us)

commit v12 on v11

--- a/solution.py
+++ b/solution.py
@@ -27,47 +27,41 @@
     return theta.astype(jnp.bfloat16)
 
 
-def energy_kernel(*refs):
-    theta_ref = refs[0]
-    chol_refs = refs[1:-3]
-    out_ref, crossed_ref, square_ref = refs[-3:]
-    n_slot, _, electrons = theta_ref.shape
+def energy_kernel(theta_ref, *refs):
+    chol_refs = refs[:-1]
+    out_ref = refs[-1]
+    s = pl.program_id(0)
+    electrons = theta_ref.shape[2]
     lanes = out_ref.shape[1]
     rows = lax.broadcasted_iota(jnp.int32, (electrons, electrons), 0)
     cols = lax.broadcasted_iota(jnp.int32, (electrons, electrons), 1)
     diagonal = rows == cols
-    crossed_ref[...] = jnp.zeros(crossed_ref.shape, jnp.float32)
-    square_ref[...] = jnp.zeros(square_ref.shape, jnp.float32)
+    carry = (jnp.zeros((electrons, electrons), jnp.float32), jnp.zeros((1, 1), jnp.float32))
     for chol_ref in chol_refs:
         def per_vector(g, carry, chol_ref=chol_ref):
-            vector = chol_ref[g]
-            for s in range(n_slot):
-                blocks = jnp.dot(vector, theta_ref[s], preferred_element_type=jnp.float32)
-                crossed_ref[s] += blocks * blocks.T
-                diag = jnp.sum(jnp.where(diagonal, blocks, 0.0), axis=0, keepdims=True)
-                trace = jnp.sum(diag, axis=1, keepdims=True)
-                square_ref[pl.ds(s, 1), :] += jnp.broadcast_to(trace * trace, (1, lanes))
-            return carry
-
-        lax.fori_loop(0, chol_ref.shape[0], per_vector, 0)
-    for s in range(n_slot):
-        crossed = jnp.sum(crossed_ref[s], keepdims=True)
-        out_ref[pl.ds(s, 1), :] = 0.5 * (square_ref[pl.ds(s, 1), :] - jnp.broadcast_to(crossed, (1, lanes)))
+            crossed, square = carry
+            blocks = jnp.dot(chol_ref[g], theta_ref[0], preferred_element_type=jnp.float32)
+            diag = jnp.sum(jnp.where(diagonal, blocks, 0.0), axis=0, keepdims=True)
+            trace = jnp.sum(diag, axis=1, keepdims=True)
+            return crossed + blocks * blocks.T, square + trace * trace
+
+        carry = lax.fori_loop(0, chol_ref.shape[0], per_vector, carry)
+    crossed, square = carry
+    value = 0.5 * (square - jnp.sum(crossed, keepdims=True))
+    out_ref[pl.ds(s, 1), :] = jnp.broadcast_to(value, (1, lanes))
 
 
 def block_energy(theta, pieces):
-    n_slot, _, electrons = theta.shape
+    n_slot, orbitals, electrons = theta.shape
     vmem = pltpu.MemorySpace.VMEM
-    held = sum(p.size * p.dtype.itemsize for p in pieces) + theta.size * theta.dtype.itemsize
+    held = sum(p.size * p.dtype.itemsize for p in pieces) + 2 * orbitals * electrons * theta.dtype.itemsize
     out = pl.pallas_call(
         energy_kernel,
         out_shape=jax.ShapeDtypeStruct((n_slot, 128), jnp.float32),
-        in_specs=[pl.BlockSpec(memory_space=vmem)] * (1 + len(pieces)),
+        grid=(n_slot,),
+        in_specs=[pl.BlockSpec((1, orbitals, electrons), lambda s: (s, 0, 0))]
+        + [pl.BlockSpec(memory_space=vmem)] * len(pieces),
         out_specs=pl.BlockSpec(memory_space=vmem),
-        scratch_shapes=[
-            pltpu.VMEM((n_slot, electrons, electrons), jnp.float32),
-            pltpu.VMEM((n_slot, 128), jnp.float32),
-        ],
         compiler_params=pltpu.CompilerParams(vmem_limit_bytes=int(held + (16 << 20))),
     )(theta, *pieces)
     return out[:, 0]

time: 86.1 us -> 90.7 us (1.053)
  Pallas kernels: 29.1 us -> 33.6 us
    pallas_call x1, Pallas kernels: 16.1 us -> 20.6 us  [block_energy(): pl.pallas_call(energy_kernel, out_shape=jax.ShapeDtypeStruct((n_slot, 128...]
  transfers between devices with their start and end apart: 17 -> 17, of which waited for: 10 -> 10; matrix products, arithmetic and copies ran while one was open for 4% -> 4% of each run, Pallas kernels for 15% -> 14%
where the time goes in v12:
time: 90.7 us; the launch traced here: 90.2 us
  waiting for transfers between devices  33.8 us (37%)
  Pallas kernels  33.6 us (37%)
  starting transfers between devices  12.5 us (14%)
  local copies, waits for them, and re-layouts  6.76 us (7%)
  other arithmetic  2.84 us (3%)
    ppermute x4, waiting for transfers between devices, body(): ahead = lax.ppermute(ahead, 'chol', forward)  25.9 us
    pallas_call x1, Pallas kernels, block_energy(): pl.pallas_call(energy_kernel, out_shape=jax.ShapeDtypeStruct((n_slot, 128...  20.6 us
    pallas_call x1, Pallas kernels, kick(): pl.pallas_call(kick_kernel, out_shape=[shape, shape], grid_spec=grid_spec)  12.9 us
    ppermute x4, starting transfers between devices, body(): ahead = lax.ppermute(ahead, 'chol', forward)  7.8 us
    unnamed x16, local copies, waits for them, and re-layouts  4.09 us
    ppermute x3, waiting for transfers between devices, body(): behind = lax.ppermute(behind, 'chol', backward)  4 us
    ppermute x10, waiting for transfers between devices, swap_pairs(): return lax.ppermute(x, axis, perm)  3.88 us
    ppermute x10, starting transfers between devices, swap_pairs(): return lax.ppermute(x, axis, perm)  3.77 us
  transfers between devices with their start and end apart: 17, of which 10 were waited for; matrix products, arithmetic and copies ran while one was open for 4% of the time, Pallas kernels for 14%

profile of v12, /device:TPU:0, one launch (start us, length us, event | category | flops | bytes accessed | tf_op | source)
XLA Modules:
  0.0 90.2 jit_solution(12434311906668331022)
XLA Ops:
  0.6 1.1 %constant_dynamic-slice_fusion = bf16[1,128,2048]{2,1,0:T(8,128)(2,1)S(1)} fusion(bf16[2,128,2048]{2,1,0:T(8,128)(2,1)} %refs_0_.3, s32[]{:T(128)S(6)} %select_n.26), kind=kLoop, calls=%fused_computation.6 | loop fusion | bytes 1048580 | tf_op jit(solution)/shard_map/dynamic_slice | solution.py:183
  1.7 3.1 %collective-permute-start = (bf16[1,128,2048]{2,1,0:T(8,128)(2,1)S(1)}, bf16[1,128,2048]{2,1,0:T(8,128)(2,1)S(1)}, u32[]{:S(2)}, u32[]{:S(2)}) collective-permute-start(bf16[1,128,2048]{2,1,0:T(8,128)(2,1)S(1)} %constant_dynamic-slice_fusion), channel_id=1, source_target_pairs={{0,2},{2,4},{4,6},{6,7},{7,5},{5,3},{3,1},{1,0},{8,10},{10,12},{12... | collective-permute-start | bytes 1572872 | tf_op jit(solution)/shard_map/ppermute | solution.py:198
  4.8 1.9 %collective-permute-start.6 = (bf16[3,2048,128]{2,1,0:T(8,128)(2,1)}, bf16[3,2048,128]{2,1,0:T(8,128)(2,1)S(1)}, u32[]{:S(2)}, u32[]{:S(2)}) collective-permute-start(bf16[3,2048,128]{2,1,0:T(8,128)(2,1)} %refs_0_.2), channel_id=1, source_target_pairs={{0,16},{8,24},{16,0},{24,8},{1,17},{9,25},{17,1},{25,9},{2,18},{10... | collective-permute-start | bytes 4718600 | tf_op jit(solution)/shard_map/ppermute | solution.py:72
  6.8 1.5 %scatter.4.refs_4_ = f32[8,2048]{1,0:T(8,128)} pad(f32[6,2048]{1,0:T(8,128)} %param.9, f32[]{:T(128)} %constant.67.clone.1), padding=0_2x0_0 | pad | bytes 114692 | tf_op jit(solution)/shard_map/scatter | solution.py:140
  8.2 1.2 %fusion.source_ref = s32[6]{0:T(128)} fusion(s32[6]{0:T(128)} %param.8, s32[]{:T(128)S(6)} %axis_index.15), kind=kLoop, calls=%fused_computation.5 | loop fusion | flops 96 | bytes 52 | tf_op jit(solution)/shard_map/add | solution.py:138
  9.4 1.1 %compare_convert_fusion.living_ref = s32[6]{0:T(128)} fusion(s32[6]{0:T(128)} %param.8), kind=kLoop, calls=%fused_computation.4 | loop fusion | flops 12 | bytes 48 | tf_op jit(solution)/shard_map/convert_element_type | solution.py:135
  10.5 6.1 %collective-permute-done.refs_1_ = bf16[1,128,2048]{2,1,0:T(8,128)(2,1)S(1)} collective-permute-done((bf16[1,128,2048]{2,1,0:T(8,128)(2,1)S(1)}, bf16[1,128,2048]{2,1,0:T(8,128)(2,1)S(1)}, u32[]{:S(2)}, u32[]{:S(2)}) %collective-permute-start) | collective-permute-done | bytes 524320 | tf_op jit(solution)/shard_map/ppermute | solution.py:198
  16.7 1.5 %collective-permute-done.1.refs_2_ = bf16[1,128,2048]{2,1,0:T(8,128)(2,1)S(1)} collective-permute-done((bf16[1,128,2048]{2,1,0:T(8,128)(2,1)S(1)}, bf16[1,128,2048]{2,1,0:T(8,128)(2,1)S(1)}, u32[]{:S(2)}, u32[]{:S(2)}) %collective-permute-start.1) | collective-permute-done | bytes 524320 | tf_op jit(solution)/shard_map/ppermute | solution.py:201
  18.2 1.6 %collective-permute-start.2 = (bf16[1,128,2048]{2,1,0:T(8,128)(2,1)S(1)}, bf16[1,128,2048]{2,1,0:T(8,128)(2,1)S(1)}, u32[]{:S(2)}, u32[]{:S(2)}) collective-permute-start(bf16[1,128,2048]{2,1,0:T(8,128)(2,1)S(1)} %collective-permute-done.refs_1_), channel_id=1, source_target_pairs={{0,2},{2,4},{4,6},{6,7},{7,5},{5,3},{3,1},{1,0},{8,10},{10,12},{12... | collective-permute-start | bytes 1572872 | tf_op jit(solution)/shard_map/ppermute | solution.py:198
  20.2 10.4 %collective-permute-done.2.refs_3_ = bf16[1,128,2048]{2,1,0:T(8,128)(2,1)S(1)} collective-permute-done((bf16[1,128,2048]{2,1,0:T(8,128)(2,1)S(1)}, bf16[1,128,2048]{2,1,0:T(8,128)(2,1)S(1)}, u32[]{:S(2)}, u32[]{:S(2)}) %collective-permute-start.2) | collective-permute-done | bytes 524320 | tf_op jit(solution)/shard_map/ppermute | solution.py:198
  30.7 1.3 %collective-permute-done.3.refs_4_ = bf16[1,128,2048]{2,1,0:T(8,128)(2,1)S(1)} collective-permute-done((bf16[1,128,2048]{2,1,0:T(8,128)(2,1)S(1)}, bf16[1,128,2048]{2,1,0:T(8,128)(2,1)S(1)}, u32[]{:S(2)}, u32[]{:S(2)}) %collective-permute-start.3) | collective-permute-done | bytes 524320 | tf_op jit(solution)/shard_map/ppermute | solution.py:201
  32.0 1.6 %collective-permute-start.4 = (bf16[1,128,2048]{2,1,0:T(8,128)(2,1)S(1)}, bf16[1,128,2048]{2,1,0:T(8,128)(2,1)}, u32[]{:S(2)}, u32[]{:S(2)}) collective-permute-start(bf16[1,128,2048]{2,1,0:T(8,128)(2,1)S(1)} %collective-permute-done.2.refs_3_), channel_id=1, source_target_pairs={{0,2},{2,4},{4,6},{6,7},{7,5},{5,3},{3,1},{1,0},{8,10},{10,12},{12... | collective-permute-start | bytes 1572872 | tf_op jit(solution)/shard_map/ppermute | solution.py:198
  34.0 9.4 %collective-permute-done.4.refs_5_ = bf16[1,128,2048]{2,1,0:T(8,128)(2,1)} collective-permute-done((bf16[1,128,2048]{2,1,0:T(8,128)(2,1)S(1)}, bf16[1,128,2048]{2,1,0:T(8,128)(2,1)}, u32[]{:S(2)}, u32[]{:S(2)}) %collective-permute-start.4) | collective-permute-done | bytes 524320 | tf_op jit(solution)/shard_map/ppermute | solution.py:198
  43.3 1.2 %collective-permute-done.5.refs_6_ = bf16[1,128,2048]{2,1,0:T(8,128)(2,1)S(1)} collective-permute-done((bf16[1,128,2048]{2,1,0:T(8,128)(2,1)S(1)}, bf16[1,128,2048]{2,1,0:T(8,128)(2,1)S(1)}, u32[]{:S(2)}, u32[]{:S(2)}) %collective-permute-start.5) | collective-permute-done | bytes 524320 | tf_op jit(solution)/shard_map/ppermute | solution.py:201
  44.6 1.6 %collective-permute-start.8 = (bf16[1,128,2048]{2,1,0:T(8,128)(2,1)}, bf16[1,128,2048]{2,1,0:T(8,128)(2,1)}, u32[]{:S(2)}, u32[]{:S(2)}) collective-permute-start(bf16[1,128,2048]{2,1,0:T(8,128)(2,1)} %collective-permute-done.4.refs_5_), channel_id=1, source_target_pairs={{0,2},{2,4},{4,6},{6,7},{7,5},{5,3},{3,1},{1,0},{8,10},{10,12},{12... | collective-permute-start | bytes 1572872 | tf_op jit(solution)/shard_map/ppermute | solution.py:198
  46.9 1.1 %collective-permute-done.9.refs_3_ = bf16[3,2048,128]{2,1,0:T(8,128)(2,1)S(1)} collective-permute-done((bf16[3,2048,128]{2,1,0:T(8,128)(2,1)S(1)}, bf16[3,2048,128]{2,1,0:T(8,128)(2,1)S(1)}, u32[]{:S(2)}, u32[]{:S(2)}) %collective-permute-start.9) | collective-permute-done | bytes 1572896 | tf_op jit(solution)/shard_map/ppermute | solution.py:72
  48.0 1.1 %copy-done.6 = bf16[3,2048,128]{2,1,0:T(8,128)(2,1)} copy-done((bf16[3,2048,128]{2,1,0:T(8,128)(2,1)}, bf16[3,2048,128]{2,1,0:T(8,128)(2,1)S(1)}, u32[]{:S(2)}) %copy-start.6) | copy-done | bytes 1572888
  49.3 12.9 %shard_map.59 = (bf16[6,2048,128]{2,1,0:T(8,128)(2,1)}, bf16[6,2048,128]{2,1,0:T(8,128)(2,1)}) custom-call(s32[6]{0:T(128)} %fusion.source_ref, s32[6]{0:T(128)} %compare_convert_fusion.living_ref, bf16[3,2048,128]{2,1,0:T(8,128)(2,1)} %refs_0_.2, bf16[3,2048,128]{2,1,0:T(8,128)(2,1)} %copy-done.5, bf16[3,2048,128]{2,1,0:T(8,128)(2,1)} %copy-done.4, ...), custom_call_target="tpu_custom_call" | custom-call | tf_op jit(solution)/shard_map/pallas_call | solution.py:165
  63.3 1.2 %collective-permute-done.14.refs_12_ = bf16[1,128,2048]{2,1,0:T(8,128)(2,1)S(1)} collective-permute-done((bf16[1,128,2048]{2,1,0:T(8,128)(2,1)}, bf16[1,128,2048]{2,1,0:T(8,128)(2,1)S(1)}, u32[]{:S(2)}, u32[]{:S(2)}) %collective-permute-start.14) | collective-permute-done | bytes 524320 | tf_op jit(solution)/shard_map/ppermute | solution.py:72
  64.5 0.7 collective-permute-done.15.refs_13_
  65.2 0.7 collective-permute-done.16.refs_14_
  66.0 1.9 %copy-done = bf16[6,2048,128]{2,1,0:T(8,128)(2,1)S(1)} copy-done((bf16[6,2048,128]{2,1,0:T(8,128)(2,1)S(1)}, bf16[6,2048,128]{2,1,0:T(8,128)(2,1)}, u32[]{:S(2)}) %copy-start) | copy-done | bytes 3145752
  67.9 1.0 %copy-done.3 = bf16[1,128,2048]{2,1,0:T(8,128)(2,1)S(1)} copy-done((bf16[1,128,2048]{2,1,0:T(8,128)(2,1)S(1)}, bf16[1,128,2048]{2,1,0:T(8,128)(2,1)}, u32[]{:S(2)}) %copy-start.3) | copy-done | bytes 524312
  68.9 20.6 %shard_map.60 = f32[6,128]{1,0:T(8,128)S(1)} custom-call(bf16[6,2048,128]{2,1,0:T(8,128)(2,1)S(1)} %copy-done, bf16[2,128,2048]{2,1,0:T(8,128)(2,1)S(1)} %copy-done.1, bf16[1,128,2048]{2,1,0:T(8,128)(2,1)S(1)} %collective-permute-done.refs_1_, bf16[1,128,2048]{2,1,0:T(8,128)(2,1)S(1)} %collective-permute-done.1.refs_2_, ...), custom_call_target="tpu_custom_call" | custom-call | tf_op jit(solution)/shard_map/pallas_call | solution.py:58
  (34 shorter events, 3.4 us)
Async XLA Ops:
  1.7 14.9 %collective-permute-start = (bf16[1,128,2048]{2,1,0:T(8,128)(2,1)S(1)}, bf16[1,128,2048]{2,1,0:T(8,128)(2,1)S(1)}, u32[]{:S(2)}, u32[]{:S(2)}) collective-permute-start(bf16[1,128,2048]{2,1,0:T(8,128)(2,1)S(1)} %constant_dynamic-slice_fusion), channel_id=1, source_target_pairs={{0,2},{2,4},{4,6},{6,7},{7,5},{5,3},{3,1},{1,0},{8,10},{10,12},{12... | collective-permute-start | bytes 1572872 | tf_op jit(solution)/shard_map/ppermute | solution.py:198
  4.8 13.4 %collective-permute-start.1 = (bf16[1,128,2048]{2,1,0:T(8,128)(2,1)S(1)}, bf16[1,128,2048]{2,1,0:T(8,128)(2,1)S(1)}, u32[]{:S(2)}, u32[]{:S(2)}) collective-permute-start(bf16[1,128,2048]{2,1,0:T(8,128)(2,1)S(1)} %constant_dynamic-slice_fusion), channel_id=1, source_target_pairs={{2,0},{4,2},{6,4},{7,6},{5,7},{3,5},{1,3},{0,1},{10,8},{12,10},{14... | collective-permute-start | bytes 1572872 | tf_op jit(solution)/shard_map/ppermute | solution.py:201
  4.8 39.7 %collective-permute-start.6 = (bf16[3,2048,128]{2,1,0:T(8,128)(2,1)}, bf16[3,2048,128]{2,1,0:T(8,128)(2,1)S(1)}, u32[]{:S(2)}, u32[]{:S(2)}) collective-permute-start(bf16[3,2048,128]{2,1,0:T(8,128)(2,1)} %refs_0_.2), channel_id=1, source_target_pairs={{0,16},{8,24},{16,0},{24,8},{1,17},{9,25},{17,1},{25,9},{2,18},{10... | collective-permute-start | bytes 4718600 | tf_op jit(solution)/shard_map/ppermute | solution.py:72
  6.8 37.8 %collective-permute-start.7 = (bf16[3,2048,128]{2,1,0:T(8,128)(2,1)}, bf16[3,2048,128]{2,1,0:T(8,128)(2,1)S(1)}, u32[]{:S(2)}, u32[]{:S(2)}) collective-permute-start(bf16[3,2048,128]{2,1,0:T(8,128)(2,1)} %refs_0_.2), channel_id=1, source_target_pairs={{0,8},{8,0},{16,24},{24,16},{1,9},{9,1},{17,25},{25,17},{2,10},{10... | collective-permute-start | bytes 4718600 | tf_op jit(solution)/shard_map/ppermute | solution.py:72
  10.5 55.4 %copy-start.1 = (bf16[2,128,2048]{2,1,0:T(8,128)(2,1)S(1)}, bf16[2,128,2048]{2,1,0:T(8,128)(2,1)}, u32[]{:S(2)}) copy-start(bf16[2,128,2048]{2,1,0:T(8,128)(2,1)} %refs_0_.3) | copy-start | bytes 3145732
  18.2 12.5 %collective-permute-start.2 = (bf16[1,128,2048]{2,1,0:T(8,128)(2,1)S(1)}, bf16[1,128,2048]{2,1,0:T(8,128)(2,1)S(1)}, u32[]{:S(2)}, u32[]{:S(2)}) collective-permute-start(bf16[1,128,2048]{2,1,0:T(8,128)(2,1)S(1)} %collective-permute-done.refs_1_), channel_id=1, source_target_pairs={{0,2},{2,4},{4,6},{6,7},{7,5},{5,3},{3,1},{1,0},{8,10},{10,12},{12... | collective-permute-start | bytes 1572872 | tf_op jit(solution)/shard_map/ppermute | solution.py:198
  19.8 12.2 %collective-permute-start.3 = (bf16[1,128,2048]{2,1,0:T(8,128)(2,1)S(1)}, bf16[1,128,2048]{2,1,0:T(8,128)(2,1)S(1)}, u32[]{:S(2)}, u32[]{:S(2)}) collective-permute-start(bf16[1,128,2048]{2,1,0:T(8,128)(2,1)S(1)} %collective-permute-done.1.refs_2_), channel_id=1, source_target_pairs={{2,0},{4,2},{6,4},{7,6},{5,7},{3,5},{1,3},{0,1},{10,8},{12,10},{14... | collective-permute-start | bytes 1572872 | tf_op jit(solution)/shard_map/ppermute | solution.py:201
  32.0 11.4 %collective-permute-start.4 = (bf16[1,128,2048]{2,1,0:T(8,128)(2,1)S(1)}, bf16[1,128,2048]{2,1,0:T(8,128)(2,1)}, u32[]{:S(2)}, u32[]{:S(2)}) collective-permute-start(bf16[1,128,2048]{2,1,0:T(8,128)(2,1)S(1)} %collective-permute-done.2.refs_3_), channel_id=1, source_target_pairs={{0,2},{2,4},{4,6},{6,7},{7,5},{5,3},{3,1},{1,0},{8,10},{10,12},{12... | collective-permute-start | bytes 1572872 | tf_op jit(solution)/shard_map/ppermute | solution.py:198
  33.5 11.0 %collective-permute-start.5 = (bf16[1,128,2048]{2,1,0:T(8,128)(2,1)S(1)}, bf16[1,128,2048]{2,1,0:T(8,128)(2,1)S(1)}, u32[]{:S(2)}, u32[]{:S(2)}) collective-permute-start(bf16[1,128,2048]{2,1,0:T(8,128)(2,1)S(1)} %collective-permute-done.3.refs_4_), channel_id=1, source_target_pairs={{2,0},{4,2},{6,4},{7,6},{5,7},{3,5},{1,3},{0,1},{10,8},{12,10},{14... | collective-permute-start | bytes 1572872 | tf_op jit(solution)/shard_map/ppermute | solution.py:201
  44.5 2.4 %copy-start.2 = (bf16[1,128,2048]{2,1,0:T(8,128)(2,1)}, bf16[1,128,2048]{2,1,0:T(8,128)(2,1)S(1)}, u32[]{:S(2)}) copy-start(bf16[1,128,2048]{2,1,0:T(8,128)(2,1)S(1)} %collective-permute-done.5.refs_6_) | copy-start | bytes 1572868
  44.5 3.5 %copy-start.4 = (bf16[3,2048,128]{2,1,0:T(8,128)(2,1)}, bf16[3,2048,128]{2,1,0:T(8,128)(2,1)S(1)}, u32[]{:S(2)}) copy-start(bf16[3,2048,128]{2,1,0:T(8,128)(2,1)S(1)} %collective-permute-done.6.refs_2_) | copy-start | bytes 4718596
  44.6 3.5 %copy-start.5 = (bf16[3,2048,128]{2,1,0:T(8,128)(2,1)}, bf16[3,2048,128]{2,1,0:T(8,128)(2,1)S(1)}, u32[]{:S(2)}) copy-start(bf16[3,2048,128]{2,1,0:T(8,128)(2,1)S(1)} %collective-permute-done.7.refs_1_) | copy-start | bytes 4718596
  44.6 3.5 %collective-permute-start.9 = (bf16[3,2048,128]{2,1,0:T(8,128)(2,1)S(1)}, bf16[3,2048,128]{2,1,0:T(8,128)(2,1)S(1)}, u32[]{:S(2)}, u32[]{:S(2)}) collective-permute-start(bf16[3,2048,128]{2,1,0:T(8,128)(2,1)S(1)} %collective-permute-done.6.refs_2_), channel_id=1, source_target_pairs={{0,8},{8,0},{16,24},{24,16},{1,9},{9,1},{17,25},{25,17},{2,10},{10... | collective-permute-start | bytes 4718600 | tf_op jit(solution)/shard_map/ppermute | solution.py:72
  44.6 17.6 %collective-permute-start.8 = (bf16[1,128,2048]{2,1,0:T(8,128)(2,1)}, bf16[1,128,2048]{2,1,0:T(8,128)(2,1)}, u32[]{:S(2)}, u32[]{:S(2)}) collective-permute-start(bf16[1,128,2048]{2,1,0:T(8,128)(2,1)} %collective-permute-done.4.refs_5_), channel_id=1, source_target_pairs={{0,2},{2,4},{4,6},{6,7},{7,5},{5,3},{3,1},{1,0},{8,10},{10,12},{12... | collective-permute-start | bytes 1572872 | tf_op jit(solution)/shard_map/ppermute | solution.py:198
  46.2 16.5 %collective-permute-start.10 = (bf16[1,128,2048]{2,1,0:T(8,128)(2,1)S(1)}, bf16[1,128,2048]{2,1,0:T(8,128)(2,1)}, u32[]{:S(2)}, u32[]{:S(2)}) collective-permute-start(bf16[1,128,2048]{2,1,0:T(8,128)(2,1)S(1)} %collective-permute-done.refs_1_), channel_id=1, source_target_pairs={{0,8},{8,0},{16,24},{24,16},{1,9},{9,1},{17,25},{25,17},{2,10},{10... | collective-permute-start | bytes 1572872 | tf_op jit(solution)/shard_map/ppermute | solution.py:72
  46.4 16.5 %collective-permute-start.11 = (bf16[1,128,2048]{2,1,0:T(8,128)(2,1)S(1)}, bf16[1,128,2048]{2,1,0:T(8,128)(2,1)}, u32[]{:S(2)}, u32[]{:S(2)}) collective-permute-start(bf16[1,128,2048]{2,1,0:T(8,128)(2,1)S(1)} %collective-permute-done.1.refs_2_), channel_id=1, source_target_pairs={{0,8},{8,0},{16,24},{24,16},{1,9},{9,1},{17,25},{25,17},{2,10},{10... | collective-permute-start | bytes 1572872 | tf_op jit(solution)/shard_map/ppermute | solution.py:72
  46.7 16.5 %collective-permute-start.12 = (bf16[1,128,2048]{2,1,0:T(8,128)(2,1)S(1)}, bf16[1,128,2048]{2,1,0:T(8,128)(2,1)}, u32[]{:S(2)}, u32[]{:S(2)}) collective-permute-start(bf16[1,128,2048]{2,1,0:T(8,128)(2,1)S(1)} %collective-permute-done.2.refs_3_), channel_id=1, source_target_pairs={{0,8},{8,0},{16,24},{24,16},{1,9},{9,1},{17,25},{25,17},{2,10},{10... | collective-permute-start | bytes 1572872 | tf_op jit(solution)/shard_map/ppermute | solution.py:72
  48.0 1.1 %copy-start.6 = (bf16[3,2048,128]{2,1,0:T(8,128)(2,1)}, bf16[3,2048,128]{2,1,0:T(8,128)(2,1)S(1)}, u32[]{:S(2)}) copy-start(bf16[3,2048,128]{2,1,0:T(8,128)(2,1)S(1)} %collective-permute-done.9.refs_3_) | copy-start | bytes 4718596
  49.2 14.1 %collective-permute-start.13 = (bf16[1,128,2048]{2,1,0:T(8,128)(2,1)S(1)}, bf16[1,128,2048]{2,1,0:T(8,128)(2,1)}, u32[]{:S(2)}, u32[]{:S(2)}) collective-permute-start(bf16[1,128,2048]{2,1,0:T(8,128)(2,1)S(1)} %collective-permute-done.3.refs_4_), channel_id=1, source_target_pairs={{0,8},{8,0},{16,24},{24,16},{1,9},{9,1},{17,25},{25,17},{2,10},{10... | collective-permute-start | bytes 1572872 | tf_op jit(solution)/shard_map/ppermute | solution.py:72
  62.3 2.2 %collective-permute-start.14 = (bf16[1,128,2048]{2,1,0:T(8,128)(2,1)}, bf16[1,128,2048]{2,1,0:T(8,128)(2,1)S(1)}, u32[]{:S(2)}, u32[]{:S(2)}) collective-permute-start(bf16[1,128,2048]{2,1,0:T(8,128)(2,1)} %collective-permute-done.4.refs_5_), channel_id=1, source_target_pairs={{0,8},{8,0},{16,24},{24,16},{1,9},{9,1},{17,25},{25,17},{2,10},{10... | collective-permute-start | bytes 1572872 | tf_op jit(solution)/shard_map/ppermute | solution.py:72
  62.7 26.9 %copy-start.7 = (s32[6]{0:T(128)S(1)}, s32[6]{0:T(128)}, u32[]{:S(2)}) copy-start(s32[6]{0:T(128)} %param.8) | copy-start | bytes 76
  62.7 2.5 %collective-permute-start.15 = (bf16[1,128,2048]{2,1,0:T(8,128)(2,1)}, bf16[1,128,2048]{2,1,0:T(8,128)(2,1)S(1)}, u32[]{:S(2)}, u32[]{:S(2)}) collective-permute-start(bf16[1,128,2048]{2,1,0:T(8,128)(2,1)} %copy-done.2), channel_id=1, source_target_pairs={{0,8},{8,0},{16,24},{24,16},{1,9},{9,1},{17,25},{25,17},{2,10},{10... | collective-permute-start | bytes 1572872 | tf_op jit(solution)/shard_map/ppermute | solution.py:72
  62.9 3.1 %collective-permute-start.16 = (bf16[1,128,2048]{2,1,0:T(8,128)(2,1)}, bf16[1,128,2048]{2,1,0:T(8,128)(2,1)S(1)}, u32[]{:S(2)}, u32[]{:S(2)}) collective-permute-start(bf16[1,128,2048]{2,1,0:T(8,128)(2,1)} %collective-permute-done.8.refs_7_), channel_id=1, source_target_pairs={{0,8},{8,0},{16,24},{24,16},{1,9},{9,1},{17,25},{25,17},{2,10},{10... | collective-permute-start | bytes 1572872 | tf_op jit(solution)/shard_map/ppermute | solution.py:72
  66.0 1.9 %copy-start = (bf16[6,2048,128]{2,1,0:T(8,128)(2,1)S(1)}, bf16[6,2048,128]{2,1,0:T(8,128)(2,1)}, u32[]{:S(2)}) copy-start(bf16[6,2048,128]{2,1,0:T(8,128)(2,1)} %get-tuple-element.43.theta_ref) | copy-start | bytes 9437188
  (1 other events, 1.0 us)

commit v13 on v11

--- a/solution.py
+++ b/solution.py
@@ -80,7 +80,7 @@
 
 def kick_kernel(source_ref, living_ref, *refs):
     walker_refs = refs[:4]
-    field_ref, new_hbm, theta_hbm, walkers, kicked_buf, new_buf, theta_buf, in_sem, out_sem = refs[4:]
+    field_ref, new_hbm, theta_out, walkers, kicked_buf, new_buf, in_sem, out_sem = refs[4:]
     old_dev = walker_refs[0].shape[0]
     n_slot, orbitals, electrons = walkers.shape
 
@@ -128,10 +128,7 @@
     for s in range(n_slot):
         widened = kicked_buf[s].astype(jnp.float32)
         theta = jnp.dot(widened, inverses[s], precision=lax.Precision.HIGHEST, preferred_element_type=jnp.float32)
-        theta_buf[s] = theta.astype(jnp.bfloat16)
-        copy = pltpu.make_async_copy(theta_buf.at[s], theta_hbm.at[s], out_sem.at[1, s])
-        copy.start()
-        out_copies.append(copy)
+        theta_out[s] = theta.astype(jnp.bfloat16)
     for copy in out_copies:
         copy.wait()
 
@@ -157,14 +154,13 @@
         num_scalar_prefetch=2,
         grid=(1,),
         in_specs=[any_space] * 4 + [pl.BlockSpec((lanes, orbitals), lambda i, *_: (0, 0))],
-        out_specs=[any_space, any_space],
+        out_specs=[any_space, pl.BlockSpec(memory_space=pltpu.MemorySpace.VMEM)],
         scratch_shapes=[
             pltpu.VMEM(slots, jnp.bfloat16),
             pltpu.VMEM(slots, jnp.bfloat16),
             pltpu.VMEM(slots, jnp.bfloat16),
-            pltpu.VMEM(slots, jnp.bfloat16),
             pltpu.SemaphoreType.DMA((slot_dev,)),
-            pltpu.SemaphoreType.DMA((2, slot_dev)),
+            pltpu.SemaphoreType.DMA((1, slot_dev)),
         ],
     )
     shape = jax.ShapeDtypeStruct(slots, jnp.bfloat16)

time: 86.1 us -> 86.7 us (level)
  transfers between devices with their start and end apart: 17 -> 17, of which waited for: 10 -> 10; matrix products, arithmetic and copies ran while one was open for 4% -> 4% of each run, Pallas kernels for 15% -> 16%
where the time goes in v13:
time: 86.7 us; the launch traced here: 86.4 us
  waiting for transfers between devices  34.1 us (39%)
  Pallas kernels  29.8 us (34%)
  starting transfers between devices  12.2 us (14%)
  local copies, waits for them, and re-layouts  6.76 us (8%)
  other arithmetic  2.84 us (3%)
    ppermute x4, waiting for transfers between devices, body(): ahead = lax.ppermute(ahead, 'chol', forward)  25.9 us
    pallas_call x1, Pallas kernels, block_energy(): pl.pallas_call(energy_kernel, out_shape=jax.ShapeDtypeStruct((n_slot, 128...  16.1 us
    pallas_call x1, Pallas kernels, kick(): pl.pallas_call(kick_kernel, out_shape=[shape, shape], grid_spec=grid_spec)  13.7 us
    ppermute x4, starting transfers between devices, body(): ahead = lax.ppermute(ahead, 'chol', forward)  7.8 us
    ppermute x10, waiting for transfers between devices, swap_pairs(): return lax.ppermute(x, axis, perm)  4.15 us
    unnamed x16, local copies, waits for them, and re-layouts  4.09 us
    ppermute x3, waiting for transfers between devices, body(): behind = lax.ppermute(behind, 'chol', backward)  4 us
    ppermute x10, starting transfers between devices, swap_pairs(): return lax.ppermute(x, axis, perm)  3.5 us
  transfers between devices with their start and end apart: 17, of which 10 were waited for; matrix products, arithmetic and copies ran while one was open for 4% of the time, Pallas kernels for 16%

profile of v13, /device:TPU:0, one launch (start us, length us, event | category | flops | bytes accessed | tf_op | source)
XLA Modules:
  0.0 86.4 jit_solution(4970887465982839898)
XLA Ops:
  0.6 1.1 %constant_dynamic-slice_fusion = bf16[1,128,2048]{2,1,0:T(8,128)(2,1)S(1)} fusion(bf16[2,128,2048]{2,1,0:T(8,128)(2,1)} %refs_1_.1, s32[]{:T(128)S(6)} %select_n.26), kind=kLoop, calls=%fused_computation.6 | loop fusion | bytes 1048580 | tf_op jit(solution)/shard_map/dynamic_slice | solution.py:185
  1.7 3.1 %collective-permute-start = (bf16[1,128,2048]{2,1,0:T(8,128)(2,1)S(1)}, bf16[1,128,2048]{2,1,0:T(8,128)(2,1)S(1)}, u32[]{:S(2)}, u32[]{:S(2)}) collective-permute-start(bf16[1,128,2048]{2,1,0:T(8,128)(2,1)S(1)} %constant_dynamic-slice_fusion), channel_id=1, source_target_pairs={{0,2},{2,4},{4,6},{6,7},{7,5},{5,3},{3,1},{1,0},{8,10},{10,12},{12... | collective-permute-start | bytes 1572872 | tf_op jit(solution)/shard_map/ppermute | solution.py:200
  4.8 1.9 %collective-permute-start.6 = (bf16[3,2048,128]{2,1,0:T(8,128)(2,1)}, bf16[3,2048,128]{2,1,0:T(8,128)(2,1)S(1)}, u32[]{:S(2)}, u32[]{:S(2)}) collective-permute-start(bf16[3,2048,128]{2,1,0:T(8,128)(2,1)} %refs_0_.1), channel_id=1, source_target_pairs={{0,16},{8,24},{16,0},{24,8},{1,17},{9,25},{17,1},{25,9},{2,18},{10... | collective-permute-start | bytes 4718600 | tf_op jit(solution)/shard_map/ppermute | solution.py:78
  6.8 1.5 %scatter.4.refs_4_ = f32[8,2048]{1,0:T(8,128)} pad(f32[6,2048]{1,0:T(8,128)} %param.9, f32[]{:T(128)} %constant.67.clone.1), padding=0_2x0_0 | pad | bytes 114692 | tf_op jit(solution)/shard_map/scatter | solution.py:143
  8.2 1.2 %fusion.source_ref = s32[6]{0:T(128)} fusion(s32[6]{0:T(128)} %param.8, s32[]{:T(128)S(6)} %axis_index.15), kind=kLoop, calls=%fused_computation.5 | loop fusion | flops 96 | bytes 52 | tf_op jit(solution)/shard_map/add | solution.py:141
  9.4 1.1 %compare_convert_fusion.living_ref = s32[6]{0:T(128)} fusion(s32[6]{0:T(128)} %param.8), kind=kLoop, calls=%fused_computation.4 | loop fusion | flops 12 | bytes 48 | tf_op jit(solution)/shard_map/convert_element_type | solution.py:138
  10.5 6.1 %collective-permute-done.refs_2_ = bf16[1,128,2048]{2,1,0:T(8,128)(2,1)S(1)} collective-permute-done((bf16[1,128,2048]{2,1,0:T(8,128)(2,1)S(1)}, bf16[1,128,2048]{2,1,0:T(8,128)(2,1)S(1)}, u32[]{:S(2)}, u32[]{:S(2)}) %collective-permute-start) | collective-permute-done | bytes 524320 | tf_op jit(solution)/shard_map/ppermute | solution.py:200
  16.7 1.5 %collective-permute-done.1.refs_3_ = bf16[1,128,2048]{2,1,0:T(8,128)(2,1)S(1)} collective-permute-done((bf16[1,128,2048]{2,1,0:T(8,128)(2,1)S(1)}, bf16[1,128,2048]{2,1,0:T(8,128)(2,1)S(1)}, u32[]{:S(2)}, u32[]{:S(2)}) %collective-permute-start.1) | collective-permute-done | bytes 524320 | tf_op jit(solution)/shard_map/ppermute | solution.py:203
  18.2 1.6 %collective-permute-start.2 = (bf16[1,128,2048]{2,1,0:T(8,128)(2,1)S(1)}, bf16[1,128,2048]{2,1,0:T(8,128)(2,1)S(1)}, u32[]{:S(2)}, u32[]{:S(2)}) collective-permute-start(bf16[1,128,2048]{2,1,0:T(8,128)(2,1)S(1)} %collective-permute-done.refs_2_), channel_id=1, source_target_pairs={{0,2},{2,4},{4,6},{6,7},{7,5},{5,3},{3,1},{1,0},{8,10},{10,12},{12... | collective-permute-start | bytes 1572872 | tf_op jit(solution)/shard_map/ppermute | solution.py:200
  20.2 10.4 %collective-permute-done.2.refs_4_ = bf16[1,128,2048]{2,1,0:T(8,128)(2,1)S(1)} collective-permute-done((bf16[1,128,2048]{2,1,0:T(8,128)(2,1)S(1)}, bf16[1,128,2048]{2,1,0:T(8,128)(2,1)S(1)}, u32[]{:S(2)}, u32[]{:S(2)}) %collective-permute-start.2) | collective-permute-done | bytes 524320 | tf_op jit(solution)/shard_map/ppermute | solution.py:200
  30.7 1.3 %collective-permute-done.3.refs_5_ = bf16[1,128,2048]{2,1,0:T(8,128)(2,1)S(1)} collective-permute-done((bf16[1,128,2048]{2,1,0:T(8,128)(2,1)S(1)}, bf16[1,128,2048]{2,1,0:T(8,128)(2,1)S(1)}, u32[]{:S(2)}, u32[]{:S(2)}) %collective-permute-start.3) | collective-permute-done | bytes 524320 | tf_op jit(solution)/shard_map/ppermute | solution.py:203
  32.0 1.6 %collective-permute-start.4 = (bf16[1,128,2048]{2,1,0:T(8,128)(2,1)S(1)}, bf16[1,128,2048]{2,1,0:T(8,128)(2,1)}, u32[]{:S(2)}, u32[]{:S(2)}) collective-permute-start(bf16[1,128,2048]{2,1,0:T(8,128)(2,1)S(1)} %collective-permute-done.2.refs_4_), channel_id=1, source_target_pairs={{0,2},{2,4},{4,6},{6,7},{7,5},{5,3},{3,1},{1,0},{8,10},{10,12},{12... | collective-permute-start | bytes 1572872 | tf_op jit(solution)/shard_map/ppermute | solution.py:200
  34.0 9.4 %collective-permute-done.4.refs_6_ = bf16[1,128,2048]{2,1,0:T(8,128)(2,1)} collective-permute-done((bf16[1,128,2048]{2,1,0:T(8,128)(2,1)S(1)}, bf16[1,128,2048]{2,1,0:T(8,128)(2,1)}, u32[]{:S(2)}, u32[]{:S(2)}) %collective-permute-start.4) | collective-permute-done | bytes 524320 | tf_op jit(solution)/shard_map/ppermute | solution.py:200
  43.3 1.2 %collective-permute-done.5.refs_7_ = bf16[1,128,2048]{2,1,0:T(8,128)(2,1)S(1)} collective-permute-done((bf16[1,128,2048]{2,1,0:T(8,128)(2,1)S(1)}, bf16[1,128,2048]{2,1,0:T(8,128)(2,1)S(1)}, u32[]{:S(2)}, u32[]{:S(2)}) %collective-permute-start.5) | collective-permute-done | bytes 524320 | tf_op jit(solution)/shard_map/ppermute | solution.py:203
  44.6 1.6 %collective-permute-start.8 = (bf16[1,128,2048]{2,1,0:T(8,128)(2,1)}, bf16[1,128,2048]{2,1,0:T(8,128)(2,1)}, u32[]{:S(2)}, u32[]{:S(2)}) collective-permute-start(bf16[1,128,2048]{2,1,0:T(8,128)(2,1)} %collective-permute-done.4.refs_6_), channel_id=1, source_target_pairs={{0,2},{2,4},{4,6},{6,7},{7,5},{5,3},{3,1},{1,0},{8,10},{10,12},{12... | collective-permute-start | bytes 1572872 | tf_op jit(solution)/shard_map/ppermute | solution.py:200
  46.9 1.1 %collective-permute-done.9.refs_3_ = bf16[3,2048,128]{2,1,0:T(8,128)(2,1)S(1)} collective-permute-done((bf16[3,2048,128]{2,1,0:T(8,128)(2,1)S(1)}, bf16[3,2048,128]{2,1,0:T(8,128)(2,1)S(1)}, u32[]{:S(2)}, u32[]{:S(2)}) %collective-permute-start.9) | collective-permute-done | bytes 1572896 | tf_op jit(solution)/shard_map/ppermute | solution.py:78
  48.0 1.1 %copy-done.6 = bf16[3,2048,128]{2,1,0:T(8,128)(2,1)} copy-done((bf16[3,2048,128]{2,1,0:T(8,128)(2,1)}, bf16[3,2048,128]{2,1,0:T(8,128)(2,1)S(1)}, u32[]{:S(2)}) %copy-start.6) | copy-done | bytes 1572888
  49.3 13.7 %shard_map.59 = (bf16[6,2048,128]{2,1,0:T(8,128)(2,1)}, bf16[6,2048,128]{2,1,0:T(8,128)(2,1)}) custom-call(s32[6]{0:T(128)} %fusion.source_ref, s32[6]{0:T(128)} %compare_convert_fusion.living_ref, bf16[3,2048,128]{2,1,0:T(8,128)(2,1)} %refs_0_.1, bf16[3,2048,128]{2,1,0:T(8,128)(2,1)} %copy-done.5, bf16[3,2048,128]{2,1,0:T(8,128)(2,1)} %copy-done.4, ...), custom_call_target="tpu_custom_call" | custom-call | tf_op jit(solution)/shard_map/pallas_call | solution.py:167
  63.7 1.5 %collective-permute-done.14.refs_13_ = bf16[1,128,2048]{2,1,0:T(8,128)(2,1)S(1)} collective-permute-done((bf16[1,128,2048]{2,1,0:T(8,128)(2,1)}, bf16[1,128,2048]{2,1,0:T(8,128)(2,1)S(1)}, u32[]{:S(2)}, u32[]{:S(2)}) %collective-permute-start.14) | collective-permute-done | bytes 524320 | tf_op jit(solution)/shard_map/ppermute | solution.py:78
  65.2 0.7 collective-permute-done.15.refs_14_
  66.0 0.7 collective-permute-done.16.refs_15_
  66.7 1.9 %copy-done = bf16[6,2048,128]{2,1,0:T(8,128)(2,1)S(1)} copy-done((bf16[6,2048,128]{2,1,0:T(8,128)(2,1)S(1)}, bf16[6,2048,128]{2,1,0:T(8,128)(2,1)}, u32[]{:S(2)}) %copy-start) | copy-done | bytes 3145752
  68.6 1.0 %copy-done.3 = bf16[1,128,2048]{2,1,0:T(8,128)(2,1)S(1)} copy-done((bf16[1,128,2048]{2,1,0:T(8,128)(2,1)S(1)}, bf16[1,128,2048]{2,1,0:T(8,128)(2,1)}, u32[]{:S(2)}) %copy-start.3) | copy-done | bytes 524312
  69.6 16.1 %shard_map.60 = f32[6,128]{1,0:T(8,128)S(1)} custom-call(bf16[6,2048,128]{2,1,0:T(8,128)(2,1)S(1)} %copy-done, bf16[2,128,2048]{2,1,0:T(8,128)(2,1)S(1)} %copy-done.1, bf16[1,128,2048]{2,1,0:T(8,128)(2,1)S(1)} %collective-permute-done.refs_2_, bf16[1,128,2048]{2,1,0:T(8,128)(2,1)S(1)} %collective-permute-done.1.refs_3_, ...), custom_call_target="tpu_custom_call" | custom-call | tf_op jit(solution)/shard_map/pallas_call | solution.py:62
  (34 shorter events, 3.1 us)
Async XLA Ops:
  1.7 14.9 %collective-permute-start = (bf16[1,128,2048]{2,1,0:T(8,128)(2,1)S(1)}, bf16[1,128,2048]{2,1,0:T(8,128)(2,1)S(1)}, u32[]{:S(2)}, u32[]{:S(2)}) collective-permute-start(bf16[1,128,2048]{2,1,0:T(8,128)(2,1)S(1)} %constant_dynamic-slice_fusion), channel_id=1, source_target_pairs={{0,2},{2,4},{4,6},{6,7},{7,5},{5,3},{3,1},{1,0},{8,10},{10,12},{12... | collective-permute-start | bytes 1572872 | tf_op jit(solution)/shard_map/ppermute | solution.py:200
  4.8 13.4 %collective-permute-start.1 = (bf16[1,128,2048]{2,1,0:T(8,128)(2,1)S(1)}, bf16[1,128,2048]{2,1,0:T(8,128)(2,1)S(1)}, u32[]{:S(2)}, u32[]{:S(2)}) collective-permute-start(bf16[1,128,2048]{2,1,0:T(8,128)(2,1)S(1)} %constant_dynamic-slice_fusion), channel_id=1, source_target_pairs={{2,0},{4,2},{6,4},{7,6},{5,7},{3,5},{1,3},{0,1},{10,8},{12,10},{14... | collective-permute-start | bytes 1572872 | tf_op jit(solution)/shard_map/ppermute | solution.py:203
  4.8 39.7 %collective-permute-start.6 = (bf16[3,2048,128]{2,1,0:T(8,128)(2,1)}, bf16[3,2048,128]{2,1,0:T(8,128)(2,1)S(1)}, u32[]{:S(2)}, u32[]{:S(2)}) collective-permute-start(bf16[3,2048,128]{2,1,0:T(8,128)(2,1)} %refs_0_.1), channel_id=1, source_target_pairs={{0,16},{8,24},{16,0},{24,8},{1,17},{9,25},{17,1},{25,9},{2,18},{10... | collective-permute-start | bytes 4718600 | tf_op jit(solution)/shard_map/ppermute | solution.py:78
  6.8 37.8 %collective-permute-start.7 = (bf16[3,2048,128]{2,1,0:T(8,128)(2,1)}, bf16[3,2048,128]{2,1,0:T(8,128)(2,1)S(1)}, u32[]{:S(2)}, u32[]{:S(2)}) collective-permute-start(bf16[3,2048,128]{2,1,0:T(8,128)(2,1)} %refs_0_.1), channel_id=1, source_target_pairs={{0,8},{8,0},{16,24},{24,16},{1,9},{9,1},{17,25},{25,17},{2,10},{10... | collective-permute-start | bytes 4718600 | tf_op jit(solution)/shard_map/ppermute | solution.py:78
  10.5 56.2 %copy-start.1 = (bf16[2,128,2048]{2,1,0:T(8,128)(2,1)S(1)}, bf16[2,128,2048]{2,1,0:T(8,128)(2,1)}, u32[]{:S(2)}) copy-start(bf16[2,128,2048]{2,1,0:T(8,128)(2,1)} %refs_1_.1) | copy-start | bytes 3145732
  18.2 12.5 %collective-permute-start.2 = (bf16[1,128,2048]{2,1,0:T(8,128)(2,1)S(1)}, bf16[1,128,2048]{2,1,0:T(8,128)(2,1)S(1)}, u32[]{:S(2)}, u32[]{:S(2)}) collective-permute-start(bf16[1,128,2048]{2,1,0:T(8,128)(2,1)S(1)} %collective-permute-done.refs_2_), channel_id=1, source_target_pairs={{0,2},{2,4},{4,6},{6,7},{7,5},{5,3},{3,1},{1,0},{8,10},{10,12},{12... | collective-permute-start | bytes 1572872 | tf_op jit(solution)/shard_map/ppermute | solution.py:200
  19.8 12.2 %collective-permute-start.3 = (bf16[1,128,2048]{2,1,0:T(8,128)(2,1)S(1)}, bf16[1,128,2048]{2,1,0:T(8,128)(2,1)S(1)}, u32[]{:S(2)}, u32[]{:S(2)}) collective-permute-start(bf16[1,128,2048]{2,1,0:T(8,128)(2,1)S(1)} %collective-permute-done.1.refs_3_), channel_id=1, source_target_pairs={{2,0},{4,2},{6,4},{7,6},{5,7},{3,5},{1,3},{0,1},{10,8},{12,10},{14... | collective-permute-start | bytes 1572872 | tf_op jit(solution)/shard_map/ppermute | solution.py:203
  32.0 11.4 %collective-permute-start.4 = (bf16[1,128,2048]{2,1,0:T(8,128)(2,1)S(1)}, bf16[1,128,2048]{2,1,0:T(8,128)(2,1)}, u32[]{:S(2)}, u32[]{:S(2)}) collective-permute-start(bf16[1,128,2048]{2,1,0:T(8,128)(2,1)S(1)} %collective-permute-done.2.refs_4_), channel_id=1, source_target_pairs={{0,2},{2,4},{4,6},{6,7},{7,5},{5,3},{3,1},{1,0},{8,10},{10,12},{12... | collective-permute-start | bytes 1572872 | tf_op jit(solution)/shard_map/ppermute | solution.py:200
  33.5 11.0 %collective-permute-start.5 = (bf16[1,128,2048]{2,1,0:T(8,128)(2,1)S(1)}, bf16[1,128,2048]{2,1,0:T(8,128)(2,1)S(1)}, u32[]{:S(2)}, u32[]{:S(2)}) collective-permute-start(bf16[1,128,2048]{2,1,0:T(8,128)(2,1)S(1)} %collective-permute-done.3.refs_5_), channel_id=1, source_target_pairs={{2,0},{4,2},{6,4},{7,6},{5,7},{3,5},{1,3},{0,1},{10,8},{12,10},{14... | collective-permute-start | bytes 1572872 | tf_op jit(solution)/shard_map/ppermute | solution.py:203
  44.5 2.4 %copy-start.2 = (bf16[1,128,2048]{2,1,0:T(8,128)(2,1)}, bf16[1,128,2048]{2,1,0:T(8,128)(2,1)S(1)}, u32[]{:S(2)}) copy-start(bf16[1,128,2048]{2,1,0:T(8,128)(2,1)S(1)} %collective-permute-done.5.refs_7_) | copy-start | bytes 1572868
  44.5 3.5 %copy-start.4 = (bf16[3,2048,128]{2,1,0:T(8,128)(2,1)}, bf16[3,2048,128]{2,1,0:T(8,128)(2,1)S(1)}, u32[]{:S(2)}) copy-start(bf16[3,2048,128]{2,1,0:T(8,128)(2,1)S(1)} %collective-permute-done.6.refs_2_) | copy-start | bytes 4718596
  44.6 3.5 %copy-start.5 = (bf16[3,2048,128]{2,1,0:T(8,128)(2,1)}, bf16[3,2048,128]{2,1,0:T(8,128)(2,1)S(1)}, u32[]{:S(2)}) copy-start(bf16[3,2048,128]{2,1,0:T(8,128)(2,1)S(1)} %collective-permute-done.7.refs_1_) | copy-start | bytes 4718596
  44.6 3.5 %collective-permute-start.9 = (bf16[3,2048,128]{2,1,0:T(8,128)(2,1)S(1)}, bf16[3,2048,128]{2,1,0:T(8,128)(2,1)S(1)}, u32[]{:S(2)}, u32[]{:S(2)}) collective-permute-start(bf16[3,2048,128]{2,1,0:T(8,128)(2,1)S(1)} %collective-permute-done.6.refs_2_), channel_id=1, source_target_pairs={{0,8},{8,0},{16,24},{24,16},{1,9},{9,1},{17,25},{25,17},{2,10},{10... | collective-permute-start | bytes 4718600 | tf_op jit(solution)/shard_map/ppermute | solution.py:78
  44.6 18.4 %collective-permute-start.8 = (bf16[1,128,2048]{2,1,0:T(8,128)(2,1)}, bf16[1,128,2048]{2,1,0:T(8,128)(2,1)}, u32[]{:S(2)}, u32[]{:S(2)}) collective-permute-start(bf16[1,128,2048]{2,1,0:T(8,128)(2,1)} %collective-permute-done.4.refs_6_), channel_id=1, source_target_pairs={{0,2},{2,4},{4,6},{6,7},{7,5},{5,3},{3,1},{1,0},{8,10},{10,12},{12... | collective-permute-start | bytes 1572872 | tf_op jit(solution)/shard_map/ppermute | solution.py:200
  46.2 17.0 %collective-permute-start.10 = (bf16[1,128,2048]{2,1,0:T(8,128)(2,1)S(1)}, bf16[1,128,2048]{2,1,0:T(8,128)(2,1)}, u32[]{:S(2)}, u32[]{:S(2)}) collective-permute-start(bf16[1,128,2048]{2,1,0:T(8,128)(2,1)S(1)} %collective-permute-done.refs_2_), channel_id=1, source_target_pairs={{0,8},{8,0},{16,24},{24,16},{1,9},{9,1},{17,25},{25,17},{2,10},{10... | collective-permute-start | bytes 1572872 | tf_op jit(solution)/shard_map/ppermute | solution.py:78
  46.4 17.2 %collective-permute-start.11 = (bf16[1,128,2048]{2,1,0:T(8,128)(2,1)S(1)}, bf16[1,128,2048]{2,1,0:T(8,128)(2,1)}, u32[]{:S(2)}, u32[]{:S(2)}) collective-permute-start(bf16[1,128,2048]{2,1,0:T(8,128)(2,1)S(1)} %collective-permute-done.1.refs_3_), channel_id=1, source_target_pairs={{0,8},{8,0},{16,24},{24,16},{1,9},{9,1},{17,25},{25,17},{2,10},{10... | collective-permute-start | bytes 1572872 | tf_op jit(solution)/shard_map/ppermute | solution.py:78
  46.7 17.0 %collective-permute-start.12 = (bf16[1,128,2048]{2,1,0:T(8,128)(2,1)S(1)}, bf16[1,128,2048]{2,1,0:T(8,128)(2,1)}, u32[]{:S(2)}, u32[]{:S(2)}) collective-permute-start(bf16[1,128,2048]{2,1,0:T(8,128)(2,1)S(1)} %collective-permute-done.2.refs_4_), channel_id=1, source_target_pairs={{0,8},{8,0},{16,24},{24,16},{1,9},{9,1},{17,25},{25,17},{2,10},{10... | collective-permute-start | bytes 1572872 | tf_op jit(solution)/shard_map/ppermute | solution.py:78
  48.0 1.1 %copy-start.6 = (bf16[3,2048,128]{2,1,0:T(8,128)(2,1)}, bf16[3,2048,128]{2,1,0:T(8,128)(2,1)S(1)}, u32[]{:S(2)}) copy-start(bf16[3,2048,128]{2,1,0:T(8,128)(2,1)S(1)} %collective-permute-done.9.refs_3_) | copy-start | bytes 4718596
  49.2 14.5 %collective-permute-start.13 = (bf16[1,128,2048]{2,1,0:T(8,128)(2,1)S(1)}, bf16[1,128,2048]{2,1,0:T(8,128)(2,1)}, u32[]{:S(2)}, u32[]{:S(2)}) collective-permute-start(bf16[1,128,2048]{2,1,0:T(8,128)(2,1)S(1)} %collective-permute-done.3.refs_5_), channel_id=1, source_target_pairs={{0,8},{8,0},{16,24},{24,16},{1,9},{9,1},{17,25},{25,17},{2,10},{10... | collective-permute-start | bytes 1572872 | tf_op jit(solution)/shard_map/ppermute | solution.py:78
  63.0 2.2 %collective-permute-start.14 = (bf16[1,128,2048]{2,1,0:T(8,128)(2,1)}, bf16[1,128,2048]{2,1,0:T(8,128)(2,1)S(1)}, u32[]{:S(2)}, u32[]{:S(2)}) collective-permute-start(bf16[1,128,2048]{2,1,0:T(8,128)(2,1)} %collective-permute-done.4.refs_6_), channel_id=1, source_target_pairs={{0,8},{8,0},{16,24},{24,16},{1,9},{9,1},{17,25},{25,17},{2,10},{10... | collective-permute-start | bytes 1572872 | tf_op jit(solution)/shard_map/ppermute | solution.py:78
  63.2 22.7 %copy-start.7 = (s32[6]{0:T(128)S(1)}, s32[6]{0:T(128)}, u32[]{:S(2)}) copy-start(s32[6]{0:T(128)} %param.8) | copy-start | bytes 76
  63.2 2.8 %collective-permute-start.15 = (bf16[1,128,2048]{2,1,0:T(8,128)(2,1)}, bf16[1,128,2048]{2,1,0:T(8,128)(2,1)S(1)}, u32[]{:S(2)}, u32[]{:S(2)}) collective-permute-start(bf16[1,128,2048]{2,1,0:T(8,128)(2,1)} %copy-done.2), channel_id=1, source_target_pairs={{0,8},{8,0},{16,24},{24,16},{1,9},{9,1},{17,25},{25,17},{2,10},{10... | collective-permute-start | bytes 1572872 | tf_op jit(solution)/shard_map/ppermute | solution.py:78
  63.6 3.1 %collective-permute-start.16 = (bf16[1,128,2048]{2,1,0:T(8,128)(2,1)}, bf16[1,128,2048]{2,1,0:T(8,128)(2,1)S(1)}, u32[]{:S(2)}, u32[]{:S(2)}) collective-permute-start(bf16[1,128,2048]{2,1,0:T(8,128)(2,1)} %collective-permute-done.8.refs_8_), channel_id=1, source_target_pairs={{0,8},{8,0},{16,24},{24,16},{1,9},{9,1},{17,25},{25,17},{2,10},{10... | collective-permute-start | bytes 1572872 | tf_op jit(solution)/shard_map/ppermute | solution.py:78
  66.7 1.9 %copy-start = (bf16[6,2048,128]{2,1,0:T(8,128)(2,1)S(1)}, bf16[6,2048,128]{2,1,0:T(8,128)(2,1)}, u32[]{:S(2)}) copy-start(bf16[6,2048,128]{2,1,0:T(8,128)(2,1)} %get-tuple-element.43.refs_0_) | copy-start | bytes 9437188
  (1 other events, 1.0 us)

commit v14 on v13

--- a/solution.py
+++ b/solution.py
@@ -230,7 +230,9 @@
         new_walkers, theta = kick(old_walkers, beside, across, diagonal_peer, *operands)
 
     living = parent >= 0
-    energy = block_energy(theta, [half_chol] + pieces + handed)
+    late = 1 if n_forward > n_backward else 2
+    energy = block_energy(theta, [half_chol] + pieces[:-late] + handed[:-late])
+    energy = energy + block_energy(theta, pieces[-late:] + handed[-late:])
     energy = jnp.where(living, energy, 0.0)
     return (new_walkers, energy)
 

time: 86.7 us -> 87.1 us (level)
  Pallas kernels: 29.8 us -> 30.8 us
  waiting for transfers between devices: 34.1 us -> 33.1 us
    pallas_call x1 -> x2, Pallas kernels: 16.1 us -> 17.3 us  [block_energy(): pl.pallas_call(energy_kernel, out_shape=jax.ShapeDtypeStruct((n_slot, 128...]
    ppermute x10, waiting for transfers between devices: 4.15 us -> 3.14 us  [swap_pairs(): return lax.ppermute(x, axis, perm)]
  transfers between devices with their start and end apart: 17 -> 17, of which waited for: 10 -> 9; matrix products, arithmetic and copies ran while one was open for 4% -> 4% of each run, Pallas kernels for 16% -> 32%
where the time goes in v14:
time: 87.1 us; the launch traced here: 86.6 us
  waiting for transfers between devices  33.1 us (38%)
  Pallas kernels  30.8 us (35%)
  starting transfers between devices  12.5 us (14%)
  local copies, waits for them, and re-layouts  6.65 us (8%)
  other arithmetic  2.95 us (3%)
    ppermute x4, waiting for transfers between devices, body(): ahead = lax.ppermute(ahead, 'chol', forward)  25.9 us
    pallas_call x2, Pallas kernels, block_energy(): pl.pallas_call(energy_kernel, out_shape=jax.ShapeDtypeStruct((n_slot, 128...  17.3 us
    pallas_call x1, Pallas kernels, kick(): pl.pallas_call(kick_kernel, out_shape=[shape, shape], grid_spec=grid_spec)  13.4 us
    ppermute x4, starting transfers between devices, body(): ahead = lax.ppermute(ahead, 'chol', forward)  7.8 us
    unnamed x16, local copies, waits for them, and re-layouts  4.1 us
    ppermute x3, waiting for transfers between devices, body(): behind = lax.ppermute(behind, 'chol', backward)  4 us
    ppermute x10, starting transfers between devices, swap_pairs(): return lax.ppermute(x, axis, perm)  3.77 us
    ppermute x10, waiting for transfers between devices, swap_pairs(): return lax.ppermute(x, axis, perm)  3.14 us
  transfers between devices with their start and end apart: 17, of which 9 were waited for; matrix products, arithmetic and copies ran while one was open for 4% of the time, Pallas kernels for 32%

profile of v14, /device:TPU:0, one launch (start us, length us, event | category | flops | bytes accessed | tf_op | source)
XLA Modules:
  0.0 86.6 jit_solution(11029014706438103980)
XLA Ops:
  0.6 1.1 %constant_dynamic-slice_fusion = bf16[1,128,2048]{2,1,0:T(8,128)(2,1)S(1)} fusion(bf16[2,128,2048]{2,1,0:T(8,128)(2,1)} %refs_1_.1, s32[]{:T(128)S(6)} %select_n.26), kind=kLoop, calls=%fused_computation.6 | loop fusion | bytes 1048580 | tf_op jit(solution)/shard_map/dynamic_slice | solution.py:185
  1.7 3.1 %collective-permute-start = (bf16[1,128,2048]{2,1,0:T(8,128)(2,1)S(1)}, bf16[1,128,2048]{2,1,0:T(8,128)(2,1)S(1)}, u32[]{:S(2)}, u32[]{:S(2)}) collective-permute-start(bf16[1,128,2048]{2,1,0:T(8,128)(2,1)S(1)} %constant_dynamic-slice_fusion), channel_id=1, source_target_pairs={{0,2},{2,4},{4,6},{6,7},{7,5},{5,3},{3,1},{1,0},{8,10},{10,12},{12... | collective-permute-start | bytes 1572872 | tf_op jit(solution)/shard_map/ppermute | solution.py:200
  4.8 1.9 %collective-permute-start.6 = (bf16[3,2048,128]{2,1,0:T(8,128)(2,1)}, bf16[3,2048,128]{2,1,0:T(8,128)(2,1)S(1)}, u32[]{:S(2)}, u32[]{:S(2)}) collective-permute-start(bf16[3,2048,128]{2,1,0:T(8,128)(2,1)} %refs_0_.1), channel_id=1, source_target_pairs={{0,16},{8,24},{16,0},{24,8},{1,17},{9,25},{17,1},{25,9},{2,18},{10... | collective-permute-start | bytes 4718600 | tf_op jit(solution)/shard_map/ppermute | solution.py:78
  6.8 1.5 %scatter.4.refs_4_ = f32[8,2048]{1,0:T(8,128)} pad(f32[6,2048]{1,0:T(8,128)} %param.9, f32[]{:T(128)} %constant.67.clone.1), padding=0_2x0_0 | pad | bytes 114692 | tf_op jit(solution)/shard_map/scatter | solution.py:143
  8.2 1.2 %fusion.source_ref = s32[6]{0:T(128)} fusion(s32[6]{0:T(128)} %param.8, s32[]{:T(128)S(6)} %axis_index.15), kind=kLoop, calls=%fused_computation.5 | loop fusion | flops 96 | bytes 52 | tf_op jit(solution)/shard_map/add | solution.py:141
  9.4 1.1 %compare_convert_fusion.living_ref = s32[6]{0:T(128)} fusion(s32[6]{0:T(128)} %param.8), kind=kLoop, calls=%fused_computation.4 | loop fusion | flops 12 | bytes 48 | tf_op jit(solution)/shard_map/convert_element_type | solution.py:138
  10.5 6.1 %collective-permute-done.refs_2_ = bf16[1,128,2048]{2,1,0:T(8,128)(2,1)S(1)} collective-permute-done((bf16[1,128,2048]{2,1,0:T(8,128)(2,1)S(1)}, bf16[1,128,2048]{2,1,0:T(8,128)(2,1)S(1)}, u32[]{:S(2)}, u32[]{:S(2)}) %collective-permute-start) | collective-permute-done | bytes 524320 | tf_op jit(solution)/shard_map/ppermute | solution.py:200
  16.7 1.5 %collective-permute-done.1.refs_3_ = bf16[1,128,2048]{2,1,0:T(8,128)(2,1)S(1)} collective-permute-done((bf16[1,128,2048]{2,1,0:T(8,128)(2,1)S(1)}, bf16[1,128,2048]{2,1,0:T(8,128)(2,1)S(1)}, u32[]{:S(2)}, u32[]{:S(2)}) %collective-permute-start.1) | collective-permute-done | bytes 524320 | tf_op jit(solution)/shard_map/ppermute | solution.py:203
  18.2 1.6 %collective-permute-start.2 = (bf16[1,128,2048]{2,1,0:T(8,128)(2,1)S(1)}, bf16[1,128,2048]{2,1,0:T(8,128)(2,1)S(1)}, u32[]{:S(2)}, u32[]{:S(2)}) collective-permute-start(bf16[1,128,2048]{2,1,0:T(8,128)(2,1)S(1)} %collective-permute-done.refs_2_), channel_id=1, source_target_pairs={{0,2},{2,4},{4,6},{6,7},{7,5},{5,3},{3,1},{1,0},{8,10},{10,12},{12... | collective-permute-start | bytes 1572872 | tf_op jit(solution)/shard_map/ppermute | solution.py:200
  20.2 10.4 %collective-permute-done.2.refs_4_ = bf16[1,128,2048]{2,1,0:T(8,128)(2,1)S(1)} collective-permute-done((bf16[1,128,2048]{2,1,0:T(8,128)(2,1)S(1)}, bf16[1,128,2048]{2,1,0:T(8,128)(2,1)S(1)}, u32[]{:S(2)}, u32[]{:S(2)}) %collective-permute-start.2) | collective-permute-done | bytes 524320 | tf_op jit(solution)/shard_map/ppermute | solution.py:200
  30.7 1.3 %collective-permute-done.3.refs_5_ = bf16[1,128,2048]{2,1,0:T(8,128)(2,1)S(1)} collective-permute-done((bf16[1,128,2048]{2,1,0:T(8,128)(2,1)S(1)}, bf16[1,128,2048]{2,1,0:T(8,128)(2,1)S(1)}, u32[]{:S(2)}, u32[]{:S(2)}) %collective-permute-start.3) | collective-permute-done | bytes 524320 | tf_op jit(solution)/shard_map/ppermute | solution.py:203
  32.0 1.6 %collective-permute-start.4 = (bf16[1,128,2048]{2,1,0:T(8,128)(2,1)S(1)}, bf16[1,128,2048]{2,1,0:T(8,128)(2,1)}, u32[]{:S(2)}, u32[]{:S(2)}) collective-permute-start(bf16[1,128,2048]{2,1,0:T(8,128)(2,1)S(1)} %collective-permute-done.2.refs_4_), channel_id=1, source_target_pairs={{0,2},{2,4},{4,6},{6,7},{7,5},{5,3},{3,1},{1,0},{8,10},{10,12},{12... | collective-permute-start | bytes 1572872 | tf_op jit(solution)/shard_map/ppermute | solution.py:200
  34.0 9.4 %collective-permute-done.4.refs_6_ = bf16[1,128,2048]{2,1,0:T(8,128)(2,1)} collective-permute-done((bf16[1,128,2048]{2,1,0:T(8,128)(2,1)S(1)}, bf16[1,128,2048]{2,1,0:T(8,128)(2,1)}, u32[]{:S(2)}, u32[]{:S(2)}) %collective-permute-start.4) | collective-permute-done | bytes 524320 | tf_op jit(solution)/shard_map/ppermute | solution.py:200
  43.3 1.2 %collective-permute-done.5.refs_7_ = bf16[1,128,2048]{2,1,0:T(8,128)(2,1)S(1)} collective-permute-done((bf16[1,128,2048]{2,1,0:T(8,128)(2,1)S(1)}, bf16[1,128,2048]{2,1,0:T(8,128)(2,1)S(1)}, u32[]{:S(2)}, u32[]{:S(2)}) %collective-permute-start.5) | collective-permute-done | bytes 524320 | tf_op jit(solution)/shard_map/ppermute | solution.py:203
  44.6 1.6 %collective-permute-start.8 = (bf16[1,128,2048]{2,1,0:T(8,128)(2,1)}, bf16[1,128,2048]{2,1,0:T(8,128)(2,1)}, u32[]{:S(2)}, u32[]{:S(2)}) collective-permute-start(bf16[1,128,2048]{2,1,0:T(8,128)(2,1)} %collective-permute-done.4.refs_6_), channel_id=1, source_target_pairs={{0,2},{2,4},{4,6},{6,7},{7,5},{5,3},{3,1},{1,0},{8,10},{10,12},{12... | collective-permute-start | bytes 1572872 | tf_op jit(solution)/shard_map/ppermute | solution.py:200
  46.9 1.1 %collective-permute-done.9.refs_3_ = bf16[3,2048,128]{2,1,0:T(8,128)(2,1)S(1)} collective-permute-done((bf16[3,2048,128]{2,1,0:T(8,128)(2,1)S(1)}, bf16[3,2048,128]{2,1,0:T(8,128)(2,1)S(1)}, u32[]{:S(2)}, u32[]{:S(2)}) %collective-permute-start.9) | collective-permute-done | bytes 1572896 | tf_op jit(solution)/shard_map/ppermute | solution.py:78
  48.0 1.1 %copy-done.6 = bf16[3,2048,128]{2,1,0:T(8,128)(2,1)} copy-done((bf16[3,2048,128]{2,1,0:T(8,128)(2,1)}, bf16[3,2048,128]{2,1,0:T(8,128)(2,1)S(1)}, u32[]{:S(2)}) %copy-start.6) | copy-done | bytes 1572888
  49.3 13.4 %shard_map.59 = (bf16[6,2048,128]{2,1,0:T(8,128)(2,1)}, bf16[6,2048,128]{2,1,0:T(8,128)(2,1)}) custom-call(s32[6]{0:T(128)} %fusion.source_ref, s32[6]{0:T(128)} %compare_convert_fusion.living_ref, bf16[3,2048,128]{2,1,0:T(8,128)(2,1)} %refs_0_.1, bf16[3,2048,128]{2,1,0:T(8,128)(2,1)} %copy-done.5, bf16[3,2048,128]{2,1,0:T(8,128)(2,1)} %copy-done.4, ...), custom_call_target="tpu_custom_call" | custom-call | tf_op jit(solution)/shard_map/pallas_call | solution.py:167
  63.7 1.2 %collective-permute-done.14.refs_12_ = bf16[1,128,2048]{2,1,0:T(8,128)(2,1)S(1)} collective-permute-done((bf16[1,128,2048]{2,1,0:T(8,128)(2,1)}, bf16[1,128,2048]{2,1,0:T(8,128)(2,1)S(1)}, u32[]{:S(2)}, u32[]{:S(2)}) %collective-permute-start.14) | collective-permute-done | bytes 524320 | tf_op jit(solution)/shard_map/ppermute | solution.py:78
  64.9 0.7 collective-permute-done.15.refs_13_
  65.7 1.9 %copy-done = bf16[6,2048,128]{2,1,0:T(8,128)(2,1)S(1)} copy-done((bf16[6,2048,128]{2,1,0:T(8,128)(2,1)S(1)}, bf16[6,2048,128]{2,1,0:T(8,128)(2,1)}, u32[]{:S(2)}) %copy-start) | copy-done | bytes 3145752
  67.6 1.0 %copy-done.3 = bf16[1,128,2048]{2,1,0:T(8,128)(2,1)S(1)} copy-done((bf16[1,128,2048]{2,1,0:T(8,128)(2,1)S(1)}, bf16[1,128,2048]{2,1,0:T(8,128)(2,1)}, u32[]{:S(2)}) %copy-start.3) | copy-done | bytes 524312
  68.6 14.3 %shard_map.60 = f32[6,128]{1,0:T(8,128)S(1)} custom-call(bf16[6,2048,128]{2,1,0:T(8,128)(2,1)S(1)} %copy-done, bf16[2,128,2048]{2,1,0:T(8,128)(2,1)S(1)} %copy-done.1, bf16[1,128,2048]{2,1,0:T(8,128)(2,1)S(1)} %collective-permute-done.refs_2_, bf16[1,128,2048]{2,1,0:T(8,128)(2,1)S(1)} %collective-permute-done.1.refs_3_, ...), custom_call_target="tpu_custom_call" | custom-call | tf_op jit(solution)/shard_map/pallas_call | solution.py:62
  83.0 3.0 %shard_map.61 = f32[6,128]{1,0:T(8,128)S(1)} custom-call(bf16[6,2048,128]{2,1,0:T(8,128)(2,1)S(1)} %copy-done, bf16[1,128,2048]{2,1,0:T(8,128)(2,1)} %collective-permute-done.8.refs_1_, bf16[1,128,2048]{2,1,0:T(8,128)(2,1)S(1)} %collective-permute-done.16.refs_2_), custom_call_target="tpu_custom_call" | custom-call | tf_op jit(solution)/shard_map/pallas_call | solution.py:62
  (35 shorter events, 3.4 us)
Async XLA Ops:
  1.7 14.9 %collective-permute-start = (bf16[1,128,2048]{2,1,0:T(8,128)(2,1)S(1)}, bf16[1,128,2048]{2,1,0:T(8,128)(2,1)S(1)}, u32[]{:S(2)}, u32[]{:S(2)}) collective-permute-start(bf16[1,128,2048]{2,1,0:T(8,128)(2,1)S(1)} %constant_dynamic-slice_fusion), channel_id=1, source_target_pairs={{0,2},{2,4},{4,6},{6,7},{7,5},{5,3},{3,1},{1,0},{8,10},{10,12},{12... | collective-permute-start | bytes 1572872 | tf_op jit(solution)/shard_map/ppermute | solution.py:200
  4.8 13.4 %collective-permute-start.1 = (bf16[1,128,2048]{2,1,0:T(8,128)(2,1)S(1)}, bf16[1,128,2048]{2,1,0:T(8,128)(2,1)S(1)}, u32[]{:S(2)}, u32[]{:S(2)}) collective-permute-start(bf16[1,128,2048]{2,1,0:T(8,128)(2,1)S(1)} %constant_dynamic-slice_fusion), channel_id=1, source_target_pairs={{2,0},{4,2},{6,4},{7,6},{5,7},{3,5},{1,3},{0,1},{10,8},{12,10},{14... | collective-permute-start | bytes 1572872 | tf_op jit(solution)/shard_map/ppermute | solution.py:203
  4.8 39.7 %collective-permute-start.6 = (bf16[3,2048,128]{2,1,0:T(8,128)(2,1)}, bf16[3,2048,128]{2,1,0:T(8,128)(2,1)S(1)}, u32[]{:S(2)}, u32[]{:S(2)}) collective-permute-start(bf16[3,2048,128]{2,1,0:T(8,128)(2,1)} %refs_0_.1), channel_id=1, source_target_pairs={{0,16},{8,24},{16,0},{24,8},{1,17},{9,25},{17,1},{25,9},{2,18},{10... | collective-permute-start | bytes 4718600 | tf_op jit(solution)/shard_map/ppermute | solution.py:78
  6.8 37.8 %collective-permute-start.7 = (bf16[3,2048,128]{2,1,0:T(8,128)(2,1)}, bf16[3,2048,128]{2,1,0:T(8,128)(2,1)S(1)}, u32[]{:S(2)}, u32[]{:S(2)}) collective-permute-start(bf16[3,2048,128]{2,1,0:T(8,128)(2,1)} %refs_0_.1), channel_id=1, source_target_pairs={{0,8},{8,0},{16,24},{24,16},{1,9},{9,1},{17,25},{25,17},{2,10},{10... | collective-permute-start | bytes 4718600 | tf_op jit(solution)/shard_map/ppermute | solution.py:78
  10.5 55.1 %copy-start.1 = (bf16[2,128,2048]{2,1,0:T(8,128)(2,1)S(1)}, bf16[2,128,2048]{2,1,0:T(8,128)(2,1)}, u32[]{:S(2)}) copy-start(bf16[2,128,2048]{2,1,0:T(8,128)(2,1)} %refs_1_.1) | copy-start | bytes 3145732
  18.2 12.5 %collective-permute-start.2 = (bf16[1,128,2048]{2,1,0:T(8,128)(2,1)S(1)}, bf16[1,128,2048]{2,1,0:T(8,128)(2,1)S(1)}, u32[]{:S(2)}, u32[]{:S(2)}) collective-permute-start(bf16[1,128,2048]{2,1,0:T(8,128)(2,1)S(1)} %collective-permute-done.refs_2_), channel_id=1, source_target_pairs={{0,2},{2,4},{4,6},{6,7},{7,5},{5,3},{3,1},{1,0},{8,10},{10,12},{12... | collective-permute-start | bytes 1572872 | tf_op jit(solution)/shard_map/ppermute | solution.py:200
  19.8 12.2 %collective-permute-start.3 = (bf16[1,128,2048]{2,1,0:T(8,128)(2,1)S(1)}, bf16[1,128,2048]{2,1,0:T(8,128)(2,1)S(1)}, u32[]{:S(2)}, u32[]{:S(2)}) collective-permute-start(bf16[1,128,2048]{2,1,0:T(8,128)(2,1)S(1)} %collective-permute-done.1.refs_3_), channel_id=1, source_target_pairs={{2,0},{4,2},{6,4},{7,6},{5,7},{3,5},{1,3},{0,1},{10,8},{12,10},{14... | collective-permute-start | bytes 1572872 | tf_op jit(solution)/shard_map/ppermute | solution.py:203
  32.0 11.4 %collective-permute-start.4 = (bf16[1,128,2048]{2,1,0:T(8,128)(2,1)S(1)}, bf16[1,128,2048]{2,1,0:T(8,128)(2,1)}, u32[]{:S(2)}, u32[]{:S(2)}) collective-permute-start(bf16[1,128,2048]{2,1,0:T(8,128)(2,1)S(1)} %collective-permute-done.2.refs_4_), channel_id=1, source_target_pairs={{0,2},{2,4},{4,6},{6,7},{7,5},{5,3},{3,1},{1,0},{8,10},{10,12},{12... | collective-permute-start | bytes 1572872 | tf_op jit(solution)/shard_map/ppermute | solution.py:200
  33.5 11.0 %collective-permute-start.5 = (bf16[1,128,2048]{2,1,0:T(8,128)(2,1)S(1)}, bf16[1,128,2048]{2,1,0:T(8,128)(2,1)S(1)}, u32[]{:S(2)}, u32[]{:S(2)}) collective-permute-start(bf16[1,128,2048]{2,1,0:T(8,128)(2,1)S(1)} %collective-permute-done.3.refs_5_), channel_id=1, source_target_pairs={{2,0},{4,2},{6,4},{7,6},{5,7},{3,5},{1,3},{0,1},{10,8},{12,10},{14... | collective-permute-start | bytes 1572872 | tf_op jit(solution)/shard_map/ppermute | solution.py:203
  44.5 2.4 %copy-start.2 = (bf16[1,128,2048]{2,1,0:T(8,128)(2,1)}, bf16[1,128,2048]{2,1,0:T(8,128)(2,1)S(1)}, u32[]{:S(2)}) copy-start(bf16[1,128,2048]{2,1,0:T(8,128)(2,1)S(1)} %collective-permute-done.5.refs_7_) | copy-start | bytes 1572868
  44.5 3.5 %copy-start.4 = (bf16[3,2048,128]{2,1,0:T(8,128)(2,1)}, bf16[3,2048,128]{2,1,0:T(8,128)(2,1)S(1)}, u32[]{:S(2)}) copy-start(bf16[3,2048,128]{2,1,0:T(8,128)(2,1)S(1)} %collective-permute-done.6.refs_2_) | copy-start | bytes 4718596
  44.6 3.5 %copy-start.5 = (bf16[3,2048,128]{2,1,0:T(8,128)(2,1)}, bf16[3,2048,128]{2,1,0:T(8,128)(2,1)S(1)}, u32[]{:S(2)}) copy-start(bf16[3,2048,128]{2,1,0:T(8,128)(2,1)S(1)} %collective-permute-done.7.refs_1_) | copy-start | bytes 4718596
  44.6 3.5 %collective-permute-start.9 = (bf16[3,2048,128]{2,1,0:T(8,128)(2,1)S(1)}, bf16[3,2048,128]{2,1,0:T(8,128)(2,1)S(1)}, u32[]{:S(2)}, u32[]{:S(2)}) collective-permute-start(bf16[3,2048,128]{2,1,0:T(8,128)(2,1)S(1)} %collective-permute-done.6.refs_2_), channel_id=1, source_target_pairs={{0,8},{8,0},{16,24},{24,16},{1,9},{9,1},{17,25},{25,17},{2,10},{10... | collective-permute-start | bytes 4718600 | tf_op jit(solution)/shard_map/ppermute | solution.py:78
  44.6 18.1 %collective-permute-start.8 = (bf16[1,128,2048]{2,1,0:T(8,128)(2,1)}, bf16[1,128,2048]{2,1,0:T(8,128)(2,1)}, u32[]{:S(2)}, u32[]{:S(2)}) collective-permute-start(bf16[1,128,2048]{2,1,0:T(8,128)(2,1)} %collective-permute-done.4.refs_6_), channel_id=1, source_target_pairs={{0,2},{2,4},{4,6},{6,7},{7,5},{5,3},{3,1},{1,0},{8,10},{10,12},{12... | collective-permute-start | bytes 1572872 | tf_op jit(solution)/shard_map/ppermute | solution.py:200
  46.2 17.0 %collective-permute-start.10 = (bf16[1,128,2048]{2,1,0:T(8,128)(2,1)S(1)}, bf16[1,128,2048]{2,1,0:T(8,128)(2,1)}, u32[]{:S(2)}, u32[]{:S(2)}) collective-permute-start(bf16[1,128,2048]{2,1,0:T(8,128)(2,1)S(1)} %collective-permute-done.refs_2_), channel_id=1, source_target_pairs={{0,8},{8,0},{16,24},{24,16},{1,9},{9,1},{17,25},{25,17},{2,10},{10... | collective-permute-start | bytes 1572872 | tf_op jit(solution)/shard_map/ppermute | solution.py:78
  46.4 17.0 %collective-permute-start.11 = (bf16[1,128,2048]{2,1,0:T(8,128)(2,1)S(1)}, bf16[1,128,2048]{2,1,0:T(8,128)(2,1)}, u32[]{:S(2)}, u32[]{:S(2)}) collective-permute-start(bf16[1,128,2048]{2,1,0:T(8,128)(2,1)S(1)} %collective-permute-done.1.refs_3_), channel_id=1, source_target_pairs={{0,8},{8,0},{16,24},{24,16},{1,9},{9,1},{17,25},{25,17},{2,10},{10... | collective-permute-start | bytes 1572872 | tf_op jit(solution)/shard_map/ppermute | solution.py:78
  46.7 17.0 %collective-permute-start.12 = (bf16[1,128,2048]{2,1,0:T(8,128)(2,1)S(1)}, bf16[1,128,2048]{2,1,0:T(8,128)(2,1)}, u32[]{:S(2)}, u32[]{:S(2)}) collective-permute-start(bf16[1,128,2048]{2,1,0:T(8,128)(2,1)S(1)} %collective-permute-done.2.refs_4_), channel_id=1, source_target_pairs={{0,8},{8,0},{16,24},{24,16},{1,9},{9,1},{17,25},{25,17},{2,10},{10... | collective-permute-start | bytes 1572872 | tf_op jit(solution)/shard_map/ppermute | solution.py:78
  48.0 1.1 %copy-start.6 = (bf16[3,2048,128]{2,1,0:T(8,128)(2,1)}, bf16[3,2048,128]{2,1,0:T(8,128)(2,1)S(1)}, u32[]{:S(2)}) copy-start(bf16[3,2048,128]{2,1,0:T(8,128)(2,1)S(1)} %collective-permute-done.9.refs_3_) | copy-start | bytes 4718596
  49.2 14.5 %collective-permute-start.13 = (bf16[1,128,2048]{2,1,0:T(8,128)(2,1)S(1)}, bf16[1,128,2048]{2,1,0:T(8,128)(2,1)}, u32[]{:S(2)}, u32[]{:S(2)}) collective-permute-start(bf16[1,128,2048]{2,1,0:T(8,128)(2,1)S(1)} %collective-permute-done.3.refs_5_), channel_id=1, source_target_pairs={{0,8},{8,0},{16,24},{24,16},{1,9},{9,1},{17,25},{25,17},{2,10},{10... | collective-permute-start | bytes 1572872 | tf_op jit(solution)/shard_map/ppermute | solution.py:78
  62.8 2.2 %collective-permute-start.14 = (bf16[1,128,2048]{2,1,0:T(8,128)(2,1)}, bf16[1,128,2048]{2,1,0:T(8,128)(2,1)S(1)}, u32[]{:S(2)}, u32[]{:S(2)}) collective-permute-start(bf16[1,128,2048]{2,1,0:T(8,128)(2,1)} %collective-permute-done.4.refs_6_), channel_id=1, source_target_pairs={{0,8},{8,0},{16,24},{24,16},{1,9},{9,1},{17,25},{25,17},{2,10},{10... | collective-permute-start | bytes 1572872 | tf_op jit(solution)/shard_map/ppermute | solution.py:78
  63.2 2.5 %collective-permute-start.15 = (bf16[1,128,2048]{2,1,0:T(8,128)(2,1)}, bf16[1,128,2048]{2,1,0:T(8,128)(2,1)S(1)}, u32[]{:S(2)}, u32[]{:S(2)}) collective-permute-start(bf16[1,128,2048]{2,1,0:T(8,128)(2,1)} %copy-done.2), channel_id=1, source_target_pairs={{0,8},{8,0},{16,24},{24,16},{1,9},{9,1},{17,25},{25,17},{2,10},{10... | collective-permute-start | bytes 1572872 | tf_op jit(solution)/shard_map/ppermute | solution.py:78
  63.3 19.6 %collective-permute-start.16 = (bf16[1,128,2048]{2,1,0:T(8,128)(2,1)}, bf16[1,128,2048]{2,1,0:T(8,128)(2,1)S(1)}, u32[]{:S(2)}, u32[]{:S(2)}) collective-permute-start(bf16[1,128,2048]{2,1,0:T(8,128)(2,1)} %collective-permute-done.8.refs_1_), channel_id=1, source_target_pairs={{0,8},{8,0},{16,24},{24,16},{1,9},{9,1},{17,25},{25,17},{2,10},{10... | collective-permute-start | bytes 1572872 | tf_op jit(solution)/shard_map/ppermute | solution.py:78
  65.7 1.9 %copy-start = (bf16[6,2048,128]{2,1,0:T(8,128)(2,1)S(1)}, bf16[6,2048,128]{2,1,0:T(8,128)(2,1)}, u32[]{:S(2)}) copy-start(bf16[6,2048,128]{2,1,0:T(8,128)(2,1)} %get-tuple-element.43.refs_0_) | copy-start | bytes 9437188
  82.9 3.2 %copy-start.7 = (s32[6]{0:T(128)S(1)}, s32[6]{0:T(128)}, u32[]{:S(2)}) copy-start(s32[6]{0:T(128)} %param.8) | copy-start | bytes 76
  (1 other events, 1.0 us)

commit v15 on v11

--- a/solution.py
+++ b/solution.py
@@ -30,33 +30,35 @@
 def energy_kernel(*refs):
     theta_ref = refs[0]
     chol_refs = refs[1:-3]
-    out_ref, crossed_ref, square_ref = refs[-3:]
+    out_ref, crossed_ref, trace_ref = refs[-3:]
     n_slot, _, electrons = theta_ref.shape
     lanes = out_ref.shape[1]
     rows = lax.broadcasted_iota(jnp.int32, (electrons, electrons), 0)
     cols = lax.broadcasted_iota(jnp.int32, (electrons, electrons), 1)
     diagonal = rows == cols
     crossed_ref[...] = jnp.zeros(crossed_ref.shape, jnp.float32)
-    square_ref[...] = jnp.zeros(square_ref.shape, jnp.float32)
+    offset = 0
     for chol_ref in chol_refs:
-        def per_vector(g, carry, chol_ref=chol_ref):
+        def per_vector(g, carry, chol_ref=chol_ref, offset=offset):
             vector = chol_ref[g]
             for s in range(n_slot):
                 blocks = jnp.dot(vector, theta_ref[s], preferred_element_type=jnp.float32)
                 crossed_ref[s] += blocks * blocks.T
-                diag = jnp.sum(jnp.where(diagonal, blocks, 0.0), axis=0, keepdims=True)
-                trace = jnp.sum(diag, axis=1, keepdims=True)
-                square_ref[pl.ds(s, 1), :] += jnp.broadcast_to(trace * trace, (1, lanes))
+                trace_ref[s, pl.ds(offset + g, 1), :] = jnp.sum(jnp.where(diagonal, blocks, 0.0), axis=0, keepdims=True)
             return carry
 
         lax.fori_loop(0, chol_ref.shape[0], per_vector, 0)
-    for s in range(n_slot):
+        offset += chol_ref.shape[0]
+    for s in range(n_slot):
+        traces = jnp.sum(trace_ref[s], axis=1, keepdims=True)
+        square = jnp.sum(traces * traces, keepdims=True)
         crossed = jnp.sum(crossed_ref[s], keepdims=True)
-        out_ref[pl.ds(s, 1), :] = 0.5 * (square_ref[pl.ds(s, 1), :] - jnp.broadcast_to(crossed, (1, lanes)))
+        out_ref[pl.ds(s, 1), :] = jnp.broadcast_to(0.5 * (square - crossed), (1, lanes))
 
 
 def block_energy(theta, pieces):
     n_slot, _, electrons = theta.shape
+    n_vectors = sum(p.shape[0] for p in pieces)
     vmem = pltpu.MemorySpace.VMEM
     held = sum(p.size * p.dtype.itemsize for p in pieces) + theta.size * theta.dtype.itemsize
     out = pl.pallas_call(
@@ -66,7 +68,7 @@
         out_specs=pl.BlockSpec(memory_space=vmem),
         scratch_shapes=[
             pltpu.VMEM((n_slot, electrons, electrons), jnp.float32),
-            pltpu.VMEM((n_slot, 128), jnp.float32),
+            pltpu.VMEM((n_slot, n_vectors, electrons), jnp.float32),
         ],
         compiler_params=pltpu.CompilerParams(vmem_limit_bytes=int(held + (16 << 20))),
     )(theta, *pieces)

time: 86.1 us -> 86 us (level)
  no operation moved by 1% of the time
where the time goes in v15:
time: 86 us; the launch traced here: 85.6 us
  waiting for transfers between devices  33.8 us (39%)
  Pallas kernels  29 us (34%)
  starting transfers between devices  12.5 us (15%)
  local copies, waits for them, and re-layouts  6.76 us (8%)
  other arithmetic  2.84 us (3%)
    ppermute x4, waiting for transfers between devices, body(): ahead = lax.ppermute(ahead, 'chol', forward)  25.9 us
    pallas_call x1, Pallas kernels, block_energy(): pl.pallas_call(energy_kernel, out_shape=jax.ShapeDtypeStruct((n_slot, 128...  16 us
    pallas_call x1, Pallas kernels, kick(): pl.pallas_call(kick_kernel, out_shape=[shape, shape], grid_spec=grid_spec)  12.9 us
    ppermute x4, starting transfers between devices, body(): ahead = lax.ppermute(ahead, 'chol', forward)  7.8 us
    unnamed x16, local copies, waits for them, and re-layouts  4.09 us
    ppermute x3, waiting for transfers between devices, body(): behind = lax.ppermute(behind, 'chol', backward)  4 us
    ppermute x10, waiting for transfers between devices, swap_pairs(): return lax.ppermute(x, axis, perm)  3.88 us
    ppermute x10, starting transfers between devices, swap_pairs(): return lax.ppermute(x, axis, perm)  3.77 us
  transfers between devices with their start and end apart: 17, of which 10 were waited for; matrix products, arithmetic and copies ran while one was open for 4% of the time, Pallas kernels for 15%

profile of v15, /device:TPU:0, one launch (start us, length us, event | category | flops | bytes accessed | tf_op | source)
XLA Modules:
  0.0 85.6 jit_solution(12632407778401375107)
XLA Ops:
  0.6 1.1 %constant_dynamic-slice_fusion = bf16[1,128,2048]{2,1,0:T(8,128)(2,1)S(1)} fusion(bf16[2,128,2048]{2,1,0:T(8,128)(2,1)} %refs_1_.1, s32[]{:T(128)S(6)} %select_n.26), kind=kLoop, calls=%fused_computation.6 | loop fusion | bytes 1048580 | tf_op jit(solution)/shard_map/dynamic_slice | solution.py:191
  1.7 3.1 %collective-permute-start = (bf16[1,128,2048]{2,1,0:T(8,128)(2,1)S(1)}, bf16[1,128,2048]{2,1,0:T(8,128)(2,1)S(1)}, u32[]{:S(2)}, u32[]{:S(2)}) collective-permute-start(bf16[1,128,2048]{2,1,0:T(8,128)(2,1)S(1)} %constant_dynamic-slice_fusion), channel_id=1, source_target_pairs={{0,2},{2,4},{4,6},{6,7},{7,5},{5,3},{3,1},{1,0},{8,10},{10,12},{12... | collective-permute-start | bytes 1572872 | tf_op jit(solution)/shard_map/ppermute | solution.py:206
  4.8 1.9 %collective-permute-start.6 = (bf16[3,2048,128]{2,1,0:T(8,128)(2,1)}, bf16[3,2048,128]{2,1,0:T(8,128)(2,1)S(1)}, u32[]{:S(2)}, u32[]{:S(2)}) collective-permute-start(bf16[3,2048,128]{2,1,0:T(8,128)(2,1)} %refs_0_.1), channel_id=1, source_target_pairs={{0,16},{8,24},{16,0},{24,8},{1,17},{9,25},{17,1},{25,9},{2,18},{10... | collective-permute-start | bytes 4718600 | tf_op jit(solution)/shard_map/ppermute | solution.py:80
  6.8 1.5 %scatter.4.refs_4_ = f32[8,2048]{1,0:T(8,128)} pad(f32[6,2048]{1,0:T(8,128)} %param.9, f32[]{:T(128)} %constant.67.clone.1), padding=0_2x0_0 | pad | bytes 114692 | tf_op jit(solution)/shard_map/scatter | solution.py:148
  8.2 1.2 %fusion.source_ref = s32[6]{0:T(128)} fusion(s32[6]{0:T(128)} %param.8, s32[]{:T(128)S(6)} %axis_index.15), kind=kLoop, calls=%fused_computation.5 | loop fusion | flops 96 | bytes 52 | tf_op jit(solution)/shard_map/add | solution.py:146
  9.4 1.1 %compare_convert_fusion.living_ref = s32[6]{0:T(128)} fusion(s32[6]{0:T(128)} %param.8), kind=kLoop, calls=%fused_computation.4 | loop fusion | flops 12 | bytes 48 | tf_op jit(solution)/shard_map/convert_element_type | solution.py:143
  10.5 6.1 %collective-permute-done.refs_2_ = bf16[1,128,2048]{2,1,0:T(8,128)(2,1)S(1)} collective-permute-done((bf16[1,128,2048]{2,1,0:T(8,128)(2,1)S(1)}, bf16[1,128,2048]{2,1,0:T(8,128)(2,1)S(1)}, u32[]{:S(2)}, u32[]{:S(2)}) %collective-permute-start) | collective-permute-done | bytes 524320 | tf_op jit(solution)/shard_map/ppermute | solution.py:206
  16.7 1.5 %collective-permute-done.1.refs_3_ = bf16[1,128,2048]{2,1,0:T(8,128)(2,1)S(1)} collective-permute-done((bf16[1,128,2048]{2,1,0:T(8,128)(2,1)S(1)}, bf16[1,128,2048]{2,1,0:T(8,128)(2,1)S(1)}, u32[]{:S(2)}, u32[]{:S(2)}) %collective-permute-start.1) | collective-permute-done | bytes 524320 | tf_op jit(solution)/shard_map/ppermute | solution.py:209
  18.2 1.6 %collective-permute-start.2 = (bf16[1,128,2048]{2,1,0:T(8,128)(2,1)S(1)}, bf16[1,128,2048]{2,1,0:T(8,128)(2,1)S(1)}, u32[]{:S(2)}, u32[]{:S(2)}) collective-permute-start(bf16[1,128,2048]{2,1,0:T(8,128)(2,1)S(1)} %collective-permute-done.refs_2_), channel_id=1, source_target_pairs={{0,2},{2,4},{4,6},{6,7},{7,5},{5,3},{3,1},{1,0},{8,10},{10,12},{12... | collective-permute-start | bytes 1572872 | tf_op jit(solution)/shard_map/ppermute | solution.py:206
  20.2 10.4 %collective-permute-done.2.refs_4_ = bf16[1,128,2048]{2,1,0:T(8,128)(2,1)S(1)} collective-permute-done((bf16[1,128,2048]{2,1,0:T(8,128)(2,1)S(1)}, bf16[1,128,2048]{2,1,0:T(8,128)(2,1)S(1)}, u32[]{:S(2)}, u32[]{:S(2)}) %collective-permute-start.2) | collective-permute-done | bytes 524320 | tf_op jit(solution)/shard_map/ppermute | solution.py:206
  30.7 1.3 %collective-permute-done.3.refs_5_ = bf16[1,128,2048]{2,1,0:T(8,128)(2,1)S(1)} collective-permute-done((bf16[1,128,2048]{2,1,0:T(8,128)(2,1)S(1)}, bf16[1,128,2048]{2,1,0:T(8,128)(2,1)S(1)}, u32[]{:S(2)}, u32[]{:S(2)}) %collective-permute-start.3) | collective-permute-done | bytes 524320 | tf_op jit(solution)/shard_map/ppermute | solution.py:209
  32.0 1.6 %collective-permute-start.4 = (bf16[1,128,2048]{2,1,0:T(8,128)(2,1)S(1)}, bf16[1,128,2048]{2,1,0:T(8,128)(2,1)}, u32[]{:S(2)}, u32[]{:S(2)}) collective-permute-start(bf16[1,128,2048]{2,1,0:T(8,128)(2,1)S(1)} %collective-permute-done.2.refs_4_), channel_id=1, source_target_pairs={{0,2},{2,4},{4,6},{6,7},{7,5},{5,3},{3,1},{1,0},{8,10},{10,12},{12... | collective-permute-start | bytes 1572872 | tf_op jit(solution)/shard_map/ppermute | solution.py:206
  34.0 9.4 %collective-permute-done.4.refs_6_ = bf16[1,128,2048]{2,1,0:T(8,128)(2,1)} collective-permute-done((bf16[1,128,2048]{2,1,0:T(8,128)(2,1)S(1)}, bf16[1,128,2048]{2,1,0:T(8,128)(2,1)}, u32[]{:S(2)}, u32[]{:S(2)}) %collective-permute-start.4) | collective-permute-done | bytes 524320 | tf_op jit(solution)/shard_map/ppermute | solution.py:206
  43.3 1.2 %collective-permute-done.5.refs_7_ = bf16[1,128,2048]{2,1,0:T(8,128)(2,1)S(1)} collective-permute-done((bf16[1,128,2048]{2,1,0:T(8,128)(2,1)S(1)}, bf16[1,128,2048]{2,1,0:T(8,128)(2,1)S(1)}, u32[]{:S(2)}, u32[]{:S(2)}) %collective-permute-start.5) | collective-permute-done | bytes 524320 | tf_op jit(solution)/shard_map/ppermute | solution.py:209
  44.6 1.6 %collective-permute-start.8 = (bf16[1,128,2048]{2,1,0:T(8,128)(2,1)}, bf16[1,128,2048]{2,1,0:T(8,128)(2,1)}, u32[]{:S(2)}, u32[]{:S(2)}) collective-permute-start(bf16[1,128,2048]{2,1,0:T(8,128)(2,1)} %collective-permute-done.4.refs_6_), channel_id=1, source_target_pairs={{0,2},{2,4},{4,6},{6,7},{7,5},{5,3},{3,1},{1,0},{8,10},{10,12},{12... | collective-permute-start | bytes 1572872 | tf_op jit(solution)/shard_map/ppermute | solution.py:206
  46.9 1.1 %collective-permute-done.9.refs_3_ = bf16[3,2048,128]{2,1,0:T(8,128)(2,1)S(1)} collective-permute-done((bf16[3,2048,128]{2,1,0:T(8,128)(2,1)S(1)}, bf16[3,2048,128]{2,1,0:T(8,128)(2,1)S(1)}, u32[]{:S(2)}, u32[]{:S(2)}) %collective-permute-start.9) | collective-permute-done | bytes 1572896 | tf_op jit(solution)/shard_map/ppermute | solution.py:80
  48.0 1.1 %copy-done.6 = bf16[3,2048,128]{2,1,0:T(8,128)(2,1)} copy-done((bf16[3,2048,128]{2,1,0:T(8,128)(2,1)}, bf16[3,2048,128]{2,1,0:T(8,128)(2,1)S(1)}, u32[]{:S(2)}) %copy-start.6) | copy-done | bytes 1572888
  49.3 12.9 %shard_map.59 = (bf16[6,2048,128]{2,1,0:T(8,128)(2,1)}, bf16[6,2048,128]{2,1,0:T(8,128)(2,1)}) custom-call(s32[6]{0:T(128)} %fusion.source_ref, s32[6]{0:T(128)} %compare_convert_fusion.living_ref, bf16[3,2048,128]{2,1,0:T(8,128)(2,1)} %refs_0_.1, bf16[3,2048,128]{2,1,0:T(8,128)(2,1)} %copy-done.5, bf16[3,2048,128]{2,1,0:T(8,128)(2,1)} %copy-done.4, ...), custom_call_target="tpu_custom_call" | custom-call | tf_op jit(solution)/shard_map/pallas_call | solution.py:173
  63.3 1.2 %collective-permute-done.14.refs_13_ = bf16[1,128,2048]{2,1,0:T(8,128)(2,1)S(1)} collective-permute-done((bf16[1,128,2048]{2,1,0:T(8,128)(2,1)}, bf16[1,128,2048]{2,1,0:T(8,128)(2,1)S(1)}, u32[]{:S(2)}, u32[]{:S(2)}) %collective-permute-start.14) | collective-permute-done | bytes 524320 | tf_op jit(solution)/shard_map/ppermute | solution.py:80
  64.5 0.7 collective-permute-done.15.refs_14_
  65.2 0.7 collective-permute-done.16.refs_15_
  66.0 1.9 %copy-done = bf16[6,2048,128]{2,1,0:T(8,128)(2,1)S(1)} copy-done((bf16[6,2048,128]{2,1,0:T(8,128)(2,1)S(1)}, bf16[6,2048,128]{2,1,0:T(8,128)(2,1)}, u32[]{:S(2)}) %copy-start) | copy-done | bytes 3145752
  67.9 1.0 %copy-done.3 = bf16[1,128,2048]{2,1,0:T(8,128)(2,1)S(1)} copy-done((bf16[1,128,2048]{2,1,0:T(8,128)(2,1)S(1)}, bf16[1,128,2048]{2,1,0:T(8,128)(2,1)}, u32[]{:S(2)}) %copy-start.3) | copy-done | bytes 524312
  68.9 16.0 %shard_map.60 = f32[6,128]{1,0:T(8,128)S(1)} custom-call(bf16[6,2048,128]{2,1,0:T(8,128)(2,1)S(1)} %copy-done, bf16[2,128,2048]{2,1,0:T(8,128)(2,1)S(1)} %copy-done.1, bf16[1,128,2048]{2,1,0:T(8,128)(2,1)S(1)} %collective-permute-done.refs_2_, bf16[1,128,2048]{2,1,0:T(8,128)(2,1)S(1)} %collective-permute-done.1.refs_3_, ...), custom_call_target="tpu_custom_call" | custom-call | tf_op jit(solution)/shard_map/pallas_call | solution.py:64
  (34 shorter events, 3.4 us)
Async XLA Ops:
  1.7 14.9 %collective-permute-start = (bf16[1,128,2048]{2,1,0:T(8,128)(2,1)S(1)}, bf16[1,128,2048]{2,1,0:T(8,128)(2,1)S(1)}, u32[]{:S(2)}, u32[]{:S(2)}) collective-permute-start(bf16[1,128,2048]{2,1,0:T(8,128)(2,1)S(1)} %constant_dynamic-slice_fusion), channel_id=1, source_target_pairs={{0,2},{2,4},{4,6},{6,7},{7,5},{5,3},{3,1},{1,0},{8,10},{10,12},{12... | collective-permute-start | bytes 1572872 | tf_op jit(solution)/shard_map/ppermute | solution.py:206
  4.8 13.4 %collective-permute-start.1 = (bf16[1,128,2048]{2,1,0:T(8,128)(2,1)S(1)}, bf16[1,128,2048]{2,1,0:T(8,128)(2,1)S(1)}, u32[]{:S(2)}, u32[]{:S(2)}) collective-permute-start(bf16[1,128,2048]{2,1,0:T(8,128)(2,1)S(1)} %constant_dynamic-slice_fusion), channel_id=1, source_target_pairs={{2,0},{4,2},{6,4},{7,6},{5,7},{3,5},{1,3},{0,1},{10,8},{12,10},{14... | collective-permute-start | bytes 1572872 | tf_op jit(solution)/shard_map/ppermute | solution.py:209
  4.8 39.7 %collective-permute-start.6 = (bf16[3,2048,128]{2,1,0:T(8,128)(2,1)}, bf16[3,2048,128]{2,1,0:T(8,128)(2,1)S(1)}, u32[]{:S(2)}, u32[]{:S(2)}) collective-permute-start(bf16[3,2048,128]{2,1,0:T(8,128)(2,1)} %refs_0_.1), channel_id=1, source_target_pairs={{0,16},{8,24},{16,0},{24,8},{1,17},{9,25},{17,1},{25,9},{2,18},{10... | collective-permute-start | bytes 4718600 | tf_op jit(solution)/shard_map/ppermute | solution.py:80
  6.8 37.8 %collective-permute-start.7 = (bf16[3,2048,128]{2,1,0:T(8,128)(2,1)}, bf16[3,2048,128]{2,1,0:T(8,128)(2,1)S(1)}, u32[]{:S(2)}, u32[]{:S(2)}) collective-permute-start(bf16[3,2048,128]{2,1,0:T(8,128)(2,1)} %refs_0_.1), channel_id=1, source_target_pairs={{0,8},{8,0},{16,24},{24,16},{1,9},{9,1},{17,25},{25,17},{2,10},{10... | collective-permute-start | bytes 4718600 | tf_op jit(solution)/shard_map/ppermute | solution.py:80
  10.5 55.4 %copy-start.1 = (bf16[2,128,2048]{2,1,0:T(8,128)(2,1)S(1)}, bf16[2,128,2048]{2,1,0:T(8,128)(2,1)}, u32[]{:S(2)}) copy-start(bf16[2,128,2048]{2,1,0:T(8,128)(2,1)} %refs_1_.1) | copy-start | bytes 3145732
  18.2 12.5 %collective-permute-start.2 = (bf16[1,128,2048]{2,1,0:T(8,128)(2,1)S(1)}, bf16[1,128,2048]{2,1,0:T(8,128)(2,1)S(1)}, u32[]{:S(2)}, u32[]{:S(2)}) collective-permute-start(bf16[1,128,2048]{2,1,0:T(8,128)(2,1)S(1)} %collective-permute-done.refs_2_), channel_id=1, source_target_pairs={{0,2},{2,4},{4,6},{6,7},{7,5},{5,3},{3,1},{1,0},{8,10},{10,12},{12... | collective-permute-start | bytes 1572872 | tf_op jit(solution)/shard_map/ppermute | solution.py:206
  19.8 12.2 %collective-permute-start.3 = (bf16[1,128,2048]{2,1,0:T(8,128)(2,1)S(1)}, bf16[1,128,2048]{2,1,0:T(8,128)(2,1)S(1)}, u32[]{:S(2)}, u32[]{:S(2)}) collective-permute-start(bf16[1,128,2048]{2,1,0:T(8,128)(2,1)S(1)} %collective-permute-done.1.refs_3_), channel_id=1, source_target_pairs={{2,0},{4,2},{6,4},{7,6},{5,7},{3,5},{1,3},{0,1},{10,8},{12,10},{14... | collective-permute-start | bytes 1572872 | tf_op jit(solution)/shard_map/ppermute | solution.py:209
  32.0 11.4 %collective-permute-start.4 = (bf16[1,128,2048]{2,1,0:T(8,128)(2,1)S(1)}, bf16[1,128,2048]{2,1,0:T(8,128)(2,1)}, u32[]{:S(2)}, u32[]{:S(2)}) collective-permute-start(bf16[1,128,2048]{2,1,0:T(8,128)(2,1)S(1)} %collective-permute-done.2.refs_4_), channel_id=1, source_target_pairs={{0,2},{2,4},{4,6},{6,7},{7,5},{5,3},{3,1},{1,0},{8,10},{10,12},{12... | collective-permute-start | bytes 1572872 | tf_op jit(solution)/shard_map/ppermute | solution.py:206
  33.5 11.0 %collective-permute-start.5 = (bf16[1,128,2048]{2,1,0:T(8,128)(2,1)S(1)}, bf16[1,128,2048]{2,1,0:T(8,128)(2,1)S(1)}, u32[]{:S(2)}, u32[]{:S(2)}) collective-permute-start(bf16[1,128,2048]{2,1,0:T(8,128)(2,1)S(1)} %collective-permute-done.3.refs_5_), channel_id=1, source_target_pairs={{2,0},{4,2},{6,4},{7,6},{5,7},{3,5},{1,3},{0,1},{10,8},{12,10},{14... | collective-permute-start | bytes 1572872 | tf_op jit(solution)/shard_map/ppermute | solution.py:209
  44.5 2.4 %copy-start.2 = (bf16[1,128,2048]{2,1,0:T(8,128)(2,1)}, bf16[1,128,2048]{2,1,0:T(8,128)(2,1)S(1)}, u32[]{:S(2)}) copy-start(bf16[1,128,2048]{2,1,0:T(8,128)(2,1)S(1)} %collective-permute-done.5.refs_7_) | copy-start | bytes 1572868
  44.5 3.5 %copy-start.4 = (bf16[3,2048,128]{2,1,0:T(8,128)(2,1)}, bf16[3,2048,128]{2,1,0:T(8,128)(2,1)S(1)}, u32[]{:S(2)}) copy-start(bf16[3,2048,128]{2,1,0:T(8,128)(2,1)S(1)} %collective-permute-done.6.refs_2_) | copy-start | bytes 4718596
  44.6 3.5 %copy-start.5 = (bf16[3,2048,128]{2,1,0:T(8,128)(2,1)}, bf16[3,2048,128]{2,1,0:T(8,128)(2,1)S(1)}, u32[]{:S(2)}) copy-start(bf16[3,2048,128]{2,1,0:T(8,128)(2,1)S(1)} %collective-permute-done.7.refs_1_) | copy-start | bytes 4718596
  44.6 3.5 %collective-permute-start.9 = (bf16[3,2048,128]{2,1,0:T(8,128)(2,1)S(1)}, bf16[3,2048,128]{2,1,0:T(8,128)(2,1)S(1)}, u32[]{:S(2)}, u32[]{:S(2)}) collective-permute-start(bf16[3,2048,128]{2,1,0:T(8,128)(2,1)S(1)} %collective-permute-done.6.refs_2_), channel_id=1, source_target_pairs={{0,8},{8,0},{16,24},{24,16},{1,9},{9,1},{17,25},{25,17},{2,10},{10... | collective-permute-start | bytes 4718600 | tf_op jit(solution)/shard_map/ppermute | solution.py:80
  44.6 17.6 %collective-permute-start.8 = (bf16[1,128,2048]{2,1,0:T(8,128)(2,1)}, bf16[1,128,2048]{2,1,0:T(8,128)(2,1)}, u32[]{:S(2)}, u32[]{:S(2)}) collective-permute-start(bf16[1,128,2048]{2,1,0:T(8,128)(2,1)} %collective-permute-done.4.refs_6_), channel_id=1, source_target_pairs={{0,2},{2,4},{4,6},{6,7},{7,5},{5,3},{3,1},{1,0},{8,10},{10,12},{12... | collective-permute-start | bytes 1572872 | tf_op jit(solution)/shard_map/ppermute | solution.py:206
  46.2 16.5 %collective-permute-start.10 = (bf16[1,128,2048]{2,1,0:T(8,128)(2,1)S(1)}, bf16[1,128,2048]{2,1,0:T(8,128)(2,1)}, u32[]{:S(2)}, u32[]{:S(2)}) collective-permute-start(bf16[1,128,2048]{2,1,0:T(8,128)(2,1)S(1)} %collective-permute-done.refs_2_), channel_id=1, source_target_pairs={{0,8},{8,0},{16,24},{24,16},{1,9},{9,1},{17,25},{25,17},{2,10},{10... | collective-permute-start | bytes 1572872 | tf_op jit(solution)/shard_map/ppermute | solution.py:80
  46.4 16.5 %collective-permute-start.11 = (bf16[1,128,2048]{2,1,0:T(8,128)(2,1)S(1)}, bf16[1,128,2048]{2,1,0:T(8,128)(2,1)}, u32[]{:S(2)}, u32[]{:S(2)}) collective-permute-start(bf16[1,128,2048]{2,1,0:T(8,128)(2,1)S(1)} %collective-permute-done.1.refs_3_), channel_id=1, source_target_pairs={{0,8},{8,0},{16,24},{24,16},{1,9},{9,1},{17,25},{25,17},{2,10},{10... | collective-permute-start | bytes 1572872 | tf_op jit(solution)/shard_map/ppermute | solution.py:80
  46.7 16.5 %collective-permute-start.12 = (bf16[1,128,2048]{2,1,0:T(8,128)(2,1)S(1)}, bf16[1,128,2048]{2,1,0:T(8,128)(2,1)}, u32[]{:S(2)}, u32[]{:S(2)}) collective-permute-start(bf16[1,128,2048]{2,1,0:T(8,128)(2,1)S(1)} %collective-permute-done.2.refs_4_), channel_id=1, source_target_pairs={{0,8},{8,0},{16,24},{24,16},{1,9},{9,1},{17,25},{25,17},{2,10},{10... | collective-permute-start | bytes 1572872 | tf_op jit(solution)/shard_map/ppermute | solution.py:80
  48.0 1.1 %copy-start.6 = (bf16[3,2048,128]{2,1,0:T(8,128)(2,1)}, bf16[3,2048,128]{2,1,0:T(8,128)(2,1)S(1)}, u32[]{:S(2)}) copy-start(bf16[3,2048,128]{2,1,0:T(8,128)(2,1)S(1)} %collective-permute-done.9.refs_3_) | copy-start | bytes 4718596
  49.2 14.1 %collective-permute-start.13 = (bf16[1,128,2048]{2,1,0:T(8,128)(2,1)S(1)}, bf16[1,128,2048]{2,1,0:T(8,128)(2,1)}, u32[]{:S(2)}, u32[]{:S(2)}) collective-permute-start(bf16[1,128,2048]{2,1,0:T(8,128)(2,1)S(1)} %collective-permute-done.3.refs_5_), channel_id=1, source_target_pairs={{0,8},{8,0},{16,24},{24,16},{1,9},{9,1},{17,25},{25,17},{2,10},{10... | collective-permute-start | bytes 1572872 | tf_op jit(solution)/shard_map/ppermute | solution.py:80
  62.3 2.2 %collective-permute-start.14 = (bf16[1,128,2048]{2,1,0:T(8,128)(2,1)}, bf16[1,128,2048]{2,1,0:T(8,128)(2,1)S(1)}, u32[]{:S(2)}, u32[]{:S(2)}) collective-permute-start(bf16[1,128,2048]{2,1,0:T(8,128)(2,1)} %collective-permute-done.4.refs_6_), channel_id=1, source_target_pairs={{0,8},{8,0},{16,24},{24,16},{1,9},{9,1},{17,25},{25,17},{2,10},{10... | collective-permute-start | bytes 1572872 | tf_op jit(solution)/shard_map/ppermute | solution.py:80
  62.7 22.3 %copy-start.7 = (s32[6]{0:T(128)S(1)}, s32[6]{0:T(128)}, u32[]{:S(2)}) copy-start(s32[6]{0:T(128)} %param.8) | copy-start | bytes 76
  62.7 2.5 %collective-permute-start.15 = (bf16[1,128,2048]{2,1,0:T(8,128)(2,1)}, bf16[1,128,2048]{2,1,0:T(8,128)(2,1)S(1)}, u32[]{:S(2)}, u32[]{:S(2)}) collective-permute-start(bf16[1,128,2048]{2,1,0:T(8,128)(2,1)} %copy-done.2), channel_id=1, source_target_pairs={{0,8},{8,0},{16,24},{24,16},{1,9},{9,1},{17,25},{25,17},{2,10},{10... | collective-permute-start | bytes 1572872 | tf_op jit(solution)/shard_map/ppermute | solution.py:80
  62.9 3.1 %collective-permute-start.16 = (bf16[1,128,2048]{2,1,0:T(8,128)(2,1)}, bf16[1,128,2048]{2,1,0:T(8,128)(2,1)S(1)}, u32[]{:S(2)}, u32[]{:S(2)}) collective-permute-start(bf16[1,128,2048]{2,1,0:T(8,128)(2,1)} %collective-permute-done.8.refs_8_), channel_id=1, source_target_pairs={{0,8},{8,0},{16,24},{24,16},{1,9},{9,1},{17,25},{25,17},{2,10},{10... | collective-permute-start | bytes 1572872 | tf_op jit(solution)/shard_map/ppermute | solution.py:80
  66.0 1.9 %copy-start = (bf16[6,2048,128]{2,1,0:T(8,128)(2,1)S(1)}, bf16[6,2048,128]{2,1,0:T(8,128)(2,1)}, u32[]{:S(2)}) copy-start(bf16[6,2048,128]{2,1,0:T(8,128)(2,1)} %get-tuple-element.43.refs_0_) | copy-start | bytes 9437188
  (1 other events, 1.0 us)

commit v16 on v15

--- a/solution.py
+++ b/solution.py
@@ -31,7 +31,7 @@
     theta_ref = refs[0]
     chol_refs = refs[1:-3]
     out_ref, crossed_ref, trace_ref = refs[-3:]
-    n_slot, _, electrons = theta_ref.shape
+    n_slot, electrons = trace_ref.shape[0], trace_ref.shape[2]
     lanes = out_ref.shape[1]
     rows = lax.broadcasted_iota(jnp.int32, (electrons, electrons), 0)
     cols = lax.broadcasted_iota(jnp.int32, (electrons, electrons), 1)
@@ -40,9 +40,9 @@
     offset = 0
     for chol_ref in chol_refs:
         def per_vector(g, carry, chol_ref=chol_ref, offset=offset):
-            vector = chol_ref[g]
+            wide = jnp.dot(chol_ref[g], theta_ref[...], preferred_element_type=jnp.float32)
             for s in range(n_slot):
-                blocks = jnp.dot(vector, theta_ref[s], preferred_element_type=jnp.float32)
+                blocks = wide[:, s * electrons:(s + 1) * electrons]
                 crossed_ref[s] += blocks * blocks.T
                 trace_ref[s, pl.ds(offset + g, 1), :] = jnp.sum(jnp.where(diagonal, blocks, 0.0), axis=0, keepdims=True)
             return carry
@@ -57,7 +57,8 @@
 
 
 def block_energy(theta, pieces):
-    n_slot, _, electrons = theta.shape
+    electrons = pieces[0].shape[1]
+    n_slot = theta.shape[1] // electrons
     n_vectors = sum(p.shape[0] for p in pieces)
     vmem = pltpu.MemorySpace.VMEM
     held = sum(p.size * p.dtype.itemsize for p in pieces) + theta.size * theta.dtype.itemsize
@@ -82,7 +83,7 @@
 
 def kick_kernel(source_ref, living_ref, *refs):
     walker_refs = refs[:4]
-    field_ref, new_hbm, theta_hbm, walkers, kicked_buf, new_buf, theta_buf, in_sem, out_sem = refs[4:]
+    field_ref, new_hbm, theta_out, walkers, kicked_buf, new_buf, in_sem, out_sem = refs[4:]
     old_dev = walker_refs[0].shape[0]
     n_slot, orbitals, electrons = walkers.shape
 
@@ -130,10 +131,7 @@
     for s in range(n_slot):
         widened = kicked_buf[s].astype(jnp.float32)
         theta = jnp.dot(widened, inverses[s], precision=lax.Precision.HIGHEST, preferred_element_type=jnp.float32)
-        theta_buf[s] = theta.astype(jnp.bfloat16)
-        copy = pltpu.make_async_copy(theta_buf.at[s], theta_hbm.at[s], out_sem.at[1, s])
-        copy.start()
-        out_copies.append(copy)
+        theta_out[:, s * electrons:(s + 1) * electrons] = theta.astype(jnp.bfloat16)
     for copy in out_copies:
         copy.wait()
 
@@ -159,20 +157,20 @@
         num_scalar_prefetch=2,
         grid=(1,),
         in_specs=[any_space] * 4 + [pl.BlockSpec((lanes, orbitals), lambda i, *_: (0, 0))],
-        out_specs=[any_space, any_space],
+        out_specs=[any_space, pl.BlockSpec(memory_space=pltpu.MemorySpace.VMEM)],
         scratch_shapes=[
             pltpu.VMEM(slots, jnp.bfloat16),
             pltpu.VMEM(slots, jnp.bfloat16),
             pltpu.VMEM(slots, jnp.bfloat16),
-            pltpu.VMEM(slots, jnp.bfloat16),
             pltpu.SemaphoreType.DMA((slot_dev,)),
-            pltpu.SemaphoreType.DMA((2, slot_dev)),
+            pltpu.SemaphoreType.DMA((1, slot_dev)),
         ],
     )
     shape = jax.ShapeDtypeStruct(slots, jnp.bfloat16)
+    wide = jax.ShapeDtypeStruct((orbitals, slot_dev * electrons), jnp.bfloat16)
     new_walkers, theta = pl.pallas_call(
         kick_kernel,
-        out_shape=[shape, shape],
+        out_shape=[shape, wide],
         grid_spec=grid_spec,
     )(index, living, old_walkers, beside, across, diagonal_peer, padded)
     return new_walkers, theta

time: 86 us -> 80.1 us (0.931)
  Pallas kernels: 29 us -> 23.2 us
    pallas_call x1, Pallas kernels: 16 us -> 9.57 us  [block_energy(): pl.pallas_call(energy_kernel, out_shape=jax.ShapeDtypeStruct((n_slot, 128...]
  transfers between devices with their start and end apart: 17 -> 17, of which waited for: 10 -> 10; matrix products, arithmetic and copies ran while one was open for 4% -> 5% of each run, Pallas kernels for 15% -> 17%
where the time goes in v16:
time: 80.1 us; the launch traced here: 79.9 us
  waiting for transfers between devices  34 us (42%)
  Pallas kernels  23.2 us (29%)
  starting transfers between devices  12.3 us (15%)
  local copies, waits for them, and re-layouts  6.76 us (8%)
  other arithmetic  2.84 us (4%)
    ppermute x4, waiting for transfers between devices, body(): ahead = lax.ppermute(ahead, 'chol', forward)  25.9 us
    pallas_call x1, Pallas kernels, kick(): pl.pallas_call(kick_kernel, out_shape=[shape, wide], grid_spec=grid_spec)  13.7 us
    pallas_call x1, Pallas kernels, block_energy(): pl.pallas_call(energy_kernel, out_shape=jax.ShapeDtypeStruct((n_slot, 128...  9.57 us
    ppermute x4, starting transfers between devices, body(): ahead = lax.ppermute(ahead, 'chol', forward)  7.8 us
    ppermute x10, waiting for transfers between devices, swap_pairs(): return lax.ppermute(x, axis, perm)  4.1 us
    unnamed x16, local copies, waits for them, and re-layouts  4.09 us
    ppermute x3, waiting for transfers between devices, body(): behind = lax.ppermute(behind, 'chol', backward)  4 us
    ppermute x10, starting transfers between devices, swap_pairs(): return lax.ppermute(x, axis, perm)  3.54 us
  transfers between devices with their start and end apart: 17, of which 10 were waited for; matrix products, arithmetic and copies ran while one was open for 5% of the time, Pallas kernels for 17%

profile of v16, /device:TPU:0, one launch (start us, length us, event | category | flops | bytes accessed | tf_op | source)
XLA Modules:
  0.0 79.9 jit_solution(2426312251921698224)
XLA Ops:
  0.6 1.1 %constant_dynamic-slice_fusion = bf16[1,128,2048]{2,1,0:T(8,128)(2,1)S(1)} fusion(bf16[2,128,2048]{2,1,0:T(8,128)(2,1)} %refs_1_.1, s32[]{:T(128)S(6)} %select_n.26), kind=kLoop, calls=%fused_computation.6 | loop fusion | bytes 1048580 | tf_op jit(solution)/shard_map/dynamic_slice | solution.py:189
  1.7 3.1 %collective-permute-start = (bf16[1,128,2048]{2,1,0:T(8,128)(2,1)S(1)}, bf16[1,128,2048]{2,1,0:T(8,128)(2,1)S(1)}, u32[]{:S(2)}, u32[]{:S(2)}) collective-permute-start(bf16[1,128,2048]{2,1,0:T(8,128)(2,1)S(1)} %constant_dynamic-slice_fusion), channel_id=1, source_target_pairs={{0,2},{2,4},{4,6},{6,7},{7,5},{5,3},{3,1},{1,0},{8,10},{10,12},{12... | collective-permute-start | bytes 1572872 | tf_op jit(solution)/shard_map/ppermute | solution.py:204
  4.8 1.9 %collective-permute-start.6 = (bf16[3,2048,128]{2,1,0:T(8,128)(2,1)}, bf16[3,2048,128]{2,1,0:T(8,128)(2,1)S(1)}, u32[]{:S(2)}, u32[]{:S(2)}) collective-permute-start(bf16[3,2048,128]{2,1,0:T(8,128)(2,1)} %refs_0_.1), channel_id=1, source_target_pairs={{0,16},{8,24},{16,0},{24,8},{1,17},{9,25},{17,1},{25,9},{2,18},{10... | collective-permute-start | bytes 4718600 | tf_op jit(solution)/shard_map/ppermute | solution.py:81
  6.8 1.5 %scatter.4.refs_4_ = f32[8,2048]{1,0:T(8,128)} pad(f32[6,2048]{1,0:T(8,128)} %param.9, f32[]{:T(128)} %constant.67.clone.1), padding=0_2x0_0 | pad | bytes 114692 | tf_op jit(solution)/shard_map/scatter | solution.py:146
  8.2 1.2 %fusion.source_ref = s32[6]{0:T(128)} fusion(s32[6]{0:T(128)} %param.8, s32[]{:T(128)S(6)} %axis_index.15), kind=kLoop, calls=%fused_computation.5 | loop fusion | flops 96 | bytes 52 | tf_op jit(solution)/shard_map/add | solution.py:144
  9.4 1.1 %compare_convert_fusion.living_ref = s32[6]{0:T(128)} fusion(s32[6]{0:T(128)} %param.8), kind=kLoop, calls=%fused_computation.4 | loop fusion | flops 12 | bytes 48 | tf_op jit(solution)/shard_map/convert_element_type | solution.py:141
  10.5 6.1 %collective-permute-done.refs_2_ = bf16[1,128,2048]{2,1,0:T(8,128)(2,1)S(1)} collective-permute-done((bf16[1,128,2048]{2,1,0:T(8,128)(2,1)S(1)}, bf16[1,128,2048]{2,1,0:T(8,128)(2,1)S(1)}, u32[]{:S(2)}, u32[]{:S(2)}) %collective-permute-start) | collective-permute-done | bytes 524320 | tf_op jit(solution)/shard_map/ppermute | solution.py:204
  16.7 1.5 %collective-permute-done.1.refs_3_ = bf16[1,128,2048]{2,1,0:T(8,128)(2,1)S(1)} collective-permute-done((bf16[1,128,2048]{2,1,0:T(8,128)(2,1)S(1)}, bf16[1,128,2048]{2,1,0:T(8,128)(2,1)S(1)}, u32[]{:S(2)}, u32[]{:S(2)}) %collective-permute-start.1) | collective-permute-done | bytes 524320 | tf_op jit(solution)/shard_map/ppermute | solution.py:207
  18.2 1.6 %collective-permute-start.2 = (bf16[1,128,2048]{2,1,0:T(8,128)(2,1)S(1)}, bf16[1,128,2048]{2,1,0:T(8,128)(2,1)S(1)}, u32[]{:S(2)}, u32[]{:S(2)}) collective-permute-start(bf16[1,128,2048]{2,1,0:T(8,128)(2,1)S(1)} %collective-permute-done.refs_2_), channel_id=1, source_target_pairs={{0,2},{2,4},{4,6},{6,7},{7,5},{5,3},{3,1},{1,0},{8,10},{10,12},{12... | collective-permute-start | bytes 1572872 | tf_op jit(solution)/shard_map/ppermute | solution.py:204
  20.2 10.4 %collective-permute-done.2.refs_4_ = bf16[1,128,2048]{2,1,0:T(8,128)(2,1)S(1)} collective-permute-done((bf16[1,128,2048]{2,1,0:T(8,128)(2,1)S(1)}, bf16[1,128,2048]{2,1,0:T(8,128)(2,1)S(1)}, u32[]{:S(2)}, u32[]{:S(2)}) %collective-permute-start.2) | collective-permute-done | bytes 524320 | tf_op jit(solution)/shard_map/ppermute | solution.py:204
  30.7 1.3 %collective-permute-done.3.refs_5_ = bf16[1,128,2048]{2,1,0:T(8,128)(2,1)S(1)} collective-permute-done((bf16[1,128,2048]{2,1,0:T(8,128)(2,1)S(1)}, bf16[1,128,2048]{2,1,0:T(8,128)(2,1)S(1)}, u32[]{:S(2)}, u32[]{:S(2)}) %collective-permute-start.3) | collective-permute-done | bytes 524320 | tf_op jit(solution)/shard_map/ppermute | solution.py:207
  32.0 1.6 %collective-permute-start.4 = (bf16[1,128,2048]{2,1,0:T(8,128)(2,1)S(1)}, bf16[1,128,2048]{2,1,0:T(8,128)(2,1)}, u32[]{:S(2)}, u32[]{:S(2)}) collective-permute-start(bf16[1,128,2048]{2,1,0:T(8,128)(2,1)S(1)} %collective-permute-done.2.refs_4_), channel_id=1, source_target_pairs={{0,2},{2,4},{4,6},{6,7},{7,5},{5,3},{3,1},{1,0},{8,10},{10,12},{12... | collective-permute-start | bytes 1572872 | tf_op jit(solution)/shard_map/ppermute | solution.py:204
  34.0 9.4 %collective-permute-done.4.refs_6_ = bf16[1,128,2048]{2,1,0:T(8,128)(2,1)} collective-permute-done((bf16[1,128,2048]{2,1,0:T(8,128)(2,1)S(1)}, bf16[1,128,2048]{2,1,0:T(8,128)(2,1)}, u32[]{:S(2)}, u32[]{:S(2)}) %collective-permute-start.4) | collective-permute-done | bytes 524320 | tf_op jit(solution)/shard_map/ppermute | solution.py:204
  43.3 1.2 %collective-permute-done.5.refs_7_ = bf16[1,128,2048]{2,1,0:T(8,128)(2,1)S(1)} collective-permute-done((bf16[1,128,2048]{2,1,0:T(8,128)(2,1)S(1)}, bf16[1,128,2048]{2,1,0:T(8,128)(2,1)S(1)}, u32[]{:S(2)}, u32[]{:S(2)}) %collective-permute-start.5) | collective-permute-done | bytes 524320 | tf_op jit(solution)/shard_map/ppermute | solution.py:207
  44.6 1.6 %collective-permute-start.8 = (bf16[1,128,2048]{2,1,0:T(8,128)(2,1)}, bf16[1,128,2048]{2,1,0:T(8,128)(2,1)}, u32[]{:S(2)}, u32[]{:S(2)}) collective-permute-start(bf16[1,128,2048]{2,1,0:T(8,128)(2,1)} %collective-permute-done.4.refs_6_), channel_id=1, source_target_pairs={{0,2},{2,4},{4,6},{6,7},{7,5},{5,3},{3,1},{1,0},{8,10},{10,12},{12... | collective-permute-start | bytes 1572872 | tf_op jit(solution)/shard_map/ppermute | solution.py:204
  46.9 1.1 %collective-permute-done.9.refs_3_ = bf16[3,2048,128]{2,1,0:T(8,128)(2,1)S(1)} collective-permute-done((bf16[3,2048,128]{2,1,0:T(8,128)(2,1)S(1)}, bf16[3,2048,128]{2,1,0:T(8,128)(2,1)S(1)}, u32[]{:S(2)}, u32[]{:S(2)}) %collective-permute-start.9) | collective-permute-done | bytes 1572896 | tf_op jit(solution)/shard_map/ppermute | solution.py:81
  48.0 1.1 %copy-done.6 = bf16[3,2048,128]{2,1,0:T(8,128)(2,1)} copy-done((bf16[3,2048,128]{2,1,0:T(8,128)(2,1)}, bf16[3,2048,128]{2,1,0:T(8,128)(2,1)S(1)}, u32[]{:S(2)}) %copy-start.6) | copy-done | bytes 1572888
  49.3 13.7 %shard_map.59 = (bf16[6,2048,128]{2,1,0:T(8,128)(2,1)}, bf16[2048,768]{1,0:T(8,128)(2,1)}) custom-call(s32[6]{0:T(128)} %fusion.source_ref, s32[6]{0:T(128)} %compare_convert_fusion.living_ref, bf16[3,2048,128]{2,1,0:T(8,128)(2,1)} %refs_0_.1, bf16[3,2048,128]{2,1,0:T(8,128)(2,1)} %copy-done.5, bf16[3,2048,128]{2,1,0:T(8,128)(2,1)} %copy-done.4, ...), custom_call_target="tpu_custom_call" | custom-call | tf_op jit(solution)/shard_map/pallas_call | solution.py:171
  63.8 1.4 %collective-permute-done.14.refs_13_ = bf16[1,128,2048]{2,1,0:T(8,128)(2,1)S(1)} collective-permute-done((bf16[1,128,2048]{2,1,0:T(8,128)(2,1)}, bf16[1,128,2048]{2,1,0:T(8,128)(2,1)S(1)}, u32[]{:S(2)}, u32[]{:S(2)}) %collective-permute-start.14) | collective-permute-done | bytes 524320 | tf_op jit(solution)/shard_map/ppermute | solution.py:81
  65.2 0.7 collective-permute-done.15.refs_14_
  66.0 0.7 collective-permute-done.16.refs_15_
  66.7 1.9 %copy-done = bf16[2048,768]{1,0:T(8,128)(2,1)S(1)} copy-done((bf16[2048,768]{1,0:T(8,128)(2,1)S(1)}, bf16[2048,768]{1,0:T(8,128)(2,1)}, u32[]{:S(2)}) %copy-start) | copy-done | bytes 3145752
  68.6 1.0 %copy-done.3 = bf16[1,128,2048]{2,1,0:T(8,128)(2,1)S(1)} copy-done((bf16[1,128,2048]{2,1,0:T(8,128)(2,1)S(1)}, bf16[1,128,2048]{2,1,0:T(8,128)(2,1)}, u32[]{:S(2)}) %copy-start.3) | copy-done | bytes 524312
  69.6 9.6 %shard_map.60 = f32[6,128]{1,0:T(8,128)S(1)} custom-call(bf16[2048,768]{1,0:T(8,128)(2,1)S(1)} %copy-done, bf16[2,128,2048]{2,1,0:T(8,128)(2,1)S(1)} %copy-done.1, bf16[1,128,2048]{2,1,0:T(8,128)(2,1)S(1)} %collective-permute-done.refs_2_, bf16[1,128,2048]{2,1,0:T(8,128)(2,1)S(1)} %collective-permute-done.1.refs_3_, ...), custom_call_target="tpu_custom_call" | custom-call | tf_op jit(solution)/shard_map/pallas_call | solution.py:65
  (34 shorter events, 3.2 us)
Async XLA Ops:
  1.7 14.9 %collective-permute-start = (bf16[1,128,2048]{2,1,0:T(8,128)(2,1)S(1)}, bf16[1,128,2048]{2,1,0:T(8,128)(2,1)S(1)}, u32[]{:S(2)}, u32[]{:S(2)}) collective-permute-start(bf16[1,128,2048]{2,1,0:T(8,128)(2,1)S(1)} %constant_dynamic-slice_fusion), channel_id=1, source_target_pairs={{0,2},{2,4},{4,6},{6,7},{7,5},{5,3},{3,1},{1,0},{8,10},{10,12},{12... | collective-permute-start | bytes 1572872 | tf_op jit(solution)/shard_map/ppermute | solution.py:204
  4.8 13.4 %collective-permute-start.1 = (bf16[1,128,2048]{2,1,0:T(8,128)(2,1)S(1)}, bf16[1,128,2048]{2,1,0:T(8,128)(2,1)S(1)}, u32[]{:S(2)}, u32[]{:S(2)}) collective-permute-start(bf16[1,128,2048]{2,1,0:T(8,128)(2,1)S(1)} %constant_dynamic-slice_fusion), channel_id=1, source_target_pairs={{2,0},{4,2},{6,4},{7,6},{5,7},{3,5},{1,3},{0,1},{10,8},{12,10},{14... | collective-permute-start | bytes 1572872 | tf_op jit(solution)/shard_map/ppermute | solution.py:207
  4.8 39.7 %collective-permute-start.6 = (bf16[3,2048,128]{2,1,0:T(8,128)(2,1)}, bf16[3,2048,128]{2,1,0:T(8,128)(2,1)S(1)}, u32[]{:S(2)}, u32[]{:S(2)}) collective-permute-start(bf16[3,2048,128]{2,1,0:T(8,128)(2,1)} %refs_0_.1), channel_id=1, source_target_pairs={{0,16},{8,24},{16,0},{24,8},{1,17},{9,25},{17,1},{25,9},{2,18},{10... | collective-permute-start | bytes 4718600 | tf_op jit(solution)/shard_map/ppermute | solution.py:81
  6.8 37.8 %collective-permute-start.7 = (bf16[3,2048,128]{2,1,0:T(8,128)(2,1)}, bf16[3,2048,128]{2,1,0:T(8,128)(2,1)S(1)}, u32[]{:S(2)}, u32[]{:S(2)}) collective-permute-start(bf16[3,2048,128]{2,1,0:T(8,128)(2,1)} %refs_0_.1), channel_id=1, source_target_pairs={{0,8},{8,0},{16,24},{24,16},{1,9},{9,1},{17,25},{25,17},{2,10},{10... | collective-permute-start | bytes 4718600 | tf_op jit(solution)/shard_map/ppermute | solution.py:81
  10.5 56.2 %copy-start.1 = (bf16[2,128,2048]{2,1,0:T(8,128)(2,1)S(1)}, bf16[2,128,2048]{2,1,0:T(8,128)(2,1)}, u32[]{:S(2)}) copy-start(bf16[2,128,2048]{2,1,0:T(8,128)(2,1)} %refs_1_.1) | copy-start | bytes 3145732
  18.2 12.5 %collective-permute-start.2 = (bf16[1,128,2048]{2,1,0:T(8,128)(2,1)S(1)}, bf16[1,128,2048]{2,1,0:T(8,128)(2,1)S(1)}, u32[]{:S(2)}, u32[]{:S(2)}) collective-permute-start(bf16[1,128,2048]{2,1,0:T(8,128)(2,1)S(1)} %collective-permute-done.refs_2_), channel_id=1, source_target_pairs={{0,2},{2,4},{4,6},{6,7},{7,5},{5,3},{3,1},{1,0},{8,10},{10,12},{12... | collective-permute-start | bytes 1572872 | tf_op jit(solution)/shard_map/ppermute | solution.py:204
  19.8 12.2 %collective-permute-start.3 = (bf16[1,128,2048]{2,1,0:T(8,128)(2,1)S(1)}, bf16[1,128,2048]{2,1,0:T(8,128)(2,1)S(1)}, u32[]{:S(2)}, u32[]{:S(2)}) collective-permute-start(bf16[1,128,2048]{2,1,0:T(8,128)(2,1)S(1)} %collective-permute-done.1.refs_3_), channel_id=1, source_target_pairs={{2,0},{4,2},{6,4},{7,6},{5,7},{3,5},{1,3},{0,1},{10,8},{12,10},{14... | collective-permute-start | bytes 1572872 | tf_op jit(solution)/shard_map/ppermute | solution.py:207
  32.0 11.4 %collective-permute-start.4 = (bf16[1,128,2048]{2,1,0:T(8,128)(2,1)S(1)}, bf16[1,128,2048]{2,1,0:T(8,128)(2,1)}, u32[]{:S(2)}, u32[]{:S(2)}) collective-permute-start(bf16[1,128,2048]{2,1,0:T(8,128)(2,1)S(1)} %collective-permute-done.2.refs_4_), channel_id=1, source_target_pairs={{0,2},{2,4},{4,6},{6,7},{7,5},{5,3},{3,1},{1,0},{8,10},{10,12},{12... | collective-permute-start | bytes 1572872 | tf_op jit(solution)/shard_map/ppermute | solution.py:204
  33.5 11.0 %collective-permute-start.5 = (bf16[1,128,2048]{2,1,0:T(8,128)(2,1)S(1)}, bf16[1,128,2048]{2,1,0:T(8,128)(2,1)S(1)}, u32[]{:S(2)}, u32[]{:S(2)}) collective-permute-start(bf16[1,128,2048]{2,1,0:T(8,128)(2,1)S(1)} %collective-permute-done.3.refs_5_), channel_id=1, source_target_pairs={{2,0},{4,2},{6,4},{7,6},{5,7},{3,5},{1,3},{0,1},{10,8},{12,10},{14... | collective-permute-start | bytes 1572872 | tf_op jit(solution)/shard_map/ppermute | solution.py:207
  44.5 2.4 %copy-start.2 = (bf16[1,128,2048]{2,1,0:T(8,128)(2,1)}, bf16[1,128,2048]{2,1,0:T(8,128)(2,1)S(1)}, u32[]{:S(2)}) copy-start(bf16[1,128,2048]{2,1,0:T(8,128)(2,1)S(1)} %collective-permute-done.5.refs_7_) | copy-start | bytes 1572868
  44.5 3.5 %copy-start.4 = (bf16[3,2048,128]{2,1,0:T(8,128)(2,1)}, bf16[3,2048,128]{2,1,0:T(8,128)(2,1)S(1)}, u32[]{:S(2)}) copy-start(bf16[3,2048,128]{2,1,0:T(8,128)(2,1)S(1)} %collective-permute-done.6.refs_2_) | copy-start | bytes 4718596
  44.6 3.5 %copy-start.5 = (bf16[3,2048,128]{2,1,0:T(8,128)(2,1)}, bf16[3,2048,128]{2,1,0:T(8,128)(2,1)S(1)}, u32[]{:S(2)}) copy-start(bf16[3,2048,128]{2,1,0:T(8,128)(2,1)S(1)} %collective-permute-done.7.refs_1_) | copy-start | bytes 4718596
  44.6 3.5 %collective-permute-start.9 = (bf16[3,2048,128]{2,1,0:T(8,128)(2,1)S(1)}, bf16[3,2048,128]{2,1,0:T(8,128)(2,1)S(1)}, u32[]{:S(2)}, u32[]{:S(2)}) collective-permute-start(bf16[3,2048,128]{2,1,0:T(8,128)(2,1)S(1)} %collective-permute-done.6.refs_2_), channel_id=1, source_target_pairs={{0,8},{8,0},{16,24},{24,16},{1,9},{9,1},{17,25},{25,17},{2,10},{10... | collective-permute-start | bytes 4718600 | tf_op jit(solution)/shard_map/ppermute | solution.py:81
  44.6 18.4 %collective-permute-start.8 = (bf16[1,128,2048]{2,1,0:T(8,128)(2,1)}, bf16[1,128,2048]{2,1,0:T(8,128)(2,1)}, u32[]{:S(2)}, u32[]{:S(2)}) collective-permute-start(bf16[1,128,2048]{2,1,0:T(8,128)(2,1)} %collective-permute-done.4.refs_6_), channel_id=1, source_target_pairs={{0,2},{2,4},{4,6},{6,7},{7,5},{5,3},{3,1},{1,0},{8,10},{10,12},{12... | collective-permute-start | bytes 1572872 | tf_op jit(solution)/shard_map/ppermute | solution.py:204
  46.2 17.0 %collective-permute-start.10 = (bf16[1,128,2048]{2,1,0:T(8,128)(2,1)S(1)}, bf16[1,128,2048]{2,1,0:T(8,128)(2,1)}, u32[]{:S(2)}, u32[]{:S(2)}) collective-permute-start(bf16[1,128,2048]{2,1,0:T(8,128)(2,1)S(1)} %collective-permute-done.refs_2_), channel_id=1, source_target_pairs={{0,8},{8,0},{16,24},{24,16},{1,9},{9,1},{17,25},{25,17},{2,10},{10... | collective-permute-start | bytes 1572872 | tf_op jit(solution)/shard_map/ppermute | solution.py:81
  46.4 17.2 %collective-permute-start.11 = (bf16[1,128,2048]{2,1,0:T(8,128)(2,1)S(1)}, bf16[1,128,2048]{2,1,0:T(8,128)(2,1)}, u32[]{:S(2)}, u32[]{:S(2)}) collective-permute-start(bf16[1,128,2048]{2,1,0:T(8,128)(2,1)S(1)} %collective-permute-done.1.refs_3_), channel_id=1, source_target_pairs={{0,8},{8,0},{16,24},{24,16},{1,9},{9,1},{17,25},{25,17},{2,10},{10... | collective-permute-start | bytes 1572872 | tf_op jit(solution)/shard_map/ppermute | solution.py:81
  46.7 17.0 %collective-permute-start.12 = (bf16[1,128,2048]{2,1,0:T(8,128)(2,1)S(1)}, bf16[1,128,2048]{2,1,0:T(8,128)(2,1)}, u32[]{:S(2)}, u32[]{:S(2)}) collective-permute-start(bf16[1,128,2048]{2,1,0:T(8,128)(2,1)S(1)} %collective-permute-done.2.refs_4_), channel_id=1, source_target_pairs={{0,8},{8,0},{16,24},{24,16},{1,9},{9,1},{17,25},{25,17},{2,10},{10... | collective-permute-start | bytes 1572872 | tf_op jit(solution)/shard_map/ppermute | solution.py:81
  48.0 1.1 %copy-start.6 = (bf16[3,2048,128]{2,1,0:T(8,128)(2,1)}, bf16[3,2048,128]{2,1,0:T(8,128)(2,1)S(1)}, u32[]{:S(2)}) copy-start(bf16[3,2048,128]{2,1,0:T(8,128)(2,1)S(1)} %collective-permute-done.9.refs_3_) | copy-start | bytes 4718596
  49.2 14.6 %collective-permute-start.13 = (bf16[1,128,2048]{2,1,0:T(8,128)(2,1)S(1)}, bf16[1,128,2048]{2,1,0:T(8,128)(2,1)}, u32[]{:S(2)}, u32[]{:S(2)}) collective-permute-start(bf16[1,128,2048]{2,1,0:T(8,128)(2,1)S(1)} %collective-permute-done.3.refs_5_), channel_id=1, source_target_pairs={{0,8},{8,0},{16,24},{24,16},{1,9},{9,1},{17,25},{25,17},{2,10},{10... | collective-permute-start | bytes 1572872 | tf_op jit(solution)/shard_map/ppermute | solution.py:81
  63.0 2.2 %collective-permute-start.14 = (bf16[1,128,2048]{2,1,0:T(8,128)(2,1)}, bf16[1,128,2048]{2,1,0:T(8,128)(2,1)S(1)}, u32[]{:S(2)}, u32[]{:S(2)}) collective-permute-start(bf16[1,128,2048]{2,1,0:T(8,128)(2,1)} %collective-permute-done.4.refs_6_), channel_id=1, source_target_pairs={{0,8},{8,0},{16,24},{24,16},{1,9},{9,1},{17,25},{25,17},{2,10},{10... | collective-permute-start | bytes 1572872 | tf_op jit(solution)/shard_map/ppermute | solution.py:81
  63.2 16.1 %copy-start.7 = (s32[6]{0:T(128)S(1)}, s32[6]{0:T(128)}, u32[]{:S(2)}) copy-start(s32[6]{0:T(128)} %param.8) | copy-start | bytes 76
  63.2 2.7 %collective-permute-start.15 = (bf16[1,128,2048]{2,1,0:T(8,128)(2,1)}, bf16[1,128,2048]{2,1,0:T(8,128)(2,1)S(1)}, u32[]{:S(2)}, u32[]{:S(2)}) collective-permute-start(bf16[1,128,2048]{2,1,0:T(8,128)(2,1)} %copy-done.2), channel_id=1, source_target_pairs={{0,8},{8,0},{16,24},{24,16},{1,9},{9,1},{17,25},{25,17},{2,10},{10... | collective-permute-start | bytes 1572872 | tf_op jit(solution)/shard_map/ppermute | solution.py:81
  63.6 3.1 %collective-permute-start.16 = (bf16[1,128,2048]{2,1,0:T(8,128)(2,1)}, bf16[1,128,2048]{2,1,0:T(8,128)(2,1)S(1)}, u32[]{:S(2)}, u32[]{:S(2)}) collective-permute-start(bf16[1,128,2048]{2,1,0:T(8,128)(2,1)} %collective-permute-done.8.refs_8_), channel_id=1, source_target_pairs={{0,8},{8,0},{16,24},{24,16},{1,9},{9,1},{17,25},{25,17},{2,10},{10... | collective-permute-start | bytes 1572872 | tf_op jit(solution)/shard_map/ppermute | solution.py:81
  66.7 1.9 %copy-start = (bf16[2048,768]{1,0:T(8,128)(2,1)S(1)}, bf16[2048,768]{1,0:T(8,128)(2,1)}, u32[]{:S(2)}) copy-start(bf16[2048,768]{1,0:T(8,128)(2,1)} %get-tuple-element.43.refs_0_) | copy-start | bytes 9437188
  (1 other events, 1.0 us)

commit v17 on v16

--- a/solution.py
+++ b/solution.py
@@ -129,8 +129,16 @@
         ]
 
     for s in range(n_slot):
-        widened = kicked_buf[s].astype(jnp.float32)
-        theta = jnp.dot(widened, inverses[s], precision=lax.Precision.HIGHEST, preferred_element_type=jnp.float32)
+        kicked = kicked_buf[s]
+        high = inverses[s].astype(jnp.bfloat16)
+        rest = inverses[s] - high.astype(jnp.float32)
+        middle = rest.astype(jnp.bfloat16)
+        low = (rest - middle.astype(jnp.float32)).astype(jnp.bfloat16)
+        theta = (
+            jnp.dot(kicked, high, preferred_element_type=jnp.float32)
+            + jnp.dot(kicked, middle, preferred_element_type=jnp.float32)
+            + jnp.dot(kicked, low, preferred_element_type=jnp.float32)
+        )
         theta_out[:, s * electrons:(s + 1) * electrons] = theta.astype(jnp.bfloat16)
     for copy in out_copies:
         copy.wait()

time: 80.1 us -> 77.5 us (0.968)
  Pallas kernels: 23.2 us -> 20.5 us
    pallas_call x1, Pallas kernels: 13.7 us -> 10.9 us  [kick(): pl.pallas_call(kick_kernel, out_shape=[shape, wide], grid_spec=grid_spec)]
  transfers between devices with their start and end apart: 17 -> 17, of which waited for: 10 -> 10; matrix products, arithmetic and copies ran while one was open for 5% -> 5% of each run, Pallas kernels for 17% -> 14%
where the time goes in v17:
time: 77.5 us; the launch traced here: 77.1 us
  waiting for transfers between devices  34 us (44%)
  Pallas kernels  20.5 us (26%)
  starting transfers between devices  12.3 us (16%)
  local copies, waits for them, and re-layouts  6.76 us (9%)
  other arithmetic  2.84 us (4%)
    ppermute x4, waiting for transfers between devices, body(): ahead = lax.ppermute(ahead, 'chol', forward)  25.9 us
    pallas_call x1, Pallas kernels, kick(): pl.pallas_call(kick_kernel, out_shape=[shape, wide], grid_spec=grid_spec)  10.9 us
    pallas_call x1, Pallas kernels, block_energy(): pl.pallas_call(energy_kernel, out_shape=jax.ShapeDtypeStruct((n_slot, 128...  9.57 us
    ppermute x4, starting transfers between devices, body(): ahead = lax.ppermute(ahead, 'chol', forward)  7.8 us
    unnamed x16, local copies, waits for them, and re-layouts  4.09 us
    ppermute x10, waiting for transfers between devices, swap_pairs(): return lax.ppermute(x, axis, perm)  4.05 us
    ppermute x3, waiting for transfers between devices, body(): behind = lax.ppermute(behind, 'chol', backward)  4 us
    ppermute x10, starting transfers between devices, swap_pairs(): return lax.ppermute(x, axis, perm)  3.6 us
  transfers between devices with their start and end apart: 17, of which 10 were waited for; matrix products, arithmetic and copies ran while one was open for 5% of the time, Pallas kernels for 14%

profile of v17, /device:TPU:0, one launch (start us, length us, event | category | flops | bytes accessed | tf_op | source)
XLA Modules:
  0.0 77.1 jit_solution(8453257563804541807)
XLA Ops:
  0.6 1.1 %constant_dynamic-slice_fusion = bf16[1,128,2048]{2,1,0:T(8,128)(2,1)S(1)} fusion(bf16[2,128,2048]{2,1,0:T(8,128)(2,1)} %refs_1_.1, s32[]{:T(128)S(6)} %select_n.26), kind=kLoop, calls=%fused_computation.6 | loop fusion | bytes 1048580 | tf_op jit(solution)/shard_map/dynamic_slice | solution.py:197
  1.7 3.1 %collective-permute-start = (bf16[1,128,2048]{2,1,0:T(8,128)(2,1)S(1)}, bf16[1,128,2048]{2,1,0:T(8,128)(2,1)S(1)}, u32[]{:S(2)}, u32[]{:S(2)}) collective-permute-start(bf16[1,128,2048]{2,1,0:T(8,128)(2,1)S(1)} %constant_dynamic-slice_fusion), channel_id=1, source_target_pairs={{0,2},{2,4},{4,6},{6,7},{7,5},{5,3},{3,1},{1,0},{8,10},{10,12},{12... | collective-permute-start | bytes 1572872 | tf_op jit(solution)/shard_map/ppermute | solution.py:212
  4.8 1.9 %collective-permute-start.6 = (bf16[3,2048,128]{2,1,0:T(8,128)(2,1)}, bf16[3,2048,128]{2,1,0:T(8,128)(2,1)S(1)}, u32[]{:S(2)}, u32[]{:S(2)}) collective-permute-start(bf16[3,2048,128]{2,1,0:T(8,128)(2,1)} %refs_0_.1), channel_id=1, source_target_pairs={{0,16},{8,24},{16,0},{24,8},{1,17},{9,25},{17,1},{25,9},{2,18},{10... | collective-permute-start | bytes 4718600 | tf_op jit(solution)/shard_map/ppermute | solution.py:81
  6.8 1.5 %scatter.4.refs_4_ = f32[8,2048]{1,0:T(8,128)} pad(f32[6,2048]{1,0:T(8,128)} %param.9, f32[]{:T(128)} %constant.67.clone.1), padding=0_2x0_0 | pad | bytes 114692 | tf_op jit(solution)/shard_map/scatter | solution.py:154
  8.2 1.2 %fusion.source_ref = s32[6]{0:T(128)} fusion(s32[6]{0:T(128)} %param.8, s32[]{:T(128)S(6)} %axis_index.15), kind=kLoop, calls=%fused_computation.5 | loop fusion | flops 96 | bytes 52 | tf_op jit(solution)/shard_map/add | solution.py:152
  9.4 1.1 %compare_convert_fusion.living_ref = s32[6]{0:T(128)} fusion(s32[6]{0:T(128)} %param.8), kind=kLoop, calls=%fused_computation.4 | loop fusion | flops 12 | bytes 48 | tf_op jit(solution)/shard_map/convert_element_type | solution.py:149
  10.5 6.1 %collective-permute-done.refs_2_ = bf16[1,128,2048]{2,1,0:T(8,128)(2,1)S(1)} collective-permute-done((bf16[1,128,2048]{2,1,0:T(8,128)(2,1)S(1)}, bf16[1,128,2048]{2,1,0:T(8,128)(2,1)S(1)}, u32[]{:S(2)}, u32[]{:S(2)}) %collective-permute-start) | collective-permute-done | bytes 524320 | tf_op jit(solution)/shard_map/ppermute | solution.py:212
  16.7 1.5 %collective-permute-done.1.refs_3_ = bf16[1,128,2048]{2,1,0:T(8,128)(2,1)S(1)} collective-permute-done((bf16[1,128,2048]{2,1,0:T(8,128)(2,1)S(1)}, bf16[1,128,2048]{2,1,0:T(8,128)(2,1)S(1)}, u32[]{:S(2)}, u32[]{:S(2)}) %collective-permute-start.1) | collective-permute-done | bytes 524320 | tf_op jit(solution)/shard_map/ppermute | solution.py:215
  18.2 1.6 %collective-permute-start.2 = (bf16[1,128,2048]{2,1,0:T(8,128)(2,1)S(1)}, bf16[1,128,2048]{2,1,0:T(8,128)(2,1)S(1)}, u32[]{:S(2)}, u32[]{:S(2)}) collective-permute-start(bf16[1,128,2048]{2,1,0:T(8,128)(2,1)S(1)} %collective-permute-done.refs_2_), channel_id=1, source_target_pairs={{0,2},{2,4},{4,6},{6,7},{7,5},{5,3},{3,1},{1,0},{8,10},{10,12},{12... | collective-permute-start | bytes 1572872 | tf_op jit(solution)/shard_map/ppermute | solution.py:212
  20.2 10.4 %collective-permute-done.2.refs_4_ = bf16[1,128,2048]{2,1,0:T(8,128)(2,1)S(1)} collective-permute-done((bf16[1,128,2048]{2,1,0:T(8,128)(2,1)S(1)}, bf16[1,128,2048]{2,1,0:T(8,128)(2,1)S(1)}, u32[]{:S(2)}, u32[]{:S(2)}) %collective-permute-start.2) | collective-permute-done | bytes 524320 | tf_op jit(solution)/shard_map/ppermute | solution.py:212
  30.7 1.3 %collective-permute-done.3.refs_5_ = bf16[1,128,2048]{2,1,0:T(8,128)(2,1)S(1)} collective-permute-done((bf16[1,128,2048]{2,1,0:T(8,128)(2,1)S(1)}, bf16[1,128,2048]{2,1,0:T(8,128)(2,1)S(1)}, u32[]{:S(2)}, u32[]{:S(2)}) %collective-permute-start.3) | collective-permute-done | bytes 524320 | tf_op jit(solution)/shard_map/ppermute | solution.py:215
  32.0 1.6 %collective-permute-start.4 = (bf16[1,128,2048]{2,1,0:T(8,128)(2,1)S(1)}, bf16[1,128,2048]{2,1,0:T(8,128)(2,1)}, u32[]{:S(2)}, u32[]{:S(2)}) collective-permute-start(bf16[1,128,2048]{2,1,0:T(8,128)(2,1)S(1)} %collective-permute-done.2.refs_4_), channel_id=1, source_target_pairs={{0,2},{2,4},{4,6},{6,7},{7,5},{5,3},{3,1},{1,0},{8,10},{10,12},{12... | collective-permute-start | bytes 1572872 | tf_op jit(solution)/shard_map/ppermute | solution.py:212
  34.0 9.4 %collective-permute-done.4.refs_6_ = bf16[1,128,2048]{2,1,0:T(8,128)(2,1)} collective-permute-done((bf16[1,128,2048]{2,1,0:T(8,128)(2,1)S(1)}, bf16[1,128,2048]{2,1,0:T(8,128)(2,1)}, u32[]{:S(2)}, u32[]{:S(2)}) %collective-permute-start.4) | collective-permute-done | bytes 524320 | tf_op jit(solution)/shard_map/ppermute | solution.py:212
  43.3 1.2 %collective-permute-done.5.refs_7_ = bf16[1,128,2048]{2,1,0:T(8,128)(2,1)S(1)} collective-permute-done((bf16[1,128,2048]{2,1,0:T(8,128)(2,1)S(1)}, bf16[1,128,2048]{2,1,0:T(8,128)(2,1)S(1)}, u32[]{:S(2)}, u32[]{:S(2)}) %collective-permute-start.5) | collective-permute-done | bytes 524320 | tf_op jit(solution)/shard_map/ppermute | solution.py:215
  44.6 1.6 %collective-permute-start.8 = (bf16[1,128,2048]{2,1,0:T(8,128)(2,1)}, bf16[1,128,2048]{2,1,0:T(8,128)(2,1)}, u32[]{:S(2)}, u32[]{:S(2)}) collective-permute-start(bf16[1,128,2048]{2,1,0:T(8,128)(2,1)} %collective-permute-done.4.refs_6_), channel_id=1, source_target_pairs={{0,2},{2,4},{4,6},{6,7},{7,5},{5,3},{3,1},{1,0},{8,10},{10,12},{12... | collective-permute-start | bytes 1572872 | tf_op jit(solution)/shard_map/ppermute | solution.py:212
  46.9 1.1 %collective-permute-done.9.refs_3_ = bf16[3,2048,128]{2,1,0:T(8,128)(2,1)S(1)} collective-permute-done((bf16[3,2048,128]{2,1,0:T(8,128)(2,1)S(1)}, bf16[3,2048,128]{2,1,0:T(8,128)(2,1)S(1)}, u32[]{:S(2)}, u32[]{:S(2)}) %collective-permute-start.9) | collective-permute-done | bytes 1572896 | tf_op jit(solution)/shard_map/ppermute | solution.py:81
  48.0 1.1 %copy-done.6 = bf16[3,2048,128]{2,1,0:T(8,128)(2,1)} copy-done((bf16[3,2048,128]{2,1,0:T(8,128)(2,1)}, bf16[3,2048,128]{2,1,0:T(8,128)(2,1)S(1)}, u32[]{:S(2)}) %copy-start.6) | copy-done | bytes 1572888
  49.3 10.9 %shard_map.59 = (bf16[6,2048,128]{2,1,0:T(8,128)(2,1)}, bf16[2048,768]{1,0:T(8,128)(2,1)}) custom-call(s32[6]{0:T(128)} %fusion.source_ref, s32[6]{0:T(128)} %compare_convert_fusion.living_ref, bf16[3,2048,128]{2,1,0:T(8,128)(2,1)} %refs_0_.1, bf16[3,2048,128]{2,1,0:T(8,128)(2,1)} %copy-done.5, bf16[3,2048,128]{2,1,0:T(8,128)(2,1)} %copy-done.4, ...), custom_call_target="tpu_custom_call" | custom-call | tf_op jit(solution)/shard_map/pallas_call | solution.py:179
  61.1 1.4 %collective-permute-done.14.refs_13_ = bf16[1,128,2048]{2,1,0:T(8,128)(2,1)S(1)} collective-permute-done((bf16[1,128,2048]{2,1,0:T(8,128)(2,1)}, bf16[1,128,2048]{2,1,0:T(8,128)(2,1)S(1)}, u32[]{:S(2)}, u32[]{:S(2)}) %collective-permute-start.14) | collective-permute-done | bytes 524320 | tf_op jit(solution)/shard_map/ppermute | solution.py:81
  62.5 0.7 collective-permute-done.15.refs_14_
  63.2 0.7 collective-permute-done.16.refs_15_
  64.0 1.9 %copy-done = bf16[2048,768]{1,0:T(8,128)(2,1)S(1)} copy-done((bf16[2048,768]{1,0:T(8,128)(2,1)S(1)}, bf16[2048,768]{1,0:T(8,128)(2,1)}, u32[]{:S(2)}) %copy-start) | copy-done | bytes 3145752
  65.9 1.0 %copy-done.3 = bf16[1,128,2048]{2,1,0:T(8,128)(2,1)S(1)} copy-done((bf16[1,128,2048]{2,1,0:T(8,128)(2,1)S(1)}, bf16[1,128,2048]{2,1,0:T(8,128)(2,1)}, u32[]{:S(2)}) %copy-start.3) | copy-done | bytes 524312
  66.9 9.6 %shard_map.60 = f32[6,128]{1,0:T(8,128)S(1)} custom-call(bf16[2048,768]{1,0:T(8,128)(2,1)S(1)} %copy-done, bf16[2,128,2048]{2,1,0:T(8,128)(2,1)S(1)} %copy-done.1, bf16[1,128,2048]{2,1,0:T(8,128)(2,1)S(1)} %collective-permute-done.refs_2_, bf16[1,128,2048]{2,1,0:T(8,128)(2,1)S(1)} %collective-permute-done.1.refs_3_, ...), custom_call_target="tpu_custom_call" | custom-call | tf_op jit(solution)/shard_map/pallas_call | solution.py:65
  (34 shorter events, 3.2 us)
Async XLA Ops:
  1.7 14.9 %collective-permute-start = (bf16[1,128,2048]{2,1,0:T(8,128)(2,1)S(1)}, bf16[1,128,2048]{2,1,0:T(8,128)(2,1)S(1)}, u32[]{:S(2)}, u32[]{:S(2)}) collective-permute-start(bf16[1,128,2048]{2,1,0:T(8,128)(2,1)S(1)} %constant_dynamic-slice_fusion), channel_id=1, source_target_pairs={{0,2},{2,4},{4,6},{6,7},{7,5},{5,3},{3,1},{1,0},{8,10},{10,12},{12... | collective-permute-start | bytes 1572872 | tf_op jit(solution)/shard_map/ppermute | solution.py:212
  4.8 13.4 %collective-permute-start.1 = (bf16[1,128,2048]{2,1,0:T(8,128)(2,1)S(1)}, bf16[1,128,2048]{2,1,0:T(8,128)(2,1)S(1)}, u32[]{:S(2)}, u32[]{:S(2)}) collective-permute-start(bf16[1,128,2048]{2,1,0:T(8,128)(2,1)S(1)} %constant_dynamic-slice_fusion), channel_id=1, source_target_pairs={{2,0},{4,2},{6,4},{7,6},{5,7},{3,5},{1,3},{0,1},{10,8},{12,10},{14... | collective-permute-start | bytes 1572872 | tf_op jit(solution)/shard_map/ppermute | solution.py:215
  4.8 39.7 %collective-permute-start.6 = (bf16[3,2048,128]{2,1,0:T(8,128)(2,1)}, bf16[3,2048,128]{2,1,0:T(8,128)(2,1)S(1)}, u32[]{:S(2)}, u32[]{:S(2)}) collective-permute-start(bf16[3,2048,128]{2,1,0:T(8,128)(2,1)} %refs_0_.1), channel_id=1, source_target_pairs={{0,16},{8,24},{16,0},{24,8},{1,17},{9,25},{17,1},{25,9},{2,18},{10... | collective-permute-start | bytes 4718600 | tf_op jit(solution)/shard_map/ppermute | solution.py:81
  6.8 37.8 %collective-permute-start.7 = (bf16[3,2048,128]{2,1,0:T(8,128)(2,1)}, bf16[3,2048,128]{2,1,0:T(8,128)(2,1)S(1)}, u32[]{:S(2)}, u32[]{:S(2)}) collective-permute-start(bf16[3,2048,128]{2,1,0:T(8,128)(2,1)} %refs_0_.1), channel_id=1, source_target_pairs={{0,8},{8,0},{16,24},{24,16},{1,9},{9,1},{17,25},{25,17},{2,10},{10... | collective-permute-start | bytes 4718600 | tf_op jit(solution)/shard_map/ppermute | solution.py:81
  10.5 53.4 %copy-start.1 = (bf16[2,128,2048]{2,1,0:T(8,128)(2,1)S(1)}, bf16[2,128,2048]{2,1,0:T(8,128)(2,1)}, u32[]{:S(2)}) copy-start(bf16[2,128,2048]{2,1,0:T(8,128)(2,1)} %refs_1_.1) | copy-start | bytes 3145732
  18.2 12.5 %collective-permute-start.2 = (bf16[1,128,2048]{2,1,0:T(8,128)(2,1)S(1)}, bf16[1,128,2048]{2,1,0:T(8,128)(2,1)S(1)}, u32[]{:S(2)}, u32[]{:S(2)}) collective-permute-start(bf16[1,128,2048]{2,1,0:T(8,128)(2,1)S(1)} %collective-permute-done.refs_2_), channel_id=1, source_target_pairs={{0,2},{2,4},{4,6},{6,7},{7,5},{5,3},{3,1},{1,0},{8,10},{10,12},{12... | collective-permute-start | bytes 1572872 | tf_op jit(solution)/shard_map/ppermute | solution.py:212
  19.8 12.2 %collective-permute-start.3 = (bf16[1,128,2048]{2,1,0:T(8,128)(2,1)S(1)}, bf16[1,128,2048]{2,1,0:T(8,128)(2,1)S(1)}, u32[]{:S(2)}, u32[]{:S(2)}) collective-permute-start(bf16[1,128,2048]{2,1,0:T(8,128)(2,1)S(1)} %collective-permute-done.1.refs_3_), channel_id=1, source_target_pairs={{2,0},{4,2},{6,4},{7,6},{5,7},{3,5},{1,3},{0,1},{10,8},{12,10},{14... | collective-permute-start | bytes 1572872 | tf_op jit(solution)/shard_map/ppermute | solution.py:215
  32.0 11.4 %collective-permute-start.4 = (bf16[1,128,2048]{2,1,0:T(8,128)(2,1)S(1)}, bf16[1,128,2048]{2,1,0:T(8,128)(2,1)}, u32[]{:S(2)}, u32[]{:S(2)}) collective-permute-start(bf16[1,128,2048]{2,1,0:T(8,128)(2,1)S(1)} %collective-permute-done.2.refs_4_), channel_id=1, source_target_pairs={{0,2},{2,4},{4,6},{6,7},{7,5},{5,3},{3,1},{1,0},{8,10},{10,12},{12... | collective-permute-start | bytes 1572872 | tf_op jit(solution)/shard_map/ppermute | solution.py:212
  33.5 11.0 %collective-permute-start.5 = (bf16[1,128,2048]{2,1,0:T(8,128)(2,1)S(1)}, bf16[1,128,2048]{2,1,0:T(8,128)(2,1)S(1)}, u32[]{:S(2)}, u32[]{:S(2)}) collective-permute-start(bf16[1,128,2048]{2,1,0:T(8,128)(2,1)S(1)} %collective-permute-done.3.refs_5_), channel_id=1, source_target_pairs={{2,0},{4,2},{6,4},{7,6},{5,7},{3,5},{1,3},{0,1},{10,8},{12,10},{14... | collective-permute-start | bytes 1572872 | tf_op jit(solution)/shard_map/ppermute | solution.py:215
  44.5 2.4 %copy-start.2 = (bf16[1,128,2048]{2,1,0:T(8,128)(2,1)}, bf16[1,128,2048]{2,1,0:T(8,128)(2,1)S(1)}, u32[]{:S(2)}) copy-start(bf16[1,128,2048]{2,1,0:T(8,128)(2,1)S(1)} %collective-permute-done.5.refs_7_) | copy-start | bytes 1572868
  44.5 3.5 %copy-start.4 = (bf16[3,2048,128]{2,1,0:T(8,128)(2,1)}, bf16[3,2048,128]{2,1,0:T(8,128)(2,1)S(1)}, u32[]{:S(2)}) copy-start(bf16[3,2048,128]{2,1,0:T(8,128)(2,1)S(1)} %collective-permute-done.6.refs_2_) | copy-start | bytes 4718596
  44.6 3.5 %copy-start.5 = (bf16[3,2048,128]{2,1,0:T(8,128)(2,1)}, bf16[3,2048,128]{2,1,0:T(8,128)(2,1)S(1)}, u32[]{:S(2)}) copy-start(bf16[3,2048,128]{2,1,0:T(8,128)(2,1)S(1)} %collective-permute-done.7.refs_1_) | copy-start | bytes 4718596
  44.6 3.5 %collective-permute-start.9 = (bf16[3,2048,128]{2,1,0:T(8,128)(2,1)S(1)}, bf16[3,2048,128]{2,1,0:T(8,128)(2,1)S(1)}, u32[]{:S(2)}, u32[]{:S(2)}) collective-permute-start(bf16[3,2048,128]{2,1,0:T(8,128)(2,1)S(1)} %collective-permute-done.6.refs_2_), channel_id=1, source_target_pairs={{0,8},{8,0},{16,24},{24,16},{1,9},{9,1},{17,25},{25,17},{2,10},{10... | collective-permute-start | bytes 4718600 | tf_op jit(solution)/shard_map/ppermute | solution.py:81
  44.6 15.6 %collective-permute-start.8 = (bf16[1,128,2048]{2,1,0:T(8,128)(2,1)}, bf16[1,128,2048]{2,1,0:T(8,128)(2,1)}, u32[]{:S(2)}, u32[]{:S(2)}) collective-permute-start(bf16[1,128,2048]{2,1,0:T(8,128)(2,1)} %collective-permute-done.4.refs_6_), channel_id=1, source_target_pairs={{0,2},{2,4},{4,6},{6,7},{7,5},{5,3},{3,1},{1,0},{8,10},{10,12},{12... | collective-permute-start | bytes 1572872 | tf_op jit(solution)/shard_map/ppermute | solution.py:212
  46.2 14.4 %collective-permute-start.10 = (bf16[1,128,2048]{2,1,0:T(8,128)(2,1)S(1)}, bf16[1,128,2048]{2,1,0:T(8,128)(2,1)}, u32[]{:S(2)}, u32[]{:S(2)}) collective-permute-start(bf16[1,128,2048]{2,1,0:T(8,128)(2,1)S(1)} %collective-permute-done.refs_2_), channel_id=1, source_target_pairs={{0,8},{8,0},{16,24},{24,16},{1,9},{9,1},{17,25},{25,17},{2,10},{10... | collective-permute-start | bytes 1572872 | tf_op jit(solution)/shard_map/ppermute | solution.py:81
  46.4 14.5 %collective-permute-start.11 = (bf16[1,128,2048]{2,1,0:T(8,128)(2,1)S(1)}, bf16[1,128,2048]{2,1,0:T(8,128)(2,1)}, u32[]{:S(2)}, u32[]{:S(2)}) collective-permute-start(bf16[1,128,2048]{2,1,0:T(8,128)(2,1)S(1)} %collective-permute-done.1.refs_3_), channel_id=1, source_target_pairs={{0,8},{8,0},{16,24},{24,16},{1,9},{9,1},{17,25},{25,17},{2,10},{10... | collective-permute-start | bytes 1572872 | tf_op jit(solution)/shard_map/ppermute | solution.py:81
  46.7 14.4 %collective-permute-start.12 = (bf16[1,128,2048]{2,1,0:T(8,128)(2,1)S(1)}, bf16[1,128,2048]{2,1,0:T(8,128)(2,1)}, u32[]{:S(2)}, u32[]{:S(2)}) collective-permute-start(bf16[1,128,2048]{2,1,0:T(8,128)(2,1)S(1)} %collective-permute-done.2.refs_4_), channel_id=1, source_target_pairs={{0,8},{8,0},{16,24},{24,16},{1,9},{9,1},{17,25},{25,17},{2,10},{10... | collective-permute-start | bytes 1572872 | tf_op jit(solution)/shard_map/ppermute | solution.py:81
  48.0 1.1 %copy-start.6 = (bf16[3,2048,128]{2,1,0:T(8,128)(2,1)}, bf16[3,2048,128]{2,1,0:T(8,128)(2,1)S(1)}, u32[]{:S(2)}) copy-start(bf16[3,2048,128]{2,1,0:T(8,128)(2,1)S(1)} %collective-permute-done.9.refs_3_) | copy-start | bytes 4718596
  49.2 11.9 %collective-permute-start.13 = (bf16[1,128,2048]{2,1,0:T(8,128)(2,1)S(1)}, bf16[1,128,2048]{2,1,0:T(8,128)(2,1)}, u32[]{:S(2)}, u32[]{:S(2)}) collective-permute-start(bf16[1,128,2048]{2,1,0:T(8,128)(2,1)S(1)} %collective-permute-done.3.refs_5_), channel_id=1, source_target_pairs={{0,8},{8,0},{16,24},{24,16},{1,9},{9,1},{17,25},{25,17},{2,10},{10... | collective-permute-start | bytes 1572872 | tf_op jit(solution)/shard_map/ppermute | solution.py:81
  60.3 2.2 %collective-permute-start.14 = (bf16[1,128,2048]{2,1,0:T(8,128)(2,1)}, bf16[1,128,2048]{2,1,0:T(8,128)(2,1)S(1)}, u32[]{:S(2)}, u32[]{:S(2)}) collective-permute-start(bf16[1,128,2048]{2,1,0:T(8,128)(2,1)} %collective-permute-done.4.refs_6_), channel_id=1, source_target_pairs={{0,8},{8,0},{16,24},{24,16},{1,9},{9,1},{17,25},{25,17},{2,10},{10... | collective-permute-start | bytes 1572872 | tf_op jit(solution)/shard_map/ppermute | solution.py:81
  60.6 16.0 %copy-start.7 = (s32[6]{0:T(128)S(1)}, s32[6]{0:T(128)}, u32[]{:S(2)}) copy-start(s32[6]{0:T(128)} %param.8) | copy-start | bytes 76
  60.6 2.7 %collective-permute-start.15 = (bf16[1,128,2048]{2,1,0:T(8,128)(2,1)}, bf16[1,128,2048]{2,1,0:T(8,128)(2,1)S(1)}, u32[]{:S(2)}, u32[]{:S(2)}) collective-permute-start(bf16[1,128,2048]{2,1,0:T(8,128)(2,1)} %copy-done.2), channel_id=1, source_target_pairs={{0,8},{8,0},{16,24},{24,16},{1,9},{9,1},{17,25},{25,17},{2,10},{10... | collective-permute-start | bytes 1572872 | tf_op jit(solution)/shard_map/ppermute | solution.py:81
  60.9 3.1 %collective-permute-start.16 = (bf16[1,128,2048]{2,1,0:T(8,128)(2,1)}, bf16[1,128,2048]{2,1,0:T(8,128)(2,1)S(1)}, u32[]{:S(2)}, u32[]{:S(2)}) collective-permute-start(bf16[1,128,2048]{2,1,0:T(8,128)(2,1)} %collective-permute-done.8.refs_8_), channel_id=1, source_target_pairs={{0,8},{8,0},{16,24},{24,16},{1,9},{9,1},{17,25},{25,17},{2,10},{10... | collective-permute-start | bytes 1572872 | tf_op jit(solution)/shard_map/ppermute | solution.py:81
  64.0 1.9 %copy-start = (bf16[2048,768]{1,0:T(8,128)(2,1)S(1)}, bf16[2048,768]{1,0:T(8,128)(2,1)}, u32[]{:S(2)}) copy-start(bf16[2048,768]{1,0:T(8,128)(2,1)} %get-tuple-element.43.refs_0_) | copy-start | bytes 9437188
  (1 other events, 1.0 us)

commit v18 on v16

--- a/solution.py
+++ b/solution.py
@@ -81,6 +81,18 @@
     return lax.ppermute(x, axis, perm)
 
 
+def exact_bf16_product(exact, wide):
+    high = wide.astype(jnp.bfloat16)
+    rest = wide - high.astype(jnp.float32)
+    middle = rest.astype(jnp.bfloat16)
+    low = (rest - middle.astype(jnp.float32)).astype(jnp.bfloat16)
+    return (
+        jnp.dot(exact, high, preferred_element_type=jnp.float32)
+        + jnp.dot(exact, middle, preferred_element_type=jnp.float32)
+        + jnp.dot(exact, low, preferred_element_type=jnp.float32)
+    )
+
+
 def kick_kernel(source_ref, living_ref, *refs):
     walker_refs = refs[:4]
     field_ref, new_hbm, theta_out, walkers, kicked_buf, new_buf, in_sem, out_sem = refs[4:]
@@ -113,24 +125,20 @@
         copy = pltpu.make_async_copy(new_buf.at[s], new_hbm.at[s], out_sem.at[0, s])
         copy.start()
         out_copies.append(copy)
-        intersection = kicked[:electrons, :].astype(jnp.float32)
-        diagonal = jnp.sum(jnp.where(eye, intersection, 0.0), axis=0, keepdims=True)
+        intersection = kicked[:electrons, :]
+        diagonal = jnp.sum(jnp.where(eye, intersection.astype(jnp.float32), 0.0), axis=0, keepdims=True)
         intersections.append(intersection)
         inverses.append(jnp.where(eye, 1.0 / diagonal, 0.0))
 
     for sweep in range(ITERS):
-        products = [
-            jnp.dot(x, inv, precision=lax.Precision.HIGHEST, preferred_element_type=jnp.float32)
-            for x, inv in zip(intersections, inverses)
-        ]
+        products = [exact_bf16_product(x, inv) for x, inv in zip(intersections, inverses)]
         inverses = [
             jnp.dot(inv, 2.0 * identity - p, precision=lax.Precision.HIGHEST, preferred_element_type=jnp.float32)
             for inv, p in zip(inverses, products)
         ]
 
     for s in range(n_slot):
-        widened = kicked_buf[s].astype(jnp.float32)
-        theta = jnp.dot(widened, inverses[s], precision=lax.Precision.HIGHEST, preferred_element_type=jnp.float32)
+        theta = exact_bf16_product(kicked_buf[s], inverses[s])
         theta_out[:, s * electrons:(s + 1) * electrons] = theta.astype(jnp.bfloat16)
     for copy in out_copies:
         copy.wait()

time: 80.1 us -> 77 us (0.961)
  Pallas kernels: 23.2 us -> 19.9 us
    pallas_call x1, Pallas kernels: 13.7 us -> 10.3 us  [kick(): pl.pallas_call(kick_kernel, out_shape=[shape, wide], grid_spec=grid_spec)]
  transfers between devices with their start and end apart: 17 -> 17, of which waited for: 10 -> 10; matrix products, arithmetic and copies ran while one was open for 5% -> 5% of each run, Pallas kernels for 17% -> 13%
where the time goes in v18:
time: 77 us; the launch traced here: 76.5 us
  waiting for transfers between devices  33.8 us (44%)
  Pallas kernels  19.9 us (26%)
  starting transfers between devices  12.5 us (16%)
  local copies, waits for them, and re-layouts  6.76 us (9%)
  other arithmetic  2.84 us (4%)
    ppermute x4, waiting for transfers between devices, body(): ahead = lax.ppermute(ahead, 'chol', forward)  25.9 us
    pallas_call x1, Pallas kernels, kick(): pl.pallas_call(kick_kernel, out_shape=[shape, wide], grid_spec=grid_spec)  10.3 us
    pallas_call x1, Pallas kernels, block_energy(): pl.pallas_call(energy_kernel, out_shape=jax.ShapeDtypeStruct((n_slot, 128...  9.56 us
    ppermute x4, starting transfers between devices, body(): ahead = lax.ppermute(ahead, 'chol', forward)  7.8 us
    unnamed x16, local copies, waits for them, and re-layouts  4.09 us
    ppermute x3, waiting for transfers between devices, body(): behind = lax.ppermute(behind, 'chol', backward)  4 us
    ppermute x10, waiting for transfers between devices, swap_pairs(): return lax.ppermute(x, axis, perm)  3.88 us
    ppermute x10, starting transfers between devices, swap_pairs(): return lax.ppermute(x, axis, perm)  3.77 us
  transfers between devices with their start and end apart: 17, of which 10 were waited for; matrix products, arithmetic and copies ran while one was open for 5% of the time, Pallas kernels for 13%

profile of v18, /device:TPU:0, one launch (start us, length us, event | category | flops | bytes accessed | tf_op | source)
XLA Modules:
  0.0 76.5 jit_solution(387581674855841162)
XLA Ops:
  0.6 1.1 %constant_dynamic-slice_fusion = bf16[1,128,2048]{2,1,0:T(8,128)(2,1)S(1)} fusion(bf16[2,128,2048]{2,1,0:T(8,128)(2,1)} %refs_1_.1, s32[]{:T(128)S(6)} %select_n.26), kind=kLoop, calls=%fused_computation.6 | loop fusion | bytes 1048580 | tf_op jit(solution)/shard_map/dynamic_slice | solution.py:197
  1.7 3.1 %collective-permute-start = (bf16[1,128,2048]{2,1,0:T(8,128)(2,1)S(1)}, bf16[1,128,2048]{2,1,0:T(8,128)(2,1)S(1)}, u32[]{:S(2)}, u32[]{:S(2)}) collective-permute-start(bf16[1,128,2048]{2,1,0:T(8,128)(2,1)S(1)} %constant_dynamic-slice_fusion), channel_id=1, source_target_pairs={{0,2},{2,4},{4,6},{6,7},{7,5},{5,3},{3,1},{1,0},{8,10},{10,12},{12... | collective-permute-start | bytes 1572872 | tf_op jit(solution)/shard_map/ppermute | solution.py:212
  4.8 1.9 %collective-permute-start.6 = (bf16[3,2048,128]{2,1,0:T(8,128)(2,1)}, bf16[3,2048,128]{2,1,0:T(8,128)(2,1)S(1)}, u32[]{:S(2)}, u32[]{:S(2)}) collective-permute-start(bf16[3,2048,128]{2,1,0:T(8,128)(2,1)} %refs_0_.1), channel_id=1, source_target_pairs={{0,16},{8,24},{16,0},{24,8},{1,17},{9,25},{17,1},{25,9},{2,18},{10... | collective-permute-start | bytes 4718600 | tf_op jit(solution)/shard_map/ppermute | solution.py:81
  6.8 1.5 %scatter.4.refs_4_ = f32[8,2048]{1,0:T(8,128)} pad(f32[6,2048]{1,0:T(8,128)} %param.9, f32[]{:T(128)} %constant.67.clone.1), padding=0_2x0_0 | pad | bytes 114692 | tf_op jit(solution)/shard_map/scatter | solution.py:154
  8.2 1.2 %fusion.source_ref = s32[6]{0:T(128)} fusion(s32[6]{0:T(128)} %param.8, s32[]{:T(128)S(6)} %axis_index.15), kind=kLoop, calls=%fused_computation.5 | loop fusion | flops 96 | bytes 52 | tf_op jit(solution)/shard_map/add | solution.py:152
  9.4 1.1 %compare_convert_fusion.living_ref = s32[6]{0:T(128)} fusion(s32[6]{0:T(128)} %param.8), kind=kLoop, calls=%fused_computation.4 | loop fusion | flops 12 | bytes 48 | tf_op jit(solution)/shard_map/convert_element_type | solution.py:149
  10.5 6.1 %collective-permute-done.refs_2_ = bf16[1,128,2048]{2,1,0:T(8,128)(2,1)S(1)} collective-permute-done((bf16[1,128,2048]{2,1,0:T(8,128)(2,1)S(1)}, bf16[1,128,2048]{2,1,0:T(8,128)(2,1)S(1)}, u32[]{:S(2)}, u32[]{:S(2)}) %collective-permute-start) | collective-permute-done | bytes 524320 | tf_op jit(solution)/shard_map/ppermute | solution.py:212
  16.7 1.5 %collective-permute-done.1.refs_3_ = bf16[1,128,2048]{2,1,0:T(8,128)(2,1)S(1)} collective-permute-done((bf16[1,128,2048]{2,1,0:T(8,128)(2,1)S(1)}, bf16[1,128,2048]{2,1,0:T(8,128)(2,1)S(1)}, u32[]{:S(2)}, u32[]{:S(2)}) %collective-permute-start.1) | collective-permute-done | bytes 524320 | tf_op jit(solution)/shard_map/ppermute | solution.py:215
  18.2 1.6 %collective-permute-start.2 = (bf16[1,128,2048]{2,1,0:T(8,128)(2,1)S(1)}, bf16[1,128,2048]{2,1,0:T(8,128)(2,1)S(1)}, u32[]{:S(2)}, u32[]{:S(2)}) collective-permute-start(bf16[1,128,2048]{2,1,0:T(8,128)(2,1)S(1)} %collective-permute-done.refs_2_), channel_id=1, source_target_pairs={{0,2},{2,4},{4,6},{6,7},{7,5},{5,3},{3,1},{1,0},{8,10},{10,12},{12... | collective-permute-start | bytes 1572872 | tf_op jit(solution)/shard_map/ppermute | solution.py:212
  20.2 10.4 %collective-permute-done.2.refs_4_ = bf16[1,128,2048]{2,1,0:T(8,128)(2,1)S(1)} collective-permute-done((bf16[1,128,2048]{2,1,0:T(8,128)(2,1)S(1)}, bf16[1,128,2048]{2,1,0:T(8,128)(2,1)S(1)}, u32[]{:S(2)}, u32[]{:S(2)}) %collective-permute-start.2) | collective-permute-done | bytes 524320 | tf_op jit(solution)/shard_map/ppermute | solution.py:212
  30.7 1.3 %collective-permute-done.3.refs_5_ = bf16[1,128,2048]{2,1,0:T(8,128)(2,1)S(1)} collective-permute-done((bf16[1,128,2048]{2,1,0:T(8,128)(2,1)S(1)}, bf16[1,128,2048]{2,1,0:T(8,128)(2,1)S(1)}, u32[]{:S(2)}, u32[]{:S(2)}) %collective-permute-start.3) | collective-permute-done | bytes 524320 | tf_op jit(solution)/shard_map/ppermute | solution.py:215
  32.0 1.6 %collective-permute-start.4 = (bf16[1,128,2048]{2,1,0:T(8,128)(2,1)S(1)}, bf16[1,128,2048]{2,1,0:T(8,128)(2,1)}, u32[]{:S(2)}, u32[]{:S(2)}) collective-permute-start(bf16[1,128,2048]{2,1,0:T(8,128)(2,1)S(1)} %collective-permute-done.2.refs_4_), channel_id=1, source_target_pairs={{0,2},{2,4},{4,6},{6,7},{7,5},{5,3},{3,1},{1,0},{8,10},{10,12},{12... | collective-permute-start | bytes 1572872 | tf_op jit(solution)/shard_map/ppermute | solution.py:212
  34.0 9.4 %collective-permute-done.4.refs_6_ = bf16[1,128,2048]{2,1,0:T(8,128)(2,1)} collective-permute-done((bf16[1,128,2048]{2,1,0:T(8,128)(2,1)S(1)}, bf16[1,128,2048]{2,1,0:T(8,128)(2,1)}, u32[]{:S(2)}, u32[]{:S(2)}) %collective-permute-start.4) | collective-permute-done | bytes 524320 | tf_op jit(solution)/shard_map/ppermute | solution.py:212
  43.3 1.2 %collective-permute-done.5.refs_7_ = bf16[1,128,2048]{2,1,0:T(8,128)(2,1)S(1)} collective-permute-done((bf16[1,128,2048]{2,1,0:T(8,128)(2,1)S(1)}, bf16[1,128,2048]{2,1,0:T(8,128)(2,1)S(1)}, u32[]{:S(2)}, u32[]{:S(2)}) %collective-permute-start.5) | collective-permute-done | bytes 524320 | tf_op jit(solution)/shard_map/ppermute | solution.py:215
  44.6 1.6 %collective-permute-start.8 = (bf16[1,128,2048]{2,1,0:T(8,128)(2,1)}, bf16[1,128,2048]{2,1,0:T(8,128)(2,1)}, u32[]{:S(2)}, u32[]{:S(2)}) collective-permute-start(bf16[1,128,2048]{2,1,0:T(8,128)(2,1)} %collective-permute-done.4.refs_6_), channel_id=1, source_target_pairs={{0,2},{2,4},{4,6},{6,7},{7,5},{5,3},{3,1},{1,0},{8,10},{10,12},{12... | collective-permute-start | bytes 1572872 | tf_op jit(solution)/shard_map/ppermute | solution.py:212
  46.9 1.1 %collective-permute-done.9.refs_3_ = bf16[3,2048,128]{2,1,0:T(8,128)(2,1)S(1)} collective-permute-done((bf16[3,2048,128]{2,1,0:T(8,128)(2,1)S(1)}, bf16[3,2048,128]{2,1,0:T(8,128)(2,1)S(1)}, u32[]{:S(2)}, u32[]{:S(2)}) %collective-permute-start.9) | collective-permute-done | bytes 1572896 | tf_op jit(solution)/shard_map/ppermute | solution.py:81
  48.0 1.1 %copy-done.6 = bf16[3,2048,128]{2,1,0:T(8,128)(2,1)} copy-done((bf16[3,2048,128]{2,1,0:T(8,128)(2,1)}, bf16[3,2048,128]{2,1,0:T(8,128)(2,1)S(1)}, u32[]{:S(2)}) %copy-start.6) | copy-done | bytes 1572888
  49.3 10.3 %shard_map.59 = (bf16[6,2048,128]{2,1,0:T(8,128)(2,1)}, bf16[2048,768]{1,0:T(8,128)(2,1)}) custom-call(s32[6]{0:T(128)} %fusion.source_ref, s32[6]{0:T(128)} %compare_convert_fusion.living_ref, bf16[3,2048,128]{2,1,0:T(8,128)(2,1)} %refs_0_.1, bf16[3,2048,128]{2,1,0:T(8,128)(2,1)} %copy-done.5, bf16[3,2048,128]{2,1,0:T(8,128)(2,1)} %copy-done.4, ...), custom_call_target="tpu_custom_call" | custom-call | tf_op jit(solution)/shard_map/pallas_call | solution.py:179
  60.6 1.2 %collective-permute-done.14.refs_13_ = bf16[1,128,2048]{2,1,0:T(8,128)(2,1)S(1)} collective-permute-done((bf16[1,128,2048]{2,1,0:T(8,128)(2,1)}, bf16[1,128,2048]{2,1,0:T(8,128)(2,1)S(1)}, u32[]{:S(2)}, u32[]{:S(2)}) %collective-permute-start.14) | collective-permute-done | bytes 524320 | tf_op jit(solution)/shard_map/ppermute | solution.py:81
  61.8 0.7 collective-permute-done.15.refs_14_
  62.6 0.7 collective-permute-done.16.refs_15_
  63.3 1.9 %copy-done = bf16[2048,768]{1,0:T(8,128)(2,1)S(1)} copy-done((bf16[2048,768]{1,0:T(8,128)(2,1)S(1)}, bf16[2048,768]{1,0:T(8,128)(2,1)}, u32[]{:S(2)}) %copy-start) | copy-done | bytes 3145752
  65.2 1.0 %copy-done.3 = bf16[1,128,2048]{2,1,0:T(8,128)(2,1)S(1)} copy-done((bf16[1,128,2048]{2,1,0:T(8,128)(2,1)S(1)}, bf16[1,128,2048]{2,1,0:T(8,128)(2,1)}, u32[]{:S(2)}) %copy-start.3) | copy-done | bytes 524312
  66.3 9.6 %shard_map.60 = f32[6,128]{1,0:T(8,128)S(1)} custom-call(bf16[2048,768]{1,0:T(8,128)(2,1)S(1)} %copy-done, bf16[2,128,2048]{2,1,0:T(8,128)(2,1)S(1)} %copy-done.1, bf16[1,128,2048]{2,1,0:T(8,128)(2,1)S(1)} %collective-permute-done.refs_2_, bf16[1,128,2048]{2,1,0:T(8,128)(2,1)S(1)} %collective-permute-done.1.refs_3_, ...), custom_call_target="tpu_custom_call" | custom-call | tf_op jit(solution)/shard_map/pallas_call | solution.py:65
  (34 shorter events, 3.4 us)
Async XLA Ops:
  1.7 14.9 %collective-permute-start = (bf16[1,128,2048]{2,1,0:T(8,128)(2,1)S(1)}, bf16[1,128,2048]{2,1,0:T(8,128)(2,1)S(1)}, u32[]{:S(2)}, u32[]{:S(2)}) collective-permute-start(bf16[1,128,2048]{2,1,0:T(8,128)(2,1)S(1)} %constant_dynamic-slice_fusion), channel_id=1, source_target_pairs={{0,2},{2,4},{4,6},{6,7},{7,5},{5,3},{3,1},{1,0},{8,10},{10,12},{12... | collective-permute-start | bytes 1572872 | tf_op jit(solution)/shard_map/ppermute | solution.py:212
  4.8 13.4 %collective-permute-start.1 = (bf16[1,128,2048]{2,1,0:T(8,128)(2,1)S(1)}, bf16[1,128,2048]{2,1,0:T(8,128)(2,1)S(1)}, u32[]{:S(2)}, u32[]{:S(2)}) collective-permute-start(bf16[1,128,2048]{2,1,0:T(8,128)(2,1)S(1)} %constant_dynamic-slice_fusion), channel_id=1, source_target_pairs={{2,0},{4,2},{6,4},{7,6},{5,7},{3,5},{1,3},{0,1},{10,8},{12,10},{14... | collective-permute-start | bytes 1572872 | tf_op jit(solution)/shard_map/ppermute | solution.py:215
  4.8 39.7 %collective-permute-start.6 = (bf16[3,2048,128]{2,1,0:T(8,128)(2,1)}, bf16[3,2048,128]{2,1,0:T(8,128)(2,1)S(1)}, u32[]{:S(2)}, u32[]{:S(2)}) collective-permute-start(bf16[3,2048,128]{2,1,0:T(8,128)(2,1)} %refs_0_.1), channel_id=1, source_target_pairs={{0,16},{8,24},{16,0},{24,8},{1,17},{9,25},{17,1},{25,9},{2,18},{10... | collective-permute-start | bytes 4718600 | tf_op jit(solution)/shard_map/ppermute | solution.py:81
  6.8 37.8 %collective-permute-start.7 = (bf16[3,2048,128]{2,1,0:T(8,128)(2,1)}, bf16[3,2048,128]{2,1,0:T(8,128)(2,1)S(1)}, u32[]{:S(2)}, u32[]{:S(2)}) collective-permute-start(bf16[3,2048,128]{2,1,0:T(8,128)(2,1)} %refs_0_.1), channel_id=1, source_target_pairs={{0,8},{8,0},{16,24},{24,16},{1,9},{9,1},{17,25},{25,17},{2,10},{10... | collective-permute-start | bytes 4718600 | tf_op jit(solution)/shard_map/ppermute | solution.py:81
  10.5 52.8 %copy-start.1 = (bf16[2,128,2048]{2,1,0:T(8,128)(2,1)S(1)}, bf16[2,128,2048]{2,1,0:T(8,128)(2,1)}, u32[]{:S(2)}) copy-start(bf16[2,128,2048]{2,1,0:T(8,128)(2,1)} %refs_1_.1) | copy-start | bytes 3145732
  18.2 12.5 %collective-permute-start.2 = (bf16[1,128,2048]{2,1,0:T(8,128)(2,1)S(1)}, bf16[1,128,2048]{2,1,0:T(8,128)(2,1)S(1)}, u32[]{:S(2)}, u32[]{:S(2)}) collective-permute-start(bf16[1,128,2048]{2,1,0:T(8,128)(2,1)S(1)} %collective-permute-done.refs_2_), channel_id=1, source_target_pairs={{0,2},{2,4},{4,6},{6,7},{7,5},{5,3},{3,1},{1,0},{8,10},{10,12},{12... | collective-permute-start | bytes 1572872 | tf_op jit(solution)/shard_map/ppermute | solution.py:212
  19.8 12.2 %collective-permute-start.3 = (bf16[1,128,2048]{2,1,0:T(8,128)(2,1)S(1)}, bf16[1,128,2048]{2,1,0:T(8,128)(2,1)S(1)}, u32[]{:S(2)}, u32[]{:S(2)}) collective-permute-start(bf16[1,128,2048]{2,1,0:T(8,128)(2,1)S(1)} %collective-permute-done.1.refs_3_), channel_id=1, source_target_pairs={{2,0},{4,2},{6,4},{7,6},{5,7},{3,5},{1,3},{0,1},{10,8},{12,10},{14... | collective-permute-start | bytes 1572872 | tf_op jit(solution)/shard_map/ppermute | solution.py:215
  32.0 11.4 %collective-permute-start.4 = (bf16[1,128,2048]{2,1,0:T(8,128)(2,1)S(1)}, bf16[1,128,2048]{2,1,0:T(8,128)(2,1)}, u32[]{:S(2)}, u32[]{:S(2)}) collective-permute-start(bf16[1,128,2048]{2,1,0:T(8,128)(2,1)S(1)} %collective-permute-done.2.refs_4_), channel_id=1, source_target_pairs={{0,2},{2,4},{4,6},{6,7},{7,5},{5,3},{3,1},{1,0},{8,10},{10,12},{12... | collective-permute-start | bytes 1572872 | tf_op jit(solution)/shard_map/ppermute | solution.py:212
  33.5 11.0 %collective-permute-start.5 = (bf16[1,128,2048]{2,1,0:T(8,128)(2,1)S(1)}, bf16[1,128,2048]{2,1,0:T(8,128)(2,1)S(1)}, u32[]{:S(2)}, u32[]{:S(2)}) collective-permute-start(bf16[1,128,2048]{2,1,0:T(8,128)(2,1)S(1)} %collective-permute-done.3.refs_5_), channel_id=1, source_target_pairs={{2,0},{4,2},{6,4},{7,6},{5,7},{3,5},{1,3},{0,1},{10,8},{12,10},{14... | collective-permute-start | bytes 1572872 | tf_op jit(solution)/shard_map/ppermute | solution.py:215
  44.5 2.4 %copy-start.2 = (bf16[1,128,2048]{2,1,0:T(8,128)(2,1)}, bf16[1,128,2048]{2,1,0:T(8,128)(2,1)S(1)}, u32[]{:S(2)}) copy-start(bf16[1,128,2048]{2,1,0:T(8,128)(2,1)S(1)} %collective-permute-done.5.refs_7_) | copy-start | bytes 1572868
  44.5 3.5 %copy-start.4 = (bf16[3,2048,128]{2,1,0:T(8,128)(2,1)}, bf16[3,2048,128]{2,1,0:T(8,128)(2,1)S(1)}, u32[]{:S(2)}) copy-start(bf16[3,2048,128]{2,1,0:T(8,128)(2,1)S(1)} %collective-permute-done.6.refs_2_) | copy-start | bytes 4718596
  44.6 3.5 %copy-start.5 = (bf16[3,2048,128]{2,1,0:T(8,128)(2,1)}, bf16[3,2048,128]{2,1,0:T(8,128)(2,1)S(1)}, u32[]{:S(2)}) copy-start(bf16[3,2048,128]{2,1,0:T(8,128)(2,1)S(1)} %collective-permute-done.7.refs_1_) | copy-start | bytes 4718596
  44.6 3.5 %collective-permute-start.9 = (bf16[3,2048,128]{2,1,0:T(8,128)(2,1)S(1)}, bf16[3,2048,128]{2,1,0:T(8,128)(2,1)S(1)}, u32[]{:S(2)}, u32[]{:S(2)}) collective-permute-start(bf16[3,2048,128]{2,1,0:T(8,128)(2,1)S(1)} %collective-permute-done.6.refs_2_), channel_id=1, source_target_pairs={{0,8},{8,0},{16,24},{24,16},{1,9},{9,1},{17,25},{25,17},{2,10},{10... | collective-permute-start | bytes 4718600 | tf_op jit(solution)/shard_map/ppermute | solution.py:81
  44.6 15.0 %collective-permute-start.8 = (bf16[1,128,2048]{2,1,0:T(8,128)(2,1)}, bf16[1,128,2048]{2,1,0:T(8,128)(2,1)}, u32[]{:S(2)}, u32[]{:S(2)}) collective-permute-start(bf16[1,128,2048]{2,1,0:T(8,128)(2,1)} %collective-permute-done.4.refs_6_), channel_id=1, source_target_pairs={{0,2},{2,4},{4,6},{6,7},{7,5},{5,3},{3,1},{1,0},{8,10},{10,12},{12... | collective-permute-start | bytes 1572872 | tf_op jit(solution)/shard_map/ppermute | solution.py:212
  46.2 13.9 %collective-permute-start.10 = (bf16[1,128,2048]{2,1,0:T(8,128)(2,1)S(1)}, bf16[1,128,2048]{2,1,0:T(8,128)(2,1)}, u32[]{:S(2)}, u32[]{:S(2)}) collective-permute-start(bf16[1,128,2048]{2,1,0:T(8,128)(2,1)S(1)} %collective-permute-done.refs_2_), channel_id=1, source_target_pairs={{0,8},{8,0},{16,24},{24,16},{1,9},{9,1},{17,25},{25,17},{2,10},{10... | collective-permute-start | bytes 1572872 | tf_op jit(solution)/shard_map/ppermute | solution.py:81
  46.4 13.9 %collective-permute-start.11 = (bf16[1,128,2048]{2,1,0:T(8,128)(2,1)S(1)}, bf16[1,128,2048]{2,1,0:T(8,128)(2,1)}, u32[]{:S(2)}, u32[]{:S(2)}) collective-permute-start(bf16[1,128,2048]{2,1,0:T(8,128)(2,1)S(1)} %collective-permute-done.1.refs_3_), channel_id=1, source_target_pairs={{0,8},{8,0},{16,24},{24,16},{1,9},{9,1},{17,25},{25,17},{2,10},{10... | collective-permute-start | bytes 1572872 | tf_op jit(solution)/shard_map/ppermute | solution.py:81
  46.7 13.9 %collective-permute-start.12 = (bf16[1,128,2048]{2,1,0:T(8,128)(2,1)S(1)}, bf16[1,128,2048]{2,1,0:T(8,128)(2,1)}, u32[]{:S(2)}, u32[]{:S(2)}) collective-permute-start(bf16[1,128,2048]{2,1,0:T(8,128)(2,1)S(1)} %collective-permute-done.2.refs_4_), channel_id=1, source_target_pairs={{0,8},{8,0},{16,24},{24,16},{1,9},{9,1},{17,25},{25,17},{2,10},{10... | collective-permute-start | bytes 1572872 | tf_op jit(solution)/shard_map/ppermute | solution.py:81
  48.0 1.1 %copy-start.6 = (bf16[3,2048,128]{2,1,0:T(8,128)(2,1)}, bf16[3,2048,128]{2,1,0:T(8,128)(2,1)S(1)}, u32[]{:S(2)}) copy-start(bf16[3,2048,128]{2,1,0:T(8,128)(2,1)S(1)} %collective-permute-done.9.refs_3_) | copy-start | bytes 4718596
  49.2 11.4 %collective-permute-start.13 = (bf16[1,128,2048]{2,1,0:T(8,128)(2,1)S(1)}, bf16[1,128,2048]{2,1,0:T(8,128)(2,1)}, u32[]{:S(2)}, u32[]{:S(2)}) collective-permute-start(bf16[1,128,2048]{2,1,0:T(8,128)(2,1)S(1)} %collective-permute-done.3.refs_5_), channel_id=1, source_target_pairs={{0,8},{8,0},{16,24},{24,16},{1,9},{9,1},{17,25},{25,17},{2,10},{10... | collective-permute-start | bytes 1572872 | tf_op jit(solution)/shard_map/ppermute | solution.py:81
  59.6 2.2 %collective-permute-start.14 = (bf16[1,128,2048]{2,1,0:T(8,128)(2,1)}, bf16[1,128,2048]{2,1,0:T(8,128)(2,1)S(1)}, u32[]{:S(2)}, u32[]{:S(2)}) collective-permute-start(bf16[1,128,2048]{2,1,0:T(8,128)(2,1)} %collective-permute-done.4.refs_6_), channel_id=1, source_target_pairs={{0,8},{8,0},{16,24},{24,16},{1,9},{9,1},{17,25},{25,17},{2,10},{10... | collective-permute-start | bytes 1572872 | tf_op jit(solution)/shard_map/ppermute | solution.py:81
  60.1 15.9 %copy-start.7 = (s32[6]{0:T(128)S(1)}, s32[6]{0:T(128)}, u32[]{:S(2)}) copy-start(s32[6]{0:T(128)} %param.8) | copy-start | bytes 76
  60.1 2.5 %collective-permute-start.15 = (bf16[1,128,2048]{2,1,0:T(8,128)(2,1)}, bf16[1,128,2048]{2,1,0:T(8,128)(2,1)S(1)}, u32[]{:S(2)}, u32[]{:S(2)}) collective-permute-start(bf16[1,128,2048]{2,1,0:T(8,128)(2,1)} %copy-done.2), channel_id=1, source_target_pairs={{0,8},{8,0},{16,24},{24,16},{1,9},{9,1},{17,25},{25,17},{2,10},{10... | collective-permute-start | bytes 1572872 | tf_op jit(solution)/shard_map/ppermute | solution.py:81
  60.2 3.1 %collective-permute-start.16 = (bf16[1,128,2048]{2,1,0:T(8,128)(2,1)}, bf16[1,128,2048]{2,1,0:T(8,128)(2,1)S(1)}, u32[]{:S(2)}, u32[]{:S(2)}) collective-permute-start(bf16[1,128,2048]{2,1,0:T(8,128)(2,1)} %collective-permute-done.8.refs_8_), channel_id=1, source_target_pairs={{0,8},{8,0},{16,24},{24,16},{1,9},{9,1},{17,25},{25,17},{2,10},{10... | collective-permute-start | bytes 1572872 | tf_op jit(solution)/shard_map/ppermute | solution.py:81
  63.3 1.9 %copy-start = (bf16[2048,768]{1,0:T(8,128)(2,1)S(1)}, bf16[2048,768]{1,0:T(8,128)(2,1)}, u32[]{:S(2)}) copy-start(bf16[2048,768]{1,0:T(8,128)(2,1)} %get-tuple-element.43.refs_0_) | copy-start | bytes 9437188
  (1 other events, 1.0 us)

commit v19 on v18

--- a/solution.py
+++ b/solution.py
@@ -93,6 +93,18 @@
     )
 
 
+def split_product(left, right):
+    left_high = left.astype(jnp.bfloat16)
+    left_low = (left - left_high.astype(jnp.float32)).astype(jnp.bfloat16)
+    right_high = right.astype(jnp.bfloat16)
+    right_low = (right - right_high.astype(jnp.float32)).astype(jnp.bfloat16)
+    return (
+        jnp.dot(left_high, right_high, preferred_element_type=jnp.float32)
+        + jnp.dot(left_high, right_low, preferred_element_type=jnp.float32)
+        + jnp.dot(left_low, right_high, preferred_element_type=jnp.float32)
+    )
+
+
 def kick_kernel(source_ref, living_ref, *refs):
     walker_refs = refs[:4]
     field_ref, new_hbm, theta_out, walkers, kicked_buf, new_buf, in_sem, out_sem = refs[4:]
@@ -132,10 +144,7 @@
 
     for sweep in range(ITERS):
         products = [exact_bf16_product(x, inv) for x, inv in zip(intersections, inverses)]
-        inverses = [
-            jnp.dot(inv, 2.0 * identity - p, precision=lax.Precision.HIGHEST, preferred_element_type=jnp.float32)
-            for inv, p in zip(inverses, products)
-        ]
+        inverses = [split_product(inv, 2.0 * identity - p) for inv, p in zip(inverses, products)]
 
     for s in range(n_slot):
         theta = exact_bf16_product(kicked_buf[s], inverses[s])

time: 77 us -> 76.3 us (level)
  no operation moved by 1% of the time
where the time goes in v19:
time: 76.3 us; the launch traced here: 75.9 us
  waiting for transfers between devices  34 us (45%)
  Pallas kernels  19.3 us (25%)
  starting transfers between devices  12.3 us (16%)
  local copies, waits for them, and re-layouts  6.76 us (9%)
  other arithmetic  2.84 us (4%)
    ppermute x4, waiting for transfers between devices, body(): ahead = lax.ppermute(ahead, 'chol', forward)  25.9 us
    pallas_call x1, Pallas kernels, kick(): pl.pallas_call(kick_kernel, out_shape=[shape, wide], grid_spec=grid_spec)  9.94 us
    pallas_call x1, Pallas kernels, block_energy(): pl.pallas_call(energy_kernel, out_shape=jax.ShapeDtypeStruct((n_slot, 128...  9.39 us
    ppermute x4, starting transfers between devices, body(): ahead = lax.ppermute(ahead, 'chol', forward)  7.8 us
    unnamed x16, local copies, waits for them, and re-layouts  4.09 us
    ppermute x10, waiting for transfers between devices, swap_pairs(): return lax.ppermute(x, axis, perm)  4.03 us
    ppermute x3, waiting for transfers between devices, body(): behind = lax.ppermute(behind, 'chol', backward)  4 us
    ppermute x10, starting transfers between devices, swap_pairs(): return lax.ppermute(x, axis, perm)  3.62 us
  transfers between devices with their start and end apart: 17, of which 10 were waited for; matrix products, arithmetic and copies ran while one was open for 5% of the time, Pallas kernels for 13%

profile of v19, /device:TPU:0, one launch (start us, length us, event | category | flops | bytes accessed | tf_op | source)
XLA Modules:
  0.0 75.9 jit_solution(360245966225982497)
XLA Ops:
  0.6 1.1 %constant_dynamic-slice_fusion = bf16[1,128,2048]{2,1,0:T(8,128)(2,1)S(1)} fusion(bf16[2,128,2048]{2,1,0:T(8,128)(2,1)} %refs_1_.1, s32[]{:T(128)S(6)} %select_n.26), kind=kLoop, calls=%fused_computation.6 | loop fusion | bytes 1048580 | tf_op jit(solution)/shard_map/dynamic_slice | solution.py:206
  1.7 3.1 %collective-permute-start = (bf16[1,128,2048]{2,1,0:T(8,128)(2,1)S(1)}, bf16[1,128,2048]{2,1,0:T(8,128)(2,1)S(1)}, u32[]{:S(2)}, u32[]{:S(2)}) collective-permute-start(bf16[1,128,2048]{2,1,0:T(8,128)(2,1)S(1)} %constant_dynamic-slice_fusion), channel_id=1, source_target_pairs={{0,2},{2,4},{4,6},{6,7},{7,5},{5,3},{3,1},{1,0},{8,10},{10,12},{12... | collective-permute-start | bytes 1572872 | tf_op jit(solution)/shard_map/ppermute | solution.py:221
  4.8 1.9 %collective-permute-start.6 = (bf16[3,2048,128]{2,1,0:T(8,128)(2,1)}, bf16[3,2048,128]{2,1,0:T(8,128)(2,1)S(1)}, u32[]{:S(2)}, u32[]{:S(2)}) collective-permute-start(bf16[3,2048,128]{2,1,0:T(8,128)(2,1)} %refs_0_.1), channel_id=1, source_target_pairs={{0,16},{8,24},{16,0},{24,8},{1,17},{9,25},{17,1},{25,9},{2,18},{10... | collective-permute-start | bytes 4718600 | tf_op jit(solution)/shard_map/ppermute | solution.py:81
  6.8 1.5 %scatter.4.refs_4_ = f32[8,2048]{1,0:T(8,128)} pad(f32[6,2048]{1,0:T(8,128)} %param.9, f32[]{:T(128)} %constant.67.clone.1), padding=0_2x0_0 | pad | bytes 114692 | tf_op jit(solution)/shard_map/scatter | solution.py:163
  8.2 1.2 %fusion.source_ref = s32[6]{0:T(128)} fusion(s32[6]{0:T(128)} %param.8, s32[]{:T(128)S(6)} %axis_index.15), kind=kLoop, calls=%fused_computation.5 | loop fusion | flops 96 | bytes 52 | tf_op jit(solution)/shard_map/add | solution.py:161
  9.4 1.1 %compare_convert_fusion.living_ref = s32[6]{0:T(128)} fusion(s32[6]{0:T(128)} %param.8), kind=kLoop, calls=%fused_computation.4 | loop fusion | flops 12 | bytes 48 | tf_op jit(solution)/shard_map/convert_element_type | solution.py:158
  10.5 6.1 %collective-permute-done.refs_2_ = bf16[1,128,2048]{2,1,0:T(8,128)(2,1)S(1)} collective-permute-done((bf16[1,128,2048]{2,1,0:T(8,128)(2,1)S(1)}, bf16[1,128,2048]{2,1,0:T(8,128)(2,1)S(1)}, u32[]{:S(2)}, u32[]{:S(2)}) %collective-permute-start) | collective-permute-done | bytes 524320 | tf_op jit(solution)/shard_map/ppermute | solution.py:221
  16.7 1.5 %collective-permute-done.1.refs_3_ = bf16[1,128,2048]{2,1,0:T(8,128)(2,1)S(1)} collective-permute-done((bf16[1,128,2048]{2,1,0:T(8,128)(2,1)S(1)}, bf16[1,128,2048]{2,1,0:T(8,128)(2,1)S(1)}, u32[]{:S(2)}, u32[]{:S(2)}) %collective-permute-start.1) | collective-permute-done | bytes 524320 | tf_op jit(solution)/shard_map/ppermute | solution.py:224
  18.2 1.6 %collective-permute-start.2 = (bf16[1,128,2048]{2,1,0:T(8,128)(2,1)S(1)}, bf16[1,128,2048]{2,1,0:T(8,128)(2,1)S(1)}, u32[]{:S(2)}, u32[]{:S(2)}) collective-permute-start(bf16[1,128,2048]{2,1,0:T(8,128)(2,1)S(1)} %collective-permute-done.refs_2_), channel_id=1, source_target_pairs={{0,2},{2,4},{4,6},{6,7},{7,5},{5,3},{3,1},{1,0},{8,10},{10,12},{12... | collective-permute-start | bytes 1572872 | tf_op jit(solution)/shard_map/ppermute | solution.py:221
  20.2 10.4 %collective-permute-done.2.refs_4_ = bf16[1,128,2048]{2,1,0:T(8,128)(2,1)S(1)} collective-permute-done((bf16[1,128,2048]{2,1,0:T(8,128)(2,1)S(1)}, bf16[1,128,2048]{2,1,0:T(8,128)(2,1)S(1)}, u32[]{:S(2)}, u32[]{:S(2)}) %collective-permute-start.2) | collective-permute-done | bytes 524320 | tf_op jit(solution)/shard_map/ppermute | solution.py:221
  30.7 1.3 %collective-permute-done.3.refs_5_ = bf16[1,128,2048]{2,1,0:T(8,128)(2,1)S(1)} collective-permute-done((bf16[1,128,2048]{2,1,0:T(8,128)(2,1)S(1)}, bf16[1,128,2048]{2,1,0:T(8,128)(2,1)S(1)}, u32[]{:S(2)}, u32[]{:S(2)}) %collective-permute-start.3) | collective-permute-done | bytes 524320 | tf_op jit(solution)/shard_map/ppermute | solution.py:224
  32.0 1.6 %collective-permute-start.4 = (bf16[1,128,2048]{2,1,0:T(8,128)(2,1)S(1)}, bf16[1,128,2048]{2,1,0:T(8,128)(2,1)}, u32[]{:S(2)}, u32[]{:S(2)}) collective-permute-start(bf16[1,128,2048]{2,1,0:T(8,128)(2,1)S(1)} %collective-permute-done.2.refs_4_), channel_id=1, source_target_pairs={{0,2},{2,4},{4,6},{6,7},{7,5},{5,3},{3,1},{1,0},{8,10},{10,12},{12... | collective-permute-start | bytes 1572872 | tf_op jit(solution)/shard_map/ppermute | solution.py:221
  34.0 9.4 %collective-permute-done.4.refs_6_ = bf16[1,128,2048]{2,1,0:T(8,128)(2,1)} collective-permute-done((bf16[1,128,2048]{2,1,0:T(8,128)(2,1)S(1)}, bf16[1,128,2048]{2,1,0:T(8,128)(2,1)}, u32[]{:S(2)}, u32[]{:S(2)}) %collective-permute-start.4) | collective-permute-done | bytes 524320 | tf_op jit(solution)/shard_map/ppermute | solution.py:221
  43.3 1.2 %collective-permute-done.5.refs_7_ = bf16[1,128,2048]{2,1,0:T(8,128)(2,1)S(1)} collective-permute-done((bf16[1,128,2048]{2,1,0:T(8,128)(2,1)S(1)}, bf16[1,128,2048]{2,1,0:T(8,128)(2,1)S(1)}, u32[]{:S(2)}, u32[]{:S(2)}) %collective-permute-start.5) | collective-permute-done | bytes 524320 | tf_op jit(solution)/shard_map/ppermute | solution.py:224
  44.6 1.6 %collective-permute-start.8 = (bf16[1,128,2048]{2,1,0:T(8,128)(2,1)}, bf16[1,128,2048]{2,1,0:T(8,128)(2,1)}, u32[]{:S(2)}, u32[]{:S(2)}) collective-permute-start(bf16[1,128,2048]{2,1,0:T(8,128)(2,1)} %collective-permute-done.4.refs_6_), channel_id=1, source_target_pairs={{0,2},{2,4},{4,6},{6,7},{7,5},{5,3},{3,1},{1,0},{8,10},{10,12},{12... | collective-permute-start | bytes 1572872 | tf_op jit(solution)/shard_map/ppermute | solution.py:221
  46.9 1.1 %collective-permute-done.9.refs_3_ = bf16[3,2048,128]{2,1,0:T(8,128)(2,1)S(1)} collective-permute-done((bf16[3,2048,128]{2,1,0:T(8,128)(2,1)S(1)}, bf16[3,2048,128]{2,1,0:T(8,128)(2,1)S(1)}, u32[]{:S(2)}, u32[]{:S(2)}) %collective-permute-start.9) | collective-permute-done | bytes 1572896 | tf_op jit(solution)/shard_map/ppermute | solution.py:81
  48.0 1.1 %copy-done.6 = bf16[3,2048,128]{2,1,0:T(8,128)(2,1)} copy-done((bf16[3,2048,128]{2,1,0:T(8,128)(2,1)}, bf16[3,2048,128]{2,1,0:T(8,128)(2,1)S(1)}, u32[]{:S(2)}) %copy-start.6) | copy-done | bytes 1572888
  49.3 9.9 %shard_map.59 = (bf16[6,2048,128]{2,1,0:T(8,128)(2,1)}, bf16[2048,768]{1,0:T(8,128)(2,1)}) custom-call(s32[6]{0:T(128)} %fusion.source_ref, s32[6]{0:T(128)} %compare_convert_fusion.living_ref, bf16[3,2048,128]{2,1,0:T(8,128)(2,1)} %refs_0_.1, bf16[3,2048,128]{2,1,0:T(8,128)(2,1)} %copy-done.5, bf16[3,2048,128]{2,1,0:T(8,128)(2,1)} %copy-done.4, ...), custom_call_target="tpu_custom_call" | custom-call | tf_op jit(solution)/shard_map/pallas_call | solution.py:188
  60.1 1.4 %collective-permute-done.14.refs_13_ = bf16[1,128,2048]{2,1,0:T(8,128)(2,1)S(1)} collective-permute-done((bf16[1,128,2048]{2,1,0:T(8,128)(2,1)}, bf16[1,128,2048]{2,1,0:T(8,128)(2,1)S(1)}, u32[]{:S(2)}, u32[]{:S(2)}) %collective-permute-start.14) | collective-permute-done | bytes 524320 | tf_op jit(solution)/shard_map/ppermute | solution.py:81
  61.5 0.7 collective-permute-done.15.refs_14_
  62.2 0.7 collective-permute-done.16.refs_15_
  63.0 1.9 %copy-done = bf16[2048,768]{1,0:T(8,128)(2,1)S(1)} copy-done((bf16[2048,768]{1,0:T(8,128)(2,1)S(1)}, bf16[2048,768]{1,0:T(8,128)(2,1)}, u32[]{:S(2)}) %copy-start) | copy-done | bytes 3145752
  64.9 1.0 %copy-done.3 = bf16[1,128,2048]{2,1,0:T(8,128)(2,1)S(1)} copy-done((bf16[1,128,2048]{2,1,0:T(8,128)(2,1)S(1)}, bf16[1,128,2048]{2,1,0:T(8,128)(2,1)}, u32[]{:S(2)}) %copy-start.3) | copy-done | bytes 524312
  65.9 9.4 %shard_map.60 = f32[6,128]{1,0:T(8,128)S(1)} custom-call(bf16[2048,768]{1,0:T(8,128)(2,1)S(1)} %copy-done, bf16[2,128,2048]{2,1,0:T(8,128)(2,1)S(1)} %copy-done.1, bf16[1,128,2048]{2,1,0:T(8,128)(2,1)S(1)} %collective-permute-done.refs_2_, bf16[1,128,2048]{2,1,0:T(8,128)(2,1)S(1)} %collective-permute-done.1.refs_3_, ...), custom_call_target="tpu_custom_call" | custom-call | tf_op jit(solution)/shard_map/pallas_call | solution.py:65
  (34 shorter events, 3.3 us)
Async XLA Ops:
  1.7 14.9 %collective-permute-start = (bf16[1,128,2048]{2,1,0:T(8,128)(2,1)S(1)}, bf16[1,128,2048]{2,1,0:T(8,128)(2,1)S(1)}, u32[]{:S(2)}, u32[]{:S(2)}) collective-permute-start(bf16[1,128,2048]{2,1,0:T(8,128)(2,1)S(1)} %constant_dynamic-slice_fusion), channel_id=1, source_target_pairs={{0,2},{2,4},{4,6},{6,7},{7,5},{5,3},{3,1},{1,0},{8,10},{10,12},{12... | collective-permute-start | bytes 1572872 | tf_op jit(solution)/shard_map/ppermute | solution.py:221
  4.8 13.4 %collective-permute-start.1 = (bf16[1,128,2048]{2,1,0:T(8,128)(2,1)S(1)}, bf16[1,128,2048]{2,1,0:T(8,128)(2,1)S(1)}, u32[]{:S(2)}, u32[]{:S(2)}) collective-permute-start(bf16[1,128,2048]{2,1,0:T(8,128)(2,1)S(1)} %constant_dynamic-slice_fusion), channel_id=1, source_target_pairs={{2,0},{4,2},{6,4},{7,6},{5,7},{3,5},{1,3},{0,1},{10,8},{12,10},{14... | collective-permute-start | bytes 1572872 | tf_op jit(solution)/shard_map/ppermute | solution.py:224
  4.8 39.7 %collective-permute-start.6 = (bf16[3,2048,128]{2,1,0:T(8,128)(2,1)}, bf16[3,2048,128]{2,1,0:T(8,128)(2,1)S(1)}, u32[]{:S(2)}, u32[]{:S(2)}) collective-permute-start(bf16[3,2048,128]{2,1,0:T(8,128)(2,1)} %refs_0_.1), channel_id=1, source_target_pairs={{0,16},{8,24},{16,0},{24,8},{1,17},{9,25},{17,1},{25,9},{2,18},{10... | collective-permute-start | bytes 4718600 | tf_op jit(solution)/shard_map/ppermute | solution.py:81
  6.8 37.8 %collective-permute-start.7 = (bf16[3,2048,128]{2,1,0:T(8,128)(2,1)}, bf16[3,2048,128]{2,1,0:T(8,128)(2,1)S(1)}, u32[]{:S(2)}, u32[]{:S(2)}) collective-permute-start(bf16[3,2048,128]{2,1,0:T(8,128)(2,1)} %refs_0_.1), channel_id=1, source_target_pairs={{0,8},{8,0},{16,24},{24,16},{1,9},{9,1},{17,25},{25,17},{2,10},{10... | collective-permute-start | bytes 4718600 | tf_op jit(solution)/shard_map/ppermute | solution.py:81
  10.5 52.4 %copy-start.1 = (bf16[2,128,2048]{2,1,0:T(8,128)(2,1)S(1)}, bf16[2,128,2048]{2,1,0:T(8,128)(2,1)}, u32[]{:S(2)}) copy-start(bf16[2,128,2048]{2,1,0:T(8,128)(2,1)} %refs_1_.1) | copy-start | bytes 3145732
  18.2 12.5 %collective-permute-start.2 = (bf16[1,128,2048]{2,1,0:T(8,128)(2,1)S(1)}, bf16[1,128,2048]{2,1,0:T(8,128)(2,1)S(1)}, u32[]{:S(2)}, u32[]{:S(2)}) collective-permute-start(bf16[1,128,2048]{2,1,0:T(8,128)(2,1)S(1)} %collective-permute-done.refs_2_), channel_id=1, source_target_pairs={{0,2},{2,4},{4,6},{6,7},{7,5},{5,3},{3,1},{1,0},{8,10},{10,12},{12... | collective-permute-start | bytes 1572872 | tf_op jit(solution)/shard_map/ppermute | solution.py:221
  19.8 12.2 %collective-permute-start.3 = (bf16[1,128,2048]{2,1,0:T(8,128)(2,1)S(1)}, bf16[1,128,2048]{2,1,0:T(8,128)(2,1)S(1)}, u32[]{:S(2)}, u32[]{:S(2)}) collective-permute-start(bf16[1,128,2048]{2,1,0:T(8,128)(2,1)S(1)} %collective-permute-done.1.refs_3_), channel_id=1, source_target_pairs={{2,0},{4,2},{6,4},{7,6},{5,7},{3,5},{1,3},{0,1},{10,8},{12,10},{14... | collective-permute-start | bytes 1572872 | tf_op jit(solution)/shard_map/ppermute | solution.py:224
  32.0 11.4 %collective-permute-start.4 = (bf16[1,128,2048]{2,1,0:T(8,128)(2,1)S(1)}, bf16[1,128,2048]{2,1,0:T(8,128)(2,1)}, u32[]{:S(2)}, u32[]{:S(2)}) collective-permute-start(bf16[1,128,2048]{2,1,0:T(8,128)(2,1)S(1)} %collective-permute-done.2.refs_4_), channel_id=1, source_target_pairs={{0,2},{2,4},{4,6},{6,7},{7,5},{5,3},{3,1},{1,0},{8,10},{10,12},{12... | collective-permute-start | bytes 1572872 | tf_op jit(solution)/shard_map/ppermute | solution.py:221
  33.5 11.0 %collective-permute-start.5 = (bf16[1,128,2048]{2,1,0:T(8,128)(2,1)S(1)}, bf16[1,128,2048]{2,1,0:T(8,128)(2,1)S(1)}, u32[]{:S(2)}, u32[]{:S(2)}) collective-permute-start(bf16[1,128,2048]{2,1,0:T(8,128)(2,1)S(1)} %collective-permute-done.3.refs_5_), channel_id=1, source_target_pairs={{2,0},{4,2},{6,4},{7,6},{5,7},{3,5},{1,3},{0,1},{10,8},{12,10},{14... | collective-permute-start | bytes 1572872 | tf_op jit(solution)/shard_map/ppermute | solution.py:224
  44.5 2.4 %copy-start.2 = (bf16[1,128,2048]{2,1,0:T(8,128)(2,1)}, bf16[1,128,2048]{2,1,0:T(8,128)(2,1)S(1)}, u32[]{:S(2)}) copy-start(bf16[1,128,2048]{2,1,0:T(8,128)(2,1)S(1)} %collective-permute-done.5.refs_7_) | copy-start | bytes 1572868
  44.5 3.5 %copy-start.4 = (bf16[3,2048,128]{2,1,0:T(8,128)(2,1)}, bf16[3,2048,128]{2,1,0:T(8,128)(2,1)S(1)}, u32[]{:S(2)}) copy-start(bf16[3,2048,128]{2,1,0:T(8,128)(2,1)S(1)} %collective-permute-done.6.refs_2_) | copy-start | bytes 4718596
  44.6 3.5 %copy-start.5 = (bf16[3,2048,128]{2,1,0:T(8,128)(2,1)}, bf16[3,2048,128]{2,1,0:T(8,128)(2,1)S(1)}, u32[]{:S(2)}) copy-start(bf16[3,2048,128]{2,1,0:T(8,128)(2,1)S(1)} %collective-permute-done.7.refs_1_) | copy-start | bytes 4718596
  44.6 3.5 %collective-permute-start.9 = (bf16[3,2048,128]{2,1,0:T(8,128)(2,1)S(1)}, bf16[3,2048,128]{2,1,0:T(8,128)(2,1)S(1)}, u32[]{:S(2)}, u32[]{:S(2)}) collective-permute-start(bf16[3,2048,128]{2,1,0:T(8,128)(2,1)S(1)} %collective-permute-done.6.refs_2_), channel_id=1, source_target_pairs={{0,8},{8,0},{16,24},{24,16},{1,9},{9,1},{17,25},{25,17},{2,10},{10... | collective-permute-start | bytes 4718600 | tf_op jit(solution)/shard_map/ppermute | solution.py:81
  44.6 14.6 %collective-permute-start.8 = (bf16[1,128,2048]{2,1,0:T(8,128)(2,1)}, bf16[1,128,2048]{2,1,0:T(8,128)(2,1)}, u32[]{:S(2)}, u32[]{:S(2)}) collective-permute-start(bf16[1,128,2048]{2,1,0:T(8,128)(2,1)} %collective-permute-done.4.refs_6_), channel_id=1, source_target_pairs={{0,2},{2,4},{4,6},{6,7},{7,5},{5,3},{3,1},{1,0},{8,10},{10,12},{12... | collective-permute-start | bytes 1572872 | tf_op jit(solution)/shard_map/ppermute | solution.py:221
  46.2 13.4 %collective-permute-start.10 = (bf16[1,128,2048]{2,1,0:T(8,128)(2,1)S(1)}, bf16[1,128,2048]{2,1,0:T(8,128)(2,1)}, u32[]{:S(2)}, u32[]{:S(2)}) collective-permute-start(bf16[1,128,2048]{2,1,0:T(8,128)(2,1)S(1)} %collective-permute-done.refs_2_), channel_id=1, source_target_pairs={{0,8},{8,0},{16,24},{24,16},{1,9},{9,1},{17,25},{25,17},{2,10},{10... | collective-permute-start | bytes 1572872 | tf_op jit(solution)/shard_map/ppermute | solution.py:81
  46.4 13.5 %collective-permute-start.11 = (bf16[1,128,2048]{2,1,0:T(8,128)(2,1)S(1)}, bf16[1,128,2048]{2,1,0:T(8,128)(2,1)}, u32[]{:S(2)}, u32[]{:S(2)}) collective-permute-start(bf16[1,128,2048]{2,1,0:T(8,128)(2,1)S(1)} %collective-permute-done.1.refs_3_), channel_id=1, source_target_pairs={{0,8},{8,0},{16,24},{24,16},{1,9},{9,1},{17,25},{25,17},{2,10},{10... | collective-permute-start | bytes 1572872 | tf_op jit(solution)/shard_map/ppermute | solution.py:81
  46.7 13.4 %collective-permute-start.12 = (bf16[1,128,2048]{2,1,0:T(8,128)(2,1)S(1)}, bf16[1,128,2048]{2,1,0:T(8,128)(2,1)}, u32[]{:S(2)}, u32[]{:S(2)}) collective-permute-start(bf16[1,128,2048]{2,1,0:T(8,128)(2,1)S(1)} %collective-permute-done.2.refs_4_), channel_id=1, source_target_pairs={{0,8},{8,0},{16,24},{24,16},{1,9},{9,1},{17,25},{25,17},{2,10},{10... | collective-permute-start | bytes 1572872 | tf_op jit(solution)/shard_map/ppermute | solution.py:81
  48.0 1.1 %copy-start.6 = (bf16[3,2048,128]{2,1,0:T(8,128)(2,1)}, bf16[3,2048,128]{2,1,0:T(8,128)(2,1)S(1)}, u32[]{:S(2)}) copy-start(bf16[3,2048,128]{2,1,0:T(8,128)(2,1)S(1)} %collective-permute-done.9.refs_3_) | copy-start | bytes 4718596
  49.2 10.9 %collective-permute-start.13 = (bf16[1,128,2048]{2,1,0:T(8,128)(2,1)S(1)}, bf16[1,128,2048]{2,1,0:T(8,128)(2,1)}, u32[]{:S(2)}, u32[]{:S(2)}) collective-permute-start(bf16[1,128,2048]{2,1,0:T(8,128)(2,1)S(1)} %collective-permute-done.3.refs_5_), channel_id=1, source_target_pairs={{0,8},{8,0},{16,24},{24,16},{1,9},{9,1},{17,25},{25,17},{2,10},{10... | collective-permute-start | bytes 1572872 | tf_op jit(solution)/shard_map/ppermute | solution.py:81
  59.3 2.2 %collective-permute-start.14 = (bf16[1,128,2048]{2,1,0:T(8,128)(2,1)}, bf16[1,128,2048]{2,1,0:T(8,128)(2,1)S(1)}, u32[]{:S(2)}, u32[]{:S(2)}) collective-permute-start(bf16[1,128,2048]{2,1,0:T(8,128)(2,1)} %collective-permute-done.4.refs_6_), channel_id=1, source_target_pairs={{0,8},{8,0},{16,24},{24,16},{1,9},{9,1},{17,25},{25,17},{2,10},{10... | collective-permute-start | bytes 1572872 | tf_op jit(solution)/shard_map/ppermute | solution.py:81
  59.6 15.8 %copy-start.7 = (s32[6]{0:T(128)S(1)}, s32[6]{0:T(128)}, u32[]{:S(2)}) copy-start(s32[6]{0:T(128)} %param.8) | copy-start | bytes 76
  59.6 2.6 %collective-permute-start.15 = (bf16[1,128,2048]{2,1,0:T(8,128)(2,1)}, bf16[1,128,2048]{2,1,0:T(8,128)(2,1)S(1)}, u32[]{:S(2)}, u32[]{:S(2)}) collective-permute-start(bf16[1,128,2048]{2,1,0:T(8,128)(2,1)} %copy-done.2), channel_id=1, source_target_pairs={{0,8},{8,0},{16,24},{24,16},{1,9},{9,1},{17,25},{25,17},{2,10},{10... | collective-permute-start | bytes 1572872 | tf_op jit(solution)/shard_map/ppermute | solution.py:81
  59.9 3.1 %collective-permute-start.16 = (bf16[1,128,2048]{2,1,0:T(8,128)(2,1)}, bf16[1,128,2048]{2,1,0:T(8,128)(2,1)S(1)}, u32[]{:S(2)}, u32[]{:S(2)}) collective-permute-start(bf16[1,128,2048]{2,1,0:T(8,128)(2,1)} %collective-permute-done.8.refs_8_), channel_id=1, source_target_pairs={{0,8},{8,0},{16,24},{24,16},{1,9},{9,1},{17,25},{25,17},{2,10},{10... | collective-permute-start | bytes 1572872 | tf_op jit(solution)/shard_map/ppermute | solution.py:81
  63.0 1.9 %copy-start = (bf16[2048,768]{1,0:T(8,128)(2,1)S(1)}, bf16[2048,768]{1,0:T(8,128)(2,1)}, u32[]{:S(2)}) copy-start(bf16[2048,768]{1,0:T(8,128)(2,1)} %get-tuple-element.43.refs_0_) | copy-start | bytes 9437188
  (1 other events, 1.0 us)
